TPU v7x, 32 devices: a whole 2x2x4 slice. The times are simulated.
32 devices in a mesh: seq: 8 (over y, x, core), head: 4 (over z).
Axes of the slice: x: 2, y: 2, z: 4, core: 2. Of those that a mesh axis runs over, the one named last changes fastest.
Arguments:
- inner_rows: bfloat16 [2048, 4096], P('seq', 'head'), may hold values from -6 to 6
- gate_rows: bfloat16 [2048, 4096], P('seq', 'head'), may hold values from -6 to 6
- input_proj: bfloat16 [2048, 512], P('seq'), may hold values from -6 to 6
- step_raw: float32 [2048, 64], P('seq', 'head'), may hold values from -8 to 8
- decay_rate: float32 [64], P('head'), may hold values from 1e-05 to 0.08
- skip_gain: float32 [64], P('head'), may hold values from 0.5 to 1.5
- conv_inner: float32 [4, 4096], P(None, 'head'), may hold values from -3 to 3
- conv_proj: float32 [4, 512], replicated, may hold values from -0.25 to 0.25
- norm_gain: float32 [4096], P('head'), may hold values from 0.1 to 1.9
Outputs:
- mixed_out: bfloat16 [2048, 4096], P('seq', 'head')
All inputs are finite; a program needn't handle non-finite values.
Results may differ from a plain program's by a relative error of at most 0.0062.
Values may be sent and summed in bfloat16 or wider, within the bound.
No kernel may reach another device: no remote copies, remote signals or barrier semaphores. Data moves between devices by JAX's collectives and lax.ppermute only.
A program may use at most 64 MiB of HBM per device.

v0:
```python
import jax
import jax.numpy as jnp
from jax import lax
from jax.sharding import PartitionSpec as P

HEAD_SIZE = 64
STATE = 128
GROUP_HEADS = 32
KERNEL = 4


def extended_2(block, sides, width):
    for axis, dim in sides:
        count = lax.axis_size(axis)
        forward = [(i, i + 1) for i in range(count - 1)]
        backward = [(target, source) for source, target in forward]
        low = lax.ppermute(
            lax.slice_in_dim(block, block.shape[dim] - width, None, axis=dim), axis, forward
        )
        high = lax.ppermute(lax.slice_in_dim(block, 0, width, axis=dim), axis, backward)
        block = jnp.concatenate([low, block, high], axis=dim)
    return block


def shifted(array, axis, by):
    devices = lax.axis_size(axis)
    pairs = [(i, i + by) for i in range(devices) if 0 <= i + by < devices]
    return lax.ppermute(array, axis, pairs)


def partner(array, axis, stride):
    return lax.ppermute(array, axis, [(i, i ^ 1 << stride) for i in range(lax.axis_size(axis))])


def combine(earlier, later):
    return (earlier[0] * later[0], later[0][:, None, None] * earlier[1] + later[1])


def reachable(seq_pos, seq_count, reach, reverse):
    if reverse:
        return seq_pos + reach < seq_count
    return seq_pos >= reach


def prefix_doubling(element, identity, mover, reverse, seq_pos, seq_count):
    levels = (seq_count - 1).bit_length()
    moved = mover(element, 1)
    valid = reachable(seq_pos, seq_count, 1, reverse)
    running = (jnp.where(valid, moved[0], identity[0]), jnp.where(valid, moved[1], identity[1]))
    for level in range(levels):
        reach = 1 << level
        moved = mover(running, reach)
        valid = reachable(seq_pos, seq_count, reach, reverse)
        candidate = combine(moved, running)
        running = (
            jnp.where(valid, candidate[0], running[0]),
            jnp.where(valid, candidate[1], running[1]),
        )
    return running


def on_device(
    inner_rows,
    gate_rows,
    input_proj,
    step_raw,
    decay_rate,
    skip_gain,
    conv_inner,
    conv_proj,
    norm_gain,
):
    tokens = inner_rows.shape[0]
    half_rows = tokens // 2
    head_count = step_raw.shape[1]
    inner_width = inner_rows.shape[1]
    group_count = input_proj.shape[1] // (2 * STATE)
    rim_rows = KERNEL - 1
    seq_count = lax.axis_size("seq")
    seq_pos = lax.axis_index("seq")
    is_last = seq_pos == seq_count - 1
    my_group = lax.axis_index("head") * head_count // GROUP_HEADS
    joined = jnp.concatenate([inner_rows, input_proj], axis=1)
    edge_rows = jnp.concatenate(
        [joined[tokens - rim_rows :], joined[half_rows - rim_rows : half_rows]], axis=0
    )
    extended = extended_2(edge_rows, (("seq", 0),), rim_rows)
    lead_first = extended[:rim_rows]
    lead_second = jnp.where(
        is_last, joined[half_rows - rim_rows : half_rows], extended[3 * rim_rows :]
    )
    conv_taps = jnp.concatenate([conv_inner, conv_proj], axis=1)
    step_size = jax.nn.softplus(step_raw)
    causal = jnp.arange(half_rows)[:, None] >= jnp.arange(half_rows)[None, :]

    def local_block(lead_rows, rows_in, block_step):
        padded = jnp.concatenate([lead_rows, rows_in], axis=0).astype(jnp.float32)
        conv_sum = jnp.zeros((half_rows, joined.shape[1]), jnp.float32)
        for offset in range(KERNEL):
            conv_sum = conv_sum + conv_taps[offset][None, :] * padded[offset : offset + half_rows]
        conv_out = jax.nn.silu(conv_sum).astype(jnp.bfloat16)
        inner_conv = conv_out[:, :inner_width].reshape(half_rows, head_count, HEAD_SIZE)
        b_rows = lax.dynamic_slice_in_dim(conv_out, inner_width + my_group * STATE, STATE, 1)
        c_rows = lax.dynamic_slice_in_dim(
            conv_out, inner_width + (group_count + my_group) * STATE, STATE, 1
        )
        log_cum = jnp.cumsum(-block_step * decay_rate[None, :], axis=0)
        score_grid = jnp.dot(c_rows, b_rows.T, preferred_element_type=jnp.float32)
        log_gap = log_cum.T[:, :, None] - log_cum.T[:, None, :]
        decay_grid = jnp.where(causal[None], jnp.exp(jnp.where(causal[None], log_gap, 0.0)), 0.0)
        weights = (score_grid[None] * decay_grid * block_step.T[:, None, :]).astype(jnp.bfloat16)
        intra_out = jnp.einsum(
            "hts,shp->thp", weights, inner_conv, preferred_element_type=jnp.float32
        )
        tail_decay = jnp.exp(log_cum[-1][None, :] - log_cum) * block_step
        x_weighted = (inner_conv.astype(jnp.float32) * tail_decay[:, :, None]).astype(jnp.bfloat16)
        local_state = jnp.einsum(
            "shp,sn->hpn", x_weighted, b_rows, preferred_element_type=jnp.float32
        )
        partial_out = intra_out + skip_gain[None, :, None] * inner_conv.astype(jnp.float32)
        return (partial_out, log_cum, c_rows, (jnp.exp(log_cum[-1]), local_state))

    def finish_block(partial_out, log_cum, c_rows, state_in):
        inter_out = jnp.einsum(
            "tn,hpn->thp", c_rows.astype(jnp.float32), state_in, precision=lax.Precision.HIGHEST
        )
        total_out = partial_out + jnp.exp(log_cum)[:, :, None] * inter_out
        return total_out.reshape(half_rows, inner_width)

    first_out, first_cum, first_c, first_elem = local_block(
        lead_first, joined[:half_rows], step_size[:half_rows]
    )
    second_out, second_cum, second_c, second_elem = local_block(
        lead_second, joined[half_rows:], step_size[half_rows:]
    )
    identity = (
        jnp.ones((head_count,), jnp.float32),
        jnp.zeros((head_count, HEAD_SIZE, STATE), jnp.float32),
    )

    def move_first(value, reach):
        return shifted((value[0], value[1]), "seq", reach)

    def move_second(value, reach):
        return shifted((value[0], value[1]), "seq", -reach)

    first_prefix = prefix_doubling(first_elem, identity, move_first, False, seq_pos, seq_count)
    first_incl = combine(first_prefix, first_elem)
    joined_elem = combine(first_incl, second_elem)
    scan_elem = (
        jnp.where(is_last, joined_elem[0], second_elem[0]),
        jnp.where(is_last, joined_elem[1], second_elem[1]),
    )
    second_prefix = prefix_doubling(scan_elem, identity, move_second, True, seq_pos, seq_count)
    second_in = jnp.where(is_last, first_incl[1], second_prefix[1])
    ssm_out = jnp.concatenate(
        [
            finish_block(first_out, first_cum, first_c, first_prefix[1]),
            finish_block(second_out, second_cum, second_c, second_in),
        ],
        axis=0,
    )
    gated = ssm_out * jax.nn.silu(gate_rows.astype(jnp.float32))
    partial_sq = jnp.sum(gated * gated, axis=1)
    other_sq = partner(partial_sq, "head", 0)
    mean_sq = (partial_sq + other_sq) / (GROUP_HEADS * HEAD_SIZE)
    normed = gated * lax.rsqrt(mean_sq + 1e-05)[:, None] * norm_gain[None, :]
    return normed.astype(jnp.bfloat16)


def solution(mesh):
    in_specs = (
        P("seq", "head"),
        P("seq", "head"),
        P("seq", None),
        P("seq", "head"),
        P("head"),
        P("head"),
        P(None, "head"),
        P(),
        P("head"),
    )
    out_specs = P("seq", "head")
    return jax.shard_map(
        on_device, mesh=mesh, in_specs=in_specs, out_specs=out_specs, check_vma=False
    )
```

profile of v0, /device:TPU:0, one launch (start us, length us, event | category | flops | bytes accessed | tf_op | source)
XLA Modules:
  0.0 136.1 jit_solution(2882980468989615667)
XLA Ops:
  0.0 1.1 constant_dynamic-update-slice_fusion.3
  1.2 1.3 collective-permute-start.8
  2.6 0.6 copy-done.11
  4.0 0.7 copy-done.8
  4.6 0.7 copy-done.9
  5.6 3.9 %collective-permute-start = (bf16[3,1536]{1,0:T(4,128)(2,1)S(1)}, bf16[3,1536]{1,0:T(4,128)(2,1)S(1)}, u32[]{:S(2)}, u32[]{:S(2)}) collective-permute-start(bf16[3,1536]{1,0:T(4,128)(2,1)S(1)} %get-tuple-element.11), channel_id=1, source_target_pairs={{0,4},{4,8},{8,12},{12,16},{16,20},{20,24},{24,28},{1,5},{5,9},{9,... | collective-permute-start | bytes 27656 | tf_op jit(solution)/shard_map/ppermute | solution.py:17
  9.6 0.7 collective-permute-done
  10.4 1.0 multiply_convert_fusion.4
  11.6 0.7 copy-done
  12.5 3.6 %collective-permute-start.4 = (f32[16,64,128]{2,1,0:T(8,128)S(1)}, f32[16,64,128]{2,1,0:T(8,128)S(1)}, u32[]{:S(2)}, u32[]{:S(2)}) collective-permute-start(f32[16,64,128]{2,1,0:T(8,128)S(1)} %fusion.32), channel_id=1, source_target_pairs={{0,4},{4,8},{8,12},{12,16},{16,20},{20,24},{24,28},{1,5},{5,9},{9,... | collective-permute-start | bytes 1572872 | tf_op jit(solution)/shard_map/ppermute | solution.py:28
  16.1 1.5 %collective-permute-done.4 = f32[16,64,128]{2,1,0:T(8,128)S(1)} collective-permute-done((f32[16,64,128]{2,1,0:T(8,128)S(1)}, f32[16,64,128]{2,1,0:T(8,128)S(1)}, u32[]{:S(2)}, u32[]{:S(2)}) %collective-permute-start.4) | collective-permute-done | bytes 524320 | tf_op jit(solution)/shard_map/ppermute | solution.py:28
  17.6 8.8 %collective-permute-start.5 = (f32[16,64,128]{2,1,0:T(8,128)S(1)}, f32[16,64,128]{2,1,0:T(8,128)S(1)}, u32[]{:S(2)}, u32[]{:S(2)}) collective-permute-start(f32[16,64,128]{2,1,0:T(8,128)S(1)} %broadcast_select_fusion.1), channel_id=1, source_target_pairs={{0,4},{4,8},{8,12},{12,16},{16,20},{20,24},{24,28},{1,5},{5,9},{9,... | collective-permute-start | bytes 1572872 | tf_op jit(solution)/shard_map/ppermute | solution.py:28
  26.5 4.4 %collective-permute-start.1 = (f32[16]{0:T(128)S(1)}, f32[16]{0:T(128)S(1)}, u32[]{:S(2)}, u32[]{:S(2)}) collective-permute-start(f32[16]{0:T(128)S(1)} %fusion.62), channel_id=1, source_target_pairs={{0,4},{4,8},{8,12},{12,16},{16,20},{20,24},{24,28},{1,5},{5,9},{9,... | collective-permute-start | bytes 200 | tf_op jit(solution)/shard_map/ppermute | solution.py:28
  30.8 0.8 collective-permute-done.1
  31.8 7.7 %collective-permute-start.6 = (f32[16,64,128]{2,1,0:T(8,128)S(1)}, f32[16,64,128]{2,1,0:T(8,128)S(1)}, u32[]{:S(2)}, u32[]{:S(2)}) collective-permute-start(f32[16,64,128]{2,1,0:T(8,128)S(1)} %add_select_fusion.6), channel_id=1, source_target_pairs={{0,8},{4,12},{8,16},{12,20},{16,24},{20,28},{1,9},{5,13},{9,17},{1... | collective-permute-start | bytes 1572872 | tf_op jit(solution)/shard_map/ppermute | solution.py:28
  39.5 3.4 %collective-permute-start.2 = (f32[16]{0:T(128)S(1)}, f32[16]{0:T(128)S(1)}, u32[]{:S(2)}, u32[]{:S(2)}) collective-permute-start(f32[16]{0:T(128)S(1)} %broadcast_select_fusion.9), channel_id=1, source_target_pairs={{0,4},{4,8},{8,12},{12,16},{16,20},{20,24},{24,28},{1,5},{5,9},{9,... | collective-permute-start | bytes 200 | tf_op jit(solution)/shard_map/ppermute | solution.py:28
  42.9 0.8 collective-permute-done.2
  43.7 7.3 %collective-permute-done.6 = f32[16,64,128]{2,1,0:T(8,128)S(1)} collective-permute-done((f32[16,64,128]{2,1,0:T(8,128)S(1)}, f32[16,64,128]{2,1,0:T(8,128)S(1)}, u32[]{:S(2)}, u32[]{:S(2)}) %collective-permute-start.6) | collective-permute-done | bytes 524320 | tf_op jit(solution)/shard_map/ppermute | solution.py:28
  51.2 6.5 %collective-permute-start.7 = (f32[16,64,128]{2,1,0:T(8,128)S(1)}, f32[16,64,128]{2,1,0:T(8,128)}, u32[]{:S(2)}, u32[]{:S(2)}) collective-permute-start(f32[16,64,128]{2,1,0:T(8,128)S(1)} %add_select_fusion.5), channel_id=1, source_target_pairs={{0,16},{4,20},{8,24},{12,28},{1,17},{5,21},{9,25},{13,29},{2,18},{... | collective-permute-start | bytes 1572872 | tf_op jit(solution)/shard_map/ppermute | solution.py:28
  57.7 1.3 collective-permute-start.3
  58.9 1.3 collective-permute-done.3
  60.2 4.3 %collective-permute-start.9 = (f32[16]{0:T(128)S(1)}, f32[16]{0:T(128)S(1)}, u32[]{:S(2)}, u32[]{:S(2)}) collective-permute-start(f32[16]{0:T(128)S(1)} %broadcast_select_fusion.10), channel_id=1, source_target_pairs={{0,16},{4,20},{8,24},{12,28},{1,17},{5,21},{9,25},{13,29},{2,18},{... | collective-permute-start | bytes 200 | tf_op jit(solution)/shard_map/ppermute | solution.py:28
  64.5 1.3 collective-permute-done.9
  66.0 1.3 add_select_fusion.4
  67.3 1.0 add_select_fusion.3
  68.3 1.3 collective-permute-start.13
  69.8 2.5 %collective-permute-done.13 = f32[16,64,128]{2,1,0:T(8,128)S(1)} collective-permute-done((f32[16,64,128]{2,1,0:T(8,128)}, f32[16,64,128]{2,1,0:T(8,128)S(1)}, u32[]{:S(2)}, u32[]{:S(2)}) %collective-permute-start.13) | collective-permute-done | bytes 524320 | tf_op jit(solution)/shard_map/ppermute | solution.py:28
  72.4 1.3 collective-permute-start.14
  73.7 1.3 collective-permute-start.10
  75.0 8.3 %collective-permute-done.10 = f32[16]{0:T(128)S(1)} collective-permute-done((f32[16]{0:T(128)S(1)}, f32[16]{0:T(128)S(1)}, u32[]{:S(2)}, u32[]{:S(2)}) %collective-permute-start.10) | collective-permute-done | bytes 96 | tf_op jit(solution)/shard_map/ppermute | solution.py:28
  83.3 1.3 collective-permute-start.11
  84.6 7.3 %collective-permute-done.11 = f32[16]{0:T(128)S(1)} collective-permute-done((f32[16]{0:T(128)S(1)}, f32[16]{0:T(128)S(1)}, u32[]{:S(2)}, u32[]{:S(2)}) %collective-permute-start.11) | collective-permute-done | bytes 96 | tf_op jit(solution)/shard_map/ppermute | solution.py:28
  92.0 1.4 %collective-permute-start.12 = (f32[16]{0:T(128)S(1)}, f32[16]{0:T(128)S(1)}, u32[]{:S(2)}, u32[]{:S(2)}) collective-permute-start(f32[16]{0:T(128)S(1)} %broadcast_select_fusion.5), channel_id=1, source_target_pairs={{8,0},{12,4},{16,8},{20,12},{24,16},{28,20},{9,1},{13,5},{17,9},{2... | collective-permute-start | bytes 200 | tf_op jit(solution)/shard_map/ppermute | solution.py:28
  93.4 1.2 add_select_fusion.2
  94.6 1.3 collective-permute-start.15
  95.9 2.8 %collective-permute-done.12 = f32[16]{0:T(128)S(1)} collective-permute-done((f32[16]{0:T(128)S(1)}, f32[16]{0:T(128)S(1)}, u32[]{:S(2)}, u32[]{:S(2)}) %collective-permute-start.12) | collective-permute-done | bytes 96 | tf_op jit(solution)/shard_map/ppermute | solution.py:28
  98.9 0.7 copy-done.12
  99.5 0.6 fusion.2
  100.1 10.4 %collective-permute-done.15 = f32[16,64,128]{2,1,0:T(8,128)S(1)} collective-permute-done((f32[16,64,128]{2,1,0:T(8,128)S(1)}, f32[16,64,128]{2,1,0:T(8,128)S(1)}, u32[]{:S(2)}, u32[]{:S(2)}) %collective-permute-start.15) | collective-permute-done | bytes 524320 | tf_op jit(solution)/shard_map/ppermute | solution.py:28
  110.6 1.3 collective-permute-start.16
  112.0 1.4 %fusion.3 = f32[128,16,64]{0,2,1:T(8,128)} fusion(bf16[128,16,64]{0,2,1:T(8,128)(2,1)S(1)} %bitcast.52, f32[16,128]{1,0:T(8,128)S(1)} %get-tuple-element.23, f32[16,128]{1,0:T(8,128)S(1)} %copy.37, f32[128,128]{1,0:T(8,128)S(1)} %fusion.44, pred[128,128]{1,0:T(8,128)(4,1)S(1)} %iota_compare_fusion, f32[16]{0:T(128)S(1)} %copy-done.12), kind=kOutput, calls=%fused_computation.9 | convolution fusion | flops 35520512 | bytes 884800 | tf_op jit(solution)/shard_map/hts,shp->thp/dot_general | solution.py:112
  114.0 14.4 %collective-permute-done.16 = f32[16,64,128]{2,1,0:T(8,128)} collective-permute-done((f32[16,64,128]{2,1,0:T(8,128)S(1)}, f32[16,64,128]{2,1,0:T(8,128)}, u32[]{:S(2)}, u32[]{:S(2)}) %collective-permute-start.16) | collective-permute-done | bytes 524320 | tf_op jit(solution)/shard_map/ppermute | solution.py:28
  128.5 1.6 %fusion = f32[128,16,64]{0,2,1:T(8,128)S(1)} fusion(f32[128,16,64]{0,2,1:T(8,128)S(1)} %copy-done.5, f32[16,64,128]{2,1,0:T(8,128)S(1)} %add_select_fusion.1, f32[16,64,128]{2,1,0:T(8,128)} %collective-permute-done.16, f32[16]{0:T(128)S(1)} %broadcast_select_fusion.7, f32[128,16]{0,1:T(8,128)S(1)} %copy.39, pred[]{:T(512)S(6)} %lt.20, pred[]{:T(512)S(6)} %eq.3, ...), kind=kOutput, calls=%fused_computation.5 | convolution fusion | flops 202375168 | bytes 3187718 | tf_op jit(solution)/shard_map/tn,hpn->thp/dot_general | solution.py:124
  130.3 0.8 copy-done.4
  131.1 0.4 multiply_reduce_fusion
  131.5 1.6 %collective-permute-start.17 = (f32[256]{0:T(256)S(1)}, f32[256]{0:T(256)S(1)}, u32[]{:S(2)}, u32[]{:S(2)}) collective-permute-start(f32[256]{0:T(256)S(1)} %get-tuple-element.9), channel_id=1, source_target_pairs={{0,1},{1,0},{2,3},{3,2},{4,5},{5,4},{6,7},{7,6},{8,9},{9,8},{10,11... | collective-permute-start | bytes 3080 | tf_op jit(solution)/shard_map/ppermute | solution.py:32
  133.1 2.0 %collective-permute-done.17 = f32[256]{0:T(256)S(1)} collective-permute-done((f32[256]{0:T(256)S(1)}, f32[256]{0:T(256)S(1)}, u32[]{:S(2)}, u32[]{:S(2)}) %collective-permute-start.17) | collective-permute-done | bytes 1056 | tf_op jit(solution)/shard_map/ppermute | solution.py:32
  135.1 1.0 multiply_convert_fusion
  (74 shorter events, 3.7 us)
Async XLA Ops:
  0.0 1.1 copy-start.6
  1.2 1.4 %copy-start.7 = (f32[256,16]{0,1:T(8,128)S(1)}, f32[256,16]{0,1:T(8,128)}, u32[]{:S(2)}) copy-start(f32[256,16]{0,1:T(8,128)} %param.12) | copy-start | bytes 49156
  1.2 4.3 %collective-permute-start.8 = (bf16[3,1536]{1,0:T(4,128)(2,1)S(1)}, bf16[3,1536]{1,0:T(4,128)(2,1)S(1)}, u32[]{:S(2)}, u32[]{:S(2)}) collective-permute-start(bf16[3,1536]{1,0:T(4,128)(2,1)S(1)} %slice.108), channel_id=1, source_target_pairs={{4,0},{8,4},{12,8},{16,12},{20,16},{24,20},{28,24},{5,1},{9,5},{13... | collective-permute-start | bytes 27656 | tf_op jit(solution)/shard_map/ppermute | solution.py:20
  2.6 0.7 copy-start.11
  3.9 0.7 copy-start.8
  4.6 0.7 copy-start.9
  5.6 4.7 %collective-permute-start = (bf16[3,1536]{1,0:T(4,128)(2,1)S(1)}, bf16[3,1536]{1,0:T(4,128)(2,1)S(1)}, u32[]{:S(2)}, u32[]{:S(2)}) collective-permute-start(bf16[3,1536]{1,0:T(4,128)(2,1)S(1)} %get-tuple-element.11), channel_id=1, source_target_pairs={{0,4},{4,8},{8,12},{12,16},{16,20},{20,24},{24,28},{1,5},{5,9},{9,... | collective-permute-start | bytes 27656 | tf_op jit(solution)/shard_map/ppermute | solution.py:17
  11.6 0.7 copy-start
  12.5 5.1 %collective-permute-start.4 = (f32[16,64,128]{2,1,0:T(8,128)S(1)}, f32[16,64,128]{2,1,0:T(8,128)S(1)}, u32[]{:S(2)}, u32[]{:S(2)}) collective-permute-start(f32[16,64,128]{2,1,0:T(8,128)S(1)} %fusion.32), channel_id=1, source_target_pairs={{0,4},{4,8},{8,12},{12,16},{16,20},{20,24},{24,28},{1,5},{5,9},{9,... | collective-permute-start | bytes 1572872 | tf_op jit(solution)/shard_map/ppermute | solution.py:28
  17.6 14.0 %collective-permute-start.5 = (f32[16,64,128]{2,1,0:T(8,128)S(1)}, f32[16,64,128]{2,1,0:T(8,128)S(1)}, u32[]{:S(2)}, u32[]{:S(2)}) collective-permute-start(f32[16,64,128]{2,1,0:T(8,128)S(1)} %broadcast_select_fusion.1), channel_id=1, source_target_pairs={{0,4},{4,8},{8,12},{12,16},{16,20},{20,24},{24,28},{1,5},{5,9},{9,... | collective-permute-start | bytes 1572872 | tf_op jit(solution)/shard_map/ppermute | solution.py:28
  26.5 5.2 %collective-permute-start.1 = (f32[16]{0:T(128)S(1)}, f32[16]{0:T(128)S(1)}, u32[]{:S(2)}, u32[]{:S(2)}) collective-permute-start(f32[16]{0:T(128)S(1)} %fusion.62), channel_id=1, source_target_pairs={{0,4},{4,8},{8,12},{12,16},{16,20},{20,24},{24,28},{1,5},{5,9},{9,... | collective-permute-start | bytes 200 | tf_op jit(solution)/shard_map/ppermute | solution.py:28
  31.8 19.3 %collective-permute-start.6 = (f32[16,64,128]{2,1,0:T(8,128)S(1)}, f32[16,64,128]{2,1,0:T(8,128)S(1)}, u32[]{:S(2)}, u32[]{:S(2)}) collective-permute-start(f32[16,64,128]{2,1,0:T(8,128)S(1)} %add_select_fusion.6), channel_id=1, source_target_pairs={{0,8},{4,12},{8,16},{12,20},{16,24},{20,28},{1,9},{5,13},{9,17},{1... | collective-permute-start | bytes 1572872 | tf_op jit(solution)/shard_map/ppermute | solution.py:28
  39.5 4.2 %collective-permute-start.2 = (f32[16]{0:T(128)S(1)}, f32[16]{0:T(128)S(1)}, u32[]{:S(2)}, u32[]{:S(2)}) collective-permute-start(f32[16]{0:T(128)S(1)} %broadcast_select_fusion.9), channel_id=1, source_target_pairs={{0,4},{4,8},{8,12},{12,16},{16,20},{20,24},{24,28},{1,5},{5,9},{9,... | collective-permute-start | bytes 200 | tf_op jit(solution)/shard_map/ppermute | solution.py:28
  51.2 14.8 %collective-permute-start.7 = (f32[16,64,128]{2,1,0:T(8,128)S(1)}, f32[16,64,128]{2,1,0:T(8,128)}, u32[]{:S(2)}, u32[]{:S(2)}) collective-permute-start(f32[16,64,128]{2,1,0:T(8,128)S(1)} %add_select_fusion.5), channel_id=1, source_target_pairs={{0,16},{4,20},{8,24},{12,28},{1,17},{5,21},{9,25},{13,29},{2,18},{... | collective-permute-start | bytes 1572872 | tf_op jit(solution)/shard_map/ppermute | solution.py:28
  57.7 2.6 %collective-permute-start.3 = (f32[16]{0:T(128)S(1)}, f32[16]{0:T(128)S(1)}, u32[]{:S(2)}, u32[]{:S(2)}) collective-permute-start(f32[16]{0:T(128)S(1)} %broadcast_select_fusion.8), channel_id=1, source_target_pairs={{0,8},{4,12},{8,16},{12,20},{16,24},{20,28},{1,9},{5,13},{9,17},{1... | collective-permute-start | bytes 200 | tf_op jit(solution)/shard_map/ppermute | solution.py:28
  60.2 5.5 %collective-permute-start.9 = (f32[16]{0:T(128)S(1)}, f32[16]{0:T(128)S(1)}, u32[]{:S(2)}, u32[]{:S(2)}) collective-permute-start(f32[16]{0:T(128)S(1)} %broadcast_select_fusion.10), channel_id=1, source_target_pairs={{0,16},{4,20},{8,24},{12,28},{1,17},{5,21},{9,25},{13,29},{2,18},{... | collective-permute-start | bytes 200 | tf_op jit(solution)/shard_map/ppermute | solution.py:28
  66.0 1.3 copy-start.2
  68.3 4.0 %collective-permute-start.13 = (f32[16,64,128]{2,1,0:T(8,128)}, f32[16,64,128]{2,1,0:T(8,128)S(1)}, u32[]{:S(2)}, u32[]{:S(2)}) collective-permute-start(f32[16,64,128]{2,1,0:T(8,128)} %add_select_fusion.3), channel_id=1, source_target_pairs={{4,0},{8,4},{12,8},{16,12},{20,16},{24,20},{28,24},{5,1},{9,5},{13... | collective-permute-start | bytes 1572872 | tf_op jit(solution)/shard_map/ppermute | solution.py:28
  72.4 21.1 %collective-permute-start.14 = (f32[16,64,128]{2,1,0:T(8,128)S(1)}, f32[16,64,128]{2,1,0:T(8,128)}, u32[]{:S(2)}, u32[]{:S(2)}) collective-permute-start(f32[16,64,128]{2,1,0:T(8,128)S(1)} %broadcast_select_fusion), channel_id=1, source_target_pairs={{4,0},{8,4},{12,8},{16,12},{20,16},{24,20},{28,24},{5,1},{9,5},{13... | collective-permute-start | bytes 1572872 | tf_op jit(solution)/shard_map/ppermute | solution.py:28
  73.7 9.7 %collective-permute-start.10 = (f32[16]{0:T(128)S(1)}, f32[16]{0:T(128)S(1)}, u32[]{:S(2)}, u32[]{:S(2)}) collective-permute-start(f32[16]{0:T(128)S(1)} %get-tuple-element.15), channel_id=1, source_target_pairs={{4,0},{8,4},{12,8},{16,12},{20,16},{24,20},{28,24},{5,1},{9,5},{13... | collective-permute-start | bytes 200 | tf_op jit(solution)/shard_map/ppermute | solution.py:28
  83.3 8.6 %collective-permute-start.11 = (f32[16]{0:T(128)S(1)}, f32[16]{0:T(128)S(1)}, u32[]{:S(2)}, u32[]{:S(2)}) collective-permute-start(f32[16]{0:T(128)S(1)} %broadcast_select_fusion.6), channel_id=1, source_target_pairs={{4,0},{8,4},{12,8},{16,12},{20,16},{24,20},{28,24},{5,1},{9,5},{13... | collective-permute-start | bytes 200 | tf_op jit(solution)/shard_map/ppermute | solution.py:28
  92.0 6.9 %copy-start.1 = (bf16[128,1024]{0,1:T(8,128)(2,1)S(1)}, bf16[128,1024]{0,1:T(8,128)(2,1)}, u32[]{:S(2)}) copy-start(bf16[128,1024]{0,1:T(8,128)(2,1)} %copy-done) | copy-start | bytes 786436
  92.0 6.7 %collective-permute-start.12 = (f32[16]{0:T(128)S(1)}, f32[16]{0:T(128)S(1)}, u32[]{:S(2)}, u32[]{:S(2)}) collective-permute-start(f32[16]{0:T(128)S(1)} %broadcast_select_fusion.5), channel_id=1, source_target_pairs={{8,0},{12,4},{16,8},{20,12},{24,16},{28,20},{9,1},{13,5},{17,9},{2... | collective-permute-start | bytes 200 | tf_op jit(solution)/shard_map/ppermute | solution.py:28
  94.6 15.9 %collective-permute-start.15 = (f32[16,64,128]{2,1,0:T(8,128)S(1)}, f32[16,64,128]{2,1,0:T(8,128)S(1)}, u32[]{:S(2)}, u32[]{:S(2)}) collective-permute-start(f32[16,64,128]{2,1,0:T(8,128)S(1)} %add_select_fusion.2), channel_id=1, source_target_pairs={{8,0},{12,4},{16,8},{20,12},{24,16},{28,20},{9,1},{13,5},{17,9},{2... | collective-permute-start | bytes 1572872 | tf_op jit(solution)/shard_map/ppermute | solution.py:28
  98.8 0.7 copy-start.12
  100.1 11.9 %copy-start.3 = (bf16[128,1024]{0,1:T(8,128)(2,1)S(1)}, bf16[128,1024]{0,1:T(8,128)(2,1)}, u32[]{:S(2)}) copy-start(bf16[128,1024]{0,1:T(8,128)(2,1)} %copy-done.2) | copy-start | bytes 786436
  110.6 17.9 %collective-permute-start.16 = (f32[16,64,128]{2,1,0:T(8,128)S(1)}, f32[16,64,128]{2,1,0:T(8,128)}, u32[]{:S(2)}, u32[]{:S(2)}) collective-permute-start(f32[16,64,128]{2,1,0:T(8,128)S(1)} %add_select_fusion.1), channel_id=1, source_target_pairs={{16,0},{20,4},{24,8},{28,12},{17,1},{21,5},{25,9},{29,13},{18,2},{... | collective-permute-start | bytes 1572872 | tf_op jit(solution)/shard_map/ppermute | solution.py:28
  113.8 14.7 %copy-start.5 = (f32[128,16,64]{0,2,1:T(8,128)S(1)}, f32[128,16,64]{0,2,1:T(8,128)}, u32[]{:S(2)}) copy-start(f32[128,16,64]{0,2,1:T(8,128)} %fusion.3) | copy-start | bytes 1572868
  130.0 1.0 copy-start.4
  131.5 3.7 %copy-start.10 = (f32[1024]{0:T(1024)S(1)}, f32[1024]{0:T(1024)}, u32[]{:S(2)}) copy-start(f32[1024]{0:T(1024)} %param.17) | copy-start | bytes 12292
  131.5 3.6 %collective-permute-start.17 = (f32[256]{0:T(256)S(1)}, f32[256]{0:T(256)S(1)}, u32[]{:S(2)}, u32[]{:S(2)}) collective-permute-start(f32[256]{0:T(256)S(1)} %get-tuple-element.9), channel_id=1, source_target_pairs={{0,1},{1,0},{2,3},{3,2},{4,5},{5,4},{6,7},{7,6},{8,9},{9,8},{10,11... | collective-permute-start | bytes 3080 | tf_op jit(solution)/shard_map/ppermute | solution.py:32
where the time goes:
time: 137 us; the launch traced here: 136 us
  waiting for transfers between devices  61.4 us (45%)
  starting transfers between devices  55.9 us (41%)
  local copies, waits for them, and re-layouts  6.87 us (5%)
  other arithmetic  6.01 us (4%)
  matrix products  5.4 us (4%)
    ppermute x15, waiting for transfers between devices, shifted(): return lax.ppermute(array, axis, pairs)  58.7 us
    ppermute x15, starting transfers between devices, shifted(): return lax.ppermute(array, axis, pairs)  49.1 us
    unnamed x28, local copies, waits for them, and re-layouts  5.34 us
    ppermute x1, starting transfers between devices, extended_2(): lax.ppermute(lax.slice_in_dim(block, block.shape[dim] - width, None, axis...  3.9 us
    select_n x5, other arithmetic, prefix_doubling(): jnp.where(valid, candidate[1], running[1])  2.81 us
  transfers between devices with their start and end apart: 18, of which 14 were waited for; matrix products, arithmetic and copies ran while one was open for 4% of the time, Pallas kernels for 0%

commit v1 on v0

--- a/solution.py
+++ b/solution.py
@@ -22,41 +22,63 @@
     return block
 
 
-def shifted(array, axis, by):
-    devices = lax.axis_size(axis)
-    pairs = [(i, i + by) for i in range(devices) if 0 <= i + by < devices]
-    return lax.ppermute(array, axis, pairs)
-
-
 def partner(array, axis, stride):
     return lax.ppermute(array, axis, [(i, i ^ 1 << stride) for i in range(lax.axis_size(axis))])
 
 
-def combine(earlier, later):
-    return (earlier[0] * later[0], later[0][:, None, None] * earlier[1] + later[1])
+def butterfly_states(first_loc, second_loc, first_log, second_log, seq_pos, seq_count):
+    levels = seq_count.bit_length() - 1
+    assert 1 << levels == seq_count
+    heads = first_loc.shape[0]
+    both = lax.all_gather(jnp.stack([first_log, second_log]), "seq")
+    block_log = jnp.concatenate([both[:, 0], both[::-1, 1]], axis=0)
+    block_ids = jnp.arange(2 * seq_count)[:, None]
 
+    def span(lo, hi):
+        inside = (block_ids >= lo) & (block_ids < hi)
+        return jnp.exp(jnp.sum(jnp.where(inside, block_log, 0.0), axis=0))[:, None, None]
 
-def reachable(seq_pos, seq_count, reach, reverse):
-    if reverse:
-        return seq_pos + reach < seq_count
-    return seq_pos >= reach
+    def pick(cond, yes, no):
+        return jnp.where(cond, yes, no)
 
-
-def prefix_doubling(element, identity, mover, reverse, seq_pos, seq_count):
-    levels = (seq_count - 1).bit_length()
-    moved = mover(element, 1)
-    valid = reachable(seq_pos, seq_count, 1, reverse)
-    running = (jnp.where(valid, moved[0], identity[0]), jnp.where(valid, moved[1], identity[1]))
+    last = 2 * seq_count
+    prefix = jnp.zeros_like(first_loc)
+    above = jnp.zeros_like(first_loc)
+    sub_f, sub_g = first_loc, second_loc
+    one = jnp.ones((heads, 1, 1), jnp.float32)
+    zero = jnp.zeros((heads, 1, 1), jnp.float32)
     for level in range(levels):
-        reach = 1 << level
-        moved = mover(running, reach)
-        valid = reachable(seq_pos, seq_count, reach, reverse)
-        candidate = combine(moved, running)
-        running = (
-            jnp.where(valid, candidate[0], running[0]),
-            jnp.where(valid, candidate[1], running[1]),
-        )
-    return running
+        size = 1 << level
+        lo = seq_pos - seq_pos % size
+        hi = lo + size
+        lower = (seq_pos // size) % 2 == 0
+        part_lo = jnp.where(lower, hi, lo - size)
+        part_hi = part_lo + size
+        pairs = [(i, i ^ size) for i in range(seq_count)]
+        e_prefix = span(lo, seq_pos)
+        e_above = span(last - hi, last - 1 - seq_pos)
+        e_f = span(lo, hi)
+        e_g = span(last - hi, last - lo)
+        if level < levels - 1:
+            got_f, got_g = lax.ppermute((sub_f, sub_g), "seq", pairs)
+            e_pf = span(part_lo, part_hi)
+            e_pg = span(last - part_hi, last - part_lo)
+            new_f = pick(lower, e_pf, one) * sub_f + pick(lower, one, e_f) * got_f
+            new_g = pick(lower, one, e_pg) * sub_g + pick(lower, e_g, one) * got_g
+            above = above + pick(lower, e_above, zero) * got_g
+            prefix = prefix + pick(lower, zero, e_prefix) * got_f
+            sub_f, sub_g = new_f, new_g
+        else:
+            message = pick(lower, one, e_g) * sub_f + pick(lower, zero, one) * sub_g
+            got = lax.ppermute(message, "seq", pairs)
+            e_pw = span(part_lo, part_hi) * span(last - part_hi, last - part_lo)
+            first_in = prefix + pick(lower, zero, e_prefix) * got
+            second_in = (
+                above
+                + pick(lower, e_above * e_pw, e_above) * sub_f
+                + pick(lower, e_above, e_above * e_f) * got
+            )
+    return first_in, second_in
 
 
 def on_device(
@@ -133,29 +155,12 @@
     second_out, second_cum, second_c, second_elem = local_block(
         lead_second, joined[half_rows:], step_size[half_rows:]
     )
-    identity = (
-        jnp.ones((head_count,), jnp.float32),
-        jnp.zeros((head_count, HEAD_SIZE, STATE), jnp.float32),
+    first_in, second_in = butterfly_states(
+        first_elem[1], second_elem[1], first_cum[-1], second_cum[-1], seq_pos, seq_count
     )
-
-    def move_first(value, reach):
-        return shifted((value[0], value[1]), "seq", reach)
-
-    def move_second(value, reach):
-        return shifted((value[0], value[1]), "seq", -reach)
-
-    first_prefix = prefix_doubling(first_elem, identity, move_first, False, seq_pos, seq_count)
-    first_incl = combine(first_prefix, first_elem)
-    joined_elem = combine(first_incl, second_elem)
-    scan_elem = (
-        jnp.where(is_last, joined_elem[0], second_elem[0]),
-        jnp.where(is_last, joined_elem[1], second_elem[1]),
-    )
-    second_prefix = prefix_doubling(scan_elem, identity, move_second, True, seq_pos, seq_count)
-    second_in = jnp.where(is_last, first_incl[1], second_prefix[1])
     ssm_out = jnp.concatenate(
         [
-            finish_block(first_out, first_cum, first_c, first_prefix[1]),
+            finish_block(first_out, first_cum, first_c, first_in),
             finish_block(second_out, second_cum, second_c, second_in),
         ],
         axis=0,

time: 137 us -> 88 us (0.64)
  starting transfers between devices: 55.9 us -> 11.4 us
  waiting for transfers between devices: 61.4 us -> 31.3 us
  blocking collectives: 0 us -> 11.8 us
  other arithmetic: 6.01 us -> 14.5 us
  local copies, waits for them, and re-layouts: 6.87 us -> 12 us
    ppermute x15 -> x5, starting transfers between devices: 49.1 us -> 6.25 us  [the longest x4 3.62 us: butterfly_states(): got_f, got_g = lax.ppermute((sub_f, sub_g), 'seq', pairs)]
    ppermute x15 -> x5, waiting for transfers between devices: 58.7 us -> 28.6 us  [the longest x4 20.5 us: butterfly_states(): got_f, got_g = lax.ppermute((sub_f, sub_g), 'seq', pairs)]
    all_gather x0 -> x1, blocking collectives: none -> 11.8 us  [butterfly_states(): both = lax.all_gather(jnp.stack([first_log, second_log]), 'seq')]
    select_n x14 -> x15, other arithmetic: 2.93 us -> 8.38 us  [pick(): return jnp.where(cond, yes, no)]
    unnamed x28 -> x90, local copies, waits for them, and re-layouts: 5.34 us -> 9.25 us
    ppermute x1, starting transfers between devices: 3.9 us -> 2.23 us  [extended_2(): lax.ppermute(lax.slice_in_dim(block, block.shape[dim] - width, None, axis...]
  transfers between devices with their start and end apart: 18 -> 8, of which waited for: 14 -> 5; matrix products, arithmetic and copies ran while one was open for 4% -> 19% of each run, Pallas kernels for 0% -> 0%
where the time goes in v1:
time: 88 us; the launch traced here: 87.5 us
  waiting for transfers between devices  31.3 us (36%)
  other arithmetic  14.5 us (16%)
  local copies, waits for them, and re-layouts  12 us (14%)
  blocking collectives  11.8 us (13%)
  starting transfers between devices  11.4 us (13%)
  matrix products  5.72 us (6%)
    ppermute x4, waiting for transfers between devices, butterfly_states(): got_f, got_g = lax.ppermute((sub_f, sub_g), 'seq', pairs)  20.5 us
    all_gather x1, blocking collectives, butterfly_states(): both = lax.all_gather(jnp.stack([first_log, second_log]), 'seq')  11.8 us
    unnamed x90, local copies, waits for them, and re-layouts  9.25 us
    select_n x15, other arithmetic, pick(): return jnp.where(cond, yes, no)  8.38 us
    ppermute x1, waiting for transfers between devices, butterfly_states(): got = lax.ppermute(message, 'seq', pairs)  8.11 us
    ppermute x4, starting transfers between devices, butterfly_states(): got_f, got_g = lax.ppermute((sub_f, sub_g), 'seq', pairs)  3.62 us
    dot_general x2, matrix products, finish_block(): jnp.einsum('tn,hpn->thp', c_rows.astype(jnp.float32), state_in, precision...  3.11 us
    ppermute x1, starting transfers between devices, butterfly_states(): got = lax.ppermute(message, 'seq', pairs)  2.63 us
  transfers between devices with their start and end apart: 8, of which 5 were waited for; matrix products, arithmetic and copies ran while one was open for 19% of the time, Pallas kernels for 0%

profile of v1, /device:TPU:0, one launch (start us, length us, event | category | flops | bytes accessed | tf_op | source)
XLA Modules:
  0.0 87.5 jit_solution(11063863065987189054)
XLA Ops:
  0.0 1.1 %constant_dynamic-update-slice_fusion.3 = bf16[256,1536]{1,0:T(8,128)(2,1)S(1)} fusion(bf16[256,1024]{1,0:T(8,128)(2,1)} %param.9), kind=kLoop, calls=%fused_computation.101 | loop fusion | bytes 1048576
  1.2 1.3 %collective-permute-start.3 = (bf16[3,1536]{1,0:T(4,128)(2,1)S(1)}, bf16[3,1536]{1,0:T(4,128)(2,1)S(1)}, u32[]{:S(2)}, u32[]{:S(2)}) collective-permute-start(bf16[3,1536]{1,0:T(4,128)(2,1)S(1)} %slice.120), channel_id=1, source_target_pairs={{4,0},{8,4},{12,8},{16,12},{20,16},{24,20},{28,24},{5,1},{9,5},{13... | collective-permute-start | bytes 27656 | tf_op jit(solution)/shard_map/ppermute | solution.py:20
  2.6 0.6 copy-done.10
  3.2 0.6 copy-done.29
  4.8 0.7 copy-done.11
  5.4 11.8 %all-gather.1 = f32[8,2,16]{2,1,0:T(2,128)S(1)} all-gather(f32[1,2,16]{2,1,0:T(2,128)S(1)} %maximum_bitcast_fusion), channel_id=2, replica_groups=mesh['seq'=8,'head'=4] {'seq'}, dimensions={0}, use_global_device_ids=true | all-gather | bytes 1152 | tf_op jit(solution)/shard_map/all_gather | solution.py:33
  17.3 0.7 select_reduce_fusion.17
  18.0 0.6 broadcast_select_fusion.14
  19.1 0.5 broadcast_select_fusion.8
  19.6 0.6 broadcast_select_fusion.9
  20.2 0.5 broadcast_select_fusion.3
  20.7 0.6 broadcast_select_fusion.7
  21.3 0.7 select_reduce_fusion.4
  22.0 0.5 broadcast_select_fusion.6
  22.6 0.5 broadcast_select_fusion.13
  23.1 0.6 broadcast_select_fusion.12
  23.7 0.5 broadcast_select_fusion.10
  24.3 0.6 broadcast_select_fusion.4
  24.8 0.6 broadcast_select_fusion.16
  25.4 0.6 slice_bitcast_fusion.1
  26.2 2.2 %collective-permute-start = (bf16[3,1536]{1,0:T(4,128)(2,1)S(1)}, bf16[3,1536]{1,0:T(4,128)(2,1)S(1)}, u32[]{:S(2)}, u32[]{:S(2)}) collective-permute-start(bf16[3,1536]{1,0:T(4,128)(2,1)S(1)} %get-tuple-element.29), channel_id=1, source_target_pairs={{0,4},{4,8},{8,12},{12,16},{16,20},{20,24},{24,28},{1,5},{5,9},{9,... | collective-permute-start | bytes 27656 | tf_op jit(solution)/shard_map/ppermute | solution.py:17
  28.5 0.7 collective-permute-done
  29.3 1.0 %multiply_convert_fusion.4 = (bf16[128,1536]{1,0:T(8,128)(2,1)S(1)}, bf16[128,1536]{1,0:T(8,128)(2,1)S(1)}) fusion(f32[131,1536]{1,0:T(8,128)S(1)} %maximum_convert_fusion, f32[1536]{0:T(1024)S(1)} %get-tuple-element.6, f32[1536]{0:T(1024)S(1)} %get-tuple-element.7, f32[1536]{0:T(1024)S(1)} %get-tuple-element.8, f32[1536]{0:T(1024)S(1)} %get-tuple-element.5, ...), kind=kLoop, calls=%fused_computation.33 | loop fusion | flops 4718592 | bytes 7102464 | tf_op jit(solution)/shard_map/convert_element_type | solution.py:123
  31.8 0.7 copy-done.6
  32.9 0.6 iota_compare_fusion
  33.6 0.7 copy.52
  34.3 0.7 copy.61
  35.0 0.6 copy-done.39
  35.7 0.5 broadcast_select_fusion.5
  36.5 2.7 %collective-permute-start.2 = (f32[16,64,128]{2,1,0:T(8,128)S(1)}, f32[16,64,128]{2,1,0:T(8,128)S(1)}, u32[]{:S(2)}, u32[]{:S(2)}) collective-permute-start(f32[16,64,128]{2,1,0:T(8,128)S(1)} %multiply_add_fusion.3), channel_id=1, source_target_pairs={{0,8},{4,12},{8,0},{12,4},{16,24},{20,28},{24,16},{28,20},{1,9},{5... | collective-permute-start | bytes 1572872 | tf_op jit(solution)/shard_map/ppermute | solution.py:63
  40.0 0.6 broadcast_select_fusion.11
  40.5 0.6 copy-done.21
  41.2 0.6 broadcast_select_fusion.2
  42.0 9.9 %collective-permute-done.2 = f32[16,64,128]{2,1,0:T(8,128)S(1)} collective-permute-done((f32[16,64,128]{2,1,0:T(8,128)S(1)}, f32[16,64,128]{2,1,0:T(8,128)S(1)}, u32[]{:S(2)}, u32[]{:S(2)}) %collective-permute-start.2) | collective-permute-done | bytes 524320 | tf_op jit(solution)/shard_map/ppermute | solution.py:63
  51.9 10.6 %collective-permute-done.5 = f32[16,64,128]{2,1,0:T(8,128)S(1)} collective-permute-done((f32[16,64,128]{2,1,0:T(8,128)S(1)}, f32[16,64,128]{2,1,0:T(8,128)S(1)}, u32[]{:S(2)}, u32[]{:S(2)}) %collective-permute-start.5) | collective-permute-done | bytes 524320 | tf_op jit(solution)/shard_map/ppermute | solution.py:63
  62.8 0.5 copy-done
  63.3 2.6 %collective-permute-start.6 = (f32[16,64,128]{2,1,0:T(8,128)S(1)}, f32[16,64,128]{2,1,0:T(8,128)S(1)}, u32[]{:S(2)}, u32[]{:S(2)}) collective-permute-start(f32[16,64,128]{2,1,0:T(8,128)S(1)} %multiply_add_fusion), channel_id=1, source_target_pairs={{0,16},{4,20},{8,24},{12,28},{16,0},{20,4},{24,8},{28,12},{1,17},{... | collective-permute-start | bytes 1572872 | tf_op jit(solution)/shard_map/ppermute | solution.py:73
  66.1 0.6 copy-done.43
  66.7 0.6 fusion.2
  67.7 1.4 %fusion.3 = f32[128,16,64]{0,2,1:T(8,128)} fusion(bf16[128,16,64]{0,2,1:T(8,128)(2,1)S(1)} %bitcast.50, f32[16,128]{1,0:T(8,128)S(1)} %copy-done.16, f32[16,128]{1,0:T(8,128)S(1)} %copy-done.14, f32[128,128]{1,0:T(8,128)S(1)} %fusion.58, pred[128,128]{1,0:T(8,128)(4,1)S(1)} %copy-done.12, f32[16]{0:T(128)S(1)} %copy-done.43), kind=kOutput, calls=%fused_computation.9 | convolution fusion | flops 35520512 | bytes 884800 | tf_op jit(solution)/shard_map/hts,shp->thp/dot_general | solution.py:134
  69.1 8.1 %collective-permute-done.6 = f32[16,64,128]{2,1,0:T(8,128)S(1)} collective-permute-done((f32[16,64,128]{2,1,0:T(8,128)S(1)}, f32[16,64,128]{2,1,0:T(8,128)S(1)}, u32[]{:S(2)}, u32[]{:S(2)}) %collective-permute-start.6) | collective-permute-done | bytes 524320 | tf_op jit(solution)/shard_map/ppermute | solution.py:73
  77.2 1.3 %fusion.1 = f32[128,16,64]{0,2,1:T(8,128)S(1)} fusion(f32[128,16,64]{0,2,1:T(8,128)S(1)} %fusion.2, f32[16,64,128]{2,1,0:T(8,128)S(1)} %collective-permute-done.6, f32[16,64,128]{2,1,0:T(8,128)S(1)} %collective-permute-done.2, f32[16,64,128]{2,1,0:T(8,128)S(1)} %collective-permute-done.1, f32[16]{0:T(128)S(1)} %copy-done.31, f32[16]{0:T(128)S(1)} %copy-done.30, ...), kind=kOutput, calls=%fused_computation.7 | convolution fusion | flops 202244096 | bytes 2662596 | tf_op jit(solution)/shard_map/tn,hpn->thp/dot_general | solution.py:146
  78.8 0.8 copy-done.1
  79.6 1.8 %fusion = f32[128,16,64]{0,2,1:T(8,128)S(1)} fusion(f32[128,16,64]{0,2,1:T(8,128)} %fusion.3, f32[16,64,128]{2,1,0:T(8,128)} %copy-done.2, f32[16,64,128]{2,1,0:T(8,128)S(1)} %copy-done.1, f32[16,64,128]{2,1,0:T(8,128)S(1)} %collective-permute-done.4, f32[16]{0:T(128)S(1)} %copy-done.20, f32[16]{0:T(128)S(1)} %copy-done.19, f32[16]{0:T(128)S(1)} %copy-done.37, ...), kind=kOutput, calls=%fused_computation.5 | convolution fusion | flops 202899456 | bytes 3713604 | tf_op jit(solution)/shard_map/tn,hpn->thp/dot_general | solution.py:146
  81.6 0.8 copy-done.8
  82.9 1.6 %collective-permute-start.7 = (f32[256]{0:T(256)S(1)}, f32[256]{0:T(256)S(1)}, u32[]{:S(2)}, u32[]{:S(2)}) collective-permute-start(f32[256]{0:T(256)S(1)} %get-tuple-element.27), channel_id=1, source_target_pairs={{0,1},{1,0},{2,3},{3,2},{4,5},{5,4},{6,7},{7,6},{8,9},{9,8},{10,11... | collective-permute-start | bytes 3080 | tf_op jit(solution)/shard_map/ppermute | solution.py:26
  84.5 2.0 %collective-permute-done.7 = f32[256]{0:T(256)S(1)} collective-permute-done((f32[256]{0:T(256)S(1)}, f32[256]{0:T(256)S(1)}, u32[]{:S(2)}, u32[]{:S(2)}) %collective-permute-start.7) | collective-permute-done | bytes 1056 | tf_op jit(solution)/shard_map/ppermute | solution.py:26
  86.5 1.0 %multiply_convert_fusion = bf16[256,1024]{1,0:T(8,128)(2,1)} fusion(f32[256,1024]{1,0:T(8,128)S(1)} %get-tuple-element.28, f32[1024]{0:T(1024)S(1)} %copy-done.18, f32[256]{0:T(256)S(1)} %add_rsqrt_fusion), kind=kLoop, calls=%fused_computation.14 | loop fusion | flops 786432 | bytes 1577984 | tf_op jit(solution)/shard_map/convert_element_type | solution.py:173
  (135 shorter events, 6.7 us)
Async XLA Ops:
  0.0 1.1 %copy-start.9 = (bf16[256,512]{1,0:T(8,128)(2,1)S(1)}, bf16[256,512]{1,0:T(8,128)(2,1)}, u32[]{:S(2)}) copy-start(bf16[256,512]{1,0:T(8,128)(2,1)} %param.11) | copy-start | bytes 786436
  1.2 24.9 %collective-permute-start.3 = (bf16[3,1536]{1,0:T(4,128)(2,1)S(1)}, bf16[3,1536]{1,0:T(4,128)(2,1)S(1)}, u32[]{:S(2)}, u32[]{:S(2)}) collective-permute-start(bf16[3,1536]{1,0:T(4,128)(2,1)S(1)} %slice.120), channel_id=1, source_target_pairs={{4,0},{8,4},{12,8},{16,12},{20,16},{24,20},{28,24},{5,1},{9,5},{13... | collective-permute-start | bytes 27656 | tf_op jit(solution)/shard_map/ppermute | solution.py:20
  2.5 0.7 copy-start.10
  4.7 0.7 copy-start.11
  23.1 2.3 %copy-start.15 = (f32[4,512]{1,0:T(4,128)S(1)}, f32[4,512]{1,0:T(4,128)}, u32[]{:S(2)}) copy-start(f32[4,512]{1,0:T(4,128)} %param.16) | copy-start | bytes 24580
  26.2 3.1 %collective-permute-start = (bf16[3,1536]{1,0:T(4,128)(2,1)S(1)}, bf16[3,1536]{1,0:T(4,128)(2,1)S(1)}, u32[]{:S(2)}, u32[]{:S(2)}) collective-permute-start(bf16[3,1536]{1,0:T(4,128)(2,1)S(1)} %get-tuple-element.29), channel_id=1, source_target_pairs={{0,4},{4,8},{8,12},{12,16},{16,20},{20,24},{24,28},{1,5},{5,9},{9,... | collective-permute-start | bytes 27656 | tf_op jit(solution)/shard_map/ppermute | solution.py:17
  30.3 11.5 %copy-start.3 = (bf16[128,1536]{1,0:T(8,128)(2,1)}, bf16[128,1536]{1,0:T(8,128)(2,1)S(1)}, u32[]{:S(2)}) copy-start(bf16[128,1536]{1,0:T(8,128)(2,1)S(1)} %get-tuple-element.37) | copy-start | bytes 1179652
  30.5 0.7 copy-start.4
  31.2 5.0 %collective-permute-start.1 = (f32[16,64,128]{2,1,0:T(8,128)S(1)}, f32[16,64,128]{2,1,0:T(8,128)S(1)}, u32[]{:S(2)}, u32[]{:S(2)}) collective-permute-start(f32[16,64,128]{2,1,0:T(8,128)S(1)} %fusion.42), channel_id=1, source_target_pairs={{0,4},{4,0},{8,12},{12,8},{16,20},{20,16},{24,28},{28,24},{1,5},{5... | collective-permute-start | bytes 1572872 | tf_op jit(solution)/shard_map/ppermute | solution.py:63
  31.8 0.7 copy-start.6
  32.8 6.4 %collective-permute-start.4 = (f32[16,64,128]{2,1,0:T(8,128)S(1)}, f32[16,64,128]{2,1,0:T(8,128)S(1)}, u32[]{:S(2)}, u32[]{:S(2)}) collective-permute-start(f32[16,64,128]{2,1,0:T(8,128)S(1)} %fusion.40), channel_id=1, source_target_pairs={{0,4},{4,0},{8,12},{12,8},{16,20},{20,16},{24,28},{28,24},{1,5},{5... | collective-permute-start | bytes 1572872 | tf_op jit(solution)/shard_map/ppermute | solution.py:63
  35.7 0.7 copy-start.34
  36.2 2.9 %copy-start.35 = (f32[16]{0:T(128)S(1)}, f32[16]{0:T(128)}, u32[]{:S(2)}) copy-start(f32[16]{0:T(128)} %broadcast_select_fusion.13) | copy-start | bytes 196
  36.2 2.9 %copy-start.36 = (f32[16]{0:T(128)S(1)}, f32[16]{0:T(128)}, u32[]{:S(2)}) copy-start(f32[16]{0:T(128)} %broadcast_select_fusion.12) | copy-start | bytes 196
  36.5 15.4 %collective-permute-start.2 = (f32[16,64,128]{2,1,0:T(8,128)S(1)}, f32[16,64,128]{2,1,0:T(8,128)S(1)}, u32[]{:S(2)}, u32[]{:S(2)}) collective-permute-start(f32[16,64,128]{2,1,0:T(8,128)S(1)} %multiply_add_fusion.3), channel_id=1, source_target_pairs={{0,8},{4,12},{8,0},{12,4},{16,24},{20,28},{24,16},{28,20},{1,9},{5... | collective-permute-start | bytes 1572872 | tf_op jit(solution)/shard_map/ppermute | solution.py:63
  39.1 1.4 %copy-start.24 = (f32[16]{0:T(128)S(1)}, f32[16]{0:T(128)}, u32[]{:S(2)}) copy-start(f32[16]{0:T(128)} %get-tuple-element.26) | copy-start | bytes 196
  39.3 0.7 copy-start.38
  39.3 23.2 %collective-permute-start.5 = (f32[16,64,128]{2,1,0:T(8,128)S(1)}, f32[16,64,128]{2,1,0:T(8,128)S(1)}, u32[]{:S(2)}, u32[]{:S(2)}) collective-permute-start(f32[16,64,128]{2,1,0:T(8,128)S(1)} %multiply_add_fusion.1), channel_id=1, source_target_pairs={{0,8},{4,12},{8,0},{12,4},{16,24},{20,28},{24,16},{28,20},{1,9},{5... | collective-permute-start | bytes 1572872 | tf_op jit(solution)/shard_map/ppermute | solution.py:63
  40.5 0.7 copy-start.22
  40.5 0.7 copy-start.23
  41.8 20.7 %copy-start.25 = (f32[16]{0:T(128)S(1)}, f32[16]{0:T(128)}, u32[]{:S(2)}) copy-start(f32[16]{0:T(128)} %broadcast_select_fusion.8) | copy-start | bytes 196
  41.8 20.7 %copy-start.27 = (f32[16]{0:T(128)S(1)}, f32[16]{0:T(128)}, u32[]{:S(2)}) copy-start(f32[16]{0:T(128)} %broadcast_select_fusion.9) | copy-start | bytes 196
  41.8 20.7 %copy-start.40 = (f32[16]{0:T(128)S(1)}, f32[16]{0:T(128)}, u32[]{:S(2)}) copy-start(f32[16]{0:T(128)} %broadcast_select_fusion.3) | copy-start | bytes 196
  41.8 20.7 %copy-start.41 = (f32[16]{0:T(128)S(1)}, f32[16]{0:T(128)}, u32[]{:S(2)}) copy-start(f32[16]{0:T(128)} %broadcast_select_fusion.7) | copy-start | bytes 196
  41.8 20.7 %copy-start.42 = (f32[16]{0:T(128)S(1)}, f32[16]{0:T(128)}, u32[]{:S(2)}) copy-start(f32[16]{0:T(128)} %broadcast_select_fusion.6) | copy-start | bytes 196
  42.0 24.1 %copy-start.5 = (bf16[128,1024]{0,1:T(8,128)(2,1)S(1)}, bf16[128,1024]{0,1:T(8,128)(2,1)}, u32[]{:S(2)}) copy-start(bf16[128,1024]{0,1:T(8,128)(2,1)} %copy-done.4) | copy-start | bytes 786436
  62.5 0.8 copy-start
  63.3 2.8 %copy-start.12 = (pred[128,128]{1,0:T(8,128)(4,1)S(1)}, pred[128,128]{1,0:T(8,128)(4,1)}, u32[]{:S(2)}) copy-start(pred[128,128]{1,0:T(8,128)(4,1)} %iota_compare_fusion) | copy-start | bytes 49156
  63.3 2.8 %copy-start.13 = (f32[16,128]{1,0:T(8,128)S(1)}, f32[16,128]{1,0:T(8,128)}, u32[]{:S(2)}) copy-start(f32[16,128]{1,0:T(8,128)} %copy.52) | copy-start | bytes 24580
  63.3 2.8 %copy-start.17 = (f32[16,128]{1,0:T(8,128)S(1)}, f32[16,128]{1,0:T(8,128)}, u32[]{:S(2)}) copy-start(f32[16,128]{1,0:T(8,128)} %get-tuple-element.41) | copy-start | bytes 24580
  63.3 13.9 %collective-permute-start.6 = (f32[16,64,128]{2,1,0:T(8,128)S(1)}, f32[16,64,128]{2,1,0:T(8,128)S(1)}, u32[]{:S(2)}, u32[]{:S(2)}) collective-permute-start(f32[16,64,128]{2,1,0:T(8,128)S(1)} %multiply_add_fusion), channel_id=1, source_target_pairs={{0,16},{4,20},{8,24},{12,28},{16,0},{20,4},{24,8},{28,12},{1,17},{... | collective-permute-start | bytes 1572872 | tf_op jit(solution)/shard_map/ppermute | solution.py:73
  66.1 0.7 copy-start.43
  66.7 0.9 %copy-start.7 = (bf16[128,1024]{0,1:T(8,128)(2,1)S(1)}, bf16[128,1024]{0,1:T(8,128)(2,1)}, u32[]{:S(2)}) copy-start(bf16[128,1024]{0,1:T(8,128)(2,1)} %copy-done.6) | copy-start | bytes 786436
  66.7 1.0 %copy-start.14 = (f32[16,128]{1,0:T(8,128)S(1)}, f32[16,128]{1,0:T(8,128)}, u32[]{:S(2)}) copy-start(f32[16,128]{1,0:T(8,128)} %copy.61) | copy-start | bytes 24580
  66.7 1.0 %copy-start.16 = (f32[16,128]{1,0:T(8,128)S(1)}, f32[16,128]{1,0:T(8,128)}, u32[]{:S(2)}) copy-start(f32[16,128]{1,0:T(8,128)} %get-tuple-element.44) | copy-start | bytes 24580
  67.7 9.5 %copy-start.30 = (f32[16]{0:T(128)S(1)}, f32[16]{0:T(128)}, u32[]{:S(2)}) copy-start(f32[16]{0:T(128)} %broadcast_select_fusion.10) | copy-start | bytes 196
  67.7 9.5 %copy-start.31 = (f32[16]{0:T(128)S(1)}, f32[16]{0:T(128)}, u32[]{:S(2)}) copy-start(f32[16]{0:T(128)} %broadcast_select_fusion.4) | copy-start | bytes 196
  67.7 9.5 %copy-start.32 = (f32[16]{0:T(128)S(1)}, f32[16]{0:T(128)}, u32[]{:S(2)}) copy-start(f32[16]{0:T(128)} %broadcast_select_fusion.16) | copy-start | bytes 196
  77.2 1.3 %copy-start.2 = (f32[16,64,128]{2,1,0:T(8,128)}, f32[16,64,128]{2,1,0:T(8,128)S(1)}, u32[]{:S(2)}) copy-start(f32[16,64,128]{2,1,0:T(8,128)S(1)} %collective-permute-done.6) | copy-start | bytes 1572868
  78.5 1.0 %copy-start.1 = (f32[16,64,128]{2,1,0:T(8,128)S(1)}, f32[16,64,128]{2,1,0:T(8,128)}, u32[]{:S(2)}) copy-start(f32[16,64,128]{2,1,0:T(8,128)} %copy-done) | copy-start | bytes 1572868
  78.5 1.0 %copy-start.28 = (f32[16]{0:T(128)S(1)}, f32[16]{0:T(128)}, u32[]{:S(2)}) copy-start(f32[16]{0:T(128)} %broadcast_select_fusion.9) | copy-start | bytes 196
  78.6 1.0 %copy-start.37 = (f32[16]{0:T(128)S(1)}, f32[16]{0:T(128)}, u32[]{:S(2)}) copy-start(f32[16]{0:T(128)} %broadcast_select_fusion.5) | copy-start | bytes 196
  78.8 0.8 copy-start.19
  78.8 0.8 copy-start.20
  78.8 0.8 copy-start.26
  81.4 1.0 %copy-start.8 = (bf16[256,1024]{1,0:T(8,128)(2,1)S(1)}, bf16[256,1024]{1,0:T(8,128)(2,1)}, u32[]{:S(2)}) copy-start(bf16[256,1024]{1,0:T(8,128)(2,1)} %param.10) | copy-start | bytes 1572868
  82.8 3.7 %copy-start.18 = (f32[1024]{0:T(1024)S(1)}, f32[1024]{0:T(1024)}, u32[]{:S(2)}) copy-start(f32[1024]{0:T(1024)} %param.17) | copy-start | bytes 12292
  82.9 3.6 %collective-permute-start.7 = (f32[256]{0:T(256)S(1)}, f32[256]{0:T(256)S(1)}, u32[]{:S(2)}, u32[]{:S(2)}) collective-permute-start(f32[256]{0:T(256)S(1)} %get-tuple-element.27), channel_id=1, source_target_pairs={{0,1},{1,0},{2,3},{3,2},{4,5},{5,4},{6,7},{7,6},{8,9},{9,8},{10,11... | collective-permute-start | bytes 3080 | tf_op jit(solution)/shard_map/ppermute | solution.py:26
  (4 other events, 2.6 us)

commit v2 on v1

--- a/solution.py
+++ b/solution.py
@@ -14,69 +14,88 @@
         count = lax.axis_size(axis)
         forward = [(i, i + 1) for i in range(count - 1)]
         backward = [(target, source) for source, target in forward]
-        low = lax.ppermute(
-            lax.slice_in_dim(block, block.shape[dim] - width, None, axis=dim), axis, forward
-        )
-        high = lax.ppermute(lax.slice_in_dim(block, 0, width, axis=dim), axis, backward)
+        tail, head = lax.optimization_barrier(
+            (
+                lax.slice_in_dim(block, block.shape[dim] - width, None, axis=dim),
+                lax.slice_in_dim(block, 0, width, axis=dim),
+            )
+        )
+        low = lax.ppermute(tail, axis, forward)
+        high = lax.ppermute(head, axis, backward)
         block = jnp.concatenate([low, block, high], axis=dim)
     return block
 
 
 def partner(array, axis, stride):
     return lax.ppermute(array, axis, [(i, i ^ 1 << stride) for i in range(lax.axis_size(axis))])
+
+
+LINK = jnp.float32
+
+
+def pack(maps, decays):
+    flat = [m.reshape(-1, m.shape[-1]) for m in maps]
+    lanes = flat[0].shape[1]
+    rows = jnp.stack(decays)
+    high = rows.astype(LINK)
+    low = (rows - high.astype(jnp.float32)).astype(LINK)
+    tail = jnp.concatenate([high, low], axis=0)
+    tail = jnp.pad(tail, ((0, 8 - tail.shape[0]), (0, lanes - tail.shape[1])))
+    return jnp.concatenate([f.astype(LINK) for f in flat] + [tail], axis=0)
+
+
+def unpack(message, count, shape):
+    rows = shape[0] * shape[1]
+    maps = [
+        message[i * rows : (i + 1) * rows].astype(jnp.float32).reshape(shape) for i in range(count)
+    ]
+    tail = message[count * rows :].astype(jnp.float32)
+    decays = [tail[i, : shape[0]] + tail[count + i, : shape[0]] for i in range(count)]
+    return maps, decays
 
 
 def butterfly_states(first_loc, second_loc, first_log, second_log, seq_pos, seq_count):
     levels = seq_count.bit_length() - 1
     assert 1 << levels == seq_count
-    heads = first_loc.shape[0]
-    both = lax.all_gather(jnp.stack([first_log, second_log]), "seq")
-    block_log = jnp.concatenate([both[:, 0], both[::-1, 1]], axis=0)
-    block_ids = jnp.arange(2 * seq_count)[:, None]
-
-    def span(lo, hi):
-        inside = (block_ids >= lo) & (block_ids < hi)
-        return jnp.exp(jnp.sum(jnp.where(inside, block_log, 0.0), axis=0))[:, None, None]
-
-    def pick(cond, yes, no):
-        return jnp.where(cond, yes, no)
-
-    last = 2 * seq_count
+    shape = first_loc.shape
+    if levels == 0:
+        return jnp.zeros_like(first_loc), first_loc
+
+    def col(v):
+        return v[:, None, None]
+
+    ones = jnp.ones((shape[0],), jnp.float32)
+    zeros = jnp.zeros((shape[0],), jnp.float32)
     prefix = jnp.zeros_like(first_loc)
     above = jnp.zeros_like(first_loc)
+    e_pre, e_abv = ones, ones
     sub_f, sub_g = first_loc, second_loc
-    one = jnp.ones((heads, 1, 1), jnp.float32)
-    zero = jnp.zeros((heads, 1, 1), jnp.float32)
+    e_f, e_g = jnp.exp(first_log), jnp.exp(second_log)
     for level in range(levels):
         size = 1 << level
-        lo = seq_pos - seq_pos % size
-        hi = lo + size
         lower = (seq_pos // size) % 2 == 0
-        part_lo = jnp.where(lower, hi, lo - size)
-        part_hi = part_lo + size
         pairs = [(i, i ^ size) for i in range(seq_count)]
-        e_prefix = span(lo, seq_pos)
-        e_above = span(last - hi, last - 1 - seq_pos)
-        e_f = span(lo, hi)
-        e_g = span(last - hi, last - lo)
         if level < levels - 1:
-            got_f, got_g = lax.ppermute((sub_f, sub_g), "seq", pairs)
-            e_pf = span(part_lo, part_hi)
-            e_pg = span(last - part_hi, last - part_lo)
-            new_f = pick(lower, e_pf, one) * sub_f + pick(lower, one, e_f) * got_f
-            new_g = pick(lower, one, e_pg) * sub_g + pick(lower, e_g, one) * got_g
-            above = above + pick(lower, e_above, zero) * got_g
-            prefix = prefix + pick(lower, zero, e_prefix) * got_f
+            got = lax.ppermute(pack((sub_f, sub_g), (e_f, e_g)), "seq", pairs)
+            (got_f, got_g), (p_f, p_g) = unpack(got, 2, shape)
+            new_f = col(jnp.where(lower, p_f, ones)) * sub_f + col(jnp.where(lower, ones, e_f)) * got_f
+            new_g = col(jnp.where(lower, ones, p_g)) * sub_g + col(jnp.where(lower, e_g, ones)) * got_g
+            above = above + col(jnp.where(lower, e_abv, zeros)) * got_g
+            prefix = prefix + col(jnp.where(lower, zeros, e_pre)) * got_f
+            e_abv = jnp.where(lower, e_abv * p_g, e_abv)
+            e_pre = jnp.where(lower, e_pre, e_pre * p_f)
             sub_f, sub_g = new_f, new_g
+            e_f, e_g = e_f * p_f, e_g * p_g
         else:
-            message = pick(lower, one, e_g) * sub_f + pick(lower, zero, one) * sub_g
-            got = lax.ppermute(message, "seq", pairs)
-            e_pw = span(part_lo, part_hi) * span(last - part_hi, last - part_lo)
-            first_in = prefix + pick(lower, zero, e_prefix) * got
+            sent = col(jnp.where(lower, ones, e_g)) * sub_f + col(jnp.where(lower, zeros, ones)) * sub_g
+            sent_e = jnp.where(lower, e_f, e_f * e_g)
+            got = lax.ppermute(pack((sent,), (sent_e,)), "seq", pairs)
+            (got_w,), (p_w,) = unpack(got, 1, shape)
+            first_in = prefix + col(jnp.where(lower, zeros, e_pre)) * got_w
             second_in = (
                 above
-                + pick(lower, e_above * e_pw, e_above) * sub_f
-                + pick(lower, e_above, e_above * e_f) * got
+                + col(jnp.where(lower, e_abv * p_w, e_abv)) * sub_f
+                + col(jnp.where(lower, e_abv, e_abv * e_f)) * got_w
             )
     return first_in, second_in
 

time: 88 us -> 77.7 us (0.88)
  blocking collectives: 11.8 us -> 0 us
  other arithmetic: 14.5 us -> 9.64 us
  waiting for transfers between devices: 31.3 us -> 35.8 us
  starting transfers between devices: 11.4 us -> 13.5 us
  local copies, waits for them, and re-layouts: 12 us -> 10.4 us
  matrix products: 5.72 us -> 7.16 us
    all_gather x1 -> x0, blocking collectives: 11.8 us -> none  [butterfly_states(): both = lax.all_gather(jnp.stack([first_log, second_log]), 'seq')]
    unnamed x90 -> x70, local copies, waits for them, and re-layouts: 9.25 us -> 2.9 us
    ppermute x7 -> x5, waiting for transfers between devices: 29.3 us -> 33.8 us  [the longest x2 24.8 us: butterfly_states(): got = lax.ppermute(pack((sub_f, sub_g), (e_f, e_g)), 'seq', pairs)]
    select_n x15 -> x10, other arithmetic: 8.38 us -> 4.34 us  [the longest x1 1.42 us: butterfly_states(): prefix = prefix + col(jnp.where(lower, zeros, e_pre)) * got_f]
    slice x1 -> x3, local copies, waits for them, and re-layouts: 0.01 us -> 2.57 us  [unpack(): message[i * rows:(i + 1) * rows].astype(jnp.float32).reshape(shape)]
    reshape x2, local copies, waits for them, and re-layouts: 0.39 us -> 2.53 us  [finish_block(): return total_out.reshape(half_rows, inner_width)]
    ppermute x7 -> x5, starting transfers between devices: 9.78 us -> 11.9 us  [the longest x2 4.99 us: butterfly_states(): got = lax.ppermute(pack((sub_f, sub_g), (e_f, e_g)), 'seq', pairs)]
    dot_general x2, matrix products: 3.11 us -> 4.55 us  [finish_block(): jnp.einsum('tn,hpn->thp', c_rows.astype(jnp.float32), state_in, precision...]
  transfers between devices with their start and end apart: 8 -> 6, of which waited for: 5 -> 4; matrix products, arithmetic and copies ran while one was open for 19% -> 7% of each run, Pallas kernels for 0% -> 0%
where the time goes in v2:
time: 77.7 us; the launch traced here: 77.1 us
  waiting for transfers between devices  35.8 us (46%)
  starting transfers between devices  13.5 us (17%)
  local copies, waits for them, and re-layouts  10.4 us (13%)
  other arithmetic  9.64 us (12%)
  matrix products  7.16 us (9%)
    ppermute x2, waiting for transfers between devices, butterfly_states(): got = lax.ppermute(pack((sub_f, sub_g), (e_f, e_g)), 'seq', pairs)  24.8 us
    ppermute x1, waiting for transfers between devices, butterfly_states(): got = lax.ppermute(pack((sent,), (sent_e,)), 'seq', pairs)  8.98 us
    ppermute x2, starting transfers between devices, butterfly_states(): got = lax.ppermute(pack((sub_f, sub_g), (e_f, e_g)), 'seq', pairs)  4.99 us
    dot_general x2, matrix products, finish_block(): jnp.einsum('tn,hpn->thp', c_rows.astype(jnp.float32), state_in, precision...  4.55 us
    ppermute x1, starting transfers between devices, extended_2(): low = lax.ppermute(tail, axis, forward)  3.03 us
    unnamed x70, local copies, waits for them, and re-layouts  2.9 us
    slice x3, local copies, waits for them, and re-layouts, unpack(): message[i * rows:(i + 1) * rows].astype(jnp.float32).reshape(shape)  2.57 us
    ppermute x1, starting transfers between devices, butterfly_states(): got = lax.ppermute(pack((sent,), (sent_e,)), 'seq', pairs)  2.54 us
  transfers between devices with their start and end apart: 6, of which 4 were waited for; matrix products, arithmetic and copies ran while one was open for 7% of the time, Pallas kernels for 0%

profile of v2, /device:TPU:0, one launch (start us, length us, event | category | flops | bytes accessed | tf_op | source)
XLA Modules:
  0.0 77.1 jit_solution(17511839289506700092)
XLA Ops:
  0.0 1.1 %constant_dynamic-update-slice_fusion.3 = bf16[256,1536]{1,0:T(8,128)(2,1)S(1)} fusion(bf16[256,1024]{1,0:T(8,128)(2,1)} %param.9), kind=kLoop, calls=%fused_computation.104 | loop fusion | bytes 1048576
  1.2 1.3 %collective-permute-start.1 = (bf16[3,1536]{1,0:T(4,128)(2,1)S(1)}, bf16[3,1536]{1,0:T(4,128)(2,1)S(1)}, u32[]{:S(2)}, u32[]{:S(2)}) collective-permute-start(bf16[3,1536]{1,0:T(4,128)(2,1)S(1)} %get-tuple-element.8), channel_id=1, source_target_pairs={{4,0},{8,4},{12,8},{16,12},{20,16},{24,20},{28,24},{5,1},{9,5},{13... | collective-permute-start | bytes 27656 | tf_op jit(solution)/shard_map/ppermute | solution.py:24
  2.5 3.0 %collective-permute-start = (bf16[3,1536]{1,0:T(4,128)(2,1)S(1)}, bf16[3,1536]{1,0:T(4,128)(2,1)S(1)}, u32[]{:S(2)}, u32[]{:S(2)}) collective-permute-start(bf16[3,1536]{1,0:T(4,128)(2,1)S(1)} %get-tuple-element.7), channel_id=1, source_target_pairs={{0,4},{4,8},{8,12},{12,16},{16,20},{20,24},{24,28},{1,5},{5,9},{9,... | collective-permute-start | bytes 27656 | tf_op jit(solution)/shard_map/ppermute | solution.py:23
  5.9 0.2 reduce_window_sum.17
  6.0 0.2 reduce_window_sum.18
  6.5 0.6 slice_bitcast_fusion.1
  7.2 0.1 maximum_convert_fusion.1
  7.3 0.1 maximum_convert_fusion
  7.5 1.0 %multiply_convert_fusion.4 = (bf16[128,1536]{1,0:T(8,128)(2,1)S(1)}, bf16[128,1536]{1,0:T(8,128)(2,1)S(1)}) fusion(f32[131,1536]{1,0:T(8,128)S(1)} %maximum_convert_fusion, f32[1536]{0:T(1024)S(1)} %get-tuple-element.10, f32[1536]{0:T(1024)S(1)} %get-tuple-element.11, f32[1536]{0:T(1024)S(1)} %get-tuple-element.12, f32[1536]{0:T(1024)S(1)} %get-tuple-element.9, ...), kind=kLoop, calls=%fused_computation.35 | loop fusion | flops 4718592 | bytes 7102464 | tf_op jit(solution)/shard_map/convert_element_type | solution.py:142
  8.5 0.2 copy.29
  8.7 0.2 copy.35
  8.9 0.2 fusion.42
  9.1 0.3 copy-done.4
  9.4 0.2 fusion.40
  9.7 2.6 %collective-permute-start.2 = (f32[2056,128]{1,0:T(8,128)S(1)}, f32[2056,128]{1,0:T(8,128)}, u32[]{:S(2)}, u32[]{:S(2)}) collective-permute-start(f32[2056,128]{1,0:T(8,128)S(1)} %pad_maximum_fusion), channel_id=1, source_target_pairs={{0,4},{4,0},{8,12},{12,8},{16,20},{20,16},{24,28},{28,24},{1,5},{5... | collective-permute-start | bytes 3158024 | tf_op jit(solution)/shard_map/ppermute | solution.py:79
  12.3 2.4 %collective-permute-done.2 = f32[2056,128]{1,0:T(8,128)} collective-permute-done((f32[2056,128]{1,0:T(8,128)S(1)}, f32[2056,128]{1,0:T(8,128)}, u32[]{:S(2)}, u32[]{:S(2)}) %collective-permute-start.2) | collective-permute-done | bytes 1052704 | tf_op jit(solution)/shard_map/ppermute | solution.py:79
  14.7 1.4 %broadcast_select_fusion.19 = (f32[16]{0:T(128)}, f32[1,16]{1,0:T(1,128)S(1)}, f32[16]{0:T(128)}, f32[1,16]{1,0:T(1,128)S(1)}) fusion(pred[]{:T(512)S(6)} %eq.18, pred[]{:T(512)S(6)} %eq.16, f32[2056,128]{1,0:T(8,128)} %collective-permute-done.2), kind=kLoop, calls=%fused_computation.151 | loop fusion | flops 96 | bytes 514 | tf_op jit(solution)/shard_map/jit(_where)/select_n | solution.py:84
  16.2 0.6 broadcast_select_fusion.16
  16.8 0.5 copy-done.19
  17.3 1.3 %fusion.82 = (f32[1024,128]{1,0:T(8,128)S(1)}, f32[1024,128]{1,0:T(8,128)S(1)}) fusion(f32[2056,128]{1,0:T(8,128)} %collective-permute-done.2), kind=kLoop, calls=%fused_computation.172 | loop fusion | bytes 2097152 | tf_op jit(solution)/shard_map/slice | solution.py:50
  18.6 0.1 multiply_add_fusion.3
  18.7 0.1 multiply_add_fusion.2
  18.9 1.0 %pad_maximum_fusion.1 = f32[2056,128]{1,0:T(8,128)} fusion(f32[8,128]{1,0:T(8,128)S(1)} %select_maximum_fusion.1, f32[1024,128]{1,0:T(8,128)S(1)} %bitcast.112, f32[1024,128]{1,0:T(8,128)S(1)} %bitcast.100), kind=kLoop, calls=%fused_computation.11 | loop fusion | flops 526336 | bytes 2105344 | tf_op jit(solution)/shard_map/concatenate | solution.py:44
  19.9 2.4 %collective-permute-start.3 = (f32[2056,128]{1,0:T(8,128)}, f32[2056,128]{1,0:T(8,128)}, u32[]{:S(2)}, u32[]{:S(2)}) collective-permute-start(f32[2056,128]{1,0:T(8,128)} %pad_maximum_fusion.1), channel_id=1, source_target_pairs={{0,8},{4,12},{8,0},{12,4},{16,24},{20,28},{24,16},{28,20},{1,9},{5... | collective-permute-start | bytes 3158024 | tf_op jit(solution)/shard_map/ppermute | solution.py:79
  22.4 0.7 copy.31
  23.1 0.7 copy.38
  23.9 0.1 fusion.63
  24.0 22.4 %collective-permute-done.3 = f32[2056,128]{1,0:T(8,128)} collective-permute-done((f32[2056,128]{1,0:T(8,128)}, f32[2056,128]{1,0:T(8,128)}, u32[]{:S(2)}, u32[]{:S(2)}) %collective-permute-start.3) | collective-permute-done | bytes 1052704 | tf_op jit(solution)/shard_map/ppermute | solution.py:79
  46.4 0.8 %broadcast_select_fusion.5 = (f32[16]{0:T(128)S(1)}, f32[1,16]{1,0:T(1,128)S(1)}, f32[16]{0:T(128)S(1)}, f32[1,16]{1,0:T(1,128)S(1)}, f32[16]{0:T(128)S(1)}) fusion(pred[]{:T(512)S(6)} %eq.19, pred[]{:T(512)S(6)} %eq.18, f32[1,16]{1,0:T(1,128)S(1)} %copy-done.15, pred[]{:T(512)S(6)} %eq.16, f32[2056,128]{1,0:T(8,128)} %collective-permute-done.3, ...), kind=kLoop, calls=%fused_computation.137 | loop fusion | flops 160 | bytes 771 | tf_op jit(solution)/shard_map/jit(_where)/select_n | solution.py:94
  47.3 0.4 copy-done.25
  47.8 1.3 %fusion.81 = (f32[1024,128]{1,0:T(8,128)S(1)}, f32[1024,128]{1,0:T(8,128)S(1)}) fusion(f32[2056,128]{1,0:T(8,128)} %collective-permute-done.3), kind=kLoop, calls=%fused_computation.171 | loop fusion | bytes 2097152 | tf_op jit(solution)/shard_map/slice | solution.py:50
  49.1 0.2 multiply_add_fusion
  49.5 2.5 %collective-permute-start.4 = (f32[1032,128]{1,0:T(8,128)S(1)}, f32[1032,128]{1,0:T(8,128)S(1)}, u32[]{:S(2)}, u32[]{:S(2)}) collective-permute-start(f32[1032,128]{1,0:T(8,128)S(1)} %pad_maximum_fusion.2), channel_id=1, source_target_pairs={{0,16},{4,20},{8,24},{12,28},{16,0},{20,4},{24,8},{28,12},{1,17},{... | collective-permute-start | bytes 1585160 | tf_op jit(solution)/shard_map/ppermute | solution.py:92
  52.0 0.1 fusion.58
  52.2 0.6 fusion.2
  52.8 0.3 copy-done.3
  53.1 1.4 %fusion.3 = f32[128,16,64]{0,2,1:T(8,128)} fusion(bf16[128,16,64]{0,2,1:T(8,128)(2,1)S(1)} %bitcast.121, f32[16,128]{1,0:T(8,128)S(1)} %copy-done.17, f32[16,128]{1,0:T(8,128)S(1)} %copy-done.11, f32[128,128]{1,0:T(8,128)S(1)} %fusion.58, pred[128,128]{1,0:T(8,128)(4,1)S(1)} %iota_compare_fusion, f32[16]{0:T(128)S(1)} %copy-done.33), kind=kOutput, calls=%fused_computation.9 | convolution fusion | flops 35520512 | bytes 884800 | tf_op jit(solution)/shard_map/hts,shp->thp/dot_general | solution.py:153
  54.5 9.0 %collective-permute-done.4 = f32[1032,128]{1,0:T(8,128)S(1)} collective-permute-done((f32[1032,128]{1,0:T(8,128)S(1)}, f32[1032,128]{1,0:T(8,128)S(1)}, u32[]{:S(2)}, u32[]{:S(2)}) %collective-permute-start.4) | collective-permute-done | bytes 528416 | tf_op jit(solution)/shard_map/ppermute | solution.py:92
  63.5 2.1 %fusion.1 = f32[128,16,64]{0,2,1:T(8,128)} fusion(f32[128,16,64]{0,2,1:T(8,128)S(1)} %fusion.2, f32[16,64,128]{2,1,0:T(8,128)S(1)} %bitcast.106, f32[16,64,128]{2,1,0:T(8,128)S(1)} %bitcast.102, f32[16,64,128]{2,1,0:T(8,128)S(1)} %bitcast.111, f32[16]{0:T(128)S(1)} %get-tuple-element.17, f32[16]{0:T(128)S(1)} %copy-done.30, f32[]{:T(128)S(6)} %select_n.253, ...), kind=kOutput, calls=%fused_computation.7 | convolution fusion | flops 202244096 | bytes 2662536 | tf_op jit(solution)/shard_map/tn,hpn->thp/dot_general | solution.py:165
  65.7 1.2 %copy.41 = f32[128,1024]{1,0:T(8,128)S(1)} copy(f32[128,1024]{0,1:T(8,128)} %bitcast.116) | data formatting | bytes 1048576 | tf_op jit(solution)/shard_map/reshape | solution.py:169
  66.9 0.8 broadcast_select_fusion.3
  67.7 0.7 broadcast_select_fusion.2
  68.4 2.4 %fusion = f32[128,16,64]{0,2,1:T(8,128)} fusion(f32[128,16,64]{0,2,1:T(8,128)} %fusion.3, f32[16,64,128]{2,1,0:T(8,128)S(1)} %bitcast.107, f32[16,64,128]{2,1,0:T(8,128)S(1)} %bitcast.114, f32[16,64,128]{2,1,0:T(8,128)S(1)} %bitcast.109, f32[16]{0:T(128)S(1)} %broadcast_select_fusion.2, f32[16]{0:T(128)S(1)} %get-tuple-element.21, f32[16]{0:T(128)} %get-tuple-element.33, ...), kind=kOutput, calls=%fused_computation.5 | convolution fusion | flops 202899456 | bytes 3712200 | tf_op jit(solution)/shard_map/tn,hpn->thp/dot_general | solution.py:165
  70.8 1.3 %copy.42 = f32[128,1024]{1,0:T(8,128)S(1)} copy(f32[128,1024]{0,1:T(8,128)} %bitcast.115) | data formatting | bytes 1048576 | tf_op jit(solution)/shard_map/reshape | solution.py:169
  72.1 0.4 multiply_reduce_fusion
  72.5 1.6 %collective-permute-start.5 = (f32[256]{0:T(256)S(1)}, f32[256]{0:T(256)S(1)}, u32[]{:S(2)}, u32[]{:S(2)}) collective-permute-start(f32[256]{0:T(256)S(1)} %get-tuple-element.13), channel_id=1, source_target_pairs={{0,1},{1,0},{2,3},{3,2},{4,5},{5,4},{6,7},{7,6},{8,9},{9,8},{10,11... | collective-permute-start | bytes 3080 | tf_op jit(solution)/shard_map/ppermute | solution.py:30
  74.2 2.0 %collective-permute-done.5 = f32[256]{0:T(256)S(1)} collective-permute-done((f32[256]{0:T(256)S(1)}, f32[256]{0:T(256)S(1)}, u32[]{:S(2)}, u32[]{:S(2)}) %collective-permute-start.5) | collective-permute-done | bytes 1056 | tf_op jit(solution)/shard_map/ppermute | solution.py:30
  76.2 1.0 %multiply_convert_fusion = bf16[256,1024]{1,0:T(8,128)(2,1)} fusion(f32[256,1024]{1,0:T(8,128)S(1)} %get-tuple-element.14, f32[1024]{0:T(1024)S(1)} %copy-done.29, f32[256]{0:T(256)S(1)} %add_rsqrt_fusion), kind=kLoop, calls=%fused_computation.16 | loop fusion | flops 786432 | bytes 1577984 | tf_op jit(solution)/shard_map/convert_element_type | solution.py:192
  (103 shorter events, 1.3 us)
Async XLA Ops:
  0.0 1.1 %copy-start.8 = (bf16[256,512]{1,0:T(8,128)(2,1)S(1)}, bf16[256,512]{1,0:T(8,128)(2,1)}, u32[]{:S(2)}) copy-start(bf16[256,512]{1,0:T(8,128)(2,1)} %param.11) | copy-start | bytes 786436
  0.0 5.5 %copy-start.9 = (f32[256,16]{0,1:T(8,128)S(1)}, f32[256,16]{0,1:T(8,128)}, u32[]{:S(2)}) copy-start(f32[256,16]{0,1:T(8,128)} %param.12) | copy-start | bytes 49156
  0.0 5.6 %copy-start.32 = (f32[16]{0:T(128)S(1)}, f32[16]{0:T(128)}, u32[]{:S(2)}) copy-start(f32[16]{0:T(128)} %param.13) | copy-start | bytes 196
  1.2 6.0 %collective-permute-start.1 = (bf16[3,1536]{1,0:T(4,128)(2,1)S(1)}, bf16[3,1536]{1,0:T(4,128)(2,1)S(1)}, u32[]{:S(2)}, u32[]{:S(2)}) collective-permute-start(bf16[3,1536]{1,0:T(4,128)(2,1)S(1)} %get-tuple-element.8), channel_id=1, source_target_pairs={{4,0},{8,4},{12,8},{16,12},{20,16},{24,20},{28,24},{5,1},{9,5},{13... | collective-permute-start | bytes 27656 | tf_op jit(solution)/shard_map/ppermute | solution.py:24
  2.5 4.8 %collective-permute-start = (bf16[3,1536]{1,0:T(4,128)(2,1)S(1)}, bf16[3,1536]{1,0:T(4,128)(2,1)S(1)}, u32[]{:S(2)}, u32[]{:S(2)}) collective-permute-start(bf16[3,1536]{1,0:T(4,128)(2,1)S(1)} %get-tuple-element.7), channel_id=1, source_target_pairs={{0,4},{4,8},{8,12},{12,16},{16,20},{20,24},{24,28},{1,5},{5,9},{9,... | collective-permute-start | bytes 27656 | tf_op jit(solution)/shard_map/ppermute | solution.py:23
  5.6 0.8 copy-start.10
  5.8 0.7 copy-start.13
  6.0 16.3 %copy-start.1 = (f32[128,16]{1,0:T(8,128)}, f32[128,16]{1,0:T(8,128)S(1)}, u32[]{:S(2)}) copy-start(f32[128,16]{1,0:T(8,128)S(1)} %reduce_window_sum.17) | copy-start | bytes 24580
  8.4 15.4 %copy-start = (bf16[128,1536]{1,0:T(8,128)(2,1)}, bf16[128,1536]{1,0:T(8,128)(2,1)S(1)}, u32[]{:S(2)}) copy-start(bf16[128,1536]{1,0:T(8,128)(2,1)S(1)} %get-tuple-element.46) | copy-start | bytes 1179652
  8.6 0.7 copy-start.4
  8.8 0.7 copy-start.2
  9.7 5.1 %collective-permute-start.2 = (f32[2056,128]{1,0:T(8,128)S(1)}, f32[2056,128]{1,0:T(8,128)}, u32[]{:S(2)}, u32[]{:S(2)}) collective-permute-start(f32[2056,128]{1,0:T(8,128)S(1)} %pad_maximum_fusion), channel_id=1, source_target_pairs={{0,4},{4,0},{8,12},{12,8},{16,20},{20,16},{24,28},{28,24},{1,5},{5... | collective-permute-start | bytes 3158024 | tf_op jit(solution)/shard_map/ppermute | solution.py:79
  16.2 0.7 copy-start.14
  16.2 0.7 copy-start.23
  16.8 0.5 copy-start.19
  16.8 0.5 copy-start.21
  18.8 27.5 %copy-start.15 = (f32[1,16]{1,0:T(1,128)S(1)}, f32[1,16]{1,0:T(1,128)}, u32[]{:S(2)}) copy-start(f32[1,16]{1,0:T(1,128)} %copy-done.14) | copy-start | bytes 196
  18.9 27.5 %copy-start.24 = (f32[1,16]{1,0:T(1,128)S(1)}, f32[1,16]{1,0:T(1,128)}, u32[]{:S(2)}) copy-start(f32[1,16]{1,0:T(1,128)} %copy-done.23) | copy-start | bytes 196
  18.9 28.4 %copy-start.20 = (f32[1,16]{1,0:T(1,128)S(1)}, f32[1,16]{1,0:T(1,128)}, u32[]{:S(2)}) copy-start(f32[1,16]{1,0:T(1,128)} %copy-done.19) | copy-start | bytes 196
  18.9 28.4 %copy-start.22 = (f32[1,16]{1,0:T(1,128)S(1)}, f32[1,16]{1,0:T(1,128)}, u32[]{:S(2)}) copy-start(f32[1,16]{1,0:T(1,128)} %copy-done.21) | copy-start | bytes 196
  19.9 26.4 %collective-permute-start.3 = (f32[2056,128]{1,0:T(8,128)}, f32[2056,128]{1,0:T(8,128)}, u32[]{:S(2)}, u32[]{:S(2)}) collective-permute-start(f32[2056,128]{1,0:T(8,128)} %pad_maximum_fusion.1), channel_id=1, source_target_pairs={{0,8},{4,12},{8,0},{12,4},{16,24},{20,28},{24,16},{28,20},{1,9},{5... | collective-permute-start | bytes 3158024 | tf_op jit(solution)/shard_map/ppermute | solution.py:79
  47.2 0.5 copy-start.25
  47.2 0.6 copy-start.26
  47.2 1.9 %copy-start.31 = (f32[16]{0:T(128)}, f32[16]{0:T(128)S(1)}, u32[]{:S(2)}) copy-start(f32[16]{0:T(128)S(1)} %broadcast_select_fusion.17) | copy-start | bytes 196
  47.8 1.3 %copy-start.28 = (f32[16]{0:T(128)S(1)}, f32[16]{0:T(128)}, u32[]{:S(2)}) copy-start(f32[16]{0:T(128)} %get-tuple-element.40) | copy-start | bytes 196
  49.4 2.8 %copy-start.5 = (bf16[128,1024]{0,1:T(8,128)(2,1)S(1)}, bf16[128,1024]{0,1:T(8,128)(2,1)}, u32[]{:S(2)}) copy-start(bf16[128,1024]{0,1:T(8,128)(2,1)} %copy-done.4) | copy-start | bytes 786436
  49.4 2.8 %copy-start.12 = (f32[16,128]{1,0:T(8,128)S(1)}, f32[16,128]{1,0:T(8,128)}, u32[]{:S(2)}) copy-start(f32[16,128]{1,0:T(8,128)} %copy.31) | copy-start | bytes 24580
  49.4 2.8 %copy-start.18 = (f32[16,128]{1,0:T(8,128)S(1)}, f32[16,128]{1,0:T(8,128)}, u32[]{:S(2)}) copy-start(f32[16,128]{1,0:T(8,128)} %get-tuple-element.50) | copy-start | bytes 24580
  49.4 2.8 %copy-start.33 = (f32[16]{0:T(128)S(1)}, f32[16]{0:T(128)}, u32[]{:S(2)}) copy-start(f32[16]{0:T(128)} %param.14) | copy-start | bytes 196
  49.5 14.0 %collective-permute-start.4 = (f32[1032,128]{1,0:T(8,128)S(1)}, f32[1032,128]{1,0:T(8,128)S(1)}, u32[]{:S(2)}, u32[]{:S(2)}) collective-permute-start(f32[1032,128]{1,0:T(8,128)S(1)} %pad_maximum_fusion.2), channel_id=1, source_target_pairs={{0,16},{4,20},{8,24},{12,28},{16,0},{20,4},{24,8},{28,12},{1,17},{... | collective-permute-start | bytes 1585160 | tf_op jit(solution)/shard_map/ppermute | solution.py:92
  52.2 1.0 %copy-start.3 = (bf16[128,1024]{0,1:T(8,128)(2,1)S(1)}, bf16[128,1024]{0,1:T(8,128)(2,1)}, u32[]{:S(2)}) copy-start(bf16[128,1024]{0,1:T(8,128)(2,1)} %copy-done.2) | copy-start | bytes 786436
  52.2 0.9 %copy-start.11 = (f32[16,128]{1,0:T(8,128)S(1)}, f32[16,128]{1,0:T(8,128)}, u32[]{:S(2)}) copy-start(f32[16,128]{1,0:T(8,128)} %copy.38) | copy-start | bytes 24580
  52.2 0.9 %copy-start.17 = (f32[16,128]{1,0:T(8,128)S(1)}, f32[16,128]{1,0:T(8,128)}, u32[]{:S(2)}) copy-start(f32[16,128]{1,0:T(8,128)} %get-tuple-element.53) | copy-start | bytes 24580
  54.5 9.0 %copy-start.30 = (f32[16]{0:T(128)S(1)}, f32[16]{0:T(128)}, u32[]{:S(2)}) copy-start(f32[16]{0:T(128)} %get-tuple-element.15) | copy-start | bytes 196
  63.5 2.2 %copy-start.7 = (f32[1032,128]{1,0:T(8,128)}, f32[1032,128]{1,0:T(8,128)S(1)}, u32[]{:S(2)}) copy-start(f32[1032,128]{1,0:T(8,128)S(1)} %collective-permute-done.4) | copy-start | bytes 1585156
  65.7 2.0 %copy-start.16 = (f32[1,16]{1,0:T(1,128)S(1)}, f32[1,16]{1,0:T(1,128)}, u32[]{:S(2)}) copy-start(f32[1,16]{1,0:T(1,128)} %copy-done.14) | copy-start | bytes 196
  65.7 2.0 %copy-start.27 = (f32[1,16]{1,0:T(1,128)S(1)}, f32[1,16]{1,0:T(1,128)}, u32[]{:S(2)}) copy-start(f32[1,16]{1,0:T(1,128)} %copy-done.26) | copy-start | bytes 196
  70.8 1.3 %copy-start.6 = (bf16[256,1024]{1,0:T(8,128)(2,1)S(1)}, bf16[256,1024]{1,0:T(8,128)(2,1)}, u32[]{:S(2)}) copy-start(bf16[256,1024]{1,0:T(8,128)(2,1)} %param.10) | copy-start | bytes 1572868
  72.1 4.1 %copy-start.29 = (f32[1024]{0:T(1024)S(1)}, f32[1024]{0:T(1024)}, u32[]{:S(2)}) copy-start(f32[1024]{0:T(1024)} %param.17) | copy-start | bytes 12292
  72.5 3.6 %collective-permute-start.5 = (f32[256]{0:T(256)S(1)}, f32[256]{0:T(256)S(1)}, u32[]{:S(2)}, u32[]{:S(2)}) collective-permute-start(f32[256]{0:T(256)S(1)} %get-tuple-element.13), channel_id=1, source_target_pairs={{0,1},{1,0},{2,3},{3,2},{4,5},{5,4},{6,7},{7,6},{8,9},{9,8},{10,11... | collective-permute-start | bytes 3080 | tf_op jit(solution)/shard_map/ppermute | solution.py:30

commit v3 on v2

--- a/solution.py
+++ b/solution.py
@@ -30,7 +30,7 @@
     return lax.ppermute(array, axis, [(i, i ^ 1 << stride) for i in range(lax.axis_size(axis))])
 
 
-LINK = jnp.float32
+LINK = jnp.bfloat16
 
 
 def pack(maps, decays):

time: 77.7 us -> 55.5 us (0.71)
  waiting for transfers between devices: 35.8 us -> 18.1 us
  local copies, waits for them, and re-layouts: 10.4 us -> 6.46 us
  matrix products: 7.16 us -> 6.02 us
    ppermute x2, waiting for transfers between devices: 24.8 us -> 11.9 us  [butterfly_states(): got = lax.ppermute(pack((sub_f, sub_g), (e_f, e_g)), 'seq', pairs)]
    ppermute x1, waiting for transfers between devices: 8.98 us -> 4.28 us  [butterfly_states(): got = lax.ppermute(pack((sent,), (sent_e,)), 'seq', pairs)]
    convert_element_type x0 -> x12, other arithmetic: none -> 2.8 us  [the longest x3 1.99 us: unpack(): tail = message[count * rows:].astype(jnp.float32)]
    dot_general x2, matrix products: 4.55 us -> 2.32 us  [finish_block(): jnp.einsum('tn,hpn->thp', c_rows.astype(jnp.float32), state_in, precision...]
    reshape x2, local copies, waits for them, and re-layouts: 2.53 us -> 0.39 us  [finish_block(): return total_out.reshape(half_rows, inner_width)]
    dot_general x2, matrix products: 1.92 us -> 2.99 us  [local_block(): jnp.einsum('hts,shp->thp', weights, inner_conv, preferred_element_type=jn...]
    select_n x1, other arithmetic: 0.84 us -> 0.01 us  [butterfly_states(): jnp.where(lower, ones, e_g)]
    select_n x1, other arithmetic: 1.42 us -> 0.6 us  [butterfly_states(): prefix = prefix + col(jnp.where(lower, zeros, e_pre)) * got_f]
  transfers between devices with their start and end apart: 6 -> 6, of which waited for: 4 -> 4; matrix products, arithmetic and copies ran while one was open for 7% -> 11% of each run, Pallas kernels for 0% -> 0%
where the time goes in v3:
time: 55.5 us; the launch traced here: 55 us
  waiting for transfers between devices  18.1 us (33%)
  starting transfers between devices  13.4 us (24%)
  other arithmetic  10.1 us (18%)
  local copies, waits for them, and re-layouts  6.46 us (12%)
  matrix products  6.02 us (11%)
  between operations  0.87 us (2%)
    ppermute x2, waiting for transfers between devices, butterfly_states(): got = lax.ppermute(pack((sub_f, sub_g), (e_f, e_g)), 'seq', pairs)  11.9 us
    ppermute x2, starting transfers between devices, butterfly_states(): got = lax.ppermute(pack((sub_f, sub_g), (e_f, e_g)), 'seq', pairs)  4.93 us
    ppermute x1, waiting for transfers between devices, butterfly_states(): got = lax.ppermute(pack((sent,), (sent_e,)), 'seq', pairs)  4.28 us
    ppermute x1, starting transfers between devices, extended_2(): low = lax.ppermute(tail, axis, forward)  3.03 us
    dot_general x2, matrix products, local_block(): jnp.einsum('hts,shp->thp', weights, inner_conv, preferred_element_type=jn...  2.99 us
    ppermute x1, starting transfers between devices, butterfly_states(): got = lax.ppermute(pack((sent,), (sent_e,)), 'seq', pairs)  2.52 us
    dot_general x2, matrix products, finish_block(): jnp.einsum('tn,hpn->thp', c_rows.astype(jnp.float32), state_in, precision...  2.32 us
    unnamed x78, local copies, waits for them, and re-layouts  2.16 us
  transfers between devices with their start and end apart: 6, of which 4 were waited for; matrix products, arithmetic and copies ran while one was open for 11% of the time, Pallas kernels for 0%

profile of v3, /device:TPU:0, one launch (start us, length us, event | category | flops | bytes accessed | tf_op | source)
XLA Modules:
  0.0 55.0 jit_solution(17132309595864987962)
XLA Ops:
  0.0 1.1 %constant_dynamic-update-slice_fusion.3 = bf16[256,1536]{1,0:T(8,128)(2,1)S(1)} fusion(bf16[256,1024]{1,0:T(8,128)(2,1)} %param.9), kind=kLoop, calls=%fused_computation.114 | loop fusion | bytes 1048576
  1.2 1.3 %collective-permute-start.1 = (bf16[3,1536]{1,0:T(4,128)(2,1)S(1)}, bf16[3,1536]{1,0:T(4,128)(2,1)S(1)}, u32[]{:S(2)}, u32[]{:S(2)}) collective-permute-start(bf16[3,1536]{1,0:T(4,128)(2,1)S(1)} %get-tuple-element.8), channel_id=1, source_target_pairs={{4,0},{8,4},{12,8},{16,12},{20,16},{24,20},{28,24},{5,1},{9,5},{13... | collective-permute-start | bytes 27656 | tf_op jit(solution)/shard_map/ppermute | solution.py:24
  2.5 3.0 %collective-permute-start = (bf16[3,1536]{1,0:T(4,128)(2,1)S(1)}, bf16[3,1536]{1,0:T(4,128)(2,1)S(1)}, u32[]{:S(2)}, u32[]{:S(2)}) collective-permute-start(bf16[3,1536]{1,0:T(4,128)(2,1)S(1)} %get-tuple-element.7), channel_id=1, source_target_pairs={{0,4},{4,8},{8,12},{12,16},{16,20},{20,24},{24,28},{1,5},{5,9},{9,... | collective-permute-start | bytes 27656 | tf_op jit(solution)/shard_map/ppermute | solution.py:23
  5.6 0.1 copy.30
  5.8 0.1 copy.36
  5.9 0.2 reduce_window_sum.17
  6.0 0.2 reduce_window_sum.18
  6.6 0.6 %slice_bitcast_fusion.1 = (f32[16,128]{1,0:T(8,128)S(1)}, f32[128,16]{0,1:T(8,128)S(1)}, f32[128,16]{0,1:T(8,128)S(1)}, f32[16,128]{1,0:T(8,128)}) fusion(f32[256,16]{0,1:T(8,128)S(1)} %compare_select_fusion, f32[128,16]{0,1:T(8,128)S(1)} %copy.34, f32[16]{0:T(128)S(1)} %get-tuple-element.60, f32[128,16]{0,1:T(8,128)S(1)} %copy.37, f32[16]{0:T(128)S(1)} %get-tuple-element.40), kind=kLoop, calls=%fused_computation.120 | loop fusion | flops 8192 | bytes 65664 | tf_op jit(solution)/shard_map/transpose | solution.py:152
  7.2 0.1 maximum_convert_fusion.1
  7.4 0.1 maximum_convert_fusion
  7.5 1.0 %multiply_convert_fusion.4 = (bf16[128,1536]{1,0:T(8,128)(2,1)S(1)}, bf16[128,1536]{1,0:T(8,128)(2,1)S(1)}) fusion(f32[131,1536]{1,0:T(8,128)S(1)} %maximum_convert_fusion, f32[1536]{0:T(1024)S(1)} %get-tuple-element.10, f32[1536]{0:T(1024)S(1)} %get-tuple-element.11, f32[1536]{0:T(1024)S(1)} %get-tuple-element.12, f32[1536]{0:T(1024)S(1)} %get-tuple-element.9, ...), kind=kLoop, calls=%fused_computation.33 | loop fusion | flops 4718592 | bytes 7102464 | tf_op jit(solution)/shard_map/convert_element_type | solution.py:142
  8.5 0.2 copy.29
  8.7 0.2 copy.35
  8.9 0.2 fusion.112
  9.1 0.2 fusion.111
  9.3 0.9 %pad_maximum_fusion = bf16[2056,128]{1,0:T(8,128)(2,1)} fusion(bf16[8,128]{1,0:T(8,128)(2,1)S(1)} %fusion.86, bf16[1024,128]{1,0:T(8,128)(2,1)S(1)} %bitcast.133, bf16[1024,128]{1,0:T(8,128)(2,1)S(1)} %bitcast.132), kind=kLoop, calls=%fused_computation.48 | loop fusion | flops 1579008 | bytes 1052672 | tf_op jit(solution)/shard_map/concatenate | solution.py:44
  10.2 2.6 %collective-permute-start.2 = (bf16[2056,128]{1,0:T(8,128)(2,1)}, bf16[2056,128]{1,0:T(8,128)(2,1)}, u32[]{:S(2)}, u32[]{:S(2)}) collective-permute-start(bf16[2056,128]{1,0:T(8,128)(2,1)} %pad_maximum_fusion), channel_id=1, source_target_pairs={{0,4},{4,0},{8,12},{12,8},{16,20},{20,16},{24,28},{28,24},{1,5},{5... | collective-permute-start | bytes 1579016 | tf_op jit(solution)/shard_map/ppermute | solution.py:79
  12.7 1.9 %collective-permute-done.2 = bf16[2056,128]{1,0:T(8,128)(2,1)} collective-permute-done((bf16[2056,128]{1,0:T(8,128)(2,1)}, bf16[2056,128]{1,0:T(8,128)(2,1)}, u32[]{:S(2)}, u32[]{:S(2)}) %collective-permute-start.2) | collective-permute-done | bytes 526368 | tf_op jit(solution)/shard_map/ppermute | solution.py:79
  14.6 0.7 %slice_convert_fusion.2 = f32[8,128]{1,0:T(8,128)S(1)} fusion(bf16[2056,128]{1,0:T(8,128)(2,1)} %collective-permute-done.2), kind=kLoop, calls=%fused_computation.147 | loop fusion | flops 1024 | bytes 6144 | tf_op jit(solution)/shard_map/convert_element_type | solution.py:52
  15.3 0.6 %broadcast_select_fusion.19 = (f32[16]{0:T(128)}, f32[1,16]{1,0:T(1,128)S(1)}, f32[16]{0:T(128)}, f32[1,16]{1,0:T(1,128)S(1)}) fusion(pred[]{:T(512)S(6)} %eq.18, pred[]{:T(512)S(6)} %eq.16, f32[8,128]{1,0:T(8,128)S(1)} %slice_convert_fusion.2), kind=kLoop, calls=%fused_computation.177 | loop fusion | flops 96 | bytes 514 | tf_op jit(solution)/shard_map/jit(_where)/select_n | solution.py:84
  15.9 0.6 %broadcast_select_fusion.16 = (f32[16]{0:T(128)}, f32[16]{0:T(128)S(1)}, f32[16]{0:T(128)S(1)}) fusion(pred[]{:T(512)S(6)} %eq.18, f32[1,16]{1,0:T(1,128)S(1)} %get-tuple-element.16, f32[128,16]{1,0:T(8,128)S(1)} %reduce_window_sum.17, pred[]{:T(512)S(6)} %eq.16), kind=kLoop, calls=%fused_computation.174 | loop fusion | flops 64 | bytes 322 | tf_op jit(solution)/shard_map/jit(_where)/select_n | solution.py:81
  16.6 1.1 %fusion.110 = (bf16[1024,128]{1,0:T(8,128)(2,1)S(1)}, bf16[1024,128]{1,0:T(8,128)(2,1)S(1)}) fusion(bf16[2056,128]{1,0:T(8,128)(2,1)} %collective-permute-done.2), kind=kLoop, calls=%fused_computation.202 | loop fusion | bytes 1048576 | tf_op jit(solution)/shard_map/slice | solution.py:50
  17.7 0.2 fusion.104
  17.9 0.2 fusion.43
  18.0 0.9 %pad_maximum_fusion.1 = bf16[2056,128]{1,0:T(8,128)(2,1)} fusion(bf16[8,128]{1,0:T(8,128)(2,1)S(1)} %fusion.90, bf16[1024,128]{1,0:T(8,128)(2,1)S(1)} %bitcast.127, bf16[1024,128]{1,0:T(8,128)(2,1)S(1)} %bitcast.126), kind=kLoop, calls=%fused_computation.49 | loop fusion | flops 1579008 | bytes 1052672 | tf_op jit(solution)/shard_map/concatenate | solution.py:44
  18.9 2.4 %collective-permute-start.3 = (bf16[2056,128]{1,0:T(8,128)(2,1)}, bf16[2056,128]{1,0:T(8,128)(2,1)}, u32[]{:S(2)}, u32[]{:S(2)}) collective-permute-start(bf16[2056,128]{1,0:T(8,128)(2,1)} %pad_maximum_fusion.1), channel_id=1, source_target_pairs={{0,8},{4,12},{8,0},{12,4},{16,24},{20,28},{24,16},{28,20},{1,9},{5... | collective-permute-start | bytes 1579016 | tf_op jit(solution)/shard_map/ppermute | solution.py:79
  21.5 0.7 %copy.38 = f32[16,128]{1,0:T(8,128)} copy(f32[16,128]{0,1:T(8,128)S(1)} %bitcast.124) | data formatting | bytes 16384 | tf_op jit(solution)/shard_map/transpose | solution.py:150
  22.2 0.1 fusion.70
  22.4 1.6 %fusion.2 = f32[128,16,64]{0,2,1:T(8,128)S(1)} fusion(bf16[128,16,64]{0,2,1:T(8,128)(2,1)} %bitcast.131, f32[16,128]{1,0:T(8,128)S(1)} %get-tuple-element.46, f32[16,128]{1,0:T(8,128)S(1)} %copy.31, f32[128,128]{1,0:T(8,128)S(1)} %fusion.70, pred[128,128]{1,0:T(8,128)(4,1)S(1)} %iota_compare_fusion, f32[16]{0:T(128)S(1)} %copy-done.36), kind=kOutput, calls=%fused_computation.8 | convolution fusion | flops 35520512 | bytes 884800 | tf_op jit(solution)/shard_map/hts,shp->thp/dot_general | solution.py:153
  24.1 10.0 %collective-permute-done.3 = bf16[2056,128]{1,0:T(8,128)(2,1)} collective-permute-done((bf16[2056,128]{1,0:T(8,128)(2,1)}, bf16[2056,128]{1,0:T(8,128)(2,1)}, u32[]{:S(2)}, u32[]{:S(2)}) %collective-permute-start.3) | collective-permute-done | bytes 526368 | tf_op jit(solution)/shard_map/ppermute | solution.py:79
  34.1 0.7 %slice_convert_fusion.1 = f32[8,128]{1,0:T(8,128)S(1)} fusion(bf16[2056,128]{1,0:T(8,128)(2,1)} %collective-permute-done.3), kind=kLoop, calls=%fused_computation.146 | loop fusion | flops 1024 | bytes 6144 | tf_op jit(solution)/shard_map/convert_element_type | solution.py:52
  34.8 1.1 %fusion.109 = (bf16[1024,128]{1,0:T(8,128)(2,1)S(1)}, bf16[1024,128]{1,0:T(8,128)(2,1)S(1)}) fusion(bf16[2056,128]{1,0:T(8,128)(2,1)} %collective-permute-done.3), kind=kLoop, calls=%fused_computation.201 | loop fusion | bytes 1048576 | tf_op jit(solution)/shard_map/slice | solution.py:50
  36.0 0.4 fusion.29
  36.5 2.5 %collective-permute-start.4 = (bf16[1032,128]{1,0:T(8,128)(2,1)S(1)}, bf16[1032,128]{1,0:T(8,128)(2,1)S(1)}, u32[]{:S(2)}, u32[]{:S(2)}) collective-permute-start(bf16[1032,128]{1,0:T(8,128)(2,1)S(1)} %pad_maximum_fusion.2), channel_id=1, source_target_pairs={{0,16},{4,20},{8,24},{12,28},{16,0},{20,4},{24,8},{28,12},{1,17},{... | collective-permute-start | bytes 792584 | tf_op jit(solution)/shard_map/ppermute | solution.py:92
  39.0 0.1 fusion.65
  39.2 1.4 %fusion.3 = f32[128,16,64]{0,2,1:T(8,128)} fusion(bf16[128,16,64]{0,2,1:T(8,128)(2,1)S(1)} %bitcast.129, f32[16,128]{1,0:T(8,128)S(1)} %copy-done.17, f32[16,128]{1,0:T(8,128)S(1)} %copy-done.13, f32[128,128]{1,0:T(8,128)S(1)} %fusion.65, pred[128,128]{1,0:T(8,128)(4,1)S(1)} %iota_compare_fusion, f32[16]{0:T(128)S(1)} %copy-done.37), kind=kOutput, calls=%fused_computation.9 | convolution fusion | flops 35520512 | bytes 884800 | tf_op jit(solution)/shard_map/hts,shp->thp/dot_general | solution.py:153
  40.6 4.3 %collective-permute-done.4 = bf16[1032,128]{1,0:T(8,128)(2,1)S(1)} collective-permute-done((bf16[1032,128]{1,0:T(8,128)(2,1)S(1)}, bf16[1032,128]{1,0:T(8,128)(2,1)S(1)}, u32[]{:S(2)}, u32[]{:S(2)}) %collective-permute-start.4) | collective-permute-done | bytes 264224 | tf_op jit(solution)/shard_map/ppermute | solution.py:92
  45.0 0.5 fusion.1
  45.6 0.2 copy.41
  45.8 0.7 %slice_convert_fusion = f32[8,128]{1,0:T(8,128)S(1)} fusion(bf16[1032,128]{1,0:T(8,128)(2,1)} %copy-done.3), kind=kLoop, calls=%fused_computation.145 | loop fusion | flops 1024 | bytes 6144 | tf_op jit(solution)/shard_map/convert_element_type | solution.py:52
  46.5 0.7 %broadcast_select_fusion.2 = f32[16]{0:T(128)S(1)} fusion(f32[16]{0:T(128)S(1)} %get-tuple-element.22, pred[]{:T(512)S(6)} %eq.19, f32[1,16]{1,0:T(1,128)S(1)} %copy-done.25, f32[1,16]{1,0:T(1,128)S(1)} %copy-done.16, f32[128,16]{1,0:T(8,128)} %copy-done), kind=kLoop, calls=%fused_computation.160 | loop fusion | flops 64 | bytes 321 | tf_op jit(solution)/shard_map/jit(_where)/select_n | solution.py:98
  47.2 1.8 %fusion = f32[128,16,64]{0,2,1:T(8,128)S(1)} fusion(f32[128,16,64]{0,2,1:T(8,128)} %fusion.3, bf16[16,64,128]{2,1,0:T(8,128)(2,1)S(1)} %bitcast.113, bf16[16,64,128]{2,1,0:T(8,128)(2,1)S(1)} %bitcast.118, bf16[16,64,128]{2,1,0:T(8,128)(2,1)S(1)} %bitcast.120, bf16[16,64,128]{2,1,0:T(8,128)(2,1)S(1)} %bitcast.116, f32[16]{0:T(128)S(1)} %broadcast_select_fusion.2, ...), kind=kOutput, calls=%fused_computation.5 | convolution fusion | flops 203948032 | bytes 2928136 | tf_op jit(solution)/shard_map/tn,hpn->thp/dot_general | solution.py:165
  49.0 0.2 copy.42
  49.2 0.8 %copy-done.2 = bf16[256,1024]{1,0:T(8,128)(2,1)S(1)} copy-done((bf16[256,1024]{1,0:T(8,128)(2,1)S(1)}, bf16[256,1024]{1,0:T(8,128)(2,1)}, u32[]{:S(2)}) %copy-start.2) | copy-done | bytes 524312
  50.0 0.4 multiply_reduce_fusion
  50.4 1.6 %collective-permute-start.5 = (f32[256]{0:T(256)S(1)}, f32[256]{0:T(256)S(1)}, u32[]{:S(2)}, u32[]{:S(2)}) collective-permute-start(f32[256]{0:T(256)S(1)} %get-tuple-element.13), channel_id=1, source_target_pairs={{0,1},{1,0},{2,3},{3,2},{4,5},{5,4},{6,7},{7,6},{8,9},{9,8},{10,11... | collective-permute-start | bytes 3080 | tf_op jit(solution)/shard_map/ppermute | solution.py:30
  52.1 2.0 %collective-permute-done.5 = f32[256]{0:T(256)S(1)} collective-permute-done((f32[256]{0:T(256)S(1)}, f32[256]{0:T(256)S(1)}, u32[]{:S(2)}, u32[]{:S(2)}) %collective-permute-start.5) | collective-permute-done | bytes 1056 | tf_op jit(solution)/shard_map/ppermute | solution.py:30
  54.1 1.0 %multiply_convert_fusion = bf16[256,1024]{1,0:T(8,128)(2,1)} fusion(f32[256,1024]{1,0:T(8,128)S(1)} %get-tuple-element.14, f32[1024]{0:T(1024)S(1)} %copy-done.26, f32[256]{0:T(256)S(1)} %add_rsqrt_fusion), kind=kLoop, calls=%fused_computation.14 | loop fusion | flops 786432 | bytes 1577984 | tf_op jit(solution)/shard_map/convert_element_type | solution.py:192
  (117 shorter events, 1.1 us)
Async XLA Ops:
  0.0 1.1 %copy-start.4 = (bf16[256,512]{1,0:T(8,128)(2,1)S(1)}, bf16[256,512]{1,0:T(8,128)(2,1)}, u32[]{:S(2)}) copy-start(bf16[256,512]{1,0:T(8,128)(2,1)} %param.11) | copy-start | bytes 786436
  0.0 5.5 %copy-start.5 = (f32[256,16]{0,1:T(8,128)S(1)}, f32[256,16]{0,1:T(8,128)}, u32[]{:S(2)}) copy-start(f32[256,16]{0,1:T(8,128)} %param.12) | copy-start | bytes 49156
  0.0 5.6 %copy-start.35 = (f32[16]{0:T(128)S(1)}, f32[16]{0:T(128)}, u32[]{:S(2)}) copy-start(f32[16]{0:T(128)} %param.13) | copy-start | bytes 196
  1.2 6.0 %collective-permute-start.1 = (bf16[3,1536]{1,0:T(4,128)(2,1)S(1)}, bf16[3,1536]{1,0:T(4,128)(2,1)S(1)}, u32[]{:S(2)}, u32[]{:S(2)}) collective-permute-start(bf16[3,1536]{1,0:T(4,128)(2,1)S(1)} %get-tuple-element.8), channel_id=1, source_target_pairs={{4,0},{8,4},{12,8},{16,12},{20,16},{24,20},{28,24},{5,1},{9,5},{13... | collective-permute-start | bytes 27656 | tf_op jit(solution)/shard_map/ppermute | solution.py:24
  2.5 4.9 %collective-permute-start = (bf16[3,1536]{1,0:T(4,128)(2,1)S(1)}, bf16[3,1536]{1,0:T(4,128)(2,1)S(1)}, u32[]{:S(2)}, u32[]{:S(2)}) collective-permute-start(bf16[3,1536]{1,0:T(4,128)(2,1)S(1)} %get-tuple-element.7), channel_id=1, source_target_pairs={{0,4},{4,8},{8,12},{12,16},{16,20},{20,24},{24,28},{1,5},{5,9},{9,... | collective-permute-start | bytes 27656 | tf_op jit(solution)/shard_map/ppermute | solution.py:23
  5.8 0.7 %copy-start.6 = (f32[4,1024]{1,0:T(4,128)S(1)}, f32[4,1024]{1,0:T(4,128)}, u32[]{:S(2)}) copy-start(f32[4,1024]{1,0:T(4,128)} %param.15) | copy-start | bytes 49156
  5.8 0.7 %copy-start.14 = (f32[4,512]{1,0:T(4,128)S(1)}, f32[4,512]{1,0:T(4,128)}, u32[]{:S(2)}) copy-start(f32[4,512]{1,0:T(4,128)} %param.16) | copy-start | bytes 24580
  6.0 15.3 %copy-start = (f32[128,16]{1,0:T(8,128)}, f32[128,16]{1,0:T(8,128)S(1)}, u32[]{:S(2)}) copy-start(f32[128,16]{1,0:T(8,128)S(1)} %reduce_window_sum.17) | copy-start | bytes 24580
  8.7 9.2 %copy-start.1 = (bf16[128,1024]{0,1:T(8,128)(2,1)}, bf16[128,1024]{0,1:T(8,128)(2,1)S(1)}, u32[]{:S(2)}) copy-start(bf16[128,1024]{0,1:T(8,128)(2,1)S(1)} %copy.29) | copy-start | bytes 786436
  10.2 4.4 %collective-permute-start.2 = (bf16[2056,128]{1,0:T(8,128)(2,1)}, bf16[2056,128]{1,0:T(8,128)(2,1)}, u32[]{:S(2)}, u32[]{:S(2)}) collective-permute-start(bf16[2056,128]{1,0:T(8,128)(2,1)} %pad_maximum_fusion), channel_id=1, source_target_pairs={{0,4},{4,0},{8,12},{12,8},{16,20},{20,16},{24,28},{28,24},{1,5},{5... | collective-permute-start | bytes 1579016 | tf_op jit(solution)/shard_map/ppermute | solution.py:79
  12.7 5.1 %copy-start.27 = (f32[16]{0:T(128)}, f32[16]{0:T(128)S(1)}, u32[]{:S(2)}) copy-start(f32[16]{0:T(128)S(1)} %broadcast_select_fusion.7) | copy-start | bytes 196
  15.9 18.8 %copy-start.15 = (f32[1,16]{1,0:T(1,128)}, f32[1,16]{1,0:T(1,128)S(1)}, u32[]{:S(2)}) copy-start(f32[1,16]{1,0:T(1,128)S(1)} %get-tuple-element.16) | copy-start | bytes 196
  15.9 18.8 %copy-start.20 = (f32[1,16]{1,0:T(1,128)}, f32[1,16]{1,0:T(1,128)S(1)}, u32[]{:S(2)}) copy-start(f32[1,16]{1,0:T(1,128)S(1)} %get-tuple-element.53) | copy-start | bytes 196
  16.5 1.3 %copy-start.7 = (f32[16]{0:T(128)}, f32[16]{0:T(128)S(1)}, u32[]{:S(2)}) copy-start(f32[16]{0:T(128)S(1)} %get-tuple-element.37) | copy-start | bytes 196
  16.5 1.3 %copy-start.10 = (f32[16]{0:T(128)}, f32[16]{0:T(128)S(1)}, u32[]{:S(2)}) copy-start(f32[16]{0:T(128)S(1)} %get-tuple-element.54) | copy-start | bytes 196
  16.5 1.3 %copy-start.29 = (f32[16]{0:T(128)}, f32[16]{0:T(128)S(1)}, u32[]{:S(2)}) copy-start(f32[16]{0:T(128)S(1)} %broadcast_select_fusion.8) | copy-start | bytes 196
  18.0 4.4 %copy-start.36 = (f32[16]{0:T(128)S(1)}, f32[16]{0:T(128)}, u32[]{:S(2)}) copy-start(f32[16]{0:T(128)} %param.14) | copy-start | bytes 196
  18.9 15.2 %collective-permute-start.3 = (bf16[2056,128]{1,0:T(8,128)(2,1)}, bf16[2056,128]{1,0:T(8,128)(2,1)}, u32[]{:S(2)}, u32[]{:S(2)}) collective-permute-start(bf16[2056,128]{1,0:T(8,128)(2,1)} %pad_maximum_fusion.1), channel_id=1, source_target_pairs={{0,8},{4,12},{8,0},{12,4},{16,24},{20,28},{24,16},{28,20},{1,9},{5... | collective-permute-start | bytes 1579016 | tf_op jit(solution)/shard_map/ppermute | solution.py:79
  24.0 11.9 %copy-start.8 = (f32[16]{0:T(128)S(1)}, f32[16]{0:T(128)}, u32[]{:S(2)}) copy-start(f32[16]{0:T(128)} %copy-done.7) | copy-start | bytes 196
  24.0 11.9 %copy-start.11 = (f32[16]{0:T(128)S(1)}, f32[16]{0:T(128)}, u32[]{:S(2)}) copy-start(f32[16]{0:T(128)} %copy-done.10) | copy-start | bytes 196
  24.0 11.9 %copy-start.18 = (f32[16]{0:T(128)S(1)}, f32[16]{0:T(128)}, u32[]{:S(2)}) copy-start(f32[16]{0:T(128)} %get-tuple-element.36) | copy-start | bytes 196
  24.0 11.9 %copy-start.28 = (f32[16]{0:T(128)S(1)}, f32[16]{0:T(128)}, u32[]{:S(2)}) copy-start(f32[16]{0:T(128)} %copy-done.27) | copy-start | bytes 196
  24.1 11.9 %copy-start.30 = (f32[16]{0:T(128)S(1)}, f32[16]{0:T(128)}, u32[]{:S(2)}) copy-start(f32[16]{0:T(128)} %copy-done.29) | copy-start | bytes 196
  34.7 1.2 %copy-start.22 = (f32[1,16]{1,0:T(1,128)}, f32[1,16]{1,0:T(1,128)S(1)}, u32[]{:S(2)}) copy-start(f32[1,16]{1,0:T(1,128)S(1)} %get-tuple-element.24) | copy-start | bytes 196
  34.7 1.2 %copy-start.24 = (f32[1,16]{1,0:T(1,128)}, f32[1,16]{1,0:T(1,128)S(1)}, u32[]{:S(2)}) copy-start(f32[1,16]{1,0:T(1,128)S(1)} %get-tuple-element.51) | copy-start | bytes 196
  34.8 1.7 %copy-start.31 = (f32[16]{0:T(128)}, f32[16]{0:T(128)S(1)}, u32[]{:S(2)}) copy-start(f32[16]{0:T(128)S(1)} %broadcast_select_fusion.17) | copy-start | bytes 196
  36.0 3.2 %copy-start.13 = (f32[16,128]{1,0:T(8,128)S(1)}, f32[16,128]{1,0:T(8,128)}, u32[]{:S(2)}) copy-start(f32[16,128]{1,0:T(8,128)} %copy.38) | copy-start | bytes 24580
  36.0 3.2 %copy-start.17 = (f32[16,128]{1,0:T(8,128)S(1)}, f32[16,128]{1,0:T(8,128)}, u32[]{:S(2)}) copy-start(f32[16,128]{1,0:T(8,128)} %get-tuple-element.49) | copy-start | bytes 24580
  36.0 3.2 %copy-start.37 = (f32[16]{0:T(128)S(1)}, f32[16]{0:T(128)}, u32[]{:S(2)}) copy-start(f32[16]{0:T(128)} %param.14) | copy-start | bytes 196
  36.5 8.3 %collective-permute-start.4 = (bf16[1032,128]{1,0:T(8,128)(2,1)S(1)}, bf16[1032,128]{1,0:T(8,128)(2,1)S(1)}, u32[]{:S(2)}, u32[]{:S(2)}) collective-permute-start(bf16[1032,128]{1,0:T(8,128)(2,1)S(1)} %pad_maximum_fusion.2), channel_id=1, source_target_pairs={{0,16},{4,20},{8,24},{12,28},{16,0},{20,4},{24,8},{28,12},{1,17},{... | collective-permute-start | bytes 792584 | tf_op jit(solution)/shard_map/ppermute | solution.py:92
  39.2 5.7 %copy-start.34 = (f32[16]{0:T(128)S(1)}, f32[16]{0:T(128)}, u32[]{:S(2)}) copy-start(f32[16]{0:T(128)} %get-tuple-element.15) | copy-start | bytes 196
  44.8 0.7 %copy-start.3 = (bf16[1032,128]{1,0:T(8,128)(2,1)}, bf16[1032,128]{1,0:T(8,128)(2,1)S(1)}, u32[]{:S(2)}) copy-start(bf16[1032,128]{1,0:T(8,128)(2,1)S(1)} %collective-permute-done.4) | copy-start | bytes 792580
  44.9 1.6 %copy-start.21 = (f32[1,16]{1,0:T(1,128)S(1)}, f32[1,16]{1,0:T(1,128)}, u32[]{:S(2)}) copy-start(f32[1,16]{1,0:T(1,128)} %copy-done.20) | copy-start | bytes 196
  44.9 1.6 %copy-start.23 = (f32[1,16]{1,0:T(1,128)S(1)}, f32[1,16]{1,0:T(1,128)}, u32[]{:S(2)}) copy-start(f32[1,16]{1,0:T(1,128)} %copy-done.22) | copy-start | bytes 196
  44.9 1.6 %copy-start.16 = (f32[1,16]{1,0:T(1,128)S(1)}, f32[1,16]{1,0:T(1,128)}, u32[]{:S(2)}) copy-start(f32[1,16]{1,0:T(1,128)} %copy-done.15) | copy-start | bytes 196
  44.9 1.6 %copy-start.25 = (f32[1,16]{1,0:T(1,128)S(1)}, f32[1,16]{1,0:T(1,128)}, u32[]{:S(2)}) copy-start(f32[1,16]{1,0:T(1,128)} %copy-done.24) | copy-start | bytes 196
  44.9 2.2 %copy-start.9 = (f32[16]{0:T(128)S(1)}, f32[16]{0:T(128)}, u32[]{:S(2)}) copy-start(f32[16]{0:T(128)} %copy-done.7) | copy-start | bytes 196
  44.9 2.2 %copy-start.12 = (f32[16]{0:T(128)S(1)}, f32[16]{0:T(128)}, u32[]{:S(2)}) copy-start(f32[16]{0:T(128)} %copy-done.10) | copy-start | bytes 196
  44.9 2.2 %copy-start.19 = (f32[16]{0:T(128)S(1)}, f32[16]{0:T(128)}, u32[]{:S(2)}) copy-start(f32[16]{0:T(128)} %get-tuple-element.36) | copy-start | bytes 196
  44.9 2.2 %copy-start.32 = (f32[16]{0:T(128)S(1)}, f32[16]{0:T(128)}, u32[]{:S(2)}) copy-start(f32[16]{0:T(128)} %copy-done.31) | copy-start | bytes 196
  45.0 2.2 %copy-start.33 = (f32[16]{0:T(128)S(1)}, f32[16]{0:T(128)}, u32[]{:S(2)}) copy-start(f32[16]{0:T(128)} %get-tuple-element.52) | copy-start | bytes 196
  49.0 1.0 %copy-start.2 = (bf16[256,1024]{1,0:T(8,128)(2,1)S(1)}, bf16[256,1024]{1,0:T(8,128)(2,1)}, u32[]{:S(2)}) copy-start(bf16[256,1024]{1,0:T(8,128)(2,1)} %param.10) | copy-start | bytes 1572868
  50.0 4.0 %copy-start.26 = (f32[1024]{0:T(1024)S(1)}, f32[1024]{0:T(1024)}, u32[]{:S(2)}) copy-start(f32[1024]{0:T(1024)} %param.17) | copy-start | bytes 12292
  50.4 3.6 %collective-permute-start.5 = (f32[256]{0:T(256)S(1)}, f32[256]{0:T(256)S(1)}, u32[]{:S(2)}, u32[]{:S(2)}) collective-permute-start(f32[256]{0:T(256)S(1)} %get-tuple-element.13), channel_id=1, source_target_pairs={{0,1},{1,0},{2,3},{3,2},{4,5},{5,4},{6,7},{7,6},{8,9},{9,8},{10,11... | collective-permute-start | bytes 3080 | tf_op jit(solution)/shard_map/ppermute | solution.py:30

commit v4 on v3

--- a/solution.py
+++ b/solution.py
@@ -33,15 +33,15 @@
 LINK = jnp.bfloat16
 
 
-def pack(maps, decays):
+def pack(maps, decays, kind):
     flat = [m.reshape(-1, m.shape[-1]) for m in maps]
     lanes = flat[0].shape[1]
     rows = jnp.stack(decays)
-    high = rows.astype(LINK)
-    low = (rows - high.astype(jnp.float32)).astype(LINK)
+    high = rows.astype(kind)
+    low = (rows - high.astype(jnp.float32)).astype(kind)
     tail = jnp.concatenate([high, low], axis=0)
     tail = jnp.pad(tail, ((0, 8 - tail.shape[0]), (0, lanes - tail.shape[1])))
-    return jnp.concatenate([f.astype(LINK) for f in flat] + [tail], axis=0)
+    return jnp.concatenate([f.astype(kind) for f in flat] + [tail], axis=0)
 
 
 def unpack(message, count, shape):
@@ -54,29 +54,27 @@
     return maps, decays
 
 
-def butterfly_states(first_loc, second_loc, first_log, second_log, seq_pos, seq_count):
-    levels = seq_count.bit_length() - 1
-    assert 1 << levels == seq_count
-    shape = first_loc.shape
+def col(v):
+    return v[:, None, None]
+
+
+def butterfly_states(sub_f, sub_g, e_f, e_g, index, count, stride, seq_count):
+    levels = count.bit_length() - 1
+    assert 1 << levels == count
+    shape = sub_f.shape
     if levels == 0:
-        return jnp.zeros_like(first_loc), first_loc
-
-    def col(v):
-        return v[:, None, None]
-
+        return jnp.zeros_like(sub_f), sub_f
     ones = jnp.ones((shape[0],), jnp.float32)
     zeros = jnp.zeros((shape[0],), jnp.float32)
-    prefix = jnp.zeros_like(first_loc)
-    above = jnp.zeros_like(first_loc)
+    prefix = jnp.zeros_like(sub_f)
+    above = jnp.zeros_like(sub_f)
     e_pre, e_abv = ones, ones
-    sub_f, sub_g = first_loc, second_loc
-    e_f, e_g = jnp.exp(first_log), jnp.exp(second_log)
     for level in range(levels):
         size = 1 << level
-        lower = (seq_pos // size) % 2 == 0
-        pairs = [(i, i ^ size) for i in range(seq_count)]
+        lower = (index // size) % 2 == 0
+        pairs = [(i, i ^ (size * stride)) for i in range(seq_count)]
         if level < levels - 1:
-            got = lax.ppermute(pack((sub_f, sub_g), (e_f, e_g)), "seq", pairs)
+            got = lax.ppermute(pack((sub_f, sub_g), (e_f, e_g), LINK), "seq", pairs)
             (got_f, got_g), (p_f, p_g) = unpack(got, 2, shape)
             new_f = col(jnp.where(lower, p_f, ones)) * sub_f + col(jnp.where(lower, ones, e_f)) * got_f
             new_g = col(jnp.where(lower, ones, p_g)) * sub_g + col(jnp.where(lower, e_g, ones)) * got_g
@@ -89,7 +87,7 @@
         else:
             sent = col(jnp.where(lower, ones, e_g)) * sub_f + col(jnp.where(lower, zeros, ones)) * sub_g
             sent_e = jnp.where(lower, e_f, e_f * e_g)
-            got = lax.ppermute(pack((sent,), (sent_e,)), "seq", pairs)
+            got = lax.ppermute(pack((sent,), (sent_e,), LINK), "seq", pairs)
             (got_w,), (p_w,) = unpack(got, 1, shape)
             first_in = prefix + col(jnp.where(lower, zeros, e_pre)) * got_w
             second_in = (
@@ -98,6 +96,54 @@
                 + col(jnp.where(lower, e_abv, e_abv * e_f)) * got_w
             )
     return first_in, second_in
+
+
+def block_states(first_loc, second_loc, first_log, second_log, seq_pos, seq_count):
+    heads = first_loc.shape[0]
+    e1, e2 = jnp.exp(first_log), jnp.exp(second_log)
+    if seq_count % 2 or heads % 2:
+        return butterfly_states(first_loc, second_loc, e1, e2, seq_pos, seq_count, 1, seq_count)
+    half = heads // 2
+    core = seq_pos % 2
+    upper = core == 1
+    pairs = [(i, i ^ 1) for i in range(seq_count)]
+    got = lax.ppermute(pack((first_loc, second_loc), (e1, e2), jnp.float32), "seq", pairs)
+    (p1, p2), (q1, q2) = unpack(got, 2, first_loc.shape)
+    ones = jnp.ones((heads,), jnp.float32)
+    pair_f = col(jnp.where(upper, ones, q1)) * first_loc + col(jnp.where(upper, e1, ones)) * p1
+    pair_g = col(jnp.where(upper, q2, ones)) * second_loc + col(jnp.where(upper, ones, e2)) * p2
+    low_f = jnp.where(upper, p1, first_loc)
+    low_fe = jnp.where(upper, q1, e1)
+    high_g = jnp.where(upper, second_loc, p2)
+    high_ge = jnp.where(upper, e2, q2)
+
+    def mine(x):
+        return lax.dynamic_slice_in_dim(x, core * half, half, 0)
+
+    prefix, wrapped = butterfly_states(
+        mine(pair_f),
+        mine(pair_g),
+        mine(e1 * q1),
+        mine(e2 * q2),
+        seq_pos // 2,
+        seq_count // 2,
+        2,
+        seq_count,
+    )
+    after_low = col(mine(low_fe)) * prefix + mine(low_f)
+    before_high = col(mine(high_ge)) * wrapped + mine(high_g)
+    own = (jnp.where(upper, after_low, prefix), jnp.where(upper, wrapped, before_high))
+    other = (jnp.where(upper, prefix, after_low), jnp.where(upper, before_high, wrapped))
+    got_1, got_2 = lax.ppermute(other, "seq", pairs)
+
+    def whole(own_half, got_half):
+        return jnp.where(
+            upper,
+            jnp.concatenate([got_half, own_half], axis=0),
+            jnp.concatenate([own_half, got_half], axis=0),
+        )
+
+    return whole(own[0], got_1), whole(own[1], got_2)
 
 
 def on_device(
@@ -174,7 +220,7 @@
     second_out, second_cum, second_c, second_elem = local_block(
         lead_second, joined[half_rows:], step_size[half_rows:]
     )
-    first_in, second_in = butterfly_states(
+    first_in, second_in = block_states(
         first_elem[1], second_elem[1], first_cum[-1], second_cum[-1], seq_pos, seq_count
     )
     ssm_out = jnp.concatenate(

time: 55.5 us -> 50.5 us (0.910)
  waiting for transfers between devices: 18.1 us -> 9.24 us
  local copies, waits for them, and re-layouts: 6.46 us -> 11.4 us
  matrix products: 6.02 us -> 3.4 us
  other arithmetic: 10.1 us -> 11.4 us
  starting transfers between devices: 13.4 us -> 14 us
    ppermute x3 -> x5, waiting for transfers between devices: 16.2 us -> 7.24 us  [the longest x1 2.58 us: butterfly_states(): got = lax.ppermute(pack((sub_f, sub_g), (e_f, e_g), LINK), 'seq', pairs)]
    exp x4, local copies, waits for them, and re-layouts: 0.15 us -> 3.03 us  [finish_block(): total_out = partial_out + jnp.exp(log_cum)[:, :, None] * inter_out]
    select_n x5 -> x3, other arithmetic: 0.62 us -> 2.51 us  [the longest x1 1.42 us: block_states(): low_fe = jnp.where(upper, q1, e1)]
    dot_general x2, matrix products: 2.32 us -> 0.78 us  [finish_block(): jnp.einsum('tn,hpn->thp', c_rows.astype(jnp.float32), state_in, precision...]
    convert_element_type x3 -> x2, other arithmetic: 1.99 us -> 0.68 us  [unpack(): tail = message[count * rows:].astype(jnp.float32)]
    dot_general x2, matrix products: 2.99 us -> 1.92 us  [local_block(): jnp.einsum('hts,shp->thp', weights, inner_conv, preferred_element_type=jn...]
    convert_element_type x9 -> x7, other arithmetic: 0.81 us -> 1.82 us  [the longest x3 1.11 us: pack(): return jnp.concatenate([f.astype(kind) for f in flat] + [tail], axis=0)]
    concatenate x3, other arithmetic: 1.73 us -> 0.8 us  [pack(): return jnp.concatenate([f.astype(kind) for f in flat] + [tail], axis=0)]
  transfers between devices with their start and end apart: 6 -> 8, of which waited for: 4 -> 4; matrix products, arithmetic and copies ran while one was open for 11% -> 18% of each run, Pallas kernels for 0% -> 0%
where the time goes in v4:
time: 50.5 us; the launch traced here: 49.9 us
  starting transfers between devices  14 us (28%)
  local copies, waits for them, and re-layouts  11.4 us (23%)
  other arithmetic  11.4 us (23%)
  waiting for transfers between devices  9.24 us (18%)
  matrix products  3.4 us (7%)
  between operations  0.51 us (1%)
    exp x4, local copies, waits for them, and re-layouts, finish_block(): total_out = partial_out + jnp.exp(log_cum)[:, :, None] * inter_out  3.03 us
    ppermute x1, starting transfers between devices, extended_2(): low = lax.ppermute(tail, axis, forward)  3.03 us
    unnamed x48, local copies, waits for them, and re-layouts  3 us
    ppermute x1, starting transfers between devices, block_states(): lax.ppermute(pack((first_loc, second_loc), (e1, e2), jnp.float32), 'seq',...  2.63 us
    ppermute x1, waiting for transfers between devices, butterfly_states(): got = lax.ppermute(pack((sub_f, sub_g), (e_f, e_g), LINK), 'seq', pairs)  2.58 us
    ppermute x1, starting transfers between devices, butterfly_states(): got = lax.ppermute(pack((sent,), (sent_e,), LINK), 'seq', pairs)  2.53 us
    ppermute x1, waiting for transfers between devices, block_states(): lax.ppermute(pack((first_loc, second_loc), (e1, e2), jnp.float32), 'seq',...  2.42 us
    ppermute x1, starting transfers between devices, butterfly_states(): got = lax.ppermute(pack((sub_f, sub_g), (e_f, e_g), LINK), 'seq', pairs)  2.37 us
  transfers between devices with their start and end apart: 8, of which 4 were waited for; matrix products, arithmetic and copies ran while one was open for 18% of the time, Pallas kernels for 0%

profile of v4, /device:TPU:0, one launch (start us, length us, event | category | flops | bytes accessed | tf_op | source)
XLA Modules:
  0.0 49.9 jit_solution(805835867188795114)
XLA Ops:
  0.0 1.1 %constant_dynamic-update-slice_fusion.3 = bf16[256,1536]{1,0:T(8,128)(2,1)S(1)} fusion(bf16[256,1024]{1,0:T(8,128)(2,1)} %param.9), kind=kLoop, calls=%fused_computation.117 | loop fusion | bytes 1048576
  1.2 1.3 %collective-permute-start.1 = (bf16[3,1536]{1,0:T(4,128)(2,1)S(1)}, bf16[3,1536]{1,0:T(4,128)(2,1)S(1)}, u32[]{:S(2)}, u32[]{:S(2)}) collective-permute-start(bf16[3,1536]{1,0:T(4,128)(2,1)S(1)} %get-tuple-element.8), channel_id=1, source_target_pairs={{4,0},{8,4},{12,8},{16,12},{20,16},{24,20},{28,24},{5,1},{9,5},{13... | collective-permute-start | bytes 27656 | tf_op jit(solution)/shard_map/ppermute | solution.py:24
  2.5 3.0 %collective-permute-start = (bf16[3,1536]{1,0:T(4,128)(2,1)S(1)}, bf16[3,1536]{1,0:T(4,128)(2,1)S(1)}, u32[]{:S(2)}, u32[]{:S(2)}) collective-permute-start(bf16[3,1536]{1,0:T(4,128)(2,1)S(1)} %get-tuple-element.7), channel_id=1, source_target_pairs={{0,4},{4,8},{8,12},{12,16},{16,20},{20,24},{24,28},{1,5},{5,9},{9,... | collective-permute-start | bytes 27656 | tf_op jit(solution)/shard_map/ppermute | solution.py:23
  5.9 0.2 reduce_window_sum.17
  6.0 0.2 reduce_window_sum.18
  6.5 0.6 %slice_bitcast_fusion.1 = (f32[16,128]{1,0:T(8,128)}, f32[128,16]{0,1:T(8,128)S(1)}, f32[128,16]{0,1:T(8,128)S(1)}, f32[16,128]{1,0:T(8,128)}) fusion(f32[256,16]{0,1:T(8,128)S(1)} %compare_select_fusion, f32[128,16]{0,1:T(8,128)S(1)} %copy.34, f32[16]{0:T(128)S(1)} %get-tuple-element.67, f32[128,16]{0,1:T(8,128)S(1)} %copy.37, f32[16]{0:T(128)S(1)} %get-tuple-element.53), kind=kLoop, calls=%fused_computation.123 | loop fusion | flops 8192 | bytes 65664 | tf_op jit(solution)/shard_map/transpose | solution.py:198
  7.5 1.0 %multiply_convert_fusion.4 = (bf16[128,1536]{1,0:T(8,128)(2,1)S(1)}, bf16[128,1536]{1,0:T(8,128)(2,1)S(1)}) fusion(f32[131,1536]{1,0:T(8,128)S(1)} %maximum_convert_fusion, f32[1536]{0:T(1024)S(1)} %get-tuple-element.10, f32[1536]{0:T(1024)S(1)} %get-tuple-element.11, f32[1536]{0:T(1024)S(1)} %get-tuple-element.12, f32[1536]{0:T(1024)S(1)} %get-tuple-element.9, ...), kind=kLoop, calls=%fused_computation.34 | loop fusion | flops 4718592 | bytes 7102464 | tf_op jit(solution)/shard_map/convert_element_type | solution.py:188
  8.9 0.2 fusion.46
  9.1 0.2 fusion.48
  9.3 0.3 copy-done
  9.6 2.6 %collective-permute-start.2 = (f32[2056,128]{1,0:T(8,128)S(1)}, f32[2056,128]{1,0:T(8,128)}, u32[]{:S(2)}, u32[]{:S(2)}) collective-permute-start(f32[2056,128]{1,0:T(8,128)S(1)} %pad_maximum_fusion), channel_id=1, source_target_pairs={{0,4},{4,0},{8,12},{12,8},{16,20},{20,16},{24,28},{28,24},{1,5},{5... | collective-permute-start | bytes 3158024 | tf_op jit(solution)/shard_map/ppermute | solution.py:110
  12.2 2.4 %collective-permute-done.2 = f32[2056,128]{1,0:T(8,128)} collective-permute-done((f32[2056,128]{1,0:T(8,128)S(1)}, f32[2056,128]{1,0:T(8,128)}, u32[]{:S(2)}, u32[]{:S(2)}) %collective-permute-start.2) | collective-permute-done | bytes 1052704 | tf_op jit(solution)/shard_map/ppermute | solution.py:110
  14.7 1.4 %broadcast_select_fusion.13 = (f32[16]{0:T(128)}, f32[16]{0:T(128)S(1)}, f32[16]{0:T(128)}, f32[16]{0:T(128)S(1)}, f32[16]{0:T(128)S(1)}, /*index=5*/f32[16]{0:T(128)S(1)}, f32[16]{0:T(128)S(1)}, f32[16]{0:T(128)S(1)}) fusion(pred[]{:T(512)S(6)} %eq.16, f32[128,16]{1,0:T(8,128)S(1)} %reduce_window_sum.17, f32[2056,128]{1,0:T(8,128)} %collective-permute-done.2, ...), kind=kLoop, calls=%fused_computation.170 | loop fusion | flops 160 | bytes 897 | tf_op jit(solution)/shard_map/jit(_where)/select_n | solution.py:116
  16.1 0.7 %broadcast_select_fusion.4 = (f32[8]{0:T(128)}, f32[8]{0:T(128)S(1)}) fusion(pred[]{:T(512)S(6)} %eq.17, f32[16]{0:T(128)S(1)} %get-tuple-element.32, s32[]{:T(128)S(6)} %select_n.259), kind=kLoop, calls=%fused_computation.161 | loop fusion | flops 8 | bytes 101 | tf_op jit(solution)/shard_map/jit(_where)/select_n | solution.py:79
  16.8 0.6 %broadcast_select_fusion.2 = (f32[8]{0:T(128)}, f32[8]{0:T(128)S(1)}) fusion(pred[]{:T(512)S(6)} %eq.17, f32[16]{0:T(128)S(1)} %get-tuple-element.36, s32[]{:T(128)S(6)} %select_n.259), kind=kLoop, calls=%fused_computation.159 | loop fusion | flops 8 | bytes 101 | tf_op jit(solution)/shard_map/jit(_where)/select_n | solution.py:80
  17.7 0.2 copy-done.16
  18.0 1.3 %fusion.100 = (f32[1024,128]{1,0:T(8,128)S(1)}, f32[1024,128]{1,0:T(8,128)S(1)}) fusion(f32[2056,128]{1,0:T(8,128)} %collective-permute-done.2), kind=kLoop, calls=%fused_computation.198 | loop fusion | bytes 2097152 | tf_op jit(solution)/shard_map/slice | solution.py:50
  19.5 0.7 %pad_maximum_fusion.1 = bf16[1032,128]{1,0:T(8,128)(2,1)} fusion(bf16[8,128]{1,0:T(8,128)(2,1)S(1)} %fusion.83, bf16[512,128]{1,0:T(8,128)(2,1)S(1)} %bitcast.129, bf16[512,128]{1,0:T(8,128)(2,1)S(1)} %bitcast.128), kind=kLoop, calls=%fused_computation.73 | loop fusion | flops 792576 | bytes 528384 | tf_op jit(solution)/shard_map/concatenate | solution.py:44
  20.2 2.4 %collective-permute-start.3 = (bf16[1032,128]{1,0:T(8,128)(2,1)}, bf16[1032,128]{1,0:T(8,128)(2,1)}, u32[]{:S(2)}, u32[]{:S(2)}) collective-permute-start(bf16[1032,128]{1,0:T(8,128)(2,1)} %pad_maximum_fusion.1), channel_id=1, source_target_pairs={{0,8},{4,12},{8,0},{12,4},{16,24},{20,28},{24,16},{28,20},{1,9},{5... | collective-permute-start | bytes 792584 | tf_op jit(solution)/shard_map/ppermute | solution.py:77
  22.6 0.6 %exp.64 = f32[128,16]{1,0:T(8,128)} exponential(f32[128,16]{1,0:T(8,128)S(1)} %reduce_window_sum.17) | non-fusion elementwise | bytes 16384 | tf_op jit(solution)/shard_map/exp | solution.py:214
  23.2 0.6 %exp.73 = f32[128,16]{1,0:T(8,128)} exponential(f32[128,16]{1,0:T(8,128)S(1)} %reduce_window_sum.18) | non-fusion elementwise | bytes 16384 | tf_op jit(solution)/shard_map/exp | solution.py:214
  23.9 0.7 %copy.31 = f32[16,128]{1,0:T(8,128)} copy(f32[16,128]{0,1:T(8,128)S(1)} %bitcast.121) | data formatting | bytes 16384 | tf_op jit(solution)/shard_map/transpose | solution.py:196
  24.5 0.9 %copy.33 = f32[128,16]{0,1:T(8,128)S(1)} copy(f32[128,16]{1,0:T(8,128)} %exp.64) | data formatting | bytes 16384 | tf_op jit(solution)/shard_map/exp | solution.py:214
  25.4 0.7 %copy.38 = f32[16,128]{1,0:T(8,128)} copy(f32[16,128]{0,1:T(8,128)S(1)} %bitcast.120) | data formatting | bytes 16384 | tf_op jit(solution)/shard_map/transpose | solution.py:196
  26.1 0.9 %copy.40 = f32[128,16]{0,1:T(8,128)S(1)} copy(f32[128,16]{1,0:T(8,128)} %exp.73) | data formatting | bytes 16384 | tf_op jit(solution)/shard_map/exp | solution.py:214
  27.2 2.6 %collective-permute-done.3 = bf16[1032,128]{1,0:T(8,128)(2,1)} collective-permute-done((bf16[1032,128]{1,0:T(8,128)(2,1)}, bf16[1032,128]{1,0:T(8,128)(2,1)}, u32[]{:S(2)}, u32[]{:S(2)}) %collective-permute-start.3) | collective-permute-done | bytes 264224 | tf_op jit(solution)/shard_map/ppermute | solution.py:77
  29.8 0.7 %slice_convert_fusion.1 = f32[8,128]{1,0:T(8,128)S(1)} fusion(bf16[1032,128]{1,0:T(8,128)(2,1)} %collective-permute-done.3), kind=kLoop, calls=%fused_computation.147 | loop fusion | flops 1024 | bytes 6144 | tf_op jit(solution)/shard_map/convert_element_type | solution.py:52
  30.5 0.6 %broadcast_select_fusion.7 = (f32[8]{0:T(128)S(1)}, f32[1,8]{1,0:T(1,128)S(1)}) fusion(pred[]{:T(512)S(6)} %eq.19, f32[8]{0:T(128)} %copy-done.13, f32[1,8]{1,0:T(1,128)S(1)} %get-tuple-element.16, pred[]{:T(512)S(6)} %eq.17, f32[8,128]{1,0:T(8,128)S(1)} %slice_convert_fusion.1), kind=kLoop, calls=%fused_computation.164 | loop fusion | flops 40 | bytes 194 | tf_op jit(solution)/shard_map/jit(_where)/select_n | solution.py:96
  31.1 0.7 %convert_bitcast_fusion.1 = (bf16[1,8]{1,0:T(2,128)(2,1)S(1)}, f32[8]{0:T(128)S(1)}, f32[8]{0:T(128)S(1)}, f32[8]{0:T(128)S(1)}, f32[8]{0:T(128)S(1)}) fusion(f32[8]{0:T(128)} %copy-done.16, f32[1,8]{1,0:T(1,128)S(1)} %get-tuple-element.18, f32[8]{0:T(128)} %copy-done.13, f32[1,8]{1,0:T(1,128)S(1)} %get-tuple-element.16, pred[]{:T(512)S(6)} %eq.19, pred[]{:T(512)S(6)} %eq.17), kind=kLoop, calls=%fused_computation.182 | loop fusion | flops 64 | bytes 274 | tf_op jit(solution)/shard_map/convert_element_type | solution.py:40
  31.8 1.0 %fusion.103 = (bf16[512,128]{1,0:T(8,128)(2,1)S(1)}, bf16[512,128]{1,0:T(8,128)(2,1)S(1)}) fusion(bf16[1032,128]{1,0:T(8,128)(2,1)} %collective-permute-done.3), kind=kLoop, calls=%fused_computation.201 | loop fusion | bytes 524288 | tf_op jit(solution)/shard_map/slice | solution.py:50
  32.8 0.9 %fusion.43 = bf16[8,64,128]{2,1,0:T(8,128)(2,1)S(1)} fusion(bf16[8,64,128]{2,1,0:T(8,128)(2,1)S(1)} %bitcast.118, bf16[8,64,128]{2,1,0:T(8,128)(2,1)S(1)} %bitcast.116, f32[8,64,128]{2,1,0:T(8,128)S(1)} %get-tuple-element.26, f32[8]{0:T(128)} %get-tuple-element.21, f32[8]{0:T(128)S(1)} %get-tuple-element.65, f32[]{:T(128)S(6)} %select_n.271, ...), kind=kLoop, calls=%fused_computation.79 | loop fusion | flops 983040 | bytes 1179880 | tf_op jit(solution)/shard_map/convert_element_type | solution.py:44
  33.7 2.5 %collective-permute-start.4 = (bf16[520,128]{1,0:T(8,128)(2,1)S(1)}, bf16[520,128]{1,0:T(8,128)(2,1)S(1)}, u32[]{:S(2)}, u32[]{:S(2)}) collective-permute-start(bf16[520,128]{1,0:T(8,128)(2,1)S(1)} %pad_maximum_fusion.2), channel_id=1, source_target_pairs={{0,16},{4,20},{8,24},{12,28},{16,0},{20,4},{24,8},{28,12},{1,17},{... | collective-permute-start | bytes 399368 | tf_op jit(solution)/shard_map/ppermute | solution.py:90
  36.3 0.6 %fusion.2 = f32[128,16,64]{0,2,1:T(8,128)S(1)} fusion(bf16[128,16,64]{0,2,1:T(8,128)(2,1)S(1)} %bitcast.125, f32[16,128]{1,0:T(8,128)S(1)} %copy-done.12, f32[16,128]{1,0:T(8,128)S(1)} %copy-done.9, f32[128,128]{1,0:T(8,128)S(1)} %fusion.68, pred[128,128]{1,0:T(8,128)(4,1)S(1)} %iota_compare_fusion, f32[16]{0:T(128)S(1)} %copy-done.22), kind=kOutput, calls=%fused_computation.8 | convolution fusion | flops 35520512 | bytes 884800 | tf_op jit(solution)/shard_map/hts,shp->thp/dot_general | solution.py:199
  37.0 2.2 %collective-permute-done.4 = bf16[520,128]{1,0:T(8,128)(2,1)S(1)} collective-permute-done((bf16[520,128]{1,0:T(8,128)(2,1)S(1)}, bf16[520,128]{1,0:T(8,128)(2,1)S(1)}, u32[]{:S(2)}, u32[]{:S(2)}) %collective-permute-start.4) | collective-permute-done | bytes 133152 | tf_op jit(solution)/shard_map/ppermute | solution.py:90
  39.3 1.1 %fusion.55 = (f32[8,64,128]{2,1,0:T(8,128)S(1)}, f32[8,64,128]{2,1,0:T(8,128)S(1)}, f32[8,64,128]{2,1,0:T(8,128)}, f32[8,64,128]{2,1,0:T(8,128)}) fusion(f32[16,64,128]{2,1,0:T(8,128)S(1)} %fusion.48, s32[]{:T(128)S(6)} %select_n.259, f32[16,64,128]{2,1,0:T(8,128)S(1)} %bitcast.115, bf16[8,64,128]{2,1,0:T(8,128)(2,1)S(1)} %bitcast.126, ...), kind=kLoop, calls=%fused_computation.93 | loop fusion | flops 1572864 | bytes 2752749 | tf_op jit(solution)/shard_map/jit(_where)/select_n | solution.py:136
  40.5 0.5 %collective-permute-start.6 = (f32[8,64,128]{2,1,0:T(8,128)}, f32[8,64,128]{2,1,0:T(8,128)S(1)}, u32[]{:S(2)}, u32[]{:S(2)}) collective-permute-start(f32[8,64,128]{2,1,0:T(8,128)} %get-tuple-element.48), channel_id=1, source_target_pairs={{0,4},{4,0},{8,12},{12,8},{16,20},{20,16},{24,28},{28,24},{1,5},{5... | collective-permute-start | bytes 786440 | tf_op jit(solution)/shard_map/ppermute | solution.py:137
  41.1 1.4 %fusion.3 = f32[128,16,64]{0,2,1:T(8,128)} fusion(bf16[128,16,64]{0,2,1:T(8,128)(2,1)S(1)} %bitcast.123, f32[16,128]{1,0:T(8,128)S(1)} %copy-done.11, f32[16,128]{1,0:T(8,128)S(1)} %copy-done.8, f32[128,128]{1,0:T(8,128)S(1)} %fusion.63, pred[128,128]{1,0:T(8,128)(4,1)S(1)} %iota_compare_fusion, f32[16]{0:T(128)S(1)} %copy-done.22), kind=kOutput, calls=%fused_computation.9 | convolution fusion | flops 35520512 | bytes 884800 | tf_op jit(solution)/shard_map/hts,shp->thp/dot_general | solution.py:199
  42.4 0.4 fusion.1
  42.8 0.2 copy.41
  43.0 0.3 copy-done.2
  43.4 0.5 %copy-done.4 = f32[128,16,64]{0,2,1:T(8,128)S(1)} copy-done((f32[128,16,64]{0,2,1:T(8,128)S(1)}, f32[128,16,64]{0,2,1:T(8,128)}, u32[]{:S(2)}) %copy-start.4) | copy-done | bytes 524312
  43.9 0.4 fusion
  44.3 0.2 copy.42
  44.5 0.4 copy-done.3
  44.9 0.4 multiply_reduce_fusion
  45.3 1.6 %collective-permute-start.7 = (f32[256]{0:T(256)S(1)}, f32[256]{0:T(256)S(1)}, u32[]{:S(2)}, u32[]{:S(2)}) collective-permute-start(f32[256]{0:T(256)S(1)} %get-tuple-element.13), channel_id=1, source_target_pairs={{0,1},{1,0},{2,3},{3,2},{4,5},{5,4},{6,7},{7,6},{8,9},{9,8},{10,11... | collective-permute-start | bytes 3080 | tf_op jit(solution)/shard_map/ppermute | solution.py:30
  47.0 2.0 %collective-permute-done.7 = f32[256]{0:T(256)S(1)} collective-permute-done((f32[256]{0:T(256)S(1)}, f32[256]{0:T(256)S(1)}, u32[]{:S(2)}, u32[]{:S(2)}) %collective-permute-start.7) | collective-permute-done | bytes 1056 | tf_op jit(solution)/shard_map/ppermute | solution.py:30
  49.0 1.0 %multiply_convert_fusion = bf16[256,1024]{1,0:T(8,128)(2,1)} fusion(f32[256,1024]{1,0:T(8,128)S(1)} %get-tuple-element.14, f32[1024]{0:T(1024)S(1)} %copy-done.15, f32[256]{0:T(256)S(1)} %add_rsqrt_fusion), kind=kLoop, calls=%fused_computation.15 | loop fusion | flops 786432 | bytes 1577984 | tf_op jit(solution)/shard_map/convert_element_type | solution.py:238
  (91 shorter events, 2.5 us)
Async XLA Ops:
  0.0 1.1 %copy-start.5 = (bf16[256,512]{1,0:T(8,128)(2,1)S(1)}, bf16[256,512]{1,0:T(8,128)(2,1)}, u32[]{:S(2)}) copy-start(bf16[256,512]{1,0:T(8,128)(2,1)} %param.11) | copy-start | bytes 786436
  0.0 5.5 %copy-start.6 = (f32[256,16]{0,1:T(8,128)S(1)}, f32[256,16]{0,1:T(8,128)}, u32[]{:S(2)}) copy-start(f32[256,16]{0,1:T(8,128)} %param.12) | copy-start | bytes 49156
  0.0 5.6 %copy-start.19 = (f32[16]{0:T(128)S(1)}, f32[16]{0:T(128)}, u32[]{:S(2)}) copy-start(f32[16]{0:T(128)} %param.13) | copy-start | bytes 196
  1.2 6.0 %collective-permute-start.1 = (bf16[3,1536]{1,0:T(4,128)(2,1)S(1)}, bf16[3,1536]{1,0:T(4,128)(2,1)S(1)}, u32[]{:S(2)}, u32[]{:S(2)}) collective-permute-start(bf16[3,1536]{1,0:T(4,128)(2,1)S(1)} %get-tuple-element.8), channel_id=1, source_target_pairs={{4,0},{8,4},{12,8},{16,12},{20,16},{24,20},{28,24},{5,1},{9,5},{13... | collective-permute-start | bytes 27656 | tf_op jit(solution)/shard_map/ppermute | solution.py:24
  2.5 4.9 %collective-permute-start = (bf16[3,1536]{1,0:T(4,128)(2,1)S(1)}, bf16[3,1536]{1,0:T(4,128)(2,1)S(1)}, u32[]{:S(2)}, u32[]{:S(2)}) collective-permute-start(bf16[3,1536]{1,0:T(4,128)(2,1)S(1)} %get-tuple-element.7), channel_id=1, source_target_pairs={{0,4},{4,8},{8,12},{12,16},{16,20},{20,24},{24,28},{1,5},{5,9},{9,... | collective-permute-start | bytes 27656 | tf_op jit(solution)/shard_map/ppermute | solution.py:23
  5.6 0.8 %copy-start.7 = (f32[4,1024]{1,0:T(4,128)S(1)}, f32[4,1024]{1,0:T(4,128)}, u32[]{:S(2)}) copy-start(f32[4,1024]{1,0:T(4,128)} %param.15) | copy-start | bytes 49156
  5.8 0.7 %copy-start.10 = (f32[4,512]{1,0:T(4,128)S(1)}, f32[4,512]{1,0:T(4,128)}, u32[]{:S(2)}) copy-start(f32[4,512]{1,0:T(4,128)} %param.16) | copy-start | bytes 24580
  8.8 0.7 %copy-start = (bf16[128,1024]{0,1:T(8,128)(2,1)}, bf16[128,1024]{0,1:T(8,128)(2,1)S(1)}, u32[]{:S(2)}) copy-start(bf16[128,1024]{0,1:T(8,128)(2,1)S(1)} %copy.29) | copy-start | bytes 786436
  9.6 5.1 %collective-permute-start.2 = (f32[2056,128]{1,0:T(8,128)S(1)}, f32[2056,128]{1,0:T(8,128)}, u32[]{:S(2)}, u32[]{:S(2)}) collective-permute-start(f32[2056,128]{1,0:T(8,128)S(1)} %pad_maximum_fusion), channel_id=1, source_target_pairs={{0,4},{4,0},{8,12},{12,8},{16,20},{20,16},{24,28},{28,24},{1,5},{5... | collective-permute-start | bytes 3158024 | tf_op jit(solution)/shard_map/ppermute | solution.py:110
  16.8 1.0 %copy-start.13 = (f32[8]{0:T(128)}, f32[8]{0:T(128)S(1)}, u32[]{:S(2)}) copy-start(f32[8]{0:T(128)S(1)} %get-tuple-element.20) | copy-start | bytes 100
  17.4 0.6 %copy-start.16 = (f32[8]{0:T(128)}, f32[8]{0:T(128)S(1)}, u32[]{:S(2)}) copy-start(f32[8]{0:T(128)S(1)} %get-tuple-element.22) | copy-start | bytes 100
  17.7 1.7 %copy-start.17 = (f32[8]{0:T(128)}, f32[8]{0:T(128)S(1)}, u32[]{:S(2)}) copy-start(f32[8]{0:T(128)S(1)} %dynamic-slice.2) | copy-start | bytes 100
  18.0 1.4 %copy-start.18 = (f32[8]{0:T(128)}, f32[8]{0:T(128)S(1)}, u32[]{:S(2)}) copy-start(f32[8]{0:T(128)S(1)} %dynamic-slice.3) | copy-start | bytes 100
  20.2 9.6 %collective-permute-start.3 = (bf16[1032,128]{1,0:T(8,128)(2,1)}, bf16[1032,128]{1,0:T(8,128)(2,1)}, u32[]{:S(2)}, u32[]{:S(2)}) collective-permute-start(bf16[1032,128]{1,0:T(8,128)(2,1)} %pad_maximum_fusion.1), channel_id=1, source_target_pairs={{0,8},{4,12},{8,0},{12,4},{16,24},{20,28},{24,16},{28,20},{1,9},{5... | collective-permute-start | bytes 792584 | tf_op jit(solution)/shard_map/ppermute | solution.py:77
  27.0 9.2 %copy-start.1 = (bf16[128,1024]{0,1:T(8,128)(2,1)S(1)}, bf16[128,1024]{0,1:T(8,128)(2,1)}, u32[]{:S(2)}) copy-start(bf16[128,1024]{0,1:T(8,128)(2,1)} %copy-done) | copy-start | bytes 786436
  27.0 9.2 %copy-start.9 = (f32[16,128]{1,0:T(8,128)S(1)}, f32[16,128]{1,0:T(8,128)}, u32[]{:S(2)}) copy-start(f32[16,128]{1,0:T(8,128)} %copy.31) | copy-start | bytes 24580
  27.1 9.2 %copy-start.12 = (f32[16,128]{1,0:T(8,128)S(1)}, f32[16,128]{1,0:T(8,128)}, u32[]{:S(2)}) copy-start(f32[16,128]{1,0:T(8,128)} %get-tuple-element.59) | copy-start | bytes 24580
  27.1 9.2 %copy-start.22 = (f32[16]{0:T(128)S(1)}, f32[16]{0:T(128)}, u32[]{:S(2)}) copy-start(f32[16]{0:T(128)} %param.14) | copy-start | bytes 196
  33.7 5.5 %collective-permute-start.4 = (bf16[520,128]{1,0:T(8,128)(2,1)S(1)}, bf16[520,128]{1,0:T(8,128)(2,1)S(1)}, u32[]{:S(2)}, u32[]{:S(2)}) collective-permute-start(bf16[520,128]{1,0:T(8,128)(2,1)S(1)} %pad_maximum_fusion.2), channel_id=1, source_target_pairs={{0,16},{4,20},{8,24},{12,28},{16,0},{20,4},{24,8},{28,12},{1,17},{... | collective-permute-start | bytes 399368 | tf_op jit(solution)/shard_map/ppermute | solution.py:90
  36.2 0.6 %copy-start.21 = (f32[16]{0:T(128)S(1)}, f32[16]{0:T(128)}, u32[]{:S(2)}) copy-start(f32[16]{0:T(128)} %get-tuple-element.31) | copy-start | bytes 196
  36.3 0.7 %copy-start.20 = (f32[16]{0:T(128)S(1)}, f32[16]{0:T(128)}, u32[]{:S(2)}) copy-start(f32[16]{0:T(128)} %get-tuple-element.35) | copy-start | bytes 196
  36.3 3.0 %copy-start.14 = (f32[8]{0:T(128)S(1)}, f32[8]{0:T(128)}, u32[]{:S(2)}) copy-start(f32[8]{0:T(128)} %get-tuple-element.19) | copy-start | bytes 100
  39.3 1.8 %copy-start.8 = (f32[16,128]{1,0:T(8,128)S(1)}, f32[16,128]{1,0:T(8,128)}, u32[]{:S(2)}) copy-start(f32[16,128]{1,0:T(8,128)} %copy.38) | copy-start | bytes 24580
  39.3 1.8 %copy-start.11 = (f32[16,128]{1,0:T(8,128)S(1)}, f32[16,128]{1,0:T(8,128)}, u32[]{:S(2)}) copy-start(f32[16,128]{1,0:T(8,128)} %get-tuple-element.62) | copy-start | bytes 24580
  40.4 2.0 %collective-permute-start.5 = (f32[8,64,128]{2,1,0:T(8,128)S(1)}, f32[8,64,128]{2,1,0:T(8,128)S(1)}, u32[]{:S(2)}, u32[]{:S(2)}) collective-permute-start(f32[8,64,128]{2,1,0:T(8,128)S(1)} %get-tuple-element.29), channel_id=1, source_target_pairs={{0,4},{4,0},{8,12},{12,8},{16,20},{20,16},{24,28},{28,24},{1,5},{5... | collective-permute-start | bytes 786440 | tf_op jit(solution)/shard_map/ppermute | solution.py:137
  40.5 2.5 %collective-permute-start.6 = (f32[8,64,128]{2,1,0:T(8,128)}, f32[8,64,128]{2,1,0:T(8,128)S(1)}, u32[]{:S(2)}, u32[]{:S(2)}) collective-permute-start(f32[8,64,128]{2,1,0:T(8,128)} %get-tuple-element.48), channel_id=1, source_target_pairs={{0,4},{4,0},{8,12},{12,8},{16,20},{20,16},{24,28},{28,24},{1,5},{5... | collective-permute-start | bytes 786440 | tf_op jit(solution)/shard_map/ppermute | solution.py:137
  42.4 1.0 %copy-start.2 = (f32[8,64,128]{2,1,0:T(8,128)S(1)}, f32[8,64,128]{2,1,0:T(8,128)}, u32[]{:S(2)}) copy-start(f32[8,64,128]{2,1,0:T(8,128)} %get-tuple-element.47) | copy-start | bytes 786436
  42.8 1.1 %copy-start.4 = (f32[128,16,64]{0,2,1:T(8,128)S(1)}, f32[128,16,64]{0,2,1:T(8,128)}, u32[]{:S(2)}) copy-start(f32[128,16,64]{0,2,1:T(8,128)} %fusion.3) | copy-start | bytes 1572868
  43.9 1.0 %copy-start.3 = (bf16[256,1024]{1,0:T(8,128)(2,1)S(1)}, bf16[256,1024]{1,0:T(8,128)(2,1)}, u32[]{:S(2)}) copy-start(bf16[256,1024]{1,0:T(8,128)(2,1)} %param.10) | copy-start | bytes 1572868
  44.9 4.0 %copy-start.15 = (f32[1024]{0:T(1024)S(1)}, f32[1024]{0:T(1024)}, u32[]{:S(2)}) copy-start(f32[1024]{0:T(1024)} %param.17) | copy-start | bytes 12292
  45.3 3.6 %collective-permute-start.7 = (f32[256]{0:T(256)S(1)}, f32[256]{0:T(256)S(1)}, u32[]{:S(2)}, u32[]{:S(2)}) collective-permute-start(f32[256]{0:T(256)S(1)} %get-tuple-element.13), channel_id=1, source_target_pairs={{0,1},{1,0},{2,3},{3,2},{4,5},{5,4},{6,7},{7,6},{8,9},{9,8},{10,11... | collective-permute-start | bytes 3080 | tf_op jit(solution)/shard_map/ppermute | solution.py:30

commit v5 on v4

--- a/solution.py
+++ b/solution.py
@@ -1,6 +1,8 @@
 import jax
 import jax.numpy as jnp
 from jax import lax
+from jax.experimental import pallas as pl
+from jax.experimental.pallas import tpu as pltpu
 from jax.sharding import PartitionSpec as P
 
 HEAD_SIZE = 64
@@ -146,6 +148,177 @@
     return whole(own[0], got_1), whole(own[1], got_2)
 
 
+class Mix:
+    def __init__(self, heads):
+        self.heads = heads
+        self.arrays = []
+        self.views = []
+
+    def view(self, array, offset):
+        for index, known in enumerate(self.arrays):
+            if known is array:
+                break
+        else:
+            self.arrays.append(array)
+            index = len(self.arrays) - 1
+        self.views.append((index, offset))
+        return [(len(self.views) - 1, jnp.ones((self.heads,), jnp.float32))]
+
+    def run(self, logical, out_arrays):
+        heads = self.heads
+        coefs, layout = [], []
+        for terms, dests in logical:
+            rows = []
+            for view, coef in terms:
+                rows.append((view, len(coefs)))
+                coefs.append(coef)
+            layout.append((rows, dests))
+        table = jnp.stack(coefs).reshape(-1)
+        offsets = jnp.stack([jnp.asarray(off, jnp.int32) for _, off in self.views])
+        inner = self.arrays[0].shape[1:]
+        views = self.views
+        count = len(self.arrays)
+
+        def kernel(table_ref, off_ref, *refs):
+            ins, outs = refs[:count], refs[count:]
+            for h in range(heads):
+                cache = {}
+                for rows, dests in layout:
+                    acc = None
+                    for view, row in rows:
+                        if view not in cache:
+                            array, _ = views[view]
+                            cache[view] = ins[array][off_ref[view] + h].astype(jnp.float32)
+                        term = table_ref[row * heads + h] * cache[view]
+                        acc = term if acc is None else acc + term
+                    for out, block in dests:
+                        outs[out][block * heads + h] = acc.astype(outs[out].dtype)
+
+        slab = heads * inner[0] * inner[1]
+        moved = sum(a.size * a.dtype.itemsize for a in self.arrays)
+        moved += sum(b * slab * jnp.dtype(d).itemsize for d, b in out_arrays)
+        smem = pl.BlockSpec(memory_space=pltpu.SMEM)
+        vmem = pl.BlockSpec(memory_space=pltpu.VMEM)
+        return pl.pallas_call(
+            kernel,
+            out_shape=[jax.ShapeDtypeStruct((b * heads, *inner), d) for d, b in out_arrays],
+            in_specs=[smem, smem] + [vmem] * count,
+            out_specs=[vmem] * len(out_arrays),
+            cost_estimate=pl.CostEstimate(
+                flops=2 * len(coefs) * slab, bytes_accessed=moved, transcendentals=0
+            ),
+        )(table, offsets, *self.arrays)
+
+
+def scale(terms, coef):
+    return [(view, c * coef) for view, c in terms]
+
+
+def next_message(f_terms, g_terms, e_f, e_g, lower, last):
+    if not last:
+        return [f_terms, g_terms], jnp.stack([e_f, e_g])
+    one = jnp.ones_like(e_f)
+    sent = scale(f_terms, jnp.where(lower, one, e_g)) + scale(g_terms, jnp.where(lower, 0.0 * one, one))
+    return [sent], jnp.stack([jnp.where(lower, e_f, e_f * e_g)])
+
+
+def kernel_states(first_loc, second_loc, first_log, second_log, seq_pos, seq_count):
+    heads = first_loc.shape[0]
+    half = heads // 2
+    units = seq_count // 2
+    levels = max(units, 1).bit_length() - 1
+    if seq_count % 2 or heads % 2 or levels < 1 or (1 << levels) != units:
+        return block_states(first_loc, second_loc, first_log, second_log, seq_pos, seq_count)
+    f32 = jnp.float32
+    e1, e2 = jnp.exp(first_log), jnp.exp(second_log)
+    core = seq_pos % 2
+    upper = core == 1
+    up = upper.astype(f32)
+    unit = seq_pos // 2
+    one = jnp.ones((half,), f32)
+    pairs = [(i, i ^ 1) for i in range(seq_count)]
+    p1, p2, got_e = lax.ppermute((first_loc, second_loc, jnp.stack([e1, e2])), "seq", pairs)
+
+    def mine(v):
+        return lax.dynamic_slice_in_dim(v, core * half, half)
+
+    e1h, e2h, q1h, q2h = mine(e1), mine(e2), mine(got_e[0]), mine(got_e[1])
+    mix = Mix(half)
+    v_p1, v_p2 = mix.view(p1, core * half), mix.view(p2, core * half)
+    v_l1, v_l2 = mix.view(first_loc, core * half), mix.view(second_loc, core * half)
+    f_terms = scale(v_l1, jnp.where(upper, one, q1h)) + scale(v_p1, jnp.where(upper, e1h, one))
+    g_terms = scale(v_l2, jnp.where(upper, q2h, one)) + scale(v_p2, jnp.where(upper, one, e2h))
+    low_terms = scale(v_p1, up * one) + scale(v_l1, (1 - up) * one)
+    high_terms = scale(v_l2, up * one) + scale(v_p2, (1 - up) * one)
+    e_f, e_g = e1h * q1h, e2h * q2h
+    low_fe = jnp.where(upper, q1h, e1h)
+    high_ge = jnp.where(upper, e2h, q2h)
+    lower = unit % 2 == 0
+    msg_terms, msg_e = next_message(f_terms, g_terms, e_f, e_g, lower, levels == 1)
+    logical = [(f_terms, [(0, 0)]), (g_terms, [(0, 1)]), (low_terms, [(1, 0)]), (high_terms, [(1, 1)])]
+    logical += [(t, [(2, b)]) for b, t in enumerate(msg_terms)]
+    state, edges, msg = mix.run(logical, [(f32, 2), (f32, 2), (LINK, len(msg_terms))])
+    zero_h = jnp.zeros((half,), f32)
+    e_pre, e_abv = one, one
+    have_acc = False
+    for level in range(levels):
+        size = 1 << level
+        lower = (unit // size) % 2 == 0
+        last = level == levels - 1
+        pairs = [(i, i ^ (2 * size)) for i in range(seq_count)]
+        got, got_e = lax.ppermute((msg, msg_e), "seq", pairs)
+        mix = Mix(half)
+        v_f, v_g = mix.view(state, 0), mix.view(state, half)
+        if have_acc:
+            v_pre, v_abv = mix.view(acc, 0), mix.view(acc, half)
+        else:
+            v_pre, v_abv = [], []
+        if not last:
+            p_f, p_g = got_e[0], got_e[1]
+            w_f, w_g = mix.view(got, 0), mix.view(got, half)
+            f_terms = scale(v_f, jnp.where(lower, p_f, one)) + scale(w_f, jnp.where(lower, one, e_f))
+            g_terms = scale(v_g, jnp.where(lower, one, p_g)) + scale(w_g, jnp.where(lower, e_g, one))
+            abv_terms = v_abv + scale(w_g, jnp.where(lower, e_abv, zero_h))
+            pre_terms = v_pre + scale(w_f, jnp.where(lower, zero_h, e_pre))
+            e_abv = jnp.where(lower, e_abv * p_g, e_abv)
+            e_pre = jnp.where(lower, e_pre, e_pre * p_f)
+            e_f, e_g = e_f * p_f, e_g * p_g
+            next_lower = (unit // (2 * size)) % 2 == 0
+            msg_terms, msg_e = next_message(f_terms, g_terms, e_f, e_g, next_lower, level + 1 == levels - 1)
+            logical = [(f_terms, [(0, 0)]), (g_terms, [(0, 1)])]
+            logical += [(pre_terms, [(1, 0)]), (abv_terms, [(1, 1)])]
+            logical += [(t, [(2, b)]) for b, t in enumerate(msg_terms)]
+            state, acc, msg = mix.run(logical, [(f32, 2), (f32, 2), (LINK, len(msg_terms))])
+            have_acc = True
+        else:
+            p_w = got_e[0]
+            w = mix.view(got, 0)
+            v_low, v_high = mix.view(edges, 0), mix.view(edges, half)
+            first_terms = v_pre + scale(w, jnp.where(lower, zero_h, e_pre))
+            second_terms = (
+                v_abv
+                + scale(v_f, jnp.where(lower, e_abv * p_w, e_abv))
+                + scale(w, jnp.where(lower, e_abv, e_abv * e_f))
+            )
+            own_first = scale(first_terms, jnp.where(upper, low_fe, one)) + scale(v_low, up * one)
+            own_second = scale(second_terms, jnp.where(upper, one, high_ge)) + scale(v_high, (1 - up) * one)
+            other_first = scale(first_terms, jnp.where(upper, one, low_fe)) + scale(v_low, (1 - up) * one)
+            other_second = scale(second_terms, jnp.where(upper, high_ge, one)) + scale(v_high, up * one)
+            logical = [(own_first, [(0, 0)]), (own_second, [(0, 1)])]
+            logical += [(other_first, [(1, 0)]), (other_second, [(1, 1)])]
+            own, other = mix.run(logical, [(f32, 2), (f32, 2)])
+    swapped = lax.ppermute(other, "seq", [(i, i ^ 1) for i in range(seq_count)])
+
+    def whole(own_half, got_half):
+        return jnp.where(
+            upper,
+            jnp.concatenate([got_half, own_half], axis=0),
+            jnp.concatenate([own_half, got_half], axis=0),
+        )
+
+    return whole(own[:half], swapped[:half]), whole(own[half:], swapped[half:])
+
+
 def on_device(
     inner_rows,
     gate_rows,
@@ -220,7 +393,7 @@
     second_out, second_cum, second_c, second_elem = local_block(
         lead_second, joined[half_rows:], step_size[half_rows:]
     )
-    first_in, second_in = block_states(
+    first_in, second_in = kernel_states(
         first_elem[1], second_elem[1], first_cum[-1], second_cum[-1], seq_pos, seq_count
     )
     ssm_out = jnp.concatenate(

time: 50.5 us -> 60.7 us (1.20)
  Pallas kernels: 0 us -> 7.51 us
  other arithmetic: 11.4 us -> 6.25 us
  local copies, waits for them, and re-layouts: 11.4 us -> 15.6 us
  waiting for transfers between devices: 9.24 us -> 12.8 us
  matrix products: 3.4 us -> 2.61 us
  starting transfers between devices: 14 us -> 14.7 us
    pallas_call x0 -> x3, Pallas kernels: none -> 7.51 us  [run(): pl.pallas_call(kernel, out_shape=[jax.ShapeDtypeStruct((b * heads, *inner...]
    unnamed x48 -> x88, local copies, waits for them, and re-layouts: 3 us -> 9.99 us
    select_n x7 -> x2, other arithmetic: 4.43 us -> 0.15 us  [the longest x1 0.08 us: kernel_states(): jnp.where(upper, q2h, one)]
    ppermute x5 -> x8, waiting for transfers between devices: 7.24 us -> 10.8 us  [the longest x4 10.4 us: kernel_states(): got, got_e = lax.ppermute((msg, msg_e), 'seq', pairs)]
    exp x4, local copies, waits for them, and re-layouts: 3.03 us -> 0.13 us  [finish_block(): total_out = partial_out + jnp.exp(log_cum)[:, :, None] * inter_out]
    convert_element_type x9 -> x0, other arithmetic: 2.49 us -> none  [the longest x3 1.11 us: pack(): return jnp.concatenate([f.astype(kind) for f in flat] + [tail], axis=0)]
    slice x3, local copies, waits for them, and re-layouts: 2.27 us -> 0.08 us  [the longest x1 0.04 us: kernel_states(): swapped[:half]]
    reshape x0 -> x3, local copies, waits for them, and re-layouts: none -> 1.96 us  [run(): table = jnp.stack(coefs).reshape(-1)]
  transfers between devices with their start and end apart: 8 -> 11, of which waited for: 4 -> 5; matrix products, arithmetic and copies ran while one was open for 18% -> 16% of each run, Pallas kernels for 0% -> 0%
where the time goes in v5:
time: 60.7 us; the launch traced here: 60.1 us
  local copies, waits for them, and re-layouts  15.6 us (26%)
  starting transfers between devices  14.7 us (24%)
  waiting for transfers between devices  12.8 us (21%)
  Pallas kernels  7.51 us (12%)
  other arithmetic  6.25 us (10%)
  matrix products  2.61 us (4%)
  between operations  0.65 us (1%)
    ppermute x4, waiting for transfers between devices, kernel_states(): got, got_e = lax.ppermute((msg, msg_e), 'seq', pairs)  10.4 us
    unnamed x88, local copies, waits for them, and re-layouts  9.99 us
    pallas_call x3, Pallas kernels, run(): pl.pallas_call(kernel, out_shape=[jax.ShapeDtypeStruct((b * heads, *inner...  7.51 us
    ppermute x4, starting transfers between devices, kernel_states(): got, got_e = lax.ppermute((msg, msg_e), 'seq', pairs)  5.96 us
    ppermute x1, starting transfers between devices, extended_2(): low = lax.ppermute(tail, axis, forward)  3.03 us
    ppermute x3, starting transfers between devices, kernel_states(): lax.ppermute((first_loc, second_loc, jnp.stack([e1, e2])), 'seq', pairs)  2.79 us
    ppermute x1, waiting for transfers between devices, partner(): lax.ppermute(array, axis, [(i, i ^ 1 << stride) for i in range(lax.axis_s...  1.99 us
    reshape x3, local copies, waits for them, and re-layouts, run(): table = jnp.stack(coefs).reshape(-1)  1.96 us
  transfers between devices with their start and end apart: 11, of which 5 were waited for; matrix products, arithmetic and copies ran while one was open for 16% of the time, Pallas kernels for 0%

profile of v5, /device:TPU:0, one launch (start us, length us, event | category | flops | bytes accessed | tf_op | source)
XLA Modules:
  0.0 60.1 jit_solution(6777068940717209321)
XLA Ops:
  0.0 1.1 %constant_dynamic-update-slice_fusion.3 = bf16[256,1536]{1,0:T(8,128)(2,1)S(1)} fusion(bf16[256,1024]{1,0:T(8,128)(2,1)} %param.9), kind=kLoop, calls=%fused_computation.92 | loop fusion | bytes 1048576
  1.2 1.3 %collective-permute-start.5 = (bf16[3,1536]{1,0:T(4,128)(2,1)S(1)}, bf16[3,1536]{1,0:T(4,128)(2,1)S(1)}, u32[]{:S(2)}, u32[]{:S(2)}) collective-permute-start(bf16[3,1536]{1,0:T(4,128)(2,1)S(1)} %get-tuple-element.16), channel_id=1, source_target_pairs={{4,0},{8,4},{12,8},{16,12},{20,16},{24,20},{28,24},{5,1},{9,5},{13... | collective-permute-start | bytes 27656 | tf_op jit(solution)/shard_map/ppermute | solution.py:26
  2.5 3.0 %collective-permute-start = (bf16[3,1536]{1,0:T(4,128)(2,1)S(1)}, bf16[3,1536]{1,0:T(4,128)(2,1)S(1)}, u32[]{:S(2)}, u32[]{:S(2)}) collective-permute-start(bf16[3,1536]{1,0:T(4,128)(2,1)S(1)} %get-tuple-element.15), channel_id=1, source_target_pairs={{0,4},{4,8},{8,12},{12,16},{16,20},{20,24},{24,28},{1,5},{5,9},{9,... | collective-permute-start | bytes 27656 | tf_op jit(solution)/shard_map/ppermute | solution.py:25
  6.2 2.6 %collective-permute-start.1 = (f32[2,16]{1,0:T(2,128)S(1)}, f32[2,16]{1,0:T(2,128)S(1)}, u32[]{:S(2)}, u32[]{:S(2)}) collective-permute-start(f32[2,16]{1,0:T(2,128)S(1)} %pad_maximum_fusion), channel_id=1, source_target_pairs={{0,4},{4,0},{8,12},{12,8},{16,20},{20,16},{24,28},{28,24},{1,5},{5... | collective-permute-start | bytes 392 | tf_op jit(solution)/shard_map/ppermute | solution.py:240
  9.2 0.6 %iota_compare_fusion = pred[128,128]{1,0:T(8,128)(4,1)} fusion(), kind=kLoop, calls=%fused_computation.72 | loop fusion | flops 16384 | bytes 16384 | tf_op jit(solution)/shard_map/ge | solution.py:354
  9.9 0.7 %copy-done.10 = f32[4,1024]{1,0:T(4,128)S(1)} copy-done((f32[4,1024]{1,0:T(4,128)S(1)}, f32[4,1024]{1,0:T(4,128)}, u32[]{:S(2)}) %copy-start.10) | copy-done | bytes 16408
  10.5 0.7 %copy-done.18 = f32[4,512]{1,0:T(4,128)S(1)} copy-done((f32[4,512]{1,0:T(4,128)S(1)}, f32[4,512]{1,0:T(4,128)}, u32[]{:S(2)}) %copy-start.18) | copy-done | bytes 8216
  11.3 0.7 %copy.50 = f32[16,128]{1,0:T(8,128)} copy(f32[16,128]{0,1:T(8,128)S(1)} %bitcast.136) | data formatting | bytes 16384 | tf_op jit(solution)/shard_map/transpose | solution.py:369
  12.1 0.7 %copy.57 = f32[16,128]{1,0:T(8,128)} copy(f32[16,128]{0,1:T(8,128)S(1)} %bitcast.135) | data formatting | bytes 16384 | tf_op jit(solution)/shard_map/transpose | solution.py:369
  12.9 0.6 %slice_bitcast_fusion.1 = (f32[16,128]{1,0:T(8,128)}, f32[128,16]{0,1:T(8,128)S(1)}, f32[128,16]{0,1:T(8,128)S(1)}, f32[16,128]{1,0:T(8,128)}) fusion(f32[256,16]{0,1:T(8,128)S(1)} %compare_select_fusion, f32[128,16]{0,1:T(8,128)S(1)} %copy.54, f32[16]{0:T(128)S(1)} %get-tuple-element.89, f32[128,16]{0,1:T(8,128)S(1)} %copy.56, f32[16]{0:T(128)S(1)} %get-tuple-element.60), kind=kLoop, calls=%fused_computation.98 | loop fusion | flops 8192 | bytes 65664 | tf_op jit(solution)/shard_map/transpose | solution.py:371
  13.7 0.6 fusion.71
  14.3 0.5 multiply_bitcast_fusion
  14.8 2.4 %collective-permute-start.2 = (f32[2,8]{1,0:T(2,128)S(1)}, f32[2,8]{1,0:T(2,128)S(1)}, u32[]{:S(2)}, u32[]{:S(2)}) collective-permute-start(f32[2,8]{1,0:T(2,128)S(1)} %pad_maximum_fusion.1), channel_id=1, source_target_pairs={{0,8},{4,12},{8,0},{12,4},{16,24},{20,28},{24,16},{28,20},{1,9},{5... | collective-permute-start | bytes 200 | tf_op jit(solution)/shard_map/ppermute | solution.py:269
  17.1 0.6 copy-done.14
  17.8 0.5 copy-done.16
  18.3 0.6 %reshape.60.table_ref = f32[96]{0:T(128)} reshape(f32[12,8]{1,0:T(8,128)S(1)} %stack.139) | data formatting | bytes 768 | tf_op jit(solution)/shard_map/reshape | solution.py:176
  18.9 0.6 %multiply_bitcast_fusion.1 = (f32[1,8]{1,0:T(1,128)}, f32[1,8]{1,0:T(1,128)}, f32[1,8]{1,0:T(1,128)}, f32[8]{0:T(128)}, f32[8]{0:T(128)}, /*index=5*/f32[1,8]{1,...) fusion(pred[]{:T(512)S(6)} %eq.19, ...), kind=kLoop, calls=%fused_computation.146 | loop fusion | flops 184 | bytes 611 | tf_op jit(solution)/shard_map/stack | solution.py:176
  19.9 1.0 %multiply_convert_fusion.4 = (bf16[128,1536]{1,0:T(8,128)(2,1)S(1)}, bf16[128,1536]{1,0:T(8,128)(2,1)S(1)}) fusion(f32[131,1536]{1,0:T(8,128)S(1)} %maximum_convert_fusion, f32[1536]{0:T(1024)S(1)} %get-tuple-element.26, f32[1536]{0:T(1024)S(1)} %get-tuple-element.27, f32[1536]{0:T(1024)S(1)} %get-tuple-element.28, f32[1536]{0:T(1024)S(1)} %get-tuple-element.25, ...), kind=kLoop, calls=%fused_computation.33 | loop fusion | flops 4718592 | bytes 7102464 | tf_op jit(solution)/shard_map/convert_element_type | solution.py:361
  21.5 0.5 copy-done
  22.4 0.4 copy-done.26
  22.8 0.6 %copy-done.35 = f32[1,8]{1,0:T(1,128)S(1)} copy-done((f32[1,8]{1,0:T(1,128)S(1)}, f32[1,8]{1,0:T(1,128)}, u32[]{:S(2)}) %copy-start.35) | copy-done | bytes 56
  23.5 0.7 %reshape.59.table_ref = f32[80]{0:T(128)} reshape(f32[10,8]{1,0:T(8,128)S(1)} %stack.136) | data formatting | bytes 640 | tf_op jit(solution)/shard_map/reshape | solution.py:176
  24.1 0.7 %copy-done.41 = f32[1,8]{1,0:T(1,128)S(1)} copy-done((f32[1,8]{1,0:T(1,128)S(1)}, f32[1,8]{1,0:T(1,128)}, u32[]{:S(2)}) %copy-start.41) | copy-done | bytes 56
  24.8 0.9 %collective-permute-start.3 = (f32[1,8]{1,0:T(1,128)S(1)}, f32[1,8]{1,0:T(1,128)S(1)}, u32[]{:S(2)}, u32[]{:S(2)}) collective-permute-start(f32[1,8]{1,0:T(1,128)S(1)} %copy-done.41), channel_id=1, source_target_pairs={{0,16},{4,20},{8,24},{12,28},{16,0},{20,4},{24,8},{28,12},{1,17},{... | collective-permute-start | bytes 104 | tf_op jit(solution)/shard_map/ppermute | solution.py:269
  25.8 2.6 %collective-permute-done.3 = f32[1,8]{1,0:T(1,128)S(1)} collective-permute-done((f32[1,8]{1,0:T(1,128)S(1)}, f32[1,8]{1,0:T(1,128)S(1)}, u32[]{:S(2)}, u32[]{:S(2)}) %collective-permute-start.3) | collective-permute-done | bytes 64 | tf_op jit(solution)/shard_map/ppermute | solution.py:269
  28.4 0.7 %stack.140.off_ref = s32[4]{0:T(128)} broadcast(s32[]{:T(128)S(6)} %mul.302), dimensions={} | broadcast | bytes 20 | tf_op jit(solution)/shard_map/stack | solution.py:177
  29.4 2.7 %shard_map.91 = (f32[16,64,128]{2,1,0:T(8,128)}, f32[16,64,128]{2,1,0:T(8,128)}, bf16[16,64,128]{2,1,0:T(8,128)(2,1)}) custom-call(f32[96]{0:T(128)} %reshape.60.table_ref, s32[4]{0:T(128)} %stack.140.off_ref, f32[16,64,128]{2,1,0:T(8,128)} %copy-done.5, f32[16,64,128]{2,1,0:T(8,128)} %copy-done.4, f32[16,64,128]{2,1,0:T(8,128)} %copy-done.1, ...), custom_call_target="tpu_custom_call" | custom-call | flops 1572864 | bytes 3407872 | tf_op jit(solution)/shard_map/pallas_call | solution.py:202
  32.0 1.8 %collective-permute-start.7 = (bf16[16,64,128]{2,1,0:T(8,128)(2,1)}, bf16[16,64,128]{2,1,0:T(8,128)(2,1)S(1)}, u32[]{:S(2)}, u32[]{:S(2)}) collective-permute-start(bf16[16,64,128]{2,1,0:T(8,128)(2,1)} %get-tuple-element.18), channel_id=1, source_target_pairs={{0,8},{4,12},{8,0},{12,4},{16,24},{20,28},{24,16},{28,20},{1,9},{5... | collective-permute-start | bytes 786440 | tf_op jit(solution)/shard_map/ppermute | solution.py:269
  33.9 0.6 %copy-done.15 = f32[1,8]{1,0:T(1,128)S(1)} copy-done((f32[1,8]{1,0:T(1,128)S(1)}, f32[1,8]{1,0:T(1,128)}, u32[]{:S(2)}) %copy-start.15) | copy-done | bytes 56
  34.5 0.7 %reshape.58.table_ref = f32[112]{0:T(128)} reshape(f32[14,8]{1,0:T(8,128)S(1)} %stack.128) | data formatting | bytes 896 | tf_op jit(solution)/shard_map/reshape | solution.py:176
  35.3 4.1 %collective-permute-done.7.refs_1_ = bf16[16,64,128]{2,1,0:T(8,128)(2,1)S(1)} collective-permute-done((bf16[16,64,128]{2,1,0:T(8,128)(2,1)}, bf16[16,64,128]{2,1,0:T(8,128)(2,1)S(1)}, u32[]{:S(2)}, u32[]{:S(2)}) %collective-permute-start.7) | collective-permute-done | bytes 262176 | tf_op jit(solution)/shard_map/ppermute | solution.py:269
  39.5 0.7 %copy-done.7 = bf16[16,64,128]{2,1,0:T(8,128)(2,1)} copy-done((bf16[16,64,128]{2,1,0:T(8,128)(2,1)}, bf16[16,64,128]{2,1,0:T(8,128)(2,1)S(1)}, u32[]{:S(2)}) %copy-start.7) | copy-done | bytes 262168
  40.2 2.2 %shard_map.92 = (f32[16,64,128]{2,1,0:T(8,128)}, f32[16,64,128]{2,1,0:T(8,128)}, bf16[8,64,128]{2,1,0:T(8,128)(2,1)}) custom-call(f32[80]{0:T(128)} %reshape.59.table_ref, s32[4]{0:T(128)} %constant.111.clone.1.off_ref, f32[16,64,128]{2,1,0:T(8,128)} %get-tuple-element.17.refs_0_, bf16[16,64,128]{2,1,0:T(8,128)(2,1)} %copy-done.7), custom_call_target="tpu_custom_call" | custom-call | flops 1310720 | bytes 1966080 | tf_op jit(solution)/shard_map/pallas_call | solution.py:202
  42.4 0.9 %collective-permute-start.8 = (bf16[8,64,128]{2,1,0:T(8,128)(2,1)}, bf16[8,64,128]{2,1,0:T(8,128)(2,1)S(1)}, u32[]{:S(2)}, u32[]{:S(2)}) collective-permute-start(bf16[8,64,128]{2,1,0:T(8,128)(2,1)} %get-tuple-element.21), channel_id=1, source_target_pairs={{0,16},{4,20},{8,24},{12,28},{16,0},{20,4},{24,8},{28,12},{1,17},{... | collective-permute-start | bytes 393224 | tf_op jit(solution)/shard_map/ppermute | solution.py:269
  43.4 0.6 fusion.2
  43.9 3.7 %collective-permute-done.8.refs_2_ = bf16[8,64,128]{2,1,0:T(8,128)(2,1)S(1)} collective-permute-done((bf16[8,64,128]{2,1,0:T(8,128)(2,1)}, bf16[8,64,128]{2,1,0:T(8,128)(2,1)S(1)}, u32[]{:S(2)}, u32[]{:S(2)}) %collective-permute-start.8) | collective-permute-done | bytes 131104 | tf_op jit(solution)/shard_map/ppermute | solution.py:269
  47.6 0.7 %copy-done.8 = bf16[8,64,128]{2,1,0:T(8,128)(2,1)} copy-done((bf16[8,64,128]{2,1,0:T(8,128)(2,1)}, bf16[8,64,128]{2,1,0:T(8,128)(2,1)S(1)}, u32[]{:S(2)}) %copy-start.8) | copy-done | bytes 131096
  48.3 2.6 %shard_map.93 = (f32[16,64,128]{2,1,0:T(8,128)}, f32[16,64,128]{2,1,0:T(8,128)}) custom-call(f32[112]{0:T(128)} %reshape.58.table_ref, s32[7]{0:T(128)} %constant.110.clone.1.off_ref, f32[16,64,128]{2,1,0:T(8,128)} %get-tuple-element.19.refs_0_, f32[16,64,128]{2,1,0:T(8,128)} %get-tuple-element.20.refs_1_, bf16[8,64,128]{2,1,0:T(8,128)(2,1)} %copy-done.8, ...), custom_call_target="tpu_custom_call" | custom-call | flops 1835008 | bytes 2752512 | tf_op jit(solution)/shard_map/pallas_call | solution.py:202
  51.0 0.5 copy-done.12
  51.6 0.6 fusion.3
  52.2 0.5 copy-done.3
  53.1 0.4 fusion.1
  53.7 0.4 fusion
  54.3 0.8 %copy-done.2 = bf16[256,1024]{1,0:T(8,128)(2,1)S(1)} copy-done((bf16[256,1024]{1,0:T(8,128)(2,1)S(1)}, bf16[256,1024]{1,0:T(8,128)(2,1)}, u32[]{:S(2)}) %copy-start.2) | copy-done | bytes 524312
  55.1 0.4 multiply_reduce_fusion
  55.5 1.6 %collective-permute-start.10 = (f32[256]{0:T(256)S(1)}, f32[256]{0:T(256)S(1)}, u32[]{:S(2)}, u32[]{:S(2)}) collective-permute-start(f32[256]{0:T(256)S(1)} %get-tuple-element.29), channel_id=1, source_target_pairs={{0,1},{1,0},{2,3},{3,2},{4,5},{5,4},{6,7},{7,6},{8,9},{9,8},{10,11... | collective-permute-start | bytes 3080 | tf_op jit(solution)/shard_map/ppermute | solution.py:32
  57.2 2.0 %collective-permute-done.10 = f32[256]{0:T(256)S(1)} collective-permute-done((f32[256]{0:T(256)S(1)}, f32[256]{0:T(256)S(1)}, u32[]{:S(2)}, u32[]{:S(2)}) %collective-permute-start.10) | collective-permute-done | bytes 1056 | tf_op jit(solution)/shard_map/ppermute | solution.py:32
  59.2 1.0 %multiply_convert_fusion = bf16[256,1024]{1,0:T(8,128)(2,1)} fusion(f32[256,1024]{1,0:T(8,128)S(1)} %get-tuple-element.30, f32[1024]{0:T(1024)S(1)} %copy-done.28, f32[256]{0:T(256)S(1)} %add_rsqrt_fusion), kind=kLoop, calls=%fused_computation.14 | loop fusion | flops 786432 | bytes 1577984 | tf_op jit(solution)/shard_map/convert_element_type | solution.py:411
  (136 shorter events, 4.3 us)
Async XLA Ops:
  0.0 1.1 %copy-start.6 = (bf16[256,512]{1,0:T(8,128)(2,1)S(1)}, bf16[256,512]{1,0:T(8,128)(2,1)}, u32[]{:S(2)}) copy-start(bf16[256,512]{1,0:T(8,128)(2,1)} %param.11) | copy-start | bytes 786436
  1.2 4.4 %copy-start.9 = (f32[256,16]{0,1:T(8,128)S(1)}, f32[256,16]{0,1:T(8,128)}, u32[]{:S(2)}) copy-start(f32[256,16]{0,1:T(8,128)} %param.12) | copy-start | bytes 49156
  1.2 4.4 %copy-start.40 = (f32[16]{0:T(128)S(1)}, f32[16]{0:T(128)}, u32[]{:S(2)}) copy-start(f32[16]{0:T(128)} %param.13) | copy-start | bytes 196
  1.2 18.4 %collective-permute-start.5 = (bf16[3,1536]{1,0:T(4,128)(2,1)S(1)}, bf16[3,1536]{1,0:T(4,128)(2,1)S(1)}, u32[]{:S(2)}, u32[]{:S(2)}) collective-permute-start(bf16[3,1536]{1,0:T(4,128)(2,1)S(1)} %get-tuple-element.16), channel_id=1, source_target_pairs={{4,0},{8,4},{12,8},{16,12},{20,16},{24,20},{28,24},{5,1},{9,5},{13... | collective-permute-start | bytes 27656 | tf_op jit(solution)/shard_map/ppermute | solution.py:26
  2.5 17.2 %collective-permute-start = (bf16[3,1536]{1,0:T(4,128)(2,1)S(1)}, bf16[3,1536]{1,0:T(4,128)(2,1)S(1)}, u32[]{:S(2)}, u32[]{:S(2)}) collective-permute-start(bf16[3,1536]{1,0:T(4,128)(2,1)S(1)} %get-tuple-element.15), channel_id=1, source_target_pairs={{0,4},{4,8},{8,12},{12,16},{16,20},{20,24},{24,28},{1,5},{5,9},{9,... | collective-permute-start | bytes 27656 | tf_op jit(solution)/shard_map/ppermute | solution.py:25
  6.2 7.3 %collective-permute-start.1 = (f32[2,16]{1,0:T(2,128)S(1)}, f32[2,16]{1,0:T(2,128)S(1)}, u32[]{:S(2)}, u32[]{:S(2)}) collective-permute-start(f32[2,16]{1,0:T(2,128)S(1)} %pad_maximum_fusion), channel_id=1, source_target_pairs={{0,4},{4,0},{8,12},{12,8},{16,20},{20,16},{24,28},{28,24},{1,5},{5... | collective-permute-start | bytes 392 | tf_op jit(solution)/shard_map/ppermute | solution.py:240
  9.8 0.7 %copy-start.10 = (f32[4,1024]{1,0:T(4,128)S(1)}, f32[4,1024]{1,0:T(4,128)}, u32[]{:S(2)}) copy-start(f32[4,1024]{1,0:T(4,128)} %param.15) | copy-start | bytes 49156
  10.5 0.7 %copy-start.18 = (f32[4,512]{1,0:T(4,128)S(1)}, f32[4,512]{1,0:T(4,128)}, u32[]{:S(2)}) copy-start(f32[4,512]{1,0:T(4,128)} %param.16) | copy-start | bytes 24580
  12.9 6.1 %copy-start.21 = (f32[8]{0:T(128)}, f32[8]{0:T(128)S(1)}, u32[]{:S(2)}) copy-start(f32[8]{0:T(128)S(1)} %get-tuple-element.91) | copy-start | bytes 100
  13.6 5.3 %copy-start.19 = (f32[1,8]{1,0:T(1,128)}, f32[1,8]{1,0:T(1,128)S(1)}, u32[]{:S(2)}) copy-start(f32[1,8]{1,0:T(1,128)S(1)} %get-tuple-element.34) | copy-start | bytes 100
  14.8 4.1 %collective-permute-start.2 = (f32[2,8]{1,0:T(2,128)S(1)}, f32[2,8]{1,0:T(2,128)S(1)}, u32[]{:S(2)}, u32[]{:S(2)}) collective-permute-start(f32[2,8]{1,0:T(2,128)S(1)} %pad_maximum_fusion.1), channel_id=1, source_target_pairs={{0,8},{4,12},{8,0},{12,4},{16,24},{20,28},{24,16},{28,20},{1,9},{5... | collective-permute-start | bytes 200 | tf_op jit(solution)/shard_map/ppermute | solution.py:269
  21.2 0.8 %copy-start = (f32[16,64,128]{2,1,0:T(8,128)}, f32[16,64,128]{2,1,0:T(8,128)S(1)}, u32[]{:S(2)}) copy-start(f32[16,64,128]{2,1,0:T(8,128)S(1)} %fusion.38.refs_3_) | copy-start | bytes 1572868
  21.3 7.1 %collective-permute-start.6 = (f32[16,64,128]{2,1,0:T(8,128)S(1)}, f32[16,64,128]{2,1,0:T(8,128)S(1)}, u32[]{:S(2)}, u32[]{:S(2)}) collective-permute-start(f32[16,64,128]{2,1,0:T(8,128)S(1)} %fusion.38.refs_3_), channel_id=1, source_target_pairs={{0,4},{4,0},{8,12},{12,8},{16,20},{20,16},{24,28},{28,24},{1,5},{5... | collective-permute-start | bytes 1572872 | tf_op jit(solution)/shard_map/ppermute | solution.py:240
  22.1 0.7 %copy-start.26 = (f32[2,8]{1,0:T(2,128)S(1)}, f32[2,8]{1,0:T(2,128)}, u32[]{:S(2)}) copy-start(f32[2,8]{1,0:T(2,128)} %copy-done.25) | copy-start | bytes 196
  22.1 0.7 %copy-start.38 = (f32[1,8]{1,0:T(1,128)S(1)}, f32[1,8]{1,0:T(1,128)}, u32[]{:S(2)}) copy-start(f32[1,8]{1,0:T(1,128)} %get-tuple-element.87) | copy-start | bytes 100
  22.1 0.7 %copy-start.39 = (f32[1,8]{1,0:T(1,128)S(1)}, f32[1,8]{1,0:T(1,128)}, u32[]{:S(2)}) copy-start(f32[1,8]{1,0:T(1,128)} %get-tuple-element.39) | copy-start | bytes 100
  22.3 6.8 %copy-start.1 = (f32[16,64,128]{2,1,0:T(8,128)}, f32[16,64,128]{2,1,0:T(8,128)S(1)}, u32[]{:S(2)}) copy-start(f32[16,64,128]{2,1,0:T(8,128)S(1)} %fusion.40.refs_2_) | copy-start | bytes 1572868
  22.3 6.1 %collective-permute-start.4 = (f32[16,64,128]{2,1,0:T(8,128)S(1)}, f32[16,64,128]{2,1,0:T(8,128)S(1)}, u32[]{:S(2)}, u32[]{:S(2)}) collective-permute-start(f32[16,64,128]{2,1,0:T(8,128)S(1)} %fusion.40.refs_2_), channel_id=1, source_target_pairs={{0,4},{4,0},{8,12},{12,8},{16,20},{20,16},{24,28},{28,24},{1,5},{5... | collective-permute-start | bytes 1572872 | tf_op jit(solution)/shard_map/ppermute | solution.py:240
  22.7 0.7 %copy-start.35 = (f32[1,8]{1,0:T(1,128)S(1)}, f32[1,8]{1,0:T(1,128)}, u32[]{:S(2)}) copy-start(f32[1,8]{1,0:T(1,128)} %get-tuple-element.43) | copy-start | bytes 100
  22.7 0.7 %copy-start.36 = (f32[1,8]{1,0:T(1,128)S(1)}, f32[1,8]{1,0:T(1,128)}, u32[]{:S(2)}) copy-start(f32[1,8]{1,0:T(1,128)} %get-tuple-element.72) | copy-start | bytes 100
  24.8 0.9 %copy-start.20 = (f32[1,8]{1,0:T(1,128)S(1)}, f32[1,8]{1,0:T(1,128)}, u32[]{:S(2)}) copy-start(f32[1,8]{1,0:T(1,128)} %copy-done.19) | copy-start | bytes 100
  24.8 0.9 %copy-start.22 = (f32[8]{0:T(128)S(1)}, f32[8]{0:T(128)}, u32[]{:S(2)}) copy-start(f32[8]{0:T(128)} %copy-done.21) | copy-start | bytes 100
  24.8 0.9 %copy-start.34 = (f32[8]{0:T(128)S(1)}, f32[8]{0:T(128)}, u32[]{:S(2)}) copy-start(f32[8]{0:T(128)} %get-tuple-element.78) | copy-start | bytes 100
  24.8 3.5 %collective-permute-start.3 = (f32[1,8]{1,0:T(1,128)S(1)}, f32[1,8]{1,0:T(1,128)S(1)}, u32[]{:S(2)}, u32[]{:S(2)}) collective-permute-start(f32[1,8]{1,0:T(1,128)S(1)} %copy-done.41), channel_id=1, source_target_pairs={{0,16},{4,20},{8,24},{12,28},{16,0},{20,4},{24,8},{28,12},{1,17},{... | collective-permute-start | bytes 104 | tf_op jit(solution)/shard_map/ppermute | solution.py:269
  25.8 2.6 %copy-start.27 = (f32[8]{0:T(128)S(1)}, f32[8]{0:T(128)}, u32[]{:S(2)}) copy-start(f32[8]{0:T(128)} %get-tuple-element.77) | copy-start | bytes 100
  28.4 0.8 %copy-start.4 = (f32[16,64,128]{2,1,0:T(8,128)}, f32[16,64,128]{2,1,0:T(8,128)S(1)}, u32[]{:S(2)}) copy-start(f32[16,64,128]{2,1,0:T(8,128)S(1)} %collective-permute-done.6.refs_1_) | copy-start | bytes 1572868
  28.4 0.9 %copy-start.5 = (f32[16,64,128]{2,1,0:T(8,128)}, f32[16,64,128]{2,1,0:T(8,128)S(1)}, u32[]{:S(2)}) copy-start(f32[16,64,128]{2,1,0:T(8,128)S(1)} %collective-permute-done.4.refs_0_) | copy-start | bytes 1572868
  29.4 4.5 %copy-start.30 = (f32[1,8]{1,0:T(1,128)S(1)}, f32[1,8]{1,0:T(1,128)}, u32[]{:S(2)}) copy-start(f32[1,8]{1,0:T(1,128)} %get-tuple-element.80) | copy-start | bytes 100
  29.4 4.5 %copy-start.31 = (f32[1,8]{1,0:T(1,128)S(1)}, f32[1,8]{1,0:T(1,128)}, u32[]{:S(2)}) copy-start(f32[1,8]{1,0:T(1,128)} %get-tuple-element.81) | copy-start | bytes 100
  29.4 4.5 %copy-start.32 = (f32[1,8]{1,0:T(1,128)S(1)}, f32[1,8]{1,0:T(1,128)}, u32[]{:S(2)}) copy-start(f32[1,8]{1,0:T(1,128)} %get-tuple-element.82) | copy-start | bytes 100
  29.4 4.5 %copy-start.33 = (f32[1,8]{1,0:T(1,128)S(1)}, f32[1,8]{1,0:T(1,128)}, u32[]{:S(2)}) copy-start(f32[1,8]{1,0:T(1,128)} %get-tuple-element.83) | copy-start | bytes 100
  32.0 7.4 %collective-permute-start.7 = (bf16[16,64,128]{2,1,0:T(8,128)(2,1)}, bf16[16,64,128]{2,1,0:T(8,128)(2,1)S(1)}, u32[]{:S(2)}, u32[]{:S(2)}) collective-permute-start(bf16[16,64,128]{2,1,0:T(8,128)(2,1)} %get-tuple-element.18), channel_id=1, source_target_pairs={{0,8},{4,12},{8,0},{12,4},{16,24},{20,28},{24,16},{28,20},{1,9},{5... | collective-permute-start | bytes 786440 | tf_op jit(solution)/shard_map/ppermute | solution.py:269
  33.8 0.7 %copy-start.15 = (f32[1,8]{1,0:T(1,128)S(1)}, f32[1,8]{1,0:T(1,128)}, u32[]{:S(2)}) copy-start(f32[1,8]{1,0:T(1,128)} %copy-done.14) | copy-start | bytes 100
  33.8 0.7 %copy-start.17 = (f32[1,8]{1,0:T(1,128)S(1)}, f32[1,8]{1,0:T(1,128)}, u32[]{:S(2)}) copy-start(f32[1,8]{1,0:T(1,128)} %copy-done.16) | copy-start | bytes 100
  33.8 0.7 %copy-start.29 = (f32[1,8]{1,0:T(1,128)S(1)}, f32[1,8]{1,0:T(1,128)}, u32[]{:S(2)}) copy-start(f32[1,8]{1,0:T(1,128)} %get-tuple-element.76) | copy-start | bytes 100
  39.5 0.7 %copy-start.7 = (bf16[16,64,128]{2,1,0:T(8,128)(2,1)}, bf16[16,64,128]{2,1,0:T(8,128)(2,1)S(1)}, u32[]{:S(2)}) copy-start(bf16[16,64,128]{2,1,0:T(8,128)(2,1)S(1)} %collective-permute-done.7.refs_1_) | copy-start | bytes 786436
  40.2 3.2 %copy-start.11 = (pred[128,128]{1,0:T(8,128)(4,1)S(1)}, pred[128,128]{1,0:T(8,128)(4,1)}, u32[]{:S(2)}) copy-start(pred[128,128]{1,0:T(8,128)(4,1)} %iota_compare_fusion) | copy-start | bytes 49156
  40.2 3.2 %copy-start.13 = (f32[16,128]{1,0:T(8,128)S(1)}, f32[16,128]{1,0:T(8,128)}, u32[]{:S(2)}) copy-start(f32[16,128]{1,0:T(8,128)} %copy.50) | copy-start | bytes 24580
  40.2 3.2 %copy-start.24 = (f32[16,128]{1,0:T(8,128)S(1)}, f32[16,128]{1,0:T(8,128)}, u32[]{:S(2)}) copy-start(f32[16,128]{1,0:T(8,128)} %get-tuple-element.68) | copy-start | bytes 24580
  42.4 0.9 %copy-start.42 = (f32[16]{0:T(128)S(1)}, f32[16]{0:T(128)}, u32[]{:S(2)}) copy-start(f32[16]{0:T(128)} %param.14) | copy-start | bytes 196
  42.4 5.2 %collective-permute-start.8 = (bf16[8,64,128]{2,1,0:T(8,128)(2,1)}, bf16[8,64,128]{2,1,0:T(8,128)(2,1)S(1)}, u32[]{:S(2)}, u32[]{:S(2)}) collective-permute-start(bf16[8,64,128]{2,1,0:T(8,128)(2,1)} %get-tuple-element.21), channel_id=1, source_target_pairs={{0,16},{4,20},{8,24},{12,28},{16,0},{20,4},{24,8},{28,12},{1,17},{... | collective-permute-start | bytes 393224 | tf_op jit(solution)/shard_map/ppermute | solution.py:269
  50.9 0.7 %copy-start.12 = (f32[16,128]{1,0:T(8,128)S(1)}, f32[16,128]{1,0:T(8,128)}, u32[]{:S(2)}) copy-start(f32[16,128]{1,0:T(8,128)} %copy.57) | copy-start | bytes 24580
  50.9 0.7 %copy-start.23 = (f32[16,128]{1,0:T(8,128)S(1)}, f32[16,128]{1,0:T(8,128)}, u32[]{:S(2)}) copy-start(f32[16,128]{1,0:T(8,128)} %get-tuple-element.71) | copy-start | bytes 24580
  50.9 2.1 %collective-permute-start.9 = (f32[16,64,128]{2,1,0:T(8,128)}, f32[16,64,128]{2,1,0:T(8,128)S(1)}, u32[]{:S(2)}, u32[]{:S(2)}) collective-permute-start(f32[16,64,128]{2,1,0:T(8,128)} %get-tuple-element.23), channel_id=1, source_target_pairs={{0,4},{4,0},{8,12},{12,8},{16,20},{20,16},{24,28},{28,24},{1,5},{5... | collective-permute-start | bytes 1572872 | tf_op jit(solution)/shard_map/ppermute | solution.py:310
  51.6 1.0 %copy-start.3 = (f32[16,64,128]{2,1,0:T(8,128)S(1)}, f32[16,64,128]{2,1,0:T(8,128)}, u32[]{:S(2)}) copy-start(f32[16,64,128]{2,1,0:T(8,128)} %get-tuple-element.24) | copy-start | bytes 1572868
  54.1 1.0 %copy-start.2 = (bf16[256,1024]{1,0:T(8,128)(2,1)S(1)}, bf16[256,1024]{1,0:T(8,128)(2,1)}, u32[]{:S(2)}) copy-start(bf16[256,1024]{1,0:T(8,128)(2,1)} %param.10) | copy-start | bytes 1572868
  55.5 3.7 %copy-start.28 = (f32[1024]{0:T(1024)S(1)}, f32[1024]{0:T(1024)}, u32[]{:S(2)}) copy-start(f32[1024]{0:T(1024)} %param.17) | copy-start | bytes 12292
  55.5 3.6 %collective-permute-start.10 = (f32[256]{0:T(256)S(1)}, f32[256]{0:T(256)S(1)}, u32[]{:S(2)}, u32[]{:S(2)}) collective-permute-start(f32[256]{0:T(256)S(1)} %get-tuple-element.29), channel_id=1, source_target_pairs={{0,1},{1,0},{2,3},{3,2},{4,5},{5,4},{6,7},{7,6},{8,9},{9,8},{10,11... | collective-permute-start | bytes 3080 | tf_op jit(solution)/shard_map/ppermute | solution.py:32
  (6 other events, 3.8 us)

commit v6 on v5

--- a/solution.py
+++ b/solution.py
@@ -164,7 +164,7 @@
         self.views.append((index, offset))
         return [(len(self.views) - 1, jnp.ones((self.heads,), jnp.float32))]
 
-    def run(self, logical, out_arrays):
+    def run(self, logical, out_arrays, tails=()):
         heads = self.heads
         coefs, layout = [], []
         for terms, dests in logical:
@@ -177,10 +177,16 @@
         offsets = jnp.stack([jnp.asarray(off, jnp.int32) for _, off in self.views])
         inner = self.arrays[0].shape[1:]
         views = self.views
-        count = len(self.arrays)
+        count = len(self.arrays) + len(tails)
+        tail_outs = [(len(self.arrays) + i, out) for i, (_, out) in enumerate(tails)]
+        extra = [0] * len(out_arrays)
+        for _, out in tails:
+            extra[out] = 1
 
         def kernel(table_ref, off_ref, *refs):
             ins, outs = refs[:count], refs[count:]
+            for source, out in tail_outs:
+                outs[out][outs[out].shape[0] - 1] = ins[source][0]
             for h in range(heads):
                 cache = {}
                 for rows, dests in layout:
@@ -197,17 +203,34 @@
         slab = heads * inner[0] * inner[1]
         moved = sum(a.size * a.dtype.itemsize for a in self.arrays)
         moved += sum(b * slab * jnp.dtype(d).itemsize for d, b in out_arrays)
+        arrays = list(self.arrays) + [t for t, _ in tails]
         smem = pl.BlockSpec(memory_space=pltpu.SMEM)
         vmem = pl.BlockSpec(memory_space=pltpu.VMEM)
         return pl.pallas_call(
             kernel,
-            out_shape=[jax.ShapeDtypeStruct((b * heads, *inner), d) for d, b in out_arrays],
+            out_shape=[
+                jax.ShapeDtypeStruct((b * heads + x, *inner), d)
+                for (d, b), x in zip(out_arrays, extra)
+            ],
             in_specs=[smem, smem] + [vmem] * count,
             out_specs=[vmem] * len(out_arrays),
             cost_estimate=pl.CostEstimate(
                 flops=2 * len(coefs) * slab, bytes_accessed=moved, transcendentals=0
             ),
-        )(table, offsets, *self.arrays)
+        )(table, offsets, *arrays)
+
+
+def tail_slot(decays, inner, kind):
+    rows = jnp.stack(decays)
+    high = rows.astype(kind)
+    low = (rows - high.astype(jnp.float32)).astype(kind)
+    both = jnp.concatenate([high, low], axis=0)
+    return jnp.pad(both, ((0, inner[0] - both.shape[0]), (0, inner[1] - both.shape[1])))[None]
+
+
+def read_tail(message, count, heads):
+    tail = message[-1].astype(jnp.float32)
+    return [tail[i, :heads] + tail[count + i, :heads] for i in range(count)]
 
 
 def scale(terms, coef):
@@ -237,14 +260,17 @@
     unit = seq_pos // 2
     one = jnp.ones((half,), f32)
     pairs = [(i, i ^ 1) for i in range(seq_count)]
-    p1, p2, got_e = lax.ppermute((first_loc, second_loc, jnp.stack([e1, e2])), "seq", pairs)
+    inner = first_loc.shape[1:]
+    sent = jnp.concatenate([first_loc, second_loc, tail_slot((e1, e2), inner, f32)], axis=0)
+    got = lax.ppermute(sent, "seq", pairs)
+    q1, q2 = read_tail(got, 2, heads)
 
     def mine(v):
         return lax.dynamic_slice_in_dim(v, core * half, half)
 
-    e1h, e2h, q1h, q2h = mine(e1), mine(e2), mine(got_e[0]), mine(got_e[1])
+    e1h, e2h, q1h, q2h = mine(e1), mine(e2), mine(q1), mine(q2)
     mix = Mix(half)
-    v_p1, v_p2 = mix.view(p1, core * half), mix.view(p2, core * half)
+    v_p1, v_p2 = mix.view(got, core * half), mix.view(got, heads + core * half)
     v_l1, v_l2 = mix.view(first_loc, core * half), mix.view(second_loc, core * half)
     f_terms = scale(v_l1, jnp.where(upper, one, q1h)) + scale(v_p1, jnp.where(upper, e1h, one))
     g_terms = scale(v_l2, jnp.where(upper, q2h, one)) + scale(v_p2, jnp.where(upper, one, e2h))
@@ -257,7 +283,11 @@
     msg_terms, msg_e = next_message(f_terms, g_terms, e_f, e_g, lower, levels == 1)
     logical = [(f_terms, [(0, 0)]), (g_terms, [(0, 1)]), (low_terms, [(1, 0)]), (high_terms, [(1, 1)])]
     logical += [(t, [(2, b)]) for b, t in enumerate(msg_terms)]
-    state, edges, msg = mix.run(logical, [(f32, 2), (f32, 2), (LINK, len(msg_terms))])
+    state, edges, msg = mix.run(
+        logical,
+        [(f32, 2), (f32, 2), (LINK, len(msg_terms))],
+        [(tail_slot(list(msg_e), inner, LINK), 2)],
+    )
     zero_h = jnp.zeros((half,), f32)
     e_pre, e_abv = one, one
     have_acc = False
@@ -266,7 +296,8 @@
         lower = (unit // size) % 2 == 0
         last = level == levels - 1
         pairs = [(i, i ^ (2 * size)) for i in range(seq_count)]
-        got, got_e = lax.ppermute((msg, msg_e), "seq", pairs)
+        got = lax.ppermute(msg, "seq", pairs)
+        got_e = read_tail(got, 1 if last else 2, half)
         mix = Mix(half)
         v_f, v_g = mix.view(state, 0), mix.view(state, half)
         if have_acc:
@@ -288,7 +319,11 @@
             logical = [(f_terms, [(0, 0)]), (g_terms, [(0, 1)])]
             logical += [(pre_terms, [(1, 0)]), (abv_terms, [(1, 1)])]
             logical += [(t, [(2, b)]) for b, t in enumerate(msg_terms)]
-            state, acc, msg = mix.run(logical, [(f32, 2), (f32, 2), (LINK, len(msg_terms))])
+            state, acc, msg = mix.run(
+                logical,
+                [(f32, 2), (f32, 2), (LINK, len(msg_terms))],
+                [(tail_slot(list(msg_e), inner, LINK), 2)],
+            )
             have_acc = True
         else:
             p_w = got_e[0]

time: 60.7 us -> 53 us (0.87)
  local copies, waits for them, and re-layouts: 15.6 us -> 6.49 us
  matrix products: 2.61 us -> 4.22 us
  starting transfers between devices: 14.7 us -> 13.9 us
    unnamed x88 -> x38, local copies, waits for them, and re-layouts: 9.99 us -> 2.77 us
    another operation x7 -> x9, other arithmetic: 1.85 us -> 0.22 us  [run(): table = jnp.stack(coefs).reshape(-1)]
    dot_general x2, matrix products: 1.13 us -> 2.76 us  [local_block(): jnp.einsum('hts,shp->thp', weights, inner_conv, preferred_element_type=jn...]
    transpose x2, local copies, waits for them, and re-layouts: 1.35 us -> 0.12 us  [local_block(): log_gap = log_cum.T[:, :, None] - log_cum.T[:, None, :]]
    broadcast_in_dim x0 -> x3, other arithmetic: none -> 1.22 us  [tail_slot(): jnp.pad(both, ((0, inner[0] - both.shape[0]), (0, inner[1] - both.shape[1...]
    concatenate x0 -> x1, other arithmetic: none -> 1.19 us  [kernel_states(): jnp.concatenate([first_loc, second_loc, tail_slot((e1, e2), inner, f32)],...]
    ppermute x7 -> x3, starting transfers between devices: 8.75 us -> 7.93 us  [the longest x2 5.37 us: kernel_states(): got = lax.ppermute(msg, 'seq', pairs)]
    another operation x2 -> x1, other arithmetic: 0.02 us -> 0.7 us  [run(): offsets = jnp.stack([jnp.asarray(off, jnp.int32) for _, off in self.views])]
  transfers between devices with their start and end apart: 11 -> 7, of which waited for: 5 -> 5; matrix products, arithmetic and copies ran while one was open for 16% -> 10% of each run, Pallas kernels for 0% -> 0%
where the time goes in v6:
time: 53 us; the launch traced here: 52.6 us
  starting transfers between devices  13.9 us (26%)
  waiting for transfers between devices  13.4 us (25%)
  Pallas kernels  7.61 us (14%)
  local copies, waits for them, and re-layouts  6.49 us (12%)
  other arithmetic  6.46 us (12%)
  matrix products  4.22 us (8%)
    ppermute x2, waiting for transfers between devices, kernel_states(): got = lax.ppermute(msg, 'seq', pairs)  9.37 us
    pallas_call x3, Pallas kernels, run(): pl.pallas_call(kernel, out_shape=[jax.ShapeDtypeStruct((b * heads + x, *i...  7.61 us
    ppermute x2, starting transfers between devices, kernel_states(): got = lax.ppermute(msg, 'seq', pairs)  5.37 us
    ppermute x1, starting transfers between devices, extended_2(): low = lax.ppermute(tail, axis, forward)  3.03 us
    unnamed x38, local copies, waits for them, and re-layouts  2.77 us
    dot_general x2, matrix products, local_block(): jnp.einsum('hts,shp->thp', weights, inner_conv, preferred_element_type=jn...  2.76 us
    ppermute x1, starting transfers between devices, kernel_states(): got = lax.ppermute(sent, 'seq', pairs)  2.56 us
    ppermute x1, waiting for transfers between devices, partner(): lax.ppermute(array, axis, [(i, i ^ 1 << stride) for i in range(lax.axis_s...  1.99 us
  transfers between devices with their start and end apart: 7, of which 5 were waited for; matrix products, arithmetic and copies ran while one was open for 10% of the time, Pallas kernels for 0%

profile of v6, /device:TPU:0, one launch (start us, length us, event | category | flops | bytes accessed | tf_op | source)
XLA Modules:
  0.0 52.6 jit_solution(7917596250088111380)
XLA Ops:
  0.0 1.1 %constant_dynamic-update-slice_fusion.3 = bf16[256,1536]{1,0:T(8,128)(2,1)S(1)} fusion(bf16[256,1024]{1,0:T(8,128)(2,1)} %param.9), kind=kLoop, calls=%fused_computation.119 | loop fusion | bytes 1048576
  1.2 1.3 %collective-permute-start.1 = (bf16[3,1536]{1,0:T(4,128)(2,1)S(1)}, bf16[3,1536]{1,0:T(4,128)(2,1)S(1)}, u32[]{:S(2)}, u32[]{:S(2)}) collective-permute-start(bf16[3,1536]{1,0:T(4,128)(2,1)S(1)} %get-tuple-element.16), channel_id=1, source_target_pairs={{4,0},{8,4},{12,8},{16,12},{20,16},{24,20},{28,24},{5,1},{9,5},{13... | collective-permute-start | bytes 27656 | tf_op jit(solution)/shard_map/ppermute | solution.py:26
  2.5 3.0 %collective-permute-start = (bf16[3,1536]{1,0:T(4,128)(2,1)S(1)}, bf16[3,1536]{1,0:T(4,128)(2,1)S(1)}, u32[]{:S(2)}, u32[]{:S(2)}) collective-permute-start(bf16[3,1536]{1,0:T(4,128)(2,1)S(1)} %get-tuple-element.15), channel_id=1, source_target_pairs={{0,4},{4,8},{8,12},{12,16},{16,20},{20,24},{24,28},{1,5},{5,9},{9,... | collective-permute-start | bytes 27656 | tf_op jit(solution)/shard_map/ppermute | solution.py:25
  5.8 0.1 copy.49
  5.9 0.2 reduce_window_sum.17
  6.1 0.1 copy.55
  6.2 0.2 reduce_window_sum.18
  6.6 0.1 slice_bitcast_fusion.4
  6.7 0.1 maximum_convert_fusion.1
  6.9 0.1 maximum_convert_fusion
  7.0 1.0 %multiply_convert_fusion.4 = (bf16[128,1536]{1,0:T(8,128)(2,1)S(1)}, bf16[128,1536]{1,0:T(8,128)(2,1)S(1)}) fusion(f32[131,1536]{1,0:T(8,128)S(1)} %maximum_convert_fusion, f32[1536]{0:T(1024)S(1)} %get-tuple-element.26, f32[1536]{0:T(1024)S(1)} %get-tuple-element.27, f32[1536]{0:T(1024)S(1)} %get-tuple-element.28, f32[1536]{0:T(1024)S(1)} %get-tuple-element.25, ...), kind=kLoop, calls=%fused_computation.34 | loop fusion | flops 4718592 | bytes 7102464 | tf_op jit(solution)/shard_map/convert_element_type | solution.py:396
  8.0 0.2 copy.48
  8.2 0.2 copy.54
  8.4 0.2 fusion.40.refs_1_
  8.6 0.3 copy-done.3
  8.9 0.2 fusion.38.refs_2_
  9.1 1.2 %pad_maximum_fusion = f32[33,64,128]{2,1,0:T(8,128)} fusion(f32[1,64,128]{2,1,0:T(8,128)S(1)} %fusion.50, f32[16,64,128]{2,1,0:T(8,128)S(1)} %fusion.38.refs_2_, f32[16,64,128]{2,1,0:T(8,128)S(1)} %fusion.40.refs_1_), kind=kLoop, calls=%fused_computation.10 | loop fusion | flops 540672 | bytes 2162688 | tf_op jit(solution)/shard_map/concatenate | solution.py:264
  10.3 2.6 %collective-permute-start.2 = (f32[33,64,128]{2,1,0:T(8,128)}, f32[33,64,128]{2,1,0:T(8,128)S(1)}, u32[]{:S(2)}, u32[]{:S(2)}) collective-permute-start(f32[33,64,128]{2,1,0:T(8,128)} %pad_maximum_fusion), channel_id=1, source_target_pairs={{0,4},{4,0},{8,12},{12,8},{16,20},{20,16},{24,28},{28,24},{1,5},{5... | collective-permute-start | bytes 3244040 | tf_op jit(solution)/shard_map/ppermute | solution.py:265
  13.2 0.7 %pad_add_fusion.off_ref = s32[4]{0:T(128)} fusion(s32[1]{0:T(128)} %bitcast.19, s32[1]{0:T(128)} %bitcast.20), kind=kLoop, calls=%fused_computation.178 | loop fusion | flops 12 | bytes 24 | tf_op jit(solution)/shard_map/stack | solution.py:177
  13.9 1.5 %collective-permute-done.2.refs_0_ = f32[33,64,128]{2,1,0:T(8,128)S(1)} collective-permute-done((f32[33,64,128]{2,1,0:T(8,128)}, f32[33,64,128]{2,1,0:T(8,128)S(1)}, u32[]{:S(2)}, u32[]{:S(2)}) %collective-permute-start.2) | collective-permute-done | bytes 1081376 | tf_op jit(solution)/shard_map/ppermute | solution.py:265
  15.7 0.7 %reshape.70.table_ref = f32[96]{0:T(128)} reshape(f32[12,8]{1,0:T(8,128)S(1)} %stack.125) | data formatting | bytes 768 | tf_op jit(solution)/shard_map/reshape | solution.py:176
  16.4 0.6 %fusion.74.refs_3_ = bf16[1,64,128]{2,1,0:T(8,128)(2,1)} fusion(bf16[2,8]{1,0:T(2,128)(2,1)S(1)} %subtract_convert_fusion, bf16[2,8]{1,0:T(2,128)(2,1)S(1)} %fusion.92), kind=kLoop, calls=%fused_computation.110 | loop fusion | flops 90112 | bytes 16448 | tf_op jit(solution)/shard_map/broadcast_in_dim | solution.py:228
  17.0 2.8 %shard_map.91 = (f32[16,64,128]{2,1,0:T(8,128)}, f32[16,64,128]{2,1,0:T(8,128)}, bf16[17,64,128]{2,1,0:T(8,128)(2,1)}) custom-call(f32[96]{0:T(128)} %reshape.70.table_ref, s32[4]{0:T(128)} %pad_add_fusion.off_ref, f32[33,64,128]{2,1,0:T(8,128)} %copy-done.2, f32[16,64,128]{2,1,0:T(8,128)} %copy-done, f32[16,64,128]{2,1,0:T(8,128)} %copy-done.1, ...), custom_call_target="tpu_custom_call" | custom-call | flops 1572864 | bytes 3440640 | tf_op jit(solution)/shard_map/pallas_call | solution.py:209
  19.7 2.4 %collective-permute-start.3 = (bf16[17,64,128]{2,1,0:T(8,128)(2,1)}, bf16[17,64,128]{2,1,0:T(8,128)(2,1)S(1)}, u32[]{:S(2)}, u32[]{:S(2)}) collective-permute-start(bf16[17,64,128]{2,1,0:T(8,128)(2,1)} %get-tuple-element.17), channel_id=1, source_target_pairs={{0,8},{4,12},{8,0},{12,4},{16,24},{20,28},{24,16},{28,20},{1,9},{5... | collective-permute-start | bytes 835592 | tf_op jit(solution)/shard_map/ppermute | solution.py:299
  22.1 0.1 fusion.63
  22.3 1.4 %fusion.2 = f32[128,16,64]{0,2,1:T(8,128)} fusion(bf16[128,16,64]{0,2,1:T(8,128)(2,1)S(1)} %bitcast.152, f32[16,128]{1,0:T(8,128)S(1)} %get-tuple-element.71, f32[16,128]{1,0:T(8,128)S(1)} %copy.50, f32[128,128]{1,0:T(8,128)S(1)} %fusion.63, pred[128,128]{1,0:T(8,128)(4,1)S(1)} %iota_compare_fusion, f32[16]{0:T(128)S(1)} %copy-done.17), kind=kOutput, calls=%fused_computation.8 | convolution fusion | flops 35520512 | bytes 884800 | tf_op jit(solution)/shard_map/hts,shp->thp/dot_general | solution.py:407
  23.6 5.8 %collective-permute-done.3.refs_1_ = bf16[17,64,128]{2,1,0:T(8,128)(2,1)S(1)} collective-permute-done((bf16[17,64,128]{2,1,0:T(8,128)(2,1)}, bf16[17,64,128]{2,1,0:T(8,128)(2,1)S(1)}, u32[]{:S(2)}, u32[]{:S(2)}) %collective-permute-start.3) | collective-permute-done | bytes 278560 | tf_op jit(solution)/shard_map/ppermute | solution.py:299
  29.6 0.6 %reshape.71.table_ref = f32[80]{0:T(128)} reshape(f32[10,8]{1,0:T(8,128)S(1)} %stack.141) | data formatting | bytes 640 | tf_op jit(solution)/shard_map/reshape | solution.py:176
  30.2 0.6 %fusion.72.refs_2_ = bf16[1,64,128]{2,1,0:T(8,128)(2,1)} fusion(bf16[1,8]{1,0:T(2,128)(2,1)S(1)} %convert_bitcast_fusion, bf16[1,8]{1,0:T(2,128)(2,1)S(1)} %get-tuple-element.82), kind=kLoop, calls=%fused_computation.108 | loop fusion | flops 90112 | bytes 16416 | tf_op jit(solution)/shard_map/broadcast_in_dim | solution.py:228
  30.8 2.2 %shard_map.92 = (f32[16,64,128]{2,1,0:T(8,128)}, f32[16,64,128]{2,1,0:T(8,128)}, bf16[9,64,128]{2,1,0:T(8,128)(2,1)}) custom-call(f32[80]{0:T(128)} %reshape.71.table_ref, s32[4]{0:T(128)} %constant.114.clone.1.off_ref, f32[16,64,128]{2,1,0:T(8,128)} %get-tuple-element.18.refs_0_, bf16[17,64,128]{2,1,0:T(8,128)(2,1)} %copy-done.9, ...), custom_call_target="tpu_custom_call" | custom-call | flops 1310720 | bytes 1982464 | tf_op jit(solution)/shard_map/pallas_call | solution.py:209
  33.1 3.0 %collective-permute-start.4 = (bf16[9,64,128]{2,1,0:T(8,128)(2,1)}, bf16[9,64,128]{2,1,0:T(8,128)(2,1)S(1)}, u32[]{:S(2)}, u32[]{:S(2)}) collective-permute-start(bf16[9,64,128]{2,1,0:T(8,128)(2,1)} %get-tuple-element.19), channel_id=1, source_target_pairs={{0,16},{4,20},{8,24},{12,28},{16,0},{20,4},{24,8},{28,12},{1,17},{... | collective-permute-start | bytes 442376 | tf_op jit(solution)/shard_map/ppermute | solution.py:299
  36.1 3.5 %collective-permute-done.4.refs_2_ = bf16[9,64,128]{2,1,0:T(8,128)(2,1)S(1)} collective-permute-done((bf16[9,64,128]{2,1,0:T(8,128)(2,1)}, bf16[9,64,128]{2,1,0:T(8,128)(2,1)S(1)}, u32[]{:S(2)}, u32[]{:S(2)}) %collective-permute-start.4) | collective-permute-done | bytes 147488 | tf_op jit(solution)/shard_map/ppermute | solution.py:299
  39.7 0.6 %reshape.72.table_ref = f32[112]{0:T(128)} reshape(f32[14,8]{1,0:T(8,128)S(1)} %stack.149) | data formatting | bytes 896 | tf_op jit(solution)/shard_map/reshape | solution.py:176
  40.3 2.6 %shard_map.93 = (f32[16,64,128]{2,1,0:T(8,128)}, f32[16,64,128]{2,1,0:T(8,128)}) custom-call(f32[112]{0:T(128)} %reshape.72.table_ref, s32[7]{0:T(128)} %constant.115.clone.1.off_ref, f32[16,64,128]{2,1,0:T(8,128)} %get-tuple-element.20.refs_0_, f32[16,64,128]{2,1,0:T(8,128)} %get-tuple-element.21.refs_1_, bf16[9,64,128]{2,1,0:T(8,128)(2,1)} %copy-done.11, ...), custom_call_target="tpu_custom_call" | custom-call | flops 1835008 | bytes 2768896 | tf_op jit(solution)/shard_map/pallas_call | solution.py:209
  42.9 0.1 fusion.58
  43.1 1.4 %fusion.3 = f32[128,16,64]{0,2,1:T(8,128)} fusion(bf16[128,16,64]{0,2,1:T(8,128)(2,1)S(1)} %bitcast.150, f32[16,128]{1,0:T(8,128)S(1)} %get-tuple-element.74, f32[16,128]{1,0:T(8,128)S(1)} %copy.57, f32[128,128]{1,0:T(8,128)S(1)} %fusion.58, pred[128,128]{1,0:T(8,128)(4,1)S(1)} %iota_compare_fusion, f32[16]{0:T(128)S(1)} %copy-done.17), kind=kOutput, calls=%fused_computation.9 | convolution fusion | flops 35520512 | bytes 884800 | tf_op jit(solution)/shard_map/hts,shp->thp/dot_general | solution.py:407
  44.5 0.6 %collective-permute-done.5 = f32[16,64,128]{2,1,0:T(8,128)S(1)} collective-permute-done((f32[16,64,128]{2,1,0:T(8,128)}, f32[16,64,128]{2,1,0:T(8,128)S(1)}, u32[]{:S(2)}, u32[]{:S(2)}) %collective-permute-start.5) | collective-permute-done | bytes 524320 | tf_op jit(solution)/shard_map/ppermute | solution.py:345
  45.1 0.4 copy-done.7
  45.5 0.4 fusion.1
  45.9 0.2 copy.60
  46.1 0.4 copy-done.8
  46.5 0.4 fusion
  46.9 0.2 copy.61
  47.1 0.4 copy-done.5
  47.6 0.4 multiply_reduce_fusion
  48.0 1.6 %collective-permute-start.6 = (f32[256]{0:T(256)S(1)}, f32[256]{0:T(256)S(1)}, u32[]{:S(2)}, u32[]{:S(2)}) collective-permute-start(f32[256]{0:T(256)S(1)} %get-tuple-element.29), channel_id=1, source_target_pairs={{0,1},{1,0},{2,3},{3,2},{4,5},{5,4},{6,7},{7,6},{8,9},{9,8},{10,11... | collective-permute-start | bytes 3080 | tf_op jit(solution)/shard_map/ppermute | solution.py:32
  49.6 2.0 %collective-permute-done.6 = f32[256]{0:T(256)S(1)} collective-permute-done((f32[256]{0:T(256)S(1)}, f32[256]{0:T(256)S(1)}, u32[]{:S(2)}, u32[]{:S(2)}) %collective-permute-start.6) | collective-permute-done | bytes 1056 | tf_op jit(solution)/shard_map/ppermute | solution.py:32
  51.6 1.0 %multiply_convert_fusion = bf16[256,1024]{1,0:T(8,128)(2,1)} fusion(f32[256,1024]{1,0:T(8,128)S(1)} %get-tuple-element.30, f32[1024]{0:T(1024)S(1)} %copy-done.15, f32[256]{0:T(256)S(1)} %add_rsqrt_fusion), kind=kLoop, calls=%fused_computation.15 | loop fusion | flops 786432 | bytes 1577984 | tf_op jit(solution)/shard_map/convert_element_type | solution.py:446
  (89 shorter events, 1.4 us)
Async XLA Ops:
  0.0 1.1 %copy-start.10 = (bf16[256,512]{1,0:T(8,128)(2,1)S(1)}, bf16[256,512]{1,0:T(8,128)(2,1)}, u32[]{:S(2)}) copy-start(bf16[256,512]{1,0:T(8,128)(2,1)} %param.11) | copy-start | bytes 786436
  1.1 4.5 %copy-start.12 = (f32[256,16]{0,1:T(8,128)S(1)}, f32[256,16]{0,1:T(8,128)}, u32[]{:S(2)}) copy-start(f32[256,16]{0,1:T(8,128)} %param.12) | copy-start | bytes 49156
  1.1 4.5 %copy-start.16 = (f32[16]{0:T(128)S(1)}, f32[16]{0:T(128)}, u32[]{:S(2)}) copy-start(f32[16]{0:T(128)} %param.13) | copy-start | bytes 196
  1.2 5.2 %copy-start.13 = (f32[4,1024]{1,0:T(4,128)S(1)}, f32[4,1024]{1,0:T(4,128)}, u32[]{:S(2)}) copy-start(f32[4,1024]{1,0:T(4,128)} %param.15) | copy-start | bytes 49156
  1.2 5.3 %copy-start.14 = (f32[4,512]{1,0:T(4,128)S(1)}, f32[4,512]{1,0:T(4,128)}, u32[]{:S(2)}) copy-start(f32[4,512]{1,0:T(4,128)} %param.16) | copy-start | bytes 24580
  1.2 5.5 %collective-permute-start.1 = (bf16[3,1536]{1,0:T(4,128)(2,1)S(1)}, bf16[3,1536]{1,0:T(4,128)(2,1)S(1)}, u32[]{:S(2)}, u32[]{:S(2)}) collective-permute-start(bf16[3,1536]{1,0:T(4,128)(2,1)S(1)} %get-tuple-element.16), channel_id=1, source_target_pairs={{4,0},{8,4},{12,8},{16,12},{20,16},{24,20},{28,24},{5,1},{9,5},{13... | collective-permute-start | bytes 27656 | tf_op jit(solution)/shard_map/ppermute | solution.py:26
  2.5 4.3 %collective-permute-start = (bf16[3,1536]{1,0:T(4,128)(2,1)S(1)}, bf16[3,1536]{1,0:T(4,128)(2,1)S(1)}, u32[]{:S(2)}, u32[]{:S(2)}) collective-permute-start(bf16[3,1536]{1,0:T(4,128)(2,1)S(1)} %get-tuple-element.15), channel_id=1, source_target_pairs={{0,4},{4,8},{8,12},{12,16},{16,20},{20,24},{24,28},{1,5},{5,9},{9,... | collective-permute-start | bytes 27656 | tf_op jit(solution)/shard_map/ppermute | solution.py:25
  8.1 0.7 %copy-start.3 = (bf16[128,1024]{0,1:T(8,128)(2,1)}, bf16[128,1024]{0,1:T(8,128)(2,1)S(1)}, u32[]{:S(2)}) copy-start(bf16[128,1024]{0,1:T(8,128)(2,1)S(1)} %copy.48) | copy-start | bytes 786436
  8.6 1.7 %copy-start = (f32[16,64,128]{2,1,0:T(8,128)}, f32[16,64,128]{2,1,0:T(8,128)S(1)}, u32[]{:S(2)}) copy-start(f32[16,64,128]{2,1,0:T(8,128)S(1)} %fusion.40.refs_1_) | copy-start | bytes 1572868
  9.1 1.2 %copy-start.1 = (f32[16,64,128]{2,1,0:T(8,128)}, f32[16,64,128]{2,1,0:T(8,128)S(1)}, u32[]{:S(2)}) copy-start(f32[16,64,128]{2,1,0:T(8,128)S(1)} %fusion.38.refs_2_) | copy-start | bytes 1572868
  10.3 5.1 %collective-permute-start.2 = (f32[33,64,128]{2,1,0:T(8,128)}, f32[33,64,128]{2,1,0:T(8,128)S(1)}, u32[]{:S(2)}, u32[]{:S(2)}) collective-permute-start(f32[33,64,128]{2,1,0:T(8,128)} %pad_maximum_fusion), channel_id=1, source_target_pairs={{0,4},{4,0},{8,12},{12,8},{16,20},{20,16},{24,28},{28,24},{1,5},{5... | collective-permute-start | bytes 3244040 | tf_op jit(solution)/shard_map/ppermute | solution.py:265
  15.4 1.6 %copy-start.2 = (f32[33,64,128]{2,1,0:T(8,128)}, f32[33,64,128]{2,1,0:T(8,128)S(1)}, u32[]{:S(2)}) copy-start(f32[33,64,128]{2,1,0:T(8,128)S(1)} %collective-permute-done.2.refs_0_) | copy-start | bytes 3244036
  17.0 5.3 %copy-start.4 = (bf16[128,1024]{0,1:T(8,128)(2,1)S(1)}, bf16[128,1024]{0,1:T(8,128)(2,1)}, u32[]{:S(2)}) copy-start(bf16[128,1024]{0,1:T(8,128)(2,1)} %copy-done.3) | copy-start | bytes 786436
  17.0 5.3 %copy-start.17 = (f32[16]{0:T(128)S(1)}, f32[16]{0:T(128)}, u32[]{:S(2)}) copy-start(f32[16]{0:T(128)} %param.14) | copy-start | bytes 196
  19.7 9.8 %collective-permute-start.3 = (bf16[17,64,128]{2,1,0:T(8,128)(2,1)}, bf16[17,64,128]{2,1,0:T(8,128)(2,1)S(1)}, u32[]{:S(2)}, u32[]{:S(2)}) collective-permute-start(bf16[17,64,128]{2,1,0:T(8,128)(2,1)} %get-tuple-element.17), channel_id=1, source_target_pairs={{0,8},{4,12},{8,0},{12,4},{16,24},{20,28},{24,16},{28,20},{1,9},{5... | collective-permute-start | bytes 835592 | tf_op jit(solution)/shard_map/ppermute | solution.py:299
  29.5 1.4 %copy-start.9 = (bf16[17,64,128]{2,1,0:T(8,128)(2,1)}, bf16[17,64,128]{2,1,0:T(8,128)(2,1)S(1)}, u32[]{:S(2)}) copy-start(bf16[17,64,128]{2,1,0:T(8,128)(2,1)S(1)} %collective-permute-done.3.refs_1_) | copy-start | bytes 835588
  33.1 6.5 %collective-permute-start.4 = (bf16[9,64,128]{2,1,0:T(8,128)(2,1)}, bf16[9,64,128]{2,1,0:T(8,128)(2,1)S(1)}, u32[]{:S(2)}, u32[]{:S(2)}) collective-permute-start(bf16[9,64,128]{2,1,0:T(8,128)(2,1)} %get-tuple-element.19), channel_id=1, source_target_pairs={{0,16},{4,20},{8,24},{12,28},{16,0},{20,4},{24,8},{28,12},{1,17},{... | collective-permute-start | bytes 442376 | tf_op jit(solution)/shard_map/ppermute | solution.py:299
  39.6 0.7 %copy-start.11 = (bf16[9,64,128]{2,1,0:T(8,128)(2,1)}, bf16[9,64,128]{2,1,0:T(8,128)(2,1)S(1)}, u32[]{:S(2)}) copy-start(bf16[9,64,128]{2,1,0:T(8,128)(2,1)S(1)} %collective-permute-done.4.refs_2_) | copy-start | bytes 442372
  42.9 2.1 %collective-permute-start.5 = (f32[16,64,128]{2,1,0:T(8,128)}, f32[16,64,128]{2,1,0:T(8,128)S(1)}, u32[]{:S(2)}, u32[]{:S(2)}) collective-permute-start(f32[16,64,128]{2,1,0:T(8,128)} %get-tuple-element.23), channel_id=1, source_target_pairs={{0,4},{4,0},{8,12},{12,8},{16,20},{20,16},{24,28},{28,24},{1,5},{5... | collective-permute-start | bytes 1572872 | tf_op jit(solution)/shard_map/ppermute | solution.py:345
  43.1 1.4 %copy-start.6 = (f32[16,64,128]{2,1,0:T(8,128)S(1)}, f32[16,64,128]{2,1,0:T(8,128)}, u32[]{:S(2)}) copy-start(f32[16,64,128]{2,1,0:T(8,128)} %get-tuple-element.24) | copy-start | bytes 1572868
  44.5 1.0 %copy-start.7 = (f32[128,16,64]{0,2,1:T(8,128)S(1)}, f32[128,16,64]{0,2,1:T(8,128)}, u32[]{:S(2)}) copy-start(f32[128,16,64]{0,2,1:T(8,128)} %fusion.2) | copy-start | bytes 1572868
  45.5 1.0 %copy-start.8 = (f32[128,16,64]{0,2,1:T(8,128)S(1)}, f32[128,16,64]{0,2,1:T(8,128)}, u32[]{:S(2)}) copy-start(f32[128,16,64]{0,2,1:T(8,128)} %fusion.3) | copy-start | bytes 1572868
  46.5 1.0 %copy-start.5 = (bf16[256,1024]{1,0:T(8,128)(2,1)S(1)}, bf16[256,1024]{1,0:T(8,128)(2,1)}, u32[]{:S(2)}) copy-start(bf16[256,1024]{1,0:T(8,128)(2,1)} %param.10) | copy-start | bytes 1572868
  47.6 4.0 %copy-start.15 = (f32[1024]{0:T(1024)S(1)}, f32[1024]{0:T(1024)}, u32[]{:S(2)}) copy-start(f32[1024]{0:T(1024)} %param.17) | copy-start | bytes 12292
  48.0 3.6 %collective-permute-start.6 = (f32[256]{0:T(256)S(1)}, f32[256]{0:T(256)S(1)}, u32[]{:S(2)}, u32[]{:S(2)}) collective-permute-start(f32[256]{0:T(256)S(1)} %get-tuple-element.29), channel_id=1, source_target_pairs={{0,1},{1,0},{2,3},{3,2},{4,5},{5,4},{6,7},{7,6},{8,9},{9,8},{10,11... | collective-permute-start | bytes 3080 | tf_op jit(solution)/shard_map/ppermute | solution.py:32

commit v7 on v4

--- a/solution.py
+++ b/solution.py
@@ -107,31 +107,30 @@
     core = seq_pos % 2
     upper = core == 1
     pairs = [(i, i ^ 1) for i in range(seq_count)]
-    got = lax.ppermute(pack((first_loc, second_loc), (e1, e2), jnp.float32), "seq", pairs)
-    (p1, p2), (q1, q2) = unpack(got, 2, first_loc.shape)
-    ones = jnp.ones((heads,), jnp.float32)
-    pair_f = col(jnp.where(upper, ones, q1)) * first_loc + col(jnp.where(upper, e1, ones)) * p1
-    pair_g = col(jnp.where(upper, q2, ones)) * second_loc + col(jnp.where(upper, ones, e2)) * p2
-    low_f = jnp.where(upper, p1, first_loc)
-    low_fe = jnp.where(upper, q1, e1)
-    high_g = jnp.where(upper, second_loc, p2)
-    high_ge = jnp.where(upper, e2, q2)
-
-    def mine(x):
-        return lax.dynamic_slice_in_dim(x, core * half, half, 0)
+
+    def part(x, which):
+        return lax.dynamic_slice_in_dim(x, which * half, half, 0)
+
+    theirs = 1 - core
+    sent = pack(
+        (part(first_loc, theirs), part(second_loc, theirs)), (part(e1, theirs), part(e2, theirs)), jnp.float32
+    )
+    got = lax.ppermute(sent, "seq", pairs)
+    (p1, p2), (q1, q2) = unpack(got, 2, (half, *first_loc.shape[1:]))
+    l1, l2, e1h, e2h = part(first_loc, core), part(second_loc, core), part(e1, core), part(e2, core)
+    ones = jnp.ones((half,), jnp.float32)
+    pair_f = col(jnp.where(upper, ones, q1)) * l1 + col(jnp.where(upper, e1h, ones)) * p1
+    pair_g = col(jnp.where(upper, q2, ones)) * l2 + col(jnp.where(upper, ones, e2h)) * p2
+    low_f = jnp.where(upper, p1, l1)
+    low_fe = jnp.where(upper, q1, e1h)
+    high_g = jnp.where(upper, l2, p2)
+    high_ge = jnp.where(upper, e2h, q2)
 
     prefix, wrapped = butterfly_states(
-        mine(pair_f),
-        mine(pair_g),
-        mine(e1 * q1),
-        mine(e2 * q2),
-        seq_pos // 2,
-        seq_count // 2,
-        2,
-        seq_count,
-    )
-    after_low = col(mine(low_fe)) * prefix + mine(low_f)
-    before_high = col(mine(high_ge)) * wrapped + mine(high_g)
+        pair_f, pair_g, e1h * q1, e2h * q2, seq_pos // 2, seq_count // 2, 2, seq_count
+    )
+    after_low = col(low_fe) * prefix + low_f
+    before_high = col(high_ge) * wrapped + high_g
     own = (jnp.where(upper, after_low, prefix), jnp.where(upper, wrapped, before_high))
     other = (jnp.where(upper, prefix, after_low), jnp.where(upper, before_high, wrapped))
     got_1, got_2 = lax.ppermute(other, "seq", pairs)

time: 50.5 us -> 49.6 us (0.982)
  other arithmetic: 11.4 us -> 7.52 us
  local copies, waits for them, and re-layouts: 11.4 us -> 14.7 us
  starting transfers between devices: 14 us -> 12.4 us
  waiting for transfers between devices: 9.24 us -> 10.4 us
    unnamed x48 -> x52, local copies, waits for them, and re-layouts: 3 us -> 8.03 us
    select_n x2 -> x0, other arithmetic: 2.06 us -> none  [the longest x1 1.42 us: block_states(): low_fe = jnp.where(upper, q1, e1)]
    ppermute x1, starting transfers between devices: 2.53 us -> 0.98 us  [butterfly_states(): got = lax.ppermute(pack((sent,), (sent_e,), LINK), 'seq', pairs)]
    ppermute x1, waiting for transfers between devices: 2.23 us -> 3.75 us  [butterfly_states(): got = lax.ppermute(pack((sent,), (sent_e,), LINK), 'seq', pairs)]
    slice x3, local copies, waits for them, and re-layouts: 2.27 us -> 1.09 us  [unpack(): message[i * rows:(i + 1) * rows].astype(jnp.float32).reshape(shape)]
    select_n x1, other arithmetic: 0.66 us -> 1.51 us  [butterfly_states(): jnp.where(lower, ones, e_f)]
    select_n x1, other arithmetic: 1.08 us -> 0.29 us  [block_states(): jnp.where(upper, prefix, after_low)]
    concatenate x3, other arithmetic: 0.8 us -> 1.57 us  [pack(): return jnp.concatenate([f.astype(kind) for f in flat] + [tail], axis=0)]
where the time goes in v7:
time: 49.6 us; the launch traced here: 49 us
  local copies, waits for them, and re-layouts  14.7 us (30%)
  starting transfers between devices  12.4 us (25%)
  waiting for transfers between devices  10.4 us (21%)
  other arithmetic  7.52 us (15%)
  matrix products  3.4 us (7%)
  between operations  0.55 us (1%)
    unnamed x52, local copies, waits for them, and re-layouts  8.03 us
    ppermute x1, waiting for transfers between devices, butterfly_states(): got = lax.ppermute(pack((sent,), (sent_e,), LINK), 'seq', pairs)  3.75 us
    ppermute x1, starting transfers between devices, extended_2(): low = lax.ppermute(tail, axis, forward)  3.03 us
    exp x4, local copies, waits for them, and re-layouts, finish_block(): total_out = partial_out + jnp.exp(log_cum)[:, :, None] * inter_out  2.84 us
    ppermute x1, waiting for transfers between devices, butterfly_states(): got = lax.ppermute(pack((sub_f, sub_g), (e_f, e_g), LINK), 'seq', pairs)  2.72 us
    ppermute x1, starting transfers between devices, block_states(): got = lax.ppermute(sent, 'seq', pairs)  2.56 us
    ppermute x1, starting transfers between devices, butterfly_states(): got = lax.ppermute(pack((sub_f, sub_g), (e_f, e_g), LINK), 'seq', pairs)  2.37 us
    ppermute x1, waiting for transfers between devices, partner(): lax.ppermute(array, axis, [(i, i ^ 1 << stride) for i in range(lax.axis_s...  1.99 us
  transfers between devices with their start and end apart: 8, of which 4 were waited for; matrix products, arithmetic and copies ran while one was open for 18% of the time, Pallas kernels for 0%

profile of v7, /device:TPU:0, one launch (start us, length us, event | category | flops | bytes accessed | tf_op | source)
XLA Modules:
  0.0 49.0 jit_solution(16660897713044433731)
XLA Ops:
  0.0 1.1 %constant_dynamic-update-slice_fusion.3 = bf16[256,1536]{1,0:T(8,128)(2,1)S(1)} fusion(bf16[256,1024]{1,0:T(8,128)(2,1)} %param.9), kind=kLoop, calls=%fused_computation.117 | loop fusion | bytes 1048576
  1.2 1.3 %collective-permute-start.1 = (bf16[3,1536]{1,0:T(4,128)(2,1)S(1)}, bf16[3,1536]{1,0:T(4,128)(2,1)S(1)}, u32[]{:S(2)}, u32[]{:S(2)}) collective-permute-start(bf16[3,1536]{1,0:T(4,128)(2,1)S(1)} %get-tuple-element.8), channel_id=1, source_target_pairs={{4,0},{8,4},{12,8},{16,12},{20,16},{24,20},{28,24},{5,1},{9,5},{13... | collective-permute-start | bytes 27656 | tf_op jit(solution)/shard_map/ppermute | solution.py:24
  2.5 3.0 %collective-permute-start = (bf16[3,1536]{1,0:T(4,128)(2,1)S(1)}, bf16[3,1536]{1,0:T(4,128)(2,1)S(1)}, u32[]{:S(2)}, u32[]{:S(2)}) collective-permute-start(bf16[3,1536]{1,0:T(4,128)(2,1)S(1)} %get-tuple-element.7), channel_id=1, source_target_pairs={{0,4},{4,8},{8,12},{12,16},{16,20},{20,24},{24,28},{1,5},{5,9},{9,... | collective-permute-start | bytes 27656 | tf_op jit(solution)/shard_map/ppermute | solution.py:23
  5.6 0.6 %copy-done.5 = f32[256,16]{0,1:T(8,128)S(1)} copy-done((f32[256,16]{0,1:T(8,128)S(1)}, f32[256,16]{0,1:T(8,128)}, u32[]{:S(2)}) %copy-start.5) | copy-done | bytes 16408
  6.3 0.6 %copy-done.23 = f32[16]{0:T(128)S(1)} copy-done((f32[16]{0:T(128)S(1)}, f32[16]{0:T(128)}, u32[]{:S(2)}) %copy-start.23) | copy-done | bytes 88
  7.1 0.2 reduce_window_sum.18
  7.4 0.2 reduce_window_sum.17
  7.7 0.7 %copy-done.6 = f32[4,1024]{1,0:T(4,128)S(1)} copy-done((f32[4,1024]{1,0:T(4,128)S(1)}, f32[4,1024]{1,0:T(4,128)}, u32[]{:S(2)}) %copy-start.6) | copy-done | bytes 16408
  8.4 0.7 %copy-done.9 = f32[4,512]{1,0:T(4,128)S(1)} copy-done((f32[4,512]{1,0:T(4,128)S(1)}, f32[4,512]{1,0:T(4,128)}, u32[]{:S(2)}) %copy-start.9) | copy-done | bytes 8216
  9.3 0.6 %slice_bitcast_fusion.1 = (f32[16,128]{1,0:T(8,128)}, f32[128,16]{0,1:T(8,128)S(1)}, f32[128,16]{0,1:T(8,128)S(1)}, f32[16,128]{1,0:T(8,128)}) fusion(f32[256,16]{0,1:T(8,128)S(1)} %compare_select_fusion, f32[128,16]{0,1:T(8,128)S(1)} %copy.34, f32[16]{0:T(128)S(1)} %slice_bitcast_fusion.3, f32[128,16]{0,1:T(8,128)S(1)} %copy.37, f32[16]{0:T(128)S(1)} %slice_bitcast_fusion.2), kind=kLoop, calls=%fused_computation.123 | loop fusion | flops 8192 | bytes 65664 | tf_op jit(solution)/shard_map/transpose | solution.py:197
  10.2 1.0 %multiply_convert_fusion.4 = (bf16[128,1536]{1,0:T(8,128)(2,1)S(1)}, bf16[128,1536]{1,0:T(8,128)(2,1)S(1)}) fusion(f32[131,1536]{1,0:T(8,128)S(1)} %maximum_convert_fusion, f32[1536]{0:T(1024)S(1)} %get-tuple-element.10, f32[1536]{0:T(1024)S(1)} %get-tuple-element.11, f32[1536]{0:T(1024)S(1)} %get-tuple-element.12, f32[1536]{0:T(1024)S(1)} %get-tuple-element.9, ...), kind=kLoop, calls=%fused_computation.33 | loop fusion | flops 4718592 | bytes 7102464 | tf_op jit(solution)/shard_map/convert_element_type | solution.py:187
  11.4 0.2 copy.35
  11.6 0.2 fusion.48
  11.8 0.2 fusion.46
  12.1 0.8 %pad_maximum_fusion = f32[1032,128]{1,0:T(8,128)} fusion(f32[8,128]{1,0:T(8,128)S(1)} %select_maximum_fusion, f32[512,128]{1,0:T(8,128)S(1)} %bitcast.122, f32[512,128]{1,0:T(8,128)S(1)} %bitcast.123), kind=kLoop, calls=%fused_computation.38 | loop fusion | flops 264192 | bytes 1056768 | tf_op jit(solution)/shard_map/concatenate | solution.py:44
  12.9 2.6 %collective-permute-start.2 = (f32[1032,128]{1,0:T(8,128)}, f32[1032,128]{1,0:T(8,128)}, u32[]{:S(2)}, u32[]{:S(2)}) collective-permute-start(f32[1032,128]{1,0:T(8,128)} %pad_maximum_fusion), channel_id=1, source_target_pairs={{0,4},{4,0},{8,12},{12,8},{16,20},{20,16},{24,28},{28,24},{1,5},{5... | collective-permute-start | bytes 1585160 | tf_op jit(solution)/shard_map/ppermute | solution.py:118
  15.5 1.9 %collective-permute-done.2 = f32[1032,128]{1,0:T(8,128)} collective-permute-done((f32[1032,128]{1,0:T(8,128)}, f32[1032,128]{1,0:T(8,128)}, u32[]{:S(2)}, u32[]{:S(2)}) %collective-permute-start.2) | collective-permute-done | bytes 528416 | tf_op jit(solution)/shard_map/ppermute | solution.py:118
  17.3 1.5 %broadcast_select_fusion.4 = (f32[8]{0:T(128)}, f32[8]{0:T(128)S(1)}, f32[8]{0:T(128)}, f32[8]{0:T(128)S(1)}, f32[8]{0:T(128)S(1)}, /*index=5*/f32[8]{0:T(128)},...) fusion(pred[]{:T(512)S(6)} %eq.17, f32[1032,128]{1,0:T(8,128)} %collective-permute-done.2, f32[16]{0:T(128)S(1)} %fusion.97, ...), kind=kLoop, calls=%fused_computation.162 | loop fusion | flops 96 | bytes 518 | tf_op jit(solution)/shard_map/jit(_where)/select_n | solution.py:79
  18.9 0.6 %copy-done.19 = f32[8]{0:T(128)} copy-done((f32[8]{0:T(128)}, f32[8]{0:T(128)S(1)}, u32[]{:S(2)}) %copy-start.19) | copy-done | bytes 56
  19.5 1.1 %fusion.104 = (f32[512,128]{1,0:T(8,128)S(1)}, f32[512,128]{1,0:T(8,128)S(1)}) fusion(f32[1032,128]{1,0:T(8,128)} %collective-permute-done.2), kind=kLoop, calls=%fused_computation.203 | loop fusion | bytes 1048576 | tf_op jit(solution)/shard_map/slice | solution.py:50
  20.8 0.7 %pad_maximum_fusion.1 = bf16[1032,128]{1,0:T(8,128)(2,1)} fusion(bf16[8,128]{1,0:T(8,128)(2,1)S(1)} %fusion.82, bf16[512,128]{1,0:T(8,128)(2,1)S(1)} %bitcast.127, bf16[512,128]{1,0:T(8,128)(2,1)S(1)} %bitcast.126), kind=kLoop, calls=%fused_computation.73 | loop fusion | flops 792576 | bytes 528384 | tf_op jit(solution)/shard_map/concatenate | solution.py:44
  21.5 2.4 %collective-permute-start.3 = (bf16[1032,128]{1,0:T(8,128)(2,1)}, bf16[1032,128]{1,0:T(8,128)(2,1)S(1)}, u32[]{:S(2)}, u32[]{:S(2)}) collective-permute-start(bf16[1032,128]{1,0:T(8,128)(2,1)} %pad_maximum_fusion.1), channel_id=1, source_target_pairs={{0,8},{4,12},{8,0},{12,4},{16,24},{20,28},{24,16},{28,20},{1,9},{5... | collective-permute-start | bytes 792584 | tf_op jit(solution)/shard_map/ppermute | solution.py:77
  23.9 0.6 %exp.50 = f32[128,16]{1,0:T(8,128)} exponential(f32[128,16]{1,0:T(8,128)S(1)} %reduce_window_sum.17) | non-fusion elementwise | bytes 16384 | tf_op jit(solution)/shard_map/exp | solution.py:213
  24.5 0.6 %exp.57 = f32[128,16]{1,0:T(8,128)} exponential(f32[128,16]{1,0:T(8,128)S(1)} %reduce_window_sum.18) | non-fusion elementwise | bytes 16384 | tf_op jit(solution)/shard_map/exp | solution.py:213
  25.1 0.7 %copy.31 = f32[16,128]{1,0:T(8,128)} copy(f32[16,128]{0,1:T(8,128)S(1)} %bitcast.117) | data formatting | bytes 16384 | tf_op jit(solution)/shard_map/transpose | solution.py:195
  25.8 1.5 %copy.33 = f32[128,16]{0,1:T(8,128)} copy(f32[128,16]{1,0:T(8,128)} %exp.50) | data formatting | bytes 16384 | tf_op jit(solution)/shard_map/exp | solution.py:213
  27.3 0.7 %copy.38 = f32[16,128]{1,0:T(8,128)} copy(f32[16,128]{0,1:T(8,128)S(1)} %bitcast.116) | data formatting | bytes 16384 | tf_op jit(solution)/shard_map/transpose | solution.py:195
  28.2 2.7 %collective-permute-done.3 = bf16[1032,128]{1,0:T(8,128)(2,1)S(1)} collective-permute-done((bf16[1032,128]{1,0:T(8,128)(2,1)}, bf16[1032,128]{1,0:T(8,128)(2,1)S(1)}, u32[]{:S(2)}, u32[]{:S(2)}) %collective-permute-start.3) | collective-permute-done | bytes 264224 | tf_op jit(solution)/shard_map/ppermute | solution.py:77
  31.0 0.7 %copy-done.20 = f32[8]{0:T(128)S(1)} copy-done((f32[8]{0:T(128)S(1)}, f32[8]{0:T(128)}, u32[]{:S(2)}) %copy-start.20) | copy-done | bytes 56
  31.8 0.6 %copy-done.18 = f32[8]{0:T(128)S(1)} copy-done((f32[8]{0:T(128)S(1)}, f32[8]{0:T(128)}, u32[]{:S(2)}) %copy-start.18) | copy-done | bytes 56
  32.4 0.2 fusion.43
  32.7 1.0 %collective-permute-start.4 = (bf16[520,128]{1,0:T(8,128)(2,1)S(1)}, bf16[520,128]{1,0:T(8,128)(2,1)S(1)}, u32[]{:S(2)}, u32[]{:S(2)}) collective-permute-start(bf16[520,128]{1,0:T(8,128)(2,1)S(1)} %pad_maximum_fusion.2), channel_id=1, source_target_pairs={{0,16},{4,20},{8,24},{12,28},{16,0},{20,4},{24,8},{28,12},{1,17},{... | collective-permute-start | bytes 399368 | tf_op jit(solution)/shard_map/ppermute | solution.py:90
  33.6 0.6 %fusion.2 = f32[128,16,64]{0,2,1:T(8,128)S(1)} fusion(bf16[128,16,64]{0,2,1:T(8,128)(2,1)S(1)} %bitcast.121, f32[16,128]{1,0:T(8,128)S(1)} %copy-done.11, f32[16,128]{1,0:T(8,128)S(1)} %copy-done.8, f32[128,128]{1,0:T(8,128)S(1)} %fusion.68, pred[128,128]{1,0:T(8,128)(4,1)S(1)} %iota_compare_fusion, f32[16]{0:T(128)S(1)} %copy-done.24), kind=kOutput, calls=%fused_computation.8 | convolution fusion | flops 35520512 | bytes 884800 | tf_op jit(solution)/shard_map/hts,shp->thp/dot_general | solution.py:198
  34.2 3.8 %collective-permute-done.4 = bf16[520,128]{1,0:T(8,128)(2,1)S(1)} collective-permute-done((bf16[520,128]{1,0:T(8,128)(2,1)S(1)}, bf16[520,128]{1,0:T(8,128)(2,1)S(1)}, u32[]{:S(2)}, u32[]{:S(2)}) %collective-permute-start.4) | collective-permute-done | bytes 133152 | tf_op jit(solution)/shard_map/ppermute | solution.py:90
  38.0 0.7 %copy-done.21 = f32[8]{0:T(128)S(1)} copy-done((f32[8]{0:T(128)S(1)}, f32[8]{0:T(128)}, u32[]{:S(2)}) %copy-start.21) | copy-done | bytes 56
  38.7 0.3 fusion.55
  39.2 0.5 %collective-permute-start.6 = (f32[8,64,128]{2,1,0:T(8,128)S(1)}, f32[8,64,128]{2,1,0:T(8,128)S(1)}, u32[]{:S(2)}, u32[]{:S(2)}) collective-permute-start(f32[8,64,128]{2,1,0:T(8,128)S(1)} %get-tuple-element.49), channel_id=1, source_target_pairs={{0,4},{4,0},{8,12},{12,8},{16,20},{20,16},{24,28},{28,24},{1,5},{5... | collective-permute-start | bytes 786440 | tf_op jit(solution)/shard_map/ppermute | solution.py:136
  39.7 1.4 %fusion.3 = f32[128,16,64]{0,2,1:T(8,128)} fusion(bf16[128,16,64]{0,2,1:T(8,128)(2,1)S(1)} %bitcast.119, f32[16,128]{1,0:T(8,128)S(1)} %copy-done.10, f32[16,128]{1,0:T(8,128)S(1)} %copy-done.7, f32[128,128]{1,0:T(8,128)S(1)} %fusion.63, pred[128,128]{1,0:T(8,128)(4,1)S(1)} %iota_compare_fusion, f32[16]{0:T(128)S(1)} %copy-done.24), kind=kOutput, calls=%fused_computation.9 | convolution fusion | flops 35520512 | bytes 884800 | tf_op jit(solution)/shard_map/hts,shp->thp/dot_general | solution.py:198
  41.1 0.4 fusion.1
  41.5 0.2 copy.41
  41.7 0.8 %copy-done.1 = f32[128,16,64]{0,2,1:T(8,128)S(1)} copy-done((f32[128,16,64]{0,2,1:T(8,128)S(1)}, f32[128,16,64]{0,2,1:T(8,128)}, u32[]{:S(2)}) %copy-start.1) | copy-done | bytes 524312
  42.5 0.4 fusion
  43.0 0.2 copy.42
  43.2 0.8 %copy-done = bf16[256,1024]{1,0:T(8,128)(2,1)S(1)} copy-done((bf16[256,1024]{1,0:T(8,128)(2,1)S(1)}, bf16[256,1024]{1,0:T(8,128)(2,1)}, u32[]{:S(2)}) %copy-start) | copy-done | bytes 524312
  44.0 0.4 multiply_reduce_fusion
  44.4 1.6 %collective-permute-start.7 = (f32[256]{0:T(256)S(1)}, f32[256]{0:T(256)S(1)}, u32[]{:S(2)}, u32[]{:S(2)}) collective-permute-start(f32[256]{0:T(256)S(1)} %get-tuple-element.13), channel_id=1, source_target_pairs={{0,1},{1,0},{2,3},{3,2},{4,5},{5,4},{6,7},{7,6},{8,9},{9,8},{10,11... | collective-permute-start | bytes 3080 | tf_op jit(solution)/shard_map/ppermute | solution.py:30
  46.0 2.0 %collective-permute-done.7 = f32[256]{0:T(256)S(1)} collective-permute-done((f32[256]{0:T(256)S(1)}, f32[256]{0:T(256)S(1)}, u32[]{:S(2)}, u32[]{:S(2)}) %collective-permute-start.7) | collective-permute-done | bytes 1056 | tf_op jit(solution)/shard_map/ppermute | solution.py:30
  48.0 1.0 %multiply_convert_fusion = bf16[256,1024]{1,0:T(8,128)(2,1)} fusion(f32[256,1024]{1,0:T(8,128)S(1)} %get-tuple-element.14, f32[1024]{0:T(1024)S(1)} %copy-done.17, f32[256]{0:T(256)S(1)} %add_rsqrt_fusion), kind=kLoop, calls=%fused_computation.14 | loop fusion | flops 786432 | bytes 1577984 | tf_op jit(solution)/shard_map/convert_element_type | solution.py:237
  (92 shorter events, 2.2 us)
Async XLA Ops:
  0.0 1.1 %copy-start.2 = (bf16[256,512]{1,0:T(8,128)(2,1)S(1)}, bf16[256,512]{1,0:T(8,128)(2,1)}, u32[]{:S(2)}) copy-start(bf16[256,512]{1,0:T(8,128)(2,1)} %param.11) | copy-start | bytes 786436
  1.2 8.7 %collective-permute-start.1 = (bf16[3,1536]{1,0:T(4,128)(2,1)S(1)}, bf16[3,1536]{1,0:T(4,128)(2,1)S(1)}, u32[]{:S(2)}, u32[]{:S(2)}) collective-permute-start(bf16[3,1536]{1,0:T(4,128)(2,1)S(1)} %get-tuple-element.8), channel_id=1, source_target_pairs={{4,0},{8,4},{12,8},{16,12},{20,16},{24,20},{28,24},{5,1},{9,5},{13... | collective-permute-start | bytes 27656 | tf_op jit(solution)/shard_map/ppermute | solution.py:24
  2.5 7.6 %collective-permute-start = (bf16[3,1536]{1,0:T(4,128)(2,1)S(1)}, bf16[3,1536]{1,0:T(4,128)(2,1)S(1)}, u32[]{:S(2)}, u32[]{:S(2)}) collective-permute-start(bf16[3,1536]{1,0:T(4,128)(2,1)S(1)} %get-tuple-element.7), channel_id=1, source_target_pairs={{0,4},{4,8},{8,12},{12,16},{16,20},{20,24},{24,28},{1,5},{5,9},{9,... | collective-permute-start | bytes 27656 | tf_op jit(solution)/shard_map/ppermute | solution.py:23
  5.5 0.7 %copy-start.5 = (f32[256,16]{0,1:T(8,128)S(1)}, f32[256,16]{0,1:T(8,128)}, u32[]{:S(2)}) copy-start(f32[256,16]{0,1:T(8,128)} %param.12) | copy-start | bytes 49156
  6.3 0.7 %copy-start.23 = (f32[16]{0:T(128)S(1)}, f32[16]{0:T(128)}, u32[]{:S(2)}) copy-start(f32[16]{0:T(128)} %param.13) | copy-start | bytes 196
  7.7 0.7 %copy-start.6 = (f32[4,1024]{1,0:T(4,128)S(1)}, f32[4,1024]{1,0:T(4,128)}, u32[]{:S(2)}) copy-start(f32[4,1024]{1,0:T(4,128)} %param.15) | copy-start | bytes 49156
  8.4 0.7 %copy-start.9 = (f32[4,512]{1,0:T(4,128)S(1)}, f32[4,512]{1,0:T(4,128)}, u32[]{:S(2)}) copy-start(f32[4,512]{1,0:T(4,128)} %param.16) | copy-start | bytes 24580
  12.9 4.4 %collective-permute-start.2 = (f32[1032,128]{1,0:T(8,128)}, f32[1032,128]{1,0:T(8,128)}, u32[]{:S(2)}, u32[]{:S(2)}) collective-permute-start(f32[1032,128]{1,0:T(8,128)} %pad_maximum_fusion), channel_id=1, source_target_pairs={{0,4},{4,0},{8,12},{12,8},{16,20},{20,16},{24,28},{28,24},{1,5},{5... | collective-permute-start | bytes 1585160 | tf_op jit(solution)/shard_map/ppermute | solution.py:118
  18.9 0.6 %copy-start.19 = (f32[8]{0:T(128)}, f32[8]{0:T(128)S(1)}, u32[]{:S(2)}) copy-start(f32[8]{0:T(128)S(1)} %get-tuple-element.45) | copy-start | bytes 100
  18.9 1.8 %copy-start.12 = (f32[8]{0:T(128)}, f32[8]{0:T(128)S(1)}, u32[]{:S(2)}) copy-start(f32[8]{0:T(128)S(1)} %get-tuple-element.41) | copy-start | bytes 100
  18.9 1.8 %copy-start.14 = (f32[8]{0:T(128)}, f32[8]{0:T(128)S(1)}, u32[]{:S(2)}) copy-start(f32[8]{0:T(128)S(1)} %get-tuple-element.60) | copy-start | bytes 100
  21.5 9.4 %collective-permute-start.3 = (bf16[1032,128]{1,0:T(8,128)(2,1)}, bf16[1032,128]{1,0:T(8,128)(2,1)S(1)}, u32[]{:S(2)}, u32[]{:S(2)}) collective-permute-start(bf16[1032,128]{1,0:T(8,128)(2,1)} %pad_maximum_fusion.1), channel_id=1, source_target_pairs={{0,8},{4,12},{8,0},{12,4},{16,24},{20,28},{24,16},{28,20},{1,9},{5... | collective-permute-start | bytes 792584 | tf_op jit(solution)/shard_map/ppermute | solution.py:77
  25.8 2.2 %copy-start.3 = (f32[128,16]{1,0:T(8,128)S(1)}, f32[128,16]{1,0:T(8,128)}, u32[]{:S(2)}) copy-start(f32[128,16]{1,0:T(8,128)} %exp.57) | copy-start | bytes 24580
  31.0 0.7 %copy-start.20 = (f32[8]{0:T(128)S(1)}, f32[8]{0:T(128)}, u32[]{:S(2)}) copy-start(f32[8]{0:T(128)} %copy-done.19) | copy-start | bytes 100
  31.7 0.6 %copy-start.18 = (f32[8]{0:T(128)S(1)}, f32[8]{0:T(128)}, u32[]{:S(2)}) copy-start(f32[8]{0:T(128)} %get-tuple-element.44) | copy-start | bytes 100
  31.7 0.6 %copy-start.13 = (f32[8]{0:T(128)S(1)}, f32[8]{0:T(128)}, u32[]{:S(2)}) copy-start(f32[8]{0:T(128)} %copy-done.12) | copy-start | bytes 100
  31.7 0.7 %copy-start.15 = (f32[8]{0:T(128)S(1)}, f32[8]{0:T(128)}, u32[]{:S(2)}) copy-start(f32[8]{0:T(128)} %copy-done.14) | copy-start | bytes 100
  31.7 0.7 %copy-start.16 = (f32[8]{0:T(128)S(1)}, f32[8]{0:T(128)}, u32[]{:S(2)}) copy-start(f32[8]{0:T(128)} %get-tuple-element.19) | copy-start | bytes 100
  32.6 1.0 %copy-start.8 = (f32[16,128]{1,0:T(8,128)S(1)}, f32[16,128]{1,0:T(8,128)}, u32[]{:S(2)}) copy-start(f32[16,128]{1,0:T(8,128)} %copy.31) | copy-start | bytes 24580
  32.6 1.0 %copy-start.11 = (f32[16,128]{1,0:T(8,128)S(1)}, f32[16,128]{1,0:T(8,128)}, u32[]{:S(2)}) copy-start(f32[16,128]{1,0:T(8,128)} %get-tuple-element.54) | copy-start | bytes 24580
  32.6 1.0 %copy-start.24 = (f32[16]{0:T(128)S(1)}, f32[16]{0:T(128)}, u32[]{:S(2)}) copy-start(f32[16]{0:T(128)} %param.14) | copy-start | bytes 196
  32.7 5.3 %collective-permute-start.4 = (bf16[520,128]{1,0:T(8,128)(2,1)S(1)}, bf16[520,128]{1,0:T(8,128)(2,1)S(1)}, u32[]{:S(2)}, u32[]{:S(2)}) collective-permute-start(bf16[520,128]{1,0:T(8,128)(2,1)S(1)} %pad_maximum_fusion.2), channel_id=1, source_target_pairs={{0,16},{4,20},{8,24},{12,28},{16,0},{20,4},{24,8},{28,12},{1,17},{... | collective-permute-start | bytes 399368 | tf_op jit(solution)/shard_map/ppermute | solution.py:90
  38.0 0.7 %copy-start.21 = (f32[8]{0:T(128)S(1)}, f32[8]{0:T(128)}, u32[]{:S(2)}) copy-start(f32[8]{0:T(128)} %get-tuple-element.35) | copy-start | bytes 100
  38.0 0.7 %copy-start.22 = (f32[8]{0:T(128)S(1)}, f32[8]{0:T(128)}, u32[]{:S(2)}) copy-start(f32[8]{0:T(128)} %get-tuple-element.43) | copy-start | bytes 100
  39.0 0.8 %copy-start.7 = (f32[16,128]{1,0:T(8,128)S(1)}, f32[16,128]{1,0:T(8,128)}, u32[]{:S(2)}) copy-start(f32[16,128]{1,0:T(8,128)} %copy.38) | copy-start | bytes 24580
  39.0 0.7 %copy-start.10 = (f32[16,128]{1,0:T(8,128)S(1)}, f32[16,128]{1,0:T(8,128)}, u32[]{:S(2)}) copy-start(f32[16,128]{1,0:T(8,128)} %get-tuple-element.57) | copy-start | bytes 24580
  39.0 2.1 %collective-permute-start.5 = (f32[8,64,128]{2,1,0:T(8,128)S(1)}, f32[8,64,128]{2,1,0:T(8,128)S(1)}, u32[]{:S(2)}, u32[]{:S(2)}) collective-permute-start(f32[8,64,128]{2,1,0:T(8,128)S(1)} %get-tuple-element.29), channel_id=1, source_target_pairs={{0,4},{4,0},{8,12},{12,8},{16,20},{20,16},{24,28},{28,24},{1,5},{5... | collective-permute-start | bytes 786440 | tf_op jit(solution)/shard_map/ppermute | solution.py:136
  39.2 2.5 %collective-permute-start.6 = (f32[8,64,128]{2,1,0:T(8,128)S(1)}, f32[8,64,128]{2,1,0:T(8,128)S(1)}, u32[]{:S(2)}, u32[]{:S(2)}) collective-permute-start(f32[8,64,128]{2,1,0:T(8,128)S(1)} %get-tuple-element.49), channel_id=1, source_target_pairs={{0,4},{4,0},{8,12},{12,8},{16,20},{20,16},{24,28},{28,24},{1,5},{5... | collective-permute-start | bytes 786440 | tf_op jit(solution)/shard_map/ppermute | solution.py:136
  39.7 1.4 %copy-start.4 = (f32[128,16]{0,1:T(8,128)S(1)}, f32[128,16]{0,1:T(8,128)}, u32[]{:S(2)}) copy-start(f32[128,16]{0,1:T(8,128)} %copy.33) | copy-start | bytes 24580
  41.5 1.0 %copy-start.1 = (f32[128,16,64]{0,2,1:T(8,128)S(1)}, f32[128,16,64]{0,2,1:T(8,128)}, u32[]{:S(2)}) copy-start(f32[128,16,64]{0,2,1:T(8,128)} %fusion.3) | copy-start | bytes 1572868
  42.9 1.0 %copy-start = (bf16[256,1024]{1,0:T(8,128)(2,1)S(1)}, bf16[256,1024]{1,0:T(8,128)(2,1)}, u32[]{:S(2)}) copy-start(bf16[256,1024]{1,0:T(8,128)(2,1)} %param.10) | copy-start | bytes 1572868
  44.4 3.7 %copy-start.17 = (f32[1024]{0:T(1024)S(1)}, f32[1024]{0:T(1024)}, u32[]{:S(2)}) copy-start(f32[1024]{0:T(1024)} %param.17) | copy-start | bytes 12292
  44.4 3.6 %collective-permute-start.7 = (f32[256]{0:T(256)S(1)}, f32[256]{0:T(256)S(1)}, u32[]{:S(2)}, u32[]{:S(2)}) collective-permute-start(f32[256]{0:T(256)S(1)} %get-tuple-element.13), channel_id=1, source_target_pairs={{0,1},{1,0},{2,3},{3,2},{4,5},{5,4},{6,7},{7,6},{8,9},{9,8},{10,11... | collective-permute-start | bytes 3080 | tf_op jit(solution)/shard_map/ppermute | solution.py:30

commit v8 on v7

--- a/solution.py
+++ b/solution.py
@@ -166,30 +166,34 @@
     seq_pos = lax.axis_index("seq")
     is_last = seq_pos == seq_count - 1
     my_group = lax.axis_index("head") * head_count // GROUP_HEADS
-    joined = jnp.concatenate([inner_rows, input_proj], axis=1)
-    edge_rows = jnp.concatenate(
-        [joined[tokens - rim_rows :], joined[half_rows - rim_rows : half_rows]], axis=0
-    )
+
+    def edges(rows):
+        return jnp.concatenate(
+            [rows[tokens - rim_rows :], rows[half_rows - rim_rows : half_rows]], axis=0
+        )
+
+    edge_rows = jnp.concatenate([edges(inner_rows), edges(input_proj)], axis=1)
     extended = extended_2(edge_rows, (("seq", 0),), rim_rows)
     lead_first = extended[:rim_rows]
     lead_second = jnp.where(
-        is_last, joined[half_rows - rim_rows : half_rows], extended[3 * rim_rows :]
-    )
-    conv_taps = jnp.concatenate([conv_inner, conv_proj], axis=1)
+        is_last, edge_rows[rim_rows:], extended[3 * rim_rows :]
+    )
     step_size = jax.nn.softplus(step_raw)
     causal = jnp.arange(half_rows)[:, None] >= jnp.arange(half_rows)[None, :]
 
-    def local_block(lead_rows, rows_in, block_step):
+    def conv(lead_rows, rows_in, taps):
         padded = jnp.concatenate([lead_rows, rows_in], axis=0).astype(jnp.float32)
-        conv_sum = jnp.zeros((half_rows, joined.shape[1]), jnp.float32)
+        conv_sum = jnp.zeros((half_rows, rows_in.shape[1]), jnp.float32)
         for offset in range(KERNEL):
-            conv_sum = conv_sum + conv_taps[offset][None, :] * padded[offset : offset + half_rows]
-        conv_out = jax.nn.silu(conv_sum).astype(jnp.bfloat16)
-        inner_conv = conv_out[:, :inner_width].reshape(half_rows, head_count, HEAD_SIZE)
-        b_rows = lax.dynamic_slice_in_dim(conv_out, inner_width + my_group * STATE, STATE, 1)
-        c_rows = lax.dynamic_slice_in_dim(
-            conv_out, inner_width + (group_count + my_group) * STATE, STATE, 1
-        )
+            conv_sum = conv_sum + taps[offset][None, :] * padded[offset : offset + half_rows]
+        return jax.nn.silu(conv_sum).astype(jnp.bfloat16)
+
+    def local_block(lead_rows, inner_in, proj_in, block_step):
+        inner_out = conv(lead_rows[:, :inner_width], inner_in, conv_inner)
+        proj_out = conv(lead_rows[:, inner_width:], proj_in, conv_proj)
+        inner_conv = inner_out.reshape(half_rows, head_count, HEAD_SIZE)
+        b_rows = lax.dynamic_slice_in_dim(proj_out, my_group * STATE, STATE, 1)
+        c_rows = lax.dynamic_slice_in_dim(proj_out, (group_count + my_group) * STATE, STATE, 1)
         log_cum = jnp.cumsum(-block_step * decay_rate[None, :], axis=0)
         score_grid = jnp.dot(c_rows, b_rows.T, preferred_element_type=jnp.float32)
         log_gap = log_cum.T[:, :, None] - log_cum.T[:, None, :]
@@ -214,10 +218,10 @@
         return total_out.reshape(half_rows, inner_width)
 
     first_out, first_cum, first_c, first_elem = local_block(
-        lead_first, joined[:half_rows], step_size[:half_rows]
+        lead_first, inner_rows[:half_rows], input_proj[:half_rows], step_size[:half_rows]
     )
     second_out, second_cum, second_c, second_elem = local_block(
-        lead_second, joined[half_rows:], step_size[half_rows:]
+        lead_second, inner_rows[half_rows:], input_proj[half_rows:], step_size[half_rows:]
     )
     first_in, second_in = block_states(
         first_elem[1], second_elem[1], first_cum[-1], second_cum[-1], seq_pos, seq_count

time: 49.6 us -> 47.3 us (0.954)
  waiting for transfers between devices: 10.4 us -> 13.4 us
  other arithmetic: 7.52 us -> 5.19 us
  local copies, waits for them, and re-layouts: 14.7 us -> 12.7 us
  matrix products: 3.4 us -> 2.61 us
    ppermute x1, waiting for transfers between devices: 2.72 us -> 5.71 us  [butterfly_states(): got = lax.ppermute(pack((sub_f, sub_g), (e_f, e_g), LINK), 'seq', pairs)]
    exp x4, local copies, waits for them, and re-layouts: 2.84 us -> 0.17 us  [finish_block(): total_out = partial_out + jnp.exp(log_cum)[:, :, None] * inter_out]
    slice x7 -> x12, local copies, waits for them, and re-layouts: 0.52 us -> 3.11 us  [the longest x2 1.53 us: edges(): rows[tokens - rim_rows:]]
    concatenate x3, other arithmetic: 1.57 us -> 0.07 us  [pack(): return jnp.concatenate([f.astype(kind) for f in flat] + [tail], axis=0)]
    transpose x2, local copies, waits for them, and re-layouts: 1.33 us -> 0.12 us  [local_block(): log_gap = log_cum.T[:, :, None] - log_cum.T[:, None, :]]
    slice x3, local copies, waits for them, and re-layouts: 1.09 us -> 0.07 us  [unpack(): message[i * rows:(i + 1) * rows].astype(jnp.float32).reshape(shape)]
    select_n x1, other arithmetic: 1.51 us -> 0.66 us  [butterfly_states(): jnp.where(lower, ones, e_f)]
    dot_general x2, matrix products: 1.92 us -> 1.15 us  [local_block(): jnp.einsum('hts,shp->thp', weights, inner_conv, preferred_element_type=jn...]
  transfers between devices with their start and end apart: 8 -> 8, of which waited for: 4 -> 6; matrix products, arithmetic and copies ran while one was open for 18% -> 11% of each run, Pallas kernels for 0% -> 0%
where the time goes in v8:
time: 47.3 us; the launch traced here: 46.6 us
  waiting for transfers between devices  13.4 us (28%)
  local copies, waits for them, and re-layouts  12.7 us (27%)
  starting transfers between devices  12.1 us (26%)
  other arithmetic  5.19 us (11%)
  matrix products  2.61 us (6%)
  between operations  0.62 us (1%)
    unnamed x52, local copies, waits for them, and re-layouts  8.08 us
    ppermute x1, waiting for transfers between devices, butterfly_states(): got = lax.ppermute(pack((sub_f, sub_g), (e_f, e_g), LINK), 'seq', pairs)  5.71 us
    ppermute x1, waiting for transfers between devices, butterfly_states(): got = lax.ppermute(pack((sent,), (sent_e,), LINK), 'seq', pairs)  3.76 us
    ppermute x1, starting transfers between devices, extended_2(): low = lax.ppermute(tail, axis, forward)  3.03 us
    ppermute x1, starting transfers between devices, block_states(): got = lax.ppermute(sent, 'seq', pairs)  2.63 us
    ppermute x1, starting transfers between devices, butterfly_states(): got = lax.ppermute(pack((sub_f, sub_g), (e_f, e_g), LINK), 'seq', pairs)  2.43 us
    ppermute x1, waiting for transfers between devices, partner(): lax.ppermute(array, axis, [(i, i ^ 1 << stride) for i in range(lax.axis_s...  1.99 us
    ppermute x1, starting transfers between devices, partner(): lax.ppermute(array, axis, [(i, i ^ 1 << stride) for i in range(lax.axis_s...  1.64 us
  transfers between devices with their start and end apart: 8, of which 6 were waited for; matrix products, arithmetic and copies ran while one was open for 11% of the time, Pallas kernels for 0%

profile of v8, /device:TPU:0, one launch (start us, length us, event | category | flops | bytes accessed | tf_op | source)
XLA Modules:
  0.0 46.6 jit_solution(9426931079078008649)
XLA Ops:
  0.0 0.8 %fusion.110 = (bf16[3,1024]{1,0:T(4,128)(2,1)S(1)}, bf16[3,1024]{1,0:T(4,128)(2,1)S(1)}) fusion(bf16[256,1024]{1,0:T(8,128)(2,1)} %param.9), kind=kLoop, calls=%fused_computation.214 | loop fusion | bytes 24576 | tf_op jit(solution)/shard_map/slice | solution.py:172
  0.8 0.7 %fusion.113 = (bf16[3,512]{1,0:T(4,128)(2,1)S(1)}, bf16[3,512]{1,0:T(4,128)(2,1)S(1)}) fusion(bf16[256,512]{1,0:T(8,128)(2,1)} %param.11), kind=kLoop, calls=%fused_computation.217 | loop fusion | bytes 12288 | tf_op jit(solution)/shard_map/slice | solution.py:172
  1.6 1.3 %collective-permute-start.1 = (bf16[3,1536]{1,0:T(4,128)(2,1)S(1)}, bf16[3,1536]{1,0:T(4,128)(2,1)S(1)}, u32[]{:S(2)}, u32[]{:S(2)}) collective-permute-start(bf16[3,1536]{1,0:T(4,128)(2,1)S(1)} %get-tuple-element.8), channel_id=1, source_target_pairs={{4,0},{8,4},{12,8},{16,12},{20,16},{24,20},{28,24},{5,1},{9,5},{13... | collective-permute-start | bytes 27656 | tf_op jit(solution)/shard_map/ppermute | solution.py:24
  2.9 3.0 %collective-permute-start = (bf16[3,1536]{1,0:T(4,128)(2,1)S(1)}, bf16[3,1536]{1,0:T(4,128)(2,1)S(1)}, u32[]{:S(2)}, u32[]{:S(2)}) collective-permute-start(bf16[3,1536]{1,0:T(4,128)(2,1)S(1)} %get-tuple-element.7), channel_id=1, source_target_pairs={{0,4},{4,8},{8,12},{12,16},{16,20},{20,24},{24,28},{1,5},{5,9},{9,... | collective-permute-start | bytes 27656 | tf_op jit(solution)/shard_map/ppermute | solution.py:23
  5.9 1.0 %fusion.112 = (bf16[128,512]{1,0:T(8,128)(2,1)S(1)}, bf16[128,512]{1,0:T(8,128)(2,1)S(1)}) fusion(bf16[256,512]{1,0:T(8,128)(2,1)} %param.11), kind=kLoop, calls=%fused_computation.216 | loop fusion | bytes 524288 | tf_op jit(solution)/shard_map/slice | solution.py:221
  7.0 0.7 %copy-done.7 = f32[256,16]{0,1:T(8,128)S(1)} copy-done((f32[256,16]{0,1:T(8,128)S(1)}, f32[256,16]{0,1:T(8,128)}, u32[]{:S(2)}) %copy-start.7) | copy-done | bytes 16408
  7.7 0.6 %copy-done.24 = f32[16]{0:T(128)S(1)} copy-done((f32[16]{0:T(128)S(1)}, f32[16]{0:T(128)}, u32[]{:S(2)}) %copy-start.24) | copy-done | bytes 88
  8.5 0.2 reduce_window_sum.18
  8.8 0.2 reduce_window_sum.17
  9.1 0.7 %copy-done.9 = f32[4,512]{1,0:T(4,128)S(1)} copy-done((f32[4,512]{1,0:T(4,128)S(1)}, f32[4,512]{1,0:T(4,128)}, u32[]{:S(2)}) %copy-start.9) | copy-done | bytes 8216
  9.9 0.6 %slice_bitcast_fusion.1 = (f32[16,128]{1,0:T(8,128)}, f32[128,16]{0,1:T(8,128)S(1)}, f32[128,16]{0,1:T(8,128)S(1)}, f32[16,128]{1,0:T(8,128)S(1)}) fusion(f32[256,16]{0,1:T(8,128)S(1)} %compare_select_fusion, f32[128,16]{0,1:T(8,128)S(1)} %copy.34, f32[16]{0:T(128)S(1)} %slice_bitcast_fusion.3, f32[128,16]{0,1:T(8,128)S(1)} %copy.37, ...), kind=kLoop, calls=%fused_computation.138 | loop fusion | flops 8192 | bytes 65664 | tf_op jit(solution)/shard_map/transpose | solution.py:201
  10.7 0.5 %copy-done.6 = bf16[3,1536]{1,0:T(4,128)(2,1)} copy-done((bf16[3,1536]{1,0:T(4,128)(2,1)}, bf16[3,1536]{1,0:T(4,128)(2,1)S(1)}, u32[]{:S(2)}) %copy-start.6) | copy-done | bytes 9240
  11.3 0.6 %multiply_convert_fusion.6 = (bf16[128,1024]{1,0:T(8,128)(2,1)S(1)}, bf16[128,1024]{1,0:T(8,128)(2,1)S(1)}) fusion(f32[131,1024]{1,0:T(8,128)S(1)} %maximum_convert_fusion, f32[1024]{0:T(1024)S(1)} %bitcast.138, f32[1024]{0:T(1024)S(1)} %bitcast.139, f32[1024]{0:T(1024)S(1)} %bitcast.137, f32[1024]{0:T(1024)S(1)} %bitcast.136, ...), kind=kLoop, calls=%fused_computation.62 | loop fusion | flops 3145728 | bytes 4734976 | tf_op jit(solution)/shard_map/convert_element_type | solution.py:189
  11.9 0.2 copy.29
  12.1 0.2 copy.35
  12.3 0.5 %slice-done = bf16[3,512]{1,0:T(4,128)(2,1)S(1)} async-done(((bf16[3,1536]{1,0:T(4,128)(2,1)}), bf16[3,512]{1,0:T(4,128)(2,1)S(1)}, s32[]{:S(2)}) %slice-start) | async-done | bytes 3096 | tf_op jit(solution)/shard_map/slice | solution.py:193
  12.9 0.3 multiply_convert_fusion.8
  13.3 0.2 fusion.48
  13.5 0.4 copy-done.4
  13.9 0.2 fusion.46
  14.3 2.6 %collective-permute-start.2 = (f32[1032,128]{1,0:T(8,128)S(1)}, f32[1032,128]{1,0:T(8,128)S(1)}, u32[]{:S(2)}, u32[]{:S(2)}) collective-permute-start(f32[1032,128]{1,0:T(8,128)S(1)} %pad_maximum_fusion), channel_id=1, source_target_pairs={{0,4},{4,0},{8,12},{12,8},{16,20},{20,16},{24,28},{28,24},{1,5},{5... | collective-permute-start | bytes 1585160 | tf_op jit(solution)/shard_map/ppermute | solution.py:118
  16.9 1.5 %collective-permute-done.2 = f32[1032,128]{1,0:T(8,128)S(1)} collective-permute-done((f32[1032,128]{1,0:T(8,128)S(1)}, f32[1032,128]{1,0:T(8,128)S(1)}, u32[]{:S(2)}, u32[]{:S(2)}) %collective-permute-start.2) | collective-permute-done | bytes 528416 | tf_op jit(solution)/shard_map/ppermute | solution.py:118
  18.4 0.7 %broadcast_select_fusion.4 = (f32[8]{0:T(128)}, f32[8]{0:T(128)S(1)}, f32[8]{0:T(128)}, f32[8]{0:T(128)S(1)}, f32[8]{0:T(128)S(1)}, /*index=5*/f32[8]{0:T(128)},...) fusion(pred[]{:T(512)S(6)} %eq.17, f32[1032,128]{1,0:T(8,128)S(1)} %collective-permute-done.2, ...), kind=kLoop, calls=%fused_computation.173 | loop fusion | flops 96 | bytes 518 | tf_op jit(solution)/shard_map/jit(_where)/select_n | solution.py:79
  19.1 0.5 %copy-done.11 = f32[8]{0:T(128)} copy-done((f32[8]{0:T(128)}, f32[8]{0:T(128)S(1)}, u32[]{:S(2)}) %copy-start.11) | copy-done | bytes 56
  20.0 2.4 %collective-permute-start.3 = (bf16[1032,128]{1,0:T(8,128)(2,1)S(1)}, bf16[1032,128]{1,0:T(8,128)(2,1)S(1)}, u32[]{:S(2)}, u32[]{:S(2)}) collective-permute-start(bf16[1032,128]{1,0:T(8,128)(2,1)S(1)} %pad_maximum_fusion.1), channel_id=1, source_target_pairs={{0,8},{4,12},{8,0},{12,4},{16,24},{20,28},{24,16},{28,20},{1,9},{5... | collective-permute-start | bytes 792584 | tf_op jit(solution)/shard_map/ppermute | solution.py:77
  22.8 0.7 %copy-done.5 = bf16[128,512]{1,0:T(8,128)(2,1)S(1)} copy-done((bf16[128,512]{1,0:T(8,128)(2,1)S(1)}, bf16[128,512]{1,0:T(8,128)(2,1)}, u32[]{:S(2)}) %copy-start.5) | copy-done | bytes 131096
  23.6 5.7 %collective-permute-done.3 = bf16[1032,128]{1,0:T(8,128)(2,1)S(1)} collective-permute-done((bf16[1032,128]{1,0:T(8,128)(2,1)S(1)}, bf16[1032,128]{1,0:T(8,128)(2,1)S(1)}, u32[]{:S(2)}, u32[]{:S(2)}) %collective-permute-start.3) | collective-permute-done | bytes 264224 | tf_op jit(solution)/shard_map/ppermute | solution.py:77
  29.3 0.6 %copy-done.12 = f32[8]{0:T(128)S(1)} copy-done((f32[8]{0:T(128)S(1)}, f32[8]{0:T(128)}, u32[]{:S(2)}) %copy-start.12) | copy-done | bytes 56
  29.9 0.6 %copy-done.21 = f32[8]{0:T(128)S(1)} copy-done((f32[8]{0:T(128)S(1)}, f32[8]{0:T(128)}, u32[]{:S(2)}) %copy-start.21) | copy-done | bytes 56
  30.6 0.5 %copy-done.19 = f32[8]{0:T(128)S(1)} copy-done((f32[8]{0:T(128)S(1)}, f32[8]{0:T(128)}, u32[]{:S(2)}) %copy-start.19) | copy-done | bytes 56
  31.3 0.2 fusion.43
  31.5 1.0 %collective-permute-start.4 = (bf16[520,128]{1,0:T(8,128)(2,1)S(1)}, bf16[520,128]{1,0:T(8,128)(2,1)S(1)}, u32[]{:S(2)}, u32[]{:S(2)}) collective-permute-start(bf16[520,128]{1,0:T(8,128)(2,1)S(1)} %pad_maximum_fusion.2), channel_id=1, source_target_pairs={{0,16},{4,20},{8,24},{12,28},{16,0},{20,4},{24,8},{28,12},{1,17},{... | collective-permute-start | bytes 399368 | tf_op jit(solution)/shard_map/ppermute | solution.py:90
  32.5 0.6 %fusion.2 = f32[128,16,64]{0,2,1:T(8,128)S(1)} fusion(bf16[128,16,64]{0,2,1:T(8,128)(2,1)S(1)} %bitcast.129, f32[16,128]{1,0:T(8,128)S(1)} %copy-done.10, f32[16,128]{1,0:T(8,128)S(1)} %copy.31, f32[128,128]{1,0:T(8,128)S(1)} %fusion.74, pred[128,128]{1,0:T(8,128)(4,1)S(1)} %iota_compare_fusion, f32[16]{0:T(128)S(1)} %copy-done.25), kind=kOutput, calls=%fused_computation.8 | convolution fusion | flops 35520512 | bytes 884800 | tf_op jit(solution)/shard_map/hts,shp->thp/dot_general | solution.py:202
  33.1 3.8 %collective-permute-done.4 = bf16[520,128]{1,0:T(8,128)(2,1)S(1)} collective-permute-done((bf16[520,128]{1,0:T(8,128)(2,1)S(1)}, bf16[520,128]{1,0:T(8,128)(2,1)S(1)}, u32[]{:S(2)}, u32[]{:S(2)}) %collective-permute-start.4) | collective-permute-done | bytes 133152 | tf_op jit(solution)/shard_map/ppermute | solution.py:90
  36.9 0.6 %copy-done.22 = f32[8]{0:T(128)S(1)} copy-done((f32[8]{0:T(128)S(1)}, f32[8]{0:T(128)}, u32[]{:S(2)}) %copy-start.22) | copy-done | bytes 56
  37.6 0.3 fusion.61
  37.9 0.5 %copy-done.3 = bf16[128,512]{1,0:T(8,128)(2,1)S(1)} copy-done((bf16[128,512]{1,0:T(8,128)(2,1)S(1)}, bf16[128,512]{1,0:T(8,128)(2,1)}, u32[]{:S(2)}) %copy-start.3) | copy-done | bytes 131096
  38.6 0.6 %fusion.3 = f32[128,16,64]{0,2,1:T(8,128)S(1)} fusion(bf16[128,16,64]{0,2,1:T(8,128)(2,1)S(1)} %bitcast.127, f32[16,128]{1,0:T(8,128)S(1)} %get-tuple-element.57, f32[16,128]{1,0:T(8,128)S(1)} %copy.38, f32[128,128]{1,0:T(8,128)S(1)} %fusion.69, pred[128,128]{1,0:T(8,128)(4,1)S(1)} %iota_compare_fusion, f32[16]{0:T(128)S(1)} %copy-done.25), kind=kOutput, calls=%fused_computation.9 | convolution fusion | flops 35520512 | bytes 884800 | tf_op jit(solution)/shard_map/hts,shp->thp/dot_general | solution.py:202
  39.2 0.3 collective-permute-done.5
  39.5 0.4 fusion.1
  39.9 0.2 copy.41
  40.2 0.4 fusion
  40.6 0.2 copy.42
  40.8 0.8 %copy-done.1 = bf16[256,1024]{1,0:T(8,128)(2,1)S(1)} copy-done((bf16[256,1024]{1,0:T(8,128)(2,1)S(1)}, bf16[256,1024]{1,0:T(8,128)(2,1)}, u32[]{:S(2)}) %copy-start.1) | copy-done | bytes 524312
  41.6 0.4 multiply_reduce_fusion
  42.0 1.6 %collective-permute-start.7 = (f32[256]{0:T(256)S(1)}, f32[256]{0:T(256)S(1)}, u32[]{:S(2)}, u32[]{:S(2)}) collective-permute-start(f32[256]{0:T(256)S(1)} %get-tuple-element.9), channel_id=1, source_target_pairs={{0,1},{1,0},{2,3},{3,2},{4,5},{5,4},{6,7},{7,6},{8,9},{9,8},{10,11... | collective-permute-start | bytes 3080 | tf_op jit(solution)/shard_map/ppermute | solution.py:30
  43.6 2.0 %collective-permute-done.7 = f32[256]{0:T(256)S(1)} collective-permute-done((f32[256]{0:T(256)S(1)}, f32[256]{0:T(256)S(1)}, u32[]{:S(2)}, u32[]{:S(2)}) %collective-permute-start.7) | collective-permute-done | bytes 1056 | tf_op jit(solution)/shard_map/ppermute | solution.py:30
  45.6 1.0 %multiply_convert_fusion = bf16[256,1024]{1,0:T(8,128)(2,1)} fusion(f32[256,1024]{1,0:T(8,128)S(1)} %get-tuple-element.10, f32[1024]{0:T(1024)S(1)} %copy-done.18, f32[256]{0:T(256)S(1)} %add_rsqrt_fusion), kind=kLoop, calls=%fused_computation.14 | loop fusion | flops 786432 | bytes 1577984 | tf_op jit(solution)/shard_map/convert_element_type | solution.py:241
  (101 shorter events, 2.4 us)
Async XLA Ops:
  0.0 6.9 %copy-start = (bf16[256,1024]{1,0:T(8,128)(2,1)S(1)}, bf16[256,1024]{1,0:T(8,128)(2,1)}, u32[]{:S(2)}) copy-start(bf16[256,1024]{1,0:T(8,128)(2,1)} %param.9) | copy-start | bytes 1572868
  1.6 9.0 %collective-permute-start.1 = (bf16[3,1536]{1,0:T(4,128)(2,1)S(1)}, bf16[3,1536]{1,0:T(4,128)(2,1)S(1)}, u32[]{:S(2)}, u32[]{:S(2)}) collective-permute-start(bf16[3,1536]{1,0:T(4,128)(2,1)S(1)} %get-tuple-element.8), channel_id=1, source_target_pairs={{4,0},{8,4},{12,8},{16,12},{20,16},{24,20},{28,24},{5,1},{9,5},{13... | collective-permute-start | bytes 27656 | tf_op jit(solution)/shard_map/ppermute | solution.py:24
  2.9 8.3 %collective-permute-start = (bf16[3,1536]{1,0:T(4,128)(2,1)S(1)}, bf16[3,1536]{1,0:T(4,128)(2,1)S(1)}, u32[]{:S(2)}, u32[]{:S(2)}) collective-permute-start(bf16[3,1536]{1,0:T(4,128)(2,1)S(1)} %get-tuple-element.7), channel_id=1, source_target_pairs={{0,4},{4,8},{8,12},{12,16},{16,20},{20,24},{24,28},{1,5},{5,9},{9,... | collective-permute-start | bytes 27656 | tf_op jit(solution)/shard_map/ppermute | solution.py:23
  6.9 0.7 %copy-start.7 = (f32[256,16]{0,1:T(8,128)S(1)}, f32[256,16]{0,1:T(8,128)}, u32[]{:S(2)}) copy-start(f32[256,16]{0,1:T(8,128)} %param.12) | copy-start | bytes 49156
  7.6 0.7 %copy-start.24 = (f32[16]{0:T(128)S(1)}, f32[16]{0:T(128)}, u32[]{:S(2)}) copy-start(f32[16]{0:T(128)} %param.13) | copy-start | bytes 196
  9.0 0.7 %copy-start.9 = (f32[4,512]{1,0:T(4,128)S(1)}, f32[4,512]{1,0:T(4,128)}, u32[]{:S(2)}) copy-start(f32[4,512]{1,0:T(4,128)} %param.16) | copy-start | bytes 24580
  9.0 0.8 %copy-start.8 = (f32[4,1024]{1,0:T(4,128)S(1)}, f32[4,1024]{1,0:T(4,128)}, u32[]{:S(2)}) copy-start(f32[4,1024]{1,0:T(4,128)} %param.15) | copy-start | bytes 49156
  10.6 0.6 %copy-start.6 = (bf16[3,1536]{1,0:T(4,128)(2,1)}, bf16[3,1536]{1,0:T(4,128)(2,1)S(1)}, u32[]{:S(2)}) copy-start(bf16[3,1536]{1,0:T(4,128)(2,1)S(1)} %broadcast_select_fusion) | copy-start | bytes 27652
  12.1 0.7 %slice-start = ((bf16[3,1536]{1,0:T(4,128)(2,1)}), bf16[3,512]{1,0:T(4,128)(2,1)S(1)}, s32[]{:S(2)}) async-start(bf16[3,1536]{1,0:T(4,128)(2,1)} %copy-done.6), calls=%async_computation | async-start | bytes 8192 | tf_op jit(solution)/shard_map/slice | solution.py:193
  13.2 0.7 %copy-start.4 = (bf16[128,512]{1,0:T(8,128)(2,1)}, bf16[128,512]{1,0:T(8,128)(2,1)S(1)}, u32[]{:S(2)}) copy-start(bf16[128,512]{1,0:T(8,128)(2,1)S(1)} %get-tuple-element.64) | copy-start | bytes 393220
  13.2 0.7 %copy-start.2 = (bf16[128,512]{1,0:T(8,128)(2,1)}, bf16[128,512]{1,0:T(8,128)(2,1)S(1)}, u32[]{:S(2)}) copy-start(bf16[128,512]{1,0:T(8,128)(2,1)S(1)} %get-tuple-element.65) | copy-start | bytes 393220
  14.3 4.2 %collective-permute-start.2 = (f32[1032,128]{1,0:T(8,128)S(1)}, f32[1032,128]{1,0:T(8,128)S(1)}, u32[]{:S(2)}, u32[]{:S(2)}) collective-permute-start(f32[1032,128]{1,0:T(8,128)S(1)} %pad_maximum_fusion), channel_id=1, source_target_pairs={{0,4},{4,0},{8,12},{12,8},{16,20},{20,16},{24,28},{28,24},{1,5},{5... | collective-permute-start | bytes 1585160 | tf_op jit(solution)/shard_map/ppermute | solution.py:118
  19.1 0.5 %copy-start.11 = (f32[8]{0:T(128)}, f32[8]{0:T(128)S(1)}, u32[]{:S(2)}) copy-start(f32[8]{0:T(128)S(1)} %get-tuple-element.16) | copy-start | bytes 100
  19.1 0.5 %copy-start.20 = (f32[8]{0:T(128)}, f32[8]{0:T(128)S(1)}, u32[]{:S(2)}) copy-start(f32[8]{0:T(128)S(1)} %get-tuple-element.37) | copy-start | bytes 100
  19.1 0.7 %copy-start.13 = (f32[8]{0:T(128)}, f32[8]{0:T(128)S(1)}, u32[]{:S(2)}) copy-start(f32[8]{0:T(128)S(1)} %get-tuple-element.33) | copy-start | bytes 100
  19.1 0.7 %copy-start.15 = (f32[8]{0:T(128)}, f32[8]{0:T(128)S(1)}, u32[]{:S(2)}) copy-start(f32[8]{0:T(128)S(1)} %get-tuple-element.72) | copy-start | bytes 100
  20.0 9.3 %collective-permute-start.3 = (bf16[1032,128]{1,0:T(8,128)(2,1)S(1)}, bf16[1032,128]{1,0:T(8,128)(2,1)S(1)}, u32[]{:S(2)}, u32[]{:S(2)}) collective-permute-start(bf16[1032,128]{1,0:T(8,128)(2,1)S(1)} %pad_maximum_fusion.1), channel_id=1, source_target_pairs={{0,8},{4,12},{8,0},{12,4},{16,24},{20,28},{24,16},{28,20},{1,9},{5... | collective-permute-start | bytes 792584 | tf_op jit(solution)/shard_map/ppermute | solution.py:77
  22.5 0.9 %copy-start.5 = (bf16[128,512]{1,0:T(8,128)(2,1)S(1)}, bf16[128,512]{1,0:T(8,128)(2,1)}, u32[]{:S(2)}) copy-start(bf16[128,512]{1,0:T(8,128)(2,1)} %copy-done.4) | copy-start | bytes 393220
  29.3 0.6 %copy-start.12 = (f32[8]{0:T(128)S(1)}, f32[8]{0:T(128)}, u32[]{:S(2)}) copy-start(f32[8]{0:T(128)} %copy-done.11) | copy-start | bytes 100
  29.9 0.6 %copy-start.21 = (f32[8]{0:T(128)S(1)}, f32[8]{0:T(128)}, u32[]{:S(2)}) copy-start(f32[8]{0:T(128)} %copy-done.20) | copy-start | bytes 100
  30.6 0.6 %copy-start.19 = (f32[8]{0:T(128)S(1)}, f32[8]{0:T(128)}, u32[]{:S(2)}) copy-start(f32[8]{0:T(128)} %get-tuple-element.36) | copy-start | bytes 100
  30.6 0.7 %copy-start.14 = (f32[8]{0:T(128)S(1)}, f32[8]{0:T(128)}, u32[]{:S(2)}) copy-start(f32[8]{0:T(128)} %copy-done.13) | copy-start | bytes 100
  30.6 0.7 %copy-start.16 = (f32[8]{0:T(128)S(1)}, f32[8]{0:T(128)}, u32[]{:S(2)}) copy-start(f32[8]{0:T(128)} %copy-done.15) | copy-start | bytes 100
  30.6 0.7 %copy-start.17 = (f32[8]{0:T(128)S(1)}, f32[8]{0:T(128)}, u32[]{:S(2)}) copy-start(f32[8]{0:T(128)} %get-tuple-element.15) | copy-start | bytes 100
  31.5 1.0 %copy-start.10 = (f32[16,128]{1,0:T(8,128)S(1)}, f32[16,128]{1,0:T(8,128)}, u32[]{:S(2)}) copy-start(f32[16,128]{1,0:T(8,128)} %get-tuple-element.54) | copy-start | bytes 24580
  31.5 1.0 %copy-start.25 = (f32[16]{0:T(128)S(1)}, f32[16]{0:T(128)}, u32[]{:S(2)}) copy-start(f32[16]{0:T(128)} %param.14) | copy-start | bytes 196
  31.5 5.3 %collective-permute-start.4 = (bf16[520,128]{1,0:T(8,128)(2,1)S(1)}, bf16[520,128]{1,0:T(8,128)(2,1)S(1)}, u32[]{:S(2)}, u32[]{:S(2)}) collective-permute-start(bf16[520,128]{1,0:T(8,128)(2,1)S(1)} %pad_maximum_fusion.2), channel_id=1, source_target_pairs={{0,16},{4,20},{8,24},{12,28},{16,0},{20,4},{24,8},{28,12},{1,17},{... | collective-permute-start | bytes 399368 | tf_op jit(solution)/shard_map/ppermute | solution.py:90
  36.9 0.6 %copy-start.22 = (f32[8]{0:T(128)S(1)}, f32[8]{0:T(128)}, u32[]{:S(2)}) copy-start(f32[8]{0:T(128)} %get-tuple-element.27) | copy-start | bytes 100
  36.9 0.7 %copy-start.23 = (f32[8]{0:T(128)S(1)}, f32[8]{0:T(128)}, u32[]{:S(2)}) copy-start(f32[8]{0:T(128)} %get-tuple-element.35) | copy-start | bytes 100
  37.6 0.9 %copy-start.3 = (bf16[128,512]{1,0:T(8,128)(2,1)S(1)}, bf16[128,512]{1,0:T(8,128)(2,1)}, u32[]{:S(2)}) copy-start(bf16[128,512]{1,0:T(8,128)(2,1)} %copy-done.2) | copy-start | bytes 393220
  37.9 1.6 %collective-permute-start.5 = (f32[8,64,128]{2,1,0:T(8,128)S(1)}, f32[8,64,128]{2,1,0:T(8,128)S(1)}, u32[]{:S(2)}, u32[]{:S(2)}) collective-permute-start(f32[8,64,128]{2,1,0:T(8,128)S(1)} %get-tuple-element.25), channel_id=1, source_target_pairs={{0,4},{4,0},{8,12},{12,8},{16,20},{20,16},{24,28},{28,24},{1,5},{5... | collective-permute-start | bytes 786440 | tf_op jit(solution)/shard_map/ppermute | solution.py:136
  38.6 1.6 %collective-permute-start.6 = (f32[8,64,128]{2,1,0:T(8,128)S(1)}, f32[8,64,128]{2,1,0:T(8,128)S(1)}, u32[]{:S(2)}, u32[]{:S(2)}) collective-permute-start(f32[8,64,128]{2,1,0:T(8,128)S(1)} %get-tuple-element.45), channel_id=1, source_target_pairs={{0,4},{4,0},{8,12},{12,8},{16,20},{20,16},{24,28},{28,24},{1,5},{5... | collective-permute-start | bytes 786440 | tf_op jit(solution)/shard_map/ppermute | solution.py:136
  40.5 1.0 %copy-start.1 = (bf16[256,1024]{1,0:T(8,128)(2,1)S(1)}, bf16[256,1024]{1,0:T(8,128)(2,1)}, u32[]{:S(2)}) copy-start(bf16[256,1024]{1,0:T(8,128)(2,1)} %param.10) | copy-start | bytes 1572868
  42.0 3.7 %copy-start.18 = (f32[1024]{0:T(1024)S(1)}, f32[1024]{0:T(1024)}, u32[]{:S(2)}) copy-start(f32[1024]{0:T(1024)} %param.17) | copy-start | bytes 12292
  42.0 3.6 %collective-permute-start.7 = (f32[256]{0:T(256)S(1)}, f32[256]{0:T(256)S(1)}, u32[]{:S(2)}, u32[]{:S(2)}) collective-permute-start(f32[256]{0:T(256)S(1)} %get-tuple-element.9), channel_id=1, source_target_pairs={{0,1},{1,0},{2,3},{3,2},{4,5},{5,4},{6,7},{7,6},{8,9},{9,8},{10,11... | collective-permute-start | bytes 3080 | tf_op jit(solution)/shard_map/ppermute | solution.py:30

commit v9 on v8

--- a/solution.py
+++ b/solution.py
@@ -58,44 +58,94 @@
     return v[:, None, None]
 
 
+def to_link(x, rows):
+    high = x.astype(LINK)
+    low = (x - high.astype(jnp.float32)).astype(LINK)
+    row = lax.broadcasted_iota(jnp.int32, x.shape, x.ndim - 2)
+    return jnp.where(row == rows + 1, low, high)
+
+
+def from_link(m, rows):
+    x = m.astype(jnp.float32)
+    return x, x[..., rows : rows + 1, :] + x[..., rows + 1 : rows + 2, :]
+
+
 def butterfly_states(sub_f, sub_g, e_f, e_g, index, count, stride, seq_count):
     levels = count.bit_length() - 1
     assert 1 << levels == count
-    shape = sub_f.shape
+    heads, rows, lanes = sub_f.shape
     if levels == 0:
         return jnp.zeros_like(sub_f), sub_f
-    ones = jnp.ones((shape[0],), jnp.float32)
-    zeros = jnp.zeros((shape[0],), jnp.float32)
-    prefix = jnp.zeros_like(sub_f)
-    above = jnp.zeros_like(sub_f)
-    e_pre, e_abv = ones, ones
+    shape = (heads, rows + 8, lanes)
+
+    def with_decay(x, e):
+        return jnp.concatenate([x, jnp.broadcast_to(e[:, None, None], (heads, 8, lanes))], axis=1)
+
+    is_map = lax.broadcasted_iota(jnp.int32, shape, 1) < rows
+
+    def decay(x):
+        return x[:, rows : rows + 1, :]
+
+    ones = jnp.ones((heads,), jnp.float32)
+    zeros = jnp.zeros((heads,), jnp.float32)
+    big_f, big_g = with_decay(sub_f, e_f), with_decay(sub_g, e_g)
+    prefix = with_decay(jnp.zeros_like(sub_f), ones)
+    above = with_decay(jnp.zeros_like(sub_f), ones)
+
+    def last_message(f, g, lower):
+        ef, eg = decay(f), decay(g)
+        body = jnp.where(lower, f, eg * f + g)
+        return jnp.where(is_map, body, jnp.where(lower, ef, ef * eg))
+
+    first_lower = index % 2 == 0
+    if levels == 1:
+        msg = to_link(last_message(big_f, big_g, first_lower)[None], rows)
+    else:
+        msg = to_link(jnp.stack([big_f, big_g]), rows)
     for level in range(levels):
         size = 1 << level
         lower = (index // size) % 2 == 0
         pairs = [(i, i ^ (size * stride)) for i in range(seq_count)]
+        got, got_e = from_link(lax.ppermute(msg, "seq", pairs), rows)
+        e_f, e_g, e_pre, e_abv = decay(big_f), decay(big_g), decay(prefix), decay(above)
         if level < levels - 1:
-            got = lax.ppermute(pack((sub_f, sub_g), (e_f, e_g), LINK), "seq", pairs)
-            (got_f, got_g), (p_f, p_g) = unpack(got, 2, shape)
-            new_f = col(jnp.where(lower, p_f, ones)) * sub_f + col(jnp.where(lower, ones, e_f)) * got_f
-            new_g = col(jnp.where(lower, ones, p_g)) * sub_g + col(jnp.where(lower, e_g, ones)) * got_g
-            above = above + col(jnp.where(lower, e_abv, zeros)) * got_g
-            prefix = prefix + col(jnp.where(lower, zeros, e_pre)) * got_f
-            e_abv = jnp.where(lower, e_abv * p_g, e_abv)
-            e_pre = jnp.where(lower, e_pre, e_pre * p_f)
-            sub_f, sub_g = new_f, new_g
-            e_f, e_g = e_f * p_f, e_g * p_g
+            got_f, got_g = got[0], got[1]
+            p_f, p_g = got_e[0], got_e[1]
+            new_f = jnp.where(
+                is_map,
+                jnp.where(lower, p_f * big_f + got_f, big_f + e_f * got_f),
+                e_f * p_f,
+            )
+            new_g = jnp.where(
+                is_map,
+                jnp.where(lower, big_g + e_g * got_g, p_g * big_g + got_g),
+                e_g * p_g,
+            )
+            above = jnp.where(
+                is_map,
+                jnp.where(lower, above + e_abv * got_g, above),
+                jnp.where(lower, e_abv * p_g, e_abv),
+            )
+            prefix = jnp.where(
+                is_map,
+                jnp.where(lower, prefix, prefix + e_pre * got_f),
+                jnp.where(lower, e_pre, e_pre * p_f),
+            )
+            big_f, big_g = new_f, new_g
+            next_lower = (index // (2 * size)) % 2 == 0
+            if level + 1 == levels - 1:
+                msg = to_link(last_message(big_f, big_g, next_lower)[None], rows)
+            else:
+                msg = to_link(jnp.stack([big_f, big_g]), rows)
         else:
-            sent = col(jnp.where(lower, ones, e_g)) * sub_f + col(jnp.where(lower, zeros, ones)) * sub_g
-            sent_e = jnp.where(lower, e_f, e_f * e_g)
-            got = lax.ppermute(pack((sent,), (sent_e,), LINK), "seq", pairs)
-            (got_w,), (p_w,) = unpack(got, 1, shape)
-            first_in = prefix + col(jnp.where(lower, zeros, e_pre)) * got_w
-            second_in = (
-                above
-                + col(jnp.where(lower, e_abv * p_w, e_abv)) * sub_f
-                + col(jnp.where(lower, e_abv, e_abv * e_f)) * got_w
-            )
-    return first_in, second_in
+            got_w, p_w = got[0], got_e[0]
+            first_in = jnp.where(lower, prefix, prefix + e_pre * got_w)
+            second_in = jnp.where(
+                lower,
+                above + e_abv * p_w * big_f + e_abv * got_w,
+                above + e_abv * big_f + e_abv * e_f * got_w,
+            )
+    return first_in[:, :rows], second_in[:, :rows]
 
 
 def block_states(first_loc, second_loc, first_log, second_log, seq_pos, seq_count):

time: 47.3 us -> 46 us (0.973)
  local copies, waits for them, and re-layouts: 12.7 us -> 10.2 us
  other arithmetic: 5.19 us -> 6.15 us
  starting transfers between devices: 12.1 us -> 12.6 us
    unnamed x52 -> x20, local copies, waits for them, and re-layouts: 8.08 us -> 3.67 us
    ppermute x1, waiting for transfers between devices: 1.54 us -> 0.01 us  [block_states(): got = lax.ppermute(sent, 'seq', pairs)]
    ppermute x2, waiting for transfers between devices: 9.47 us -> 10.8 us  [butterfly_states(): got, got_e = from_link(lax.ppermute(msg, 'seq', pairs), rows)]
    broadcast_in_dim x0 -> x1, other arithmetic: none -> 0.75 us  [last_message(): return jnp.where(is_map, body, jnp.where(lower, ef, ef * eg))]
    slice x0 -> x5, local copies, waits for them, and re-layouts: none -> 0.73 us  [the longest x1 0.65 us: decay(): return x[:, rows:rows + 1, :]]
    add x0 -> x6, other arithmetic: none -> 0.67 us  [the longest x1 0.3 us: block_states(): col(jnp.where(upper, ones, q1)) * l1 + col(jnp.where(upper, e1h, ones)) * p1]
    exp x4, local copies, waits for them, and re-layouts: 0.17 us -> 0.79 us  [finish_block(): total_out = partial_out + jnp.exp(log_cum)[:, :, None] * inter_out]
    ppermute x2, starting transfers between devices: 0.07 us -> 0.63 us  [block_states(): got_1, got_2 = lax.ppermute(other, 'seq', pairs)]
  transfers between devices with their start and end apart: 8 -> 8, of which waited for: 6 -> 4; matrix products, arithmetic and copies ran while one was open for 11% -> 13% of each run, Pallas kernels for 0% -> 0%
where the time goes in v9:
time: 46 us; the launch traced here: 45.3 us
  waiting for transfers between devices  13.1 us (28%)
  starting transfers between devices  12.6 us (27%)
  local copies, waits for them, and re-layouts  10.2 us (22%)
  other arithmetic  6.15 us (13%)
  matrix products  2.62 us (6%)
  between operations  0.63 us (1%)
    ppermute x2, waiting for transfers between devices, butterfly_states(): got, got_e = from_link(lax.ppermute(msg, 'seq', pairs), rows)  10.8 us
    unnamed x20, local copies, waits for them, and re-layouts  3.67 us
    ppermute x2, starting transfers between devices, butterfly_states(): got, got_e = from_link(lax.ppermute(msg, 'seq', pairs), rows)  3.39 us
    ppermute x1, starting transfers between devices, extended_2(): low = lax.ppermute(tail, axis, forward)  3.03 us
    ppermute x1, starting transfers between devices, block_states(): got = lax.ppermute(sent, 'seq', pairs)  2.62 us
    ppermute x1, waiting for transfers between devices, partner(): lax.ppermute(array, axis, [(i, i ^ 1 << stride) for i in range(lax.axis_s...  1.99 us
    ppermute x1, starting transfers between devices, partner(): lax.ppermute(array, axis, [(i, i ^ 1 << stride) for i in range(lax.axis_s...  1.64 us
    slice x2, local copies, waits for them, and re-layouts, edges(): rows[tokens - rim_rows:]  1.53 us
  transfers between devices with their start and end apart: 8, of which 4 were waited for; matrix products, arithmetic and copies ran while one was open for 13% of the time, Pallas kernels for 0%

profile of v9, /device:TPU:0, one launch (start us, length us, event | category | flops | bytes accessed | tf_op | source)
XLA Modules:
  0.0 45.3 jit_solution(9140916831482674522)
XLA Ops:
  0.0 0.8 %fusion.106 = (bf16[3,1024]{1,0:T(4,128)(2,1)S(1)}, bf16[3,1024]{1,0:T(4,128)(2,1)S(1)}) fusion(bf16[256,1024]{1,0:T(8,128)(2,1)} %param.9), kind=kLoop, calls=%fused_computation.222 | loop fusion | bytes 24576 | tf_op jit(solution)/shard_map/slice | solution.py:222
  0.8 0.7 %fusion.108 = (bf16[3,512]{1,0:T(4,128)(2,1)S(1)}, bf16[3,512]{1,0:T(4,128)(2,1)S(1)}) fusion(bf16[256,512]{1,0:T(8,128)(2,1)} %param.11), kind=kLoop, calls=%fused_computation.224 | loop fusion | bytes 12288 | tf_op jit(solution)/shard_map/slice | solution.py:222
  1.6 1.3 %collective-permute-start.1 = (bf16[3,1536]{1,0:T(4,128)(2,1)S(1)}, bf16[3,1536]{1,0:T(4,128)(2,1)S(1)}, u32[]{:S(2)}, u32[]{:S(2)}) collective-permute-start(bf16[3,1536]{1,0:T(4,128)(2,1)S(1)} %get-tuple-element.8), channel_id=1, source_target_pairs={{4,0},{8,4},{12,8},{16,12},{20,16},{24,20},{28,24},{5,1},{9,5},{13... | collective-permute-start | bytes 27656 | tf_op jit(solution)/shard_map/ppermute | solution.py:24
  2.9 3.0 %collective-permute-start = (bf16[3,1536]{1,0:T(4,128)(2,1)S(1)}, bf16[3,1536]{1,0:T(4,128)(2,1)S(1)}, u32[]{:S(2)}, u32[]{:S(2)}) collective-permute-start(bf16[3,1536]{1,0:T(4,128)(2,1)S(1)} %get-tuple-element.7), channel_id=1, source_target_pairs={{0,4},{4,8},{8,12},{12,16},{16,20},{20,24},{24,28},{1,5},{5,9},{9,... | collective-permute-start | bytes 27656 | tf_op jit(solution)/shard_map/ppermute | solution.py:23
  5.9 1.0 %fusion.107 = (bf16[128,512]{1,0:T(8,128)(2,1)S(1)}, bf16[128,512]{1,0:T(8,128)(2,1)S(1)}) fusion(bf16[256,512]{1,0:T(8,128)(2,1)} %param.11), kind=kLoop, calls=%fused_computation.223 | loop fusion | bytes 524288 | tf_op jit(solution)/shard_map/slice | solution.py:271
  7.0 0.7 %copy-done.4 = f32[256,16]{0,1:T(8,128)S(1)} copy-done((f32[256,16]{0,1:T(8,128)S(1)}, f32[256,16]{0,1:T(8,128)}, u32[]{:S(2)}) %copy-start.4) | copy-done | bytes 16408
  7.7 0.6 %copy-done.8 = f32[16]{0:T(128)S(1)} copy-done((f32[16]{0:T(128)S(1)}, f32[16]{0:T(128)}, u32[]{:S(2)}) %copy-start.8) | copy-done | bytes 88
  8.5 0.2 reduce_window_sum.18
  8.8 0.2 reduce_window_sum.17
  9.1 0.7 %copy-done.6 = f32[4,512]{1,0:T(4,128)S(1)} copy-done((f32[4,512]{1,0:T(4,128)S(1)}, f32[4,512]{1,0:T(4,128)}, u32[]{:S(2)}) %copy-start.6) | copy-done | bytes 8216
  10.2 0.5 %copy-done.2 = bf16[3,1536]{1,0:T(4,128)(2,1)} copy-done((bf16[3,1536]{1,0:T(4,128)(2,1)}, bf16[3,1536]{1,0:T(4,128)(2,1)S(1)}, u32[]{:S(2)}) %copy-start.2) | copy-done | bytes 9240
  10.8 0.6 %multiply_convert_fusion.6 = (bf16[128,1024]{1,0:T(8,128)(2,1)S(1)}, bf16[128,1024]{1,0:T(8,128)(2,1)S(1)}) fusion(f32[131,1024]{1,0:T(8,128)S(1)} %maximum_convert_fusion, f32[1024]{0:T(1024)S(1)} %bitcast.145, f32[1024]{0:T(1024)S(1)} %bitcast.146, f32[1024]{0:T(1024)S(1)} %bitcast.144, f32[1024]{0:T(1024)S(1)} %bitcast.143, ...), kind=kLoop, calls=%fused_computation.64 | loop fusion | flops 3145728 | bytes 4734976 | tf_op jit(solution)/shard_map/convert_element_type | solution.py:239
  11.4 0.2 copy.86
  11.6 0.2 copy.80
  11.8 0.5 %slice-done = bf16[3,512]{1,0:T(4,128)(2,1)S(1)} async-done(((bf16[3,1536]{1,0:T(4,128)(2,1)}), bf16[3,512]{1,0:T(4,128)(2,1)S(1)}, s32[]{:S(2)}) %slice-start) | async-done | bytes 3096 | tf_op jit(solution)/shard_map/slice | solution.py:243
  12.4 0.3 multiply_convert_fusion.8
  12.7 0.2 fusion.49
  13.0 0.2 fusion.51
  13.3 2.6 %collective-permute-start.2 = (f32[1032,128]{1,0:T(8,128)S(1)}, f32[1032,128]{1,0:T(8,128)S(1)}, u32[]{:S(2)}, u32[]{:S(2)}) collective-permute-start(f32[1032,128]{1,0:T(8,128)S(1)} %pad_maximum_fusion.1), channel_id=1, source_target_pairs={{0,4},{4,0},{8,12},{12,8},{16,20},{20,16},{24,28},{28,24},{1,5},{5... | collective-permute-start | bytes 1585160 | tf_op jit(solution)/shard_map/ppermute | solution.py:168
  16.0 0.6 %slice.315 = pred[1]{0:T(512)(128)(4,1)} slice(pred[72]{0:T(512)(128)(4,1)S(1)} %iota_compare_fusion.4), slice={[64:65]} | slice | bytes 2 | tf_op jit(solution)/shard_map/slice | solution.py:87
  16.7 0.7 %copy.84 = f32[128,16]{0,1:T(8,128)} copy(f32[128,16]{1,0:T(8,128)S(1)} %exp.58) | data formatting | bytes 16384 | tf_op jit(solution)/shard_map/exp | solution.py:267
  18.0 0.2 copy.91
  18.1 0.3 fusion.60
  18.6 0.1 fusion.39
  18.8 2.4 %collective-permute-start.3 = (bf16[2,8,72,128]{3,1,2,0:T(8,128)(2,1)S(1)}, bf16[2,8,72,128]{3,1,2,0:T(8,128)(2,1)S(1)}, u32[]{:S(2)}, u32[]{:S(2)}) collective-permute-start(bf16[2,8,72,128]{3,1,2,0:T(8,128)(2,1)S(1)} %fusion.39), channel_id=1, source_target_pairs={{0,8},{4,12},{8,0},{12,4},{16,24},{20,28},{24,16},{28,20},{1,9},{5... | collective-permute-start | bytes 884744 | tf_op jit(solution)/shard_map/ppermute | solution.py:109
  21.2 0.6 %fusion.2 = f32[128,16,64]{0,2,1:T(8,128)S(1)} fusion(bf16[128,16,64]{0,2,1:T(8,128)(2,1)S(1)} %bitcast.139, f32[16,128]{1,0:T(8,128)S(1)} %get-tuple-element.54, f32[16,128]{1,0:T(8,128)S(1)} %copy.82, f32[128,128]{1,0:T(8,128)S(1)} %fusion.81, pred[128,128]{1,0:T(8,128)(4,1)S(1)} %iota_compare_fusion, f32[16]{0:T(128)S(1)} %copy-done.9), kind=kOutput, calls=%fused_computation.8 | convolution fusion | flops 35520512 | bytes 884800 | tf_op jit(solution)/shard_map/hts,shp->thp/dot_general | solution.py:252
  22.1 6.4 %collective-permute-done.3 = bf16[2,8,72,128]{3,1,2,0:T(8,128)(2,1)S(1)} collective-permute-done((bf16[2,8,72,128]{3,1,2,0:T(8,128)(2,1)S(1)}, bf16[2,8,72,128]{3,1,2,0:T(8,128)(2,1)S(1)}, u32[]{:S(2)}, u32[]{:S(2)}) %collective-permute-start.3) | collective-permute-done | bytes 294944 | tf_op jit(solution)/shard_map/ppermute | solution.py:109
  28.7 0.2 fusion.42
  28.9 0.2 multiply_add_fusion
  29.1 0.7 %fusion.86 = (f32[8,128]{1,0:T(8,128)S(1)}, f32[8,1,128]{2,0,1:T(8,128)S(1)}) fusion(f32[8,72,128]{2,0,1:T(8,128)S(1)} %get-tuple-element.18, pred[]{:T(512)S(6)} %eq.31, f32[8,128]{1,0:T(8,128)S(1)} %get-tuple-element.65, f32[8,128]{1,0:T(8,128)S(1)} %get-tuple-element.68, f32[8,72,128]{2,0,1:T(8,128)S(1)} %slice_bitcast_fusion.8, ...), kind=kLoop, calls=%fused_computation.167 | loop fusion | flops 9216 | bytes 319523 | tf_op jit(solution)/shard_map/jit(_where)/broadcast_in_dim | solution.py:98
  29.9 0.2 broadcast_multiply_fusion
  30.1 0.3 fusion.66
  30.4 1.0 %collective-permute-start.4 = (bf16[1,8,72,128]{3,2,1,0:T(8,128)(2,1)S(1)}, bf16[1,8,72,128]{3,2,1,0:T(8,128)(2,1)S(1)}, u32[]{:S(2)}, u32[]{:S(2)}) collective-permute-start(bf16[1,8,72,128]{3,2,1,0:T(8,128)(2,1)S(1)} %fusion.66), channel_id=1, source_target_pairs={{0,16},{4,20},{8,24},{12,28},{16,0},{20,4},{24,8},{28,12},{1,17},{... | collective-permute-start | bytes 442376 | tf_op jit(solution)/shard_map/ppermute | solution.py:109
  31.4 4.4 %collective-permute-done.4 = bf16[1,8,72,128]{3,2,1,0:T(8,128)(2,1)S(1)} collective-permute-done((bf16[1,8,72,128]{3,2,1,0:T(8,128)(2,1)S(1)}, bf16[1,8,72,128]{3,2,1,0:T(8,128)(2,1)S(1)}, u32[]{:S(2)}, u32[]{:S(2)}) %collective-permute-start.4) | collective-permute-done | bytes 147488 | tf_op jit(solution)/shard_map/ppermute | solution.py:109
  36.0 0.3 fusion.68
  36.4 0.6 %fusion.3 = f32[128,16,64]{0,2,1:T(8,128)S(1)} fusion(bf16[128,16,64]{0,2,1:T(8,128)(2,1)S(1)} %bitcast.137, f32[16,128]{1,0:T(8,128)S(1)} %get-tuple-element.57, f32[16,128]{1,0:T(8,128)S(1)} %copy.102, f32[128,128]{1,0:T(8,128)S(1)} %fusion.76, pred[128,128]{1,0:T(8,128)(4,1)S(1)} %iota_compare_fusion, f32[16]{0:T(128)S(1)} %copy-done.9), kind=kOutput, calls=%fused_computation.9 | convolution fusion | flops 35520512 | bytes 884800 | tf_op jit(solution)/shard_map/hts,shp->thp/dot_general | solution.py:252
  36.9 0.6 %collective-permute-start.6 = (f32[8,64,128]{2,1,0:T(8,128)S(1)}, f32[8,64,128]{2,1,0:T(8,128)S(1)}, u32[]{:S(2)}, u32[]{:S(2)}) collective-permute-start(f32[8,64,128]{2,1,0:T(8,128)S(1)} %get-tuple-element.40), channel_id=1, source_target_pairs={{0,4},{4,0},{8,12},{12,8},{16,20},{20,16},{24,28},{28,24},{1,5},{5... | collective-permute-start | bytes 786440 | tf_op jit(solution)/shard_map/ppermute | solution.py:186
  37.6 0.3 collective-permute-done.5
  37.9 0.3 copy-done.3
  38.2 0.4 fusion.1
  38.6 0.2 copy.108
  38.8 0.4 fusion
  39.2 0.2 copy.109
  39.4 0.8 %copy-done.1 = bf16[256,1024]{1,0:T(8,128)(2,1)S(1)} copy-done((bf16[256,1024]{1,0:T(8,128)(2,1)S(1)}, bf16[256,1024]{1,0:T(8,128)(2,1)}, u32[]{:S(2)}) %copy-start.1) | copy-done | bytes 524312
  40.2 0.4 multiply_reduce_fusion
  40.7 1.6 %collective-permute-start.7 = (f32[256]{0:T(256)S(1)}, f32[256]{0:T(256)S(1)}, u32[]{:S(2)}, u32[]{:S(2)}) collective-permute-start(f32[256]{0:T(256)S(1)} %get-tuple-element.9), channel_id=1, source_target_pairs={{0,1},{1,0},{2,3},{3,2},{4,5},{5,4},{6,7},{7,6},{8,9},{9,8},{10,11... | collective-permute-start | bytes 3080 | tf_op jit(solution)/shard_map/ppermute | solution.py:30
  42.3 2.0 %collective-permute-done.7 = f32[256]{0:T(256)S(1)} collective-permute-done((f32[256]{0:T(256)S(1)}, f32[256]{0:T(256)S(1)}, u32[]{:S(2)}, u32[]{:S(2)}) %collective-permute-start.7) | collective-permute-done | bytes 1056 | tf_op jit(solution)/shard_map/ppermute | solution.py:30
  44.3 1.0 %multiply_convert_fusion = bf16[256,1024]{1,0:T(8,128)(2,1)} fusion(f32[256,1024]{1,0:T(8,128)S(1)} %get-tuple-element.10, f32[1024]{0:T(1024)S(1)} %copy-done.7, f32[256]{0:T(256)S(1)} %add_rsqrt_fusion), kind=kLoop, calls=%fused_computation.14 | loop fusion | flops 786432 | bytes 1577984 | tf_op jit(solution)/shard_map/convert_element_type | solution.py:291
  (88 shorter events, 2.8 us)
Async XLA Ops:
  0.0 6.9 %copy-start = (bf16[256,1024]{1,0:T(8,128)(2,1)S(1)}, bf16[256,1024]{1,0:T(8,128)(2,1)}, u32[]{:S(2)}) copy-start(bf16[256,1024]{1,0:T(8,128)(2,1)} %param.9) | copy-start | bytes 1572868
  1.6 8.5 %collective-permute-start.1 = (bf16[3,1536]{1,0:T(4,128)(2,1)S(1)}, bf16[3,1536]{1,0:T(4,128)(2,1)S(1)}, u32[]{:S(2)}, u32[]{:S(2)}) collective-permute-start(bf16[3,1536]{1,0:T(4,128)(2,1)S(1)} %get-tuple-element.8), channel_id=1, source_target_pairs={{4,0},{8,4},{12,8},{16,12},{20,16},{24,20},{28,24},{5,1},{9,5},{13... | collective-permute-start | bytes 27656 | tf_op jit(solution)/shard_map/ppermute | solution.py:24
  2.9 7.8 %collective-permute-start = (bf16[3,1536]{1,0:T(4,128)(2,1)S(1)}, bf16[3,1536]{1,0:T(4,128)(2,1)S(1)}, u32[]{:S(2)}, u32[]{:S(2)}) collective-permute-start(bf16[3,1536]{1,0:T(4,128)(2,1)S(1)} %get-tuple-element.7), channel_id=1, source_target_pairs={{0,4},{4,8},{8,12},{12,16},{16,20},{20,24},{24,28},{1,5},{5,9},{9,... | collective-permute-start | bytes 27656 | tf_op jit(solution)/shard_map/ppermute | solution.py:23
  6.9 0.7 %copy-start.4 = (f32[256,16]{0,1:T(8,128)S(1)}, f32[256,16]{0,1:T(8,128)}, u32[]{:S(2)}) copy-start(f32[256,16]{0,1:T(8,128)} %param.12) | copy-start | bytes 49156
  7.6 0.7 %copy-start.8 = (f32[16]{0:T(128)S(1)}, f32[16]{0:T(128)}, u32[]{:S(2)}) copy-start(f32[16]{0:T(128)} %param.13) | copy-start | bytes 196
  9.0 0.7 %copy-start.6 = (f32[4,512]{1,0:T(4,128)S(1)}, f32[4,512]{1,0:T(4,128)}, u32[]{:S(2)}) copy-start(f32[4,512]{1,0:T(4,128)} %param.16) | copy-start | bytes 24580
  9.0 0.8 %copy-start.5 = (f32[4,1024]{1,0:T(4,128)S(1)}, f32[4,1024]{1,0:T(4,128)}, u32[]{:S(2)}) copy-start(f32[4,1024]{1,0:T(4,128)} %param.15) | copy-start | bytes 49156
  10.1 0.6 %copy-start.2 = (bf16[3,1536]{1,0:T(4,128)(2,1)}, bf16[3,1536]{1,0:T(4,128)(2,1)S(1)}, u32[]{:S(2)}) copy-start(bf16[3,1536]{1,0:T(4,128)(2,1)S(1)} %broadcast_select_fusion) | copy-start | bytes 27652
  11.6 0.7 %slice-start = ((bf16[3,1536]{1,0:T(4,128)(2,1)}), bf16[3,512]{1,0:T(4,128)(2,1)S(1)}, s32[]{:S(2)}) async-start(bf16[3,1536]{1,0:T(4,128)(2,1)} %copy-done.2), calls=%async_computation | async-start | bytes 8192 | tf_op jit(solution)/shard_map/slice | solution.py:243
  13.3 4.4 %collective-permute-start.2 = (f32[1032,128]{1,0:T(8,128)S(1)}, f32[1032,128]{1,0:T(8,128)S(1)}, u32[]{:S(2)}, u32[]{:S(2)}) collective-permute-start(f32[1032,128]{1,0:T(8,128)S(1)} %pad_maximum_fusion.1), channel_id=1, source_target_pairs={{0,4},{4,0},{8,12},{12,8},{16,20},{20,16},{24,28},{28,24},{1,5},{5... | collective-permute-start | bytes 1585160 | tf_op jit(solution)/shard_map/ppermute | solution.py:168
  18.8 2.4 %copy-start.9 = (f32[16]{0:T(128)S(1)}, f32[16]{0:T(128)}, u32[]{:S(2)}) copy-start(f32[16]{0:T(128)} %param.14) | copy-start | bytes 196
  18.8 9.7 %collective-permute-start.3 = (bf16[2,8,72,128]{3,1,2,0:T(8,128)(2,1)S(1)}, bf16[2,8,72,128]{3,1,2,0:T(8,128)(2,1)S(1)}, u32[]{:S(2)}, u32[]{:S(2)}) collective-permute-start(bf16[2,8,72,128]{3,1,2,0:T(8,128)(2,1)S(1)} %fusion.39), channel_id=1, source_target_pairs={{0,8},{4,12},{8,0},{12,4},{16,24},{20,28},{24,16},{28,20},{1,9},{5... | collective-permute-start | bytes 884744 | tf_op jit(solution)/shard_map/ppermute | solution.py:109
  30.4 5.4 %collective-permute-start.4 = (bf16[1,8,72,128]{3,2,1,0:T(8,128)(2,1)S(1)}, bf16[1,8,72,128]{3,2,1,0:T(8,128)(2,1)S(1)}, u32[]{:S(2)}, u32[]{:S(2)}) collective-permute-start(bf16[1,8,72,128]{3,2,1,0:T(8,128)(2,1)S(1)} %fusion.66), channel_id=1, source_target_pairs={{0,16},{4,20},{8,24},{12,28},{16,0},{20,4},{24,8},{28,12},{1,17},{... | collective-permute-start | bytes 442376 | tf_op jit(solution)/shard_map/ppermute | solution.py:109
  36.3 1.6 %collective-permute-start.5 = (f32[8,64,128]{2,1,0:T(8,128)S(1)}, f32[8,64,128]{2,1,0:T(8,128)S(1)}, u32[]{:S(2)}, u32[]{:S(2)}) collective-permute-start(f32[8,64,128]{2,1,0:T(8,128)S(1)} %get-tuple-element.19), channel_id=1, source_target_pairs={{0,4},{4,0},{8,12},{12,8},{16,20},{20,16},{24,28},{28,24},{1,5},{5... | collective-permute-start | bytes 786440 | tf_op jit(solution)/shard_map/ppermute | solution.py:186
  36.9 1.9 %collective-permute-start.6 = (f32[8,64,128]{2,1,0:T(8,128)S(1)}, f32[8,64,128]{2,1,0:T(8,128)S(1)}, u32[]{:S(2)}, u32[]{:S(2)}) collective-permute-start(f32[8,64,128]{2,1,0:T(8,128)S(1)} %get-tuple-element.40), channel_id=1, source_target_pairs={{0,4},{4,0},{8,12},{12,8},{16,20},{20,16},{24,28},{28,24},{1,5},{5... | collective-permute-start | bytes 786440 | tf_op jit(solution)/shard_map/ppermute | solution.py:186
  37.5 0.7 %copy-start.3 = (f32[128,16]{0,1:T(8,128)S(1)}, f32[128,16]{0,1:T(8,128)}, u32[]{:S(2)}) copy-start(f32[128,16]{0,1:T(8,128)} %copy.84) | copy-start | bytes 24580
  39.2 1.0 %copy-start.1 = (bf16[256,1024]{1,0:T(8,128)(2,1)S(1)}, bf16[256,1024]{1,0:T(8,128)(2,1)}, u32[]{:S(2)}) copy-start(bf16[256,1024]{1,0:T(8,128)(2,1)} %param.10) | copy-start | bytes 1572868
  40.6 3.7 %copy-start.7 = (f32[1024]{0:T(1024)S(1)}, f32[1024]{0:T(1024)}, u32[]{:S(2)}) copy-start(f32[1024]{0:T(1024)} %param.17) | copy-start | bytes 12292
  40.7 3.6 %collective-permute-start.7 = (f32[256]{0:T(256)S(1)}, f32[256]{0:T(256)S(1)}, u32[]{:S(2)}, u32[]{:S(2)}) collective-permute-start(f32[256]{0:T(256)S(1)} %get-tuple-element.9), channel_id=1, source_target_pairs={{0,1},{1,0},{2,3},{3,2},{4,5},{5,4},{6,7},{7,6},{8,9},{9,8},{10,11... | collective-permute-start | bytes 3080 | tf_op jit(solution)/shard_map/ppermute | solution.py:30

commit v10 on v9

--- a/solution.py
+++ b/solution.py
@@ -273,6 +273,9 @@
     second_out, second_cum, second_c, second_elem = local_block(
         lead_second, inner_rows[half_rows:], input_proj[half_rows:], step_size[half_rows:]
     )
+    gate_act, first_out, second_out = lax.optimization_barrier(
+        (jax.nn.silu(gate_rows.astype(jnp.float32)), first_out, second_out)
+    )
     first_in, second_in = block_states(
         first_elem[1], second_elem[1], first_cum[-1], second_cum[-1], seq_pos, seq_count
     )
@@ -283,7 +286,7 @@
         ],
         axis=0,
     )
-    gated = ssm_out * jax.nn.silu(gate_rows.astype(jnp.float32))
+    gated = ssm_out * gate_act
     partial_sq = jnp.sum(gated * gated, axis=1)
     other_sq = partner(partial_sq, "head", 0)
     mean_sq = (partial_sq + other_sq) / (GROUP_HEADS * HEAD_SIZE)

time: 46 us -> 54.1 us (1.18)
  local copies, waits for them, and re-layouts: 10.2 us -> 14.7 us
  other arithmetic: 6.15 us -> 9.02 us
  matrix products: 2.62 us -> 3.63 us
    unnamed x20 -> x50, local copies, waits for them, and re-layouts: 3.67 us -> 6.39 us
    mul x0 -> x2, other arithmetic: none -> 1.96 us  [the longest x1 1.36 us: on_device(): jax.nn.silu(gate_rows.astype(jnp.float32))]
    transpose x2, local copies, waits for them, and re-layouts: 0.1 us -> 1.34 us  [local_block(): log_gap = log_cum.T[:, :, None] - log_cum.T[:, None, :]]
    dot_general x2, matrix products: 0.78 us -> 1.81 us  [finish_block(): jnp.einsum('tn,hpn->thp', c_rows.astype(jnp.float32), state_in, precision...]
    select_n x1, other arithmetic: 0.29 us -> 0.98 us  [block_states(): jnp.where(upper, prefix, after_low)]
    concatenate x1, local copies, waits for them, and re-layouts: 0.01 us -> 0.61 us  [with_decay(): jnp.concatenate([x, jnp.broadcast_to(e[:, None, None], (heads, 8, lanes))...]
  transfers between devices with their start and end apart: 8 -> 8, of which waited for: 4 -> 5; matrix products, arithmetic and copies ran while one was open for 13% -> 19% of each run, Pallas kernels for 0% -> 0%
where the time goes in v10:
time: 54.1 us; the launch traced here: 53.3 us
  local copies, waits for them, and re-layouts  14.7 us (27%)
  waiting for transfers between devices  12.8 us (24%)
  starting transfers between devices  12.6 us (23%)
  other arithmetic  9.02 us (17%)
  matrix products  3.63 us (7%)
  between operations  0.65 us (1%)
    ppermute x2, waiting for transfers between devices, butterfly_states(): got, got_e = from_link(lax.ppermute(msg, 'seq', pairs), rows)  10.3 us
    unnamed x50, local copies, waits for them, and re-layouts  6.39 us
    ppermute x2, starting transfers between devices, butterfly_states(): got, got_e = from_link(lax.ppermute(msg, 'seq', pairs), rows)  3.39 us
    ppermute x1, starting transfers between devices, extended_2(): low = lax.ppermute(tail, axis, forward)  3.03 us
    ppermute x1, starting transfers between devices, block_states(): got = lax.ppermute(sent, 'seq', pairs)  2.62 us
    ppermute x1, waiting for transfers between devices, partner(): lax.ppermute(array, axis, [(i, i ^ 1 << stride) for i in range(lax.axis_s...  1.99 us
    dot_general x2, matrix products, finish_block(): jnp.einsum('tn,hpn->thp', c_rows.astype(jnp.float32), state_in, precision...  1.81 us
    ppermute x1, starting transfers between devices, partner(): lax.ppermute(array, axis, [(i, i ^ 1 << stride) for i in range(lax.axis_s...  1.66 us
  transfers between devices with their start and end apart: 8, of which 5 were waited for; matrix products, arithmetic and copies ran while one was open for 19% of the time, Pallas kernels for 0%

profile of v10, /device:TPU:0, one launch (start us, length us, event | category | flops | bytes accessed | tf_op | source)
XLA Modules:
  0.0 53.3 jit_solution(16957081895431234243)
XLA Ops:
  0.0 0.8 %fusion.104 = (bf16[3,1024]{1,0:T(4,128)(2,1)S(1)}, bf16[3,1024]{1,0:T(4,128)(2,1)S(1)}) fusion(bf16[256,1024]{1,0:T(8,128)(2,1)} %param.9), kind=kLoop, calls=%fused_computation.222 | loop fusion | bytes 24576 | tf_op jit(solution)/shard_map/slice | solution.py:222
  0.8 0.7 %fusion.106 = (bf16[3,512]{1,0:T(4,128)(2,1)S(1)}, bf16[3,512]{1,0:T(4,128)(2,1)S(1)}) fusion(bf16[256,512]{1,0:T(8,128)(2,1)} %param.11), kind=kLoop, calls=%fused_computation.224 | loop fusion | bytes 12288 | tf_op jit(solution)/shard_map/slice | solution.py:222
  1.6 1.3 %collective-permute-start.1 = (bf16[3,1536]{1,0:T(4,128)(2,1)S(1)}, bf16[3,1536]{1,0:T(4,128)(2,1)S(1)}, u32[]{:S(2)}, u32[]{:S(2)}) collective-permute-start(bf16[3,1536]{1,0:T(4,128)(2,1)S(1)} %get-tuple-element.11), channel_id=1, source_target_pairs={{4,0},{8,4},{12,8},{16,12},{20,16},{24,20},{28,24},{5,1},{9,5},{13... | collective-permute-start | bytes 27656 | tf_op jit(solution)/shard_map/ppermute | solution.py:24
  2.9 3.0 %collective-permute-start = (bf16[3,1536]{1,0:T(4,128)(2,1)S(1)}, bf16[3,1536]{1,0:T(4,128)(2,1)S(1)}, u32[]{:S(2)}, u32[]{:S(2)}) collective-permute-start(bf16[3,1536]{1,0:T(4,128)(2,1)S(1)} %get-tuple-element.10), channel_id=1, source_target_pairs={{0,4},{4,8},{8,12},{12,16},{16,20},{20,24},{24,28},{1,5},{5,9},{9,... | collective-permute-start | bytes 27656 | tf_op jit(solution)/shard_map/ppermute | solution.py:23
  5.9 1.0 %fusion.105 = (bf16[128,512]{1,0:T(8,128)(2,1)S(1)}, bf16[128,512]{1,0:T(8,128)(2,1)S(1)}) fusion(bf16[256,512]{1,0:T(8,128)(2,1)} %param.11), kind=kLoop, calls=%fused_computation.223 | loop fusion | bytes 524288 | tf_op jit(solution)/shard_map/slice | solution.py:274
  7.0 0.7 %copy-done.7 = f32[256,16]{0,1:T(8,128)S(1)} copy-done((f32[256,16]{0,1:T(8,128)S(1)}, f32[256,16]{0,1:T(8,128)}, u32[]{:S(2)}) %copy-start.7) | copy-done | bytes 16408
  7.7 0.6 %copy-done.23 = f32[16]{0:T(128)S(1)} copy-done((f32[16]{0:T(128)S(1)}, f32[16]{0:T(128)}, u32[]{:S(2)}) %copy-start.23) | copy-done | bytes 88
  9.1 0.7 %copy-done.13 = f32[4,512]{1,0:T(4,128)S(1)} copy-done((f32[4,512]{1,0:T(4,128)S(1)}, f32[4,512]{1,0:T(4,128)}, u32[]{:S(2)}) %copy-start.13) | copy-done | bytes 8216
  9.8 0.4 copy-done.20
  10.4 0.6 %exponential_multiply_fusion.1 = (f32[128,16]{0,1:T(8,128)S(1)}, f32[16,128]{1,0:T(8,128)}, f32[16,128]{1,0:T(8,128)}, f32[128,16]{0,1:T(8,128)S(1)}) fusion(f32[128,16]{0,1:T(8,128)S(1)} %copy.89, f32[256,16]{0,1:T(8,128)S(1)} %compare_select_fusion, f32[16]{0:T(128)S(1)} %slice_bitcast_fusion.7, f32[128,16]{0,1:T(8,128)S(1)} %copy.90, ...), kind=kLoop, calls=%fused_computation.160 | loop fusion | flops 8192 | bytes 65664 | tf_op jit(solution)/shard_map/mul | solution.py:255
  11.0 0.5 iota_compare_fusion.3
  11.6 0.5 copy-done.5
  12.2 0.6 %multiply_convert_fusion.5 = (bf16[128,1024]{1,0:T(8,128)(2,1)S(1)}, bf16[128,1024]{1,0:T(8,128)(2,1)S(1)}) fusion(f32[131,1024]{1,0:T(8,128)S(1)} %maximum_convert_fusion.1, f32[1024]{0:T(1024)S(1)} %bitcast.145, f32[1024]{0:T(1024)S(1)} %bitcast.146, f32[1024]{0:T(1024)S(1)} %bitcast.144, f32[1024]{0:T(1024)S(1)} %bitcast.143, ...), kind=kLoop, calls=%fused_computation.57 | loop fusion | flops 3145728 | bytes 4734976 | tf_op jit(solution)/shard_map/convert_element_type | solution.py:239
  13.2 0.5 slice-done
  13.8 0.3 multiply_convert_fusion.7
  14.4 0.4 copy-done.1
  15.2 2.6 %collective-permute-start.2 = (f32[1032,128]{1,0:T(8,128)S(1)}, f32[1032,128]{1,0:T(8,128)S(1)}, u32[]{:S(2)}, u32[]{:S(2)}) collective-permute-start(f32[1032,128]{1,0:T(8,128)S(1)} %pad_maximum_fusion.1), channel_id=1, source_target_pairs={{0,4},{4,0},{8,12},{12,8},{16,20},{20,16},{24,28},{28,24},{1,5},{5... | collective-permute-start | bytes 1585160 | tf_op jit(solution)/shard_map/ppermute | solution.py:168
  17.9 0.5 copy-done.9
  18.3 0.7 %slice.315 = pred[1]{0:T(512)(128)(4,1)} slice(pred[72]{0:T(512)(128)(4,1)S(1)} %iota_compare_fusion.4), slice={[64:65]} | slice | bytes 2 | tf_op jit(solution)/shard_map/slice | solution.py:87
  19.0 0.7 %copy.86 = f32[16,128]{1,0:T(8,128)} copy(f32[16,128]{0,1:T(8,128)S(1)} %bitcast.134) | data formatting | bytes 16384 | tf_op jit(solution)/shard_map/transpose | solution.py:249
  19.7 0.7 %copy.82 = f32[16,128]{1,0:T(8,128)} copy(f32[16,128]{0,1:T(8,128)S(1)} %bitcast.135) | data formatting | bytes 16384 | tf_op jit(solution)/shard_map/transpose | solution.py:249
  20.3 0.7 %copy.88 = f32[128,16]{0,1:T(8,128)} copy(f32[128,16]{1,0:T(8,128)S(1)} %exp.62) | data formatting | bytes 16384 | tf_op jit(solution)/shard_map/exp | solution.py:267
  21.1 0.6 %concatenate.84 = f32[72]{0:T(128)} pad(f32[64]{0:T(128)S(1)} %broadcast.164, f32[]{:T(128)} %constant.95.clone.1), padding=0_8 | pad | bytes 548 | tf_op jit(solution)/shard_map/concatenate | solution.py:82
  21.7 1.4 %convert_multiply_fusion = f32[256,1024]{1,0:T(8,128)S(1)} fusion(bf16[256,1024]{1,0:T(8,128)(2,1)} %param.10), kind=kLoop, calls=%fused_computation | loop fusion | flops 1310720 | bytes 1572864 | tf_op jit(solution)/shard_map/jit(silu)/mul | solution.py:277
  23.3 0.6 %copy-done.19 = f32[16]{0:T(128)S(1)} copy-done((f32[16]{0:T(128)S(1)}, f32[16]{0:T(128)}, u32[]{:S(2)}) %copy-start.19) | copy-done | bytes 88
  24.3 0.3 fusion.59
  24.8 0.6 %copy-done.17 = pred[72]{0:T(512)(128)(4,1)S(1)} copy-done((pred[72]{0:T(512)(128)(4,1)S(1)}, pred[72]{0:T(512)(128)(4,1)}, u32[]{:S(2)}) %copy-start.17) | copy-done | bytes 96
  25.5 2.4 %collective-permute-start.3 = (bf16[2,8,72,128]{3,1,2,0:T(8,128)(2,1)S(1)}, bf16[2,8,72,128]{3,1,2,0:T(8,128)(2,1)S(1)}, u32[]{:S(2)}, u32[]{:S(2)}) collective-permute-start(bf16[2,8,72,128]{3,1,2,0:T(8,128)(2,1)S(1)} %fusion.38), channel_id=1, source_target_pairs={{0,8},{4,12},{8,0},{12,4},{16,24},{20,28},{24,16},{28,20},{1,9},{5... | collective-permute-start | bytes 884744 | tf_op jit(solution)/shard_map/ppermute | solution.py:109
  27.9 0.6 %fusion.3 = f32[128,16,64]{0,2,1:T(8,128)S(1)} fusion(bf16[128,16,64]{0,2,1:T(8,128)(2,1)S(1)} %bitcast.139, f32[16,128]{1,0:T(8,128)S(1)} %copy-done.15, f32[16,128]{1,0:T(8,128)S(1)} %copy-done.12, f32[128,128]{1,0:T(8,128)S(1)} %fusion.75, pred[128,128]{1,0:T(8,128)(4,1)S(1)} %iota_compare_fusion, f32[16]{0:T(128)S(1)} %copy-done.24), kind=kOutput, calls=%fused_computation.9 | convolution fusion | flops 35520512 | bytes 884800 | tf_op jit(solution)/shard_map/hts,shp->thp/dot_general | solution.py:252
  28.5 0.3 copy-done.4
  29.1 6.0 %collective-permute-done.3 = bf16[2,8,72,128]{3,1,2,0:T(8,128)(2,1)S(1)} collective-permute-done((bf16[2,8,72,128]{3,1,2,0:T(8,128)(2,1)S(1)}, bf16[2,8,72,128]{3,1,2,0:T(8,128)(2,1)S(1)}, u32[]{:S(2)}, u32[]{:S(2)}) %collective-permute-start.3) | collective-permute-done | bytes 294944 | tf_op jit(solution)/shard_map/ppermute | solution.py:109
  35.3 0.6 %copy-done.10 = pred[72]{0:T(512)(128)(4,1)S(1)} copy-done((pred[72]{0:T(512)(128)(4,1)S(1)}, pred[72]{0:T(512)(128)(4,1)}, u32[]{:S(2)}) %copy-start.10) | copy-done | bytes 96
  35.9 0.2 fusion.41
  36.3 0.8 %fusion.85 = (f32[8,128]{1,0:T(8,128)S(1)}, f32[8,1,128]{2,0,1:T(8,128)S(1)}) fusion(f32[8,72,128]{2,0,1:T(8,128)S(1)} %get-tuple-element.22, pred[]{:T(512)S(6)} %eq.32, f32[8,128]{1,0:T(8,128)S(1)} %get-tuple-element.69, f32[8,128]{1,0:T(8,128)S(1)} %get-tuple-element.72, f32[8,72,128]{2,0,1:T(8,128)S(1)} %slice_bitcast_fusion.8, ...), kind=kLoop, calls=%fused_computation.167 | loop fusion | flops 9216 | bytes 319523 | tf_op jit(solution)/shard_map/jit(_where)/broadcast_in_dim | solution.py:98
  37.2 0.2 broadcast_multiply_fusion
  37.4 0.3 fusion.65
  37.7 1.0 %collective-permute-start.4 = (bf16[1,8,72,128]{3,2,1,0:T(8,128)(2,1)S(1)}, bf16[1,8,72,128]{3,2,1,0:T(8,128)(2,1)S(1)}, u32[]{:S(2)}, u32[]{:S(2)}) collective-permute-start(bf16[1,8,72,128]{3,2,1,0:T(8,128)(2,1)S(1)} %fusion.65), channel_id=1, source_target_pairs={{0,16},{4,20},{8,24},{12,28},{16,0},{20,4},{24,8},{28,12},{1,17},{... | collective-permute-start | bytes 442376 | tf_op jit(solution)/shard_map/ppermute | solution.py:109
  38.7 4.3 %collective-permute-done.4 = bf16[1,8,72,128]{3,2,1,0:T(8,128)(2,1)S(1)} collective-permute-done((bf16[1,8,72,128]{3,2,1,0:T(8,128)(2,1)S(1)}, bf16[1,8,72,128]{3,2,1,0:T(8,128)(2,1)S(1)}, u32[]{:S(2)}, u32[]{:S(2)}) %collective-permute-start.4) | collective-permute-done | bytes 147488 | tf_op jit(solution)/shard_map/ppermute | solution.py:109
  43.2 1.0 %fusion.67 = (f32[8,64,128]{2,1,0:T(8,128)S(1)}, f32[8,64,128]{2,1,0:T(8,128)S(1)}, f32[8,64,128]{2,1,0:T(8,128)}, f32[8,64,128]{2,1,0:T(8,128)S(1)}) fusion(f32[8,64,128]{2,1,0:T(8,128)S(1)} %bitcast.131, f32[8,64,128]{2,1,0:T(8,128)S(1)} %get-tuple-element.38, f32[8]{0:T(128)S(1)} %get-tuple-element.28, pred[]{:T(512)S(6)} %eq.31, ...), kind=kLoop, calls=%fused_computation.133 | loop fusion | flops 983040 | bytes 3153990 | tf_op jit(solution)/shard_map/jit(_where)/select_n | solution.py:185
  44.2 0.6 %fusion.2 = f32[128,16,64]{0,2,1:T(8,128)S(1)} fusion(bf16[128,16,64]{0,2,1:T(8,128)(2,1)S(1)} %bitcast.137, f32[16,128]{1,0:T(8,128)S(1)} %copy-done.14, f32[16,128]{1,0:T(8,128)S(1)} %copy-done.11, f32[128,128]{1,0:T(8,128)S(1)} %fusion.80, pred[128,128]{1,0:T(8,128)(4,1)S(1)} %iota_compare_fusion, f32[16]{0:T(128)S(1)} %copy-done.24), kind=kOutput, calls=%fused_computation.8 | convolution fusion | flops 35520512 | bytes 884800 | tf_op jit(solution)/shard_map/hts,shp->thp/dot_general | solution.py:252
  44.8 0.6 %collective-permute-start.6 = (f32[8,64,128]{2,1,0:T(8,128)}, f32[8,64,128]{2,1,0:T(8,128)}, u32[]{:S(2)}, u32[]{:S(2)}) collective-permute-start(f32[8,64,128]{2,1,0:T(8,128)} %get-tuple-element.44), channel_id=1, source_target_pairs={{0,4},{4,0},{8,12},{12,8},{16,20},{20,16},{24,28},{28,24},{1,5},{5... | collective-permute-start | bytes 786440 | tf_op jit(solution)/shard_map/ppermute | solution.py:186
  45.5 0.3 collective-permute-done.5
  45.7 0.3 copy-done.6
  46.0 0.4 fusion.1
  46.9 1.4 %fusion = f32[128,16,64]{0,2,1:T(8,128)S(1)} fusion(f32[128,16,64]{0,2,1:T(8,128)S(1)} %fusion.3, f32[8,64,128]{2,1,0:T(8,128)S(1)} %fusion.68, f32[8,64,128]{2,1,0:T(8,128)} %collective-permute-done.6, f32[128,16]{0,1:T(8,128)S(1)} %copy.104, pred[]{:T(512)S(6)} %eq.31, bf16[128,512]{1,0:T(8,128)(2,1)S(1)} %copy-done.2, s32[]{:T(128)S(6)} %select_n.257), kind=kOutput, calls=%fused_computation.5 | convolution fusion | flops 201981952 | bytes 1613829 | tf_op jit(solution)/shard_map/tn,hpn->thp/dot_general | solution.py:264
  48.7 1.7 %collective-permute-start.7 = (f32[256]{0:T(256)S(1)}, f32[256]{0:T(256)S(1)}, u32[]{:S(2)}, u32[]{:S(2)}) collective-permute-start(f32[256]{0:T(256)S(1)} %multiply_reduce_fusion), channel_id=1, source_target_pairs={{0,1},{1,0},{2,3},{3,2},{4,5},{5,4},{6,7},{7,6},{8,9},{9,8},{10,11... | collective-permute-start | bytes 3080 | tf_op jit(solution)/shard_map/ppermute | solution.py:30
  50.3 2.0 %collective-permute-done.7 = f32[256]{0:T(256)S(1)} collective-permute-done((f32[256]{0:T(256)S(1)}, f32[256]{0:T(256)S(1)}, u32[]{:S(2)}, u32[]{:S(2)}) %collective-permute-start.7) | collective-permute-done | bytes 1056 | tf_op jit(solution)/shard_map/ppermute | solution.py:30
  52.3 1.0 %multiply_convert_fusion = bf16[256,1024]{1,0:T(8,128)(2,1)} fusion(f32[1024]{0:T(1024)S(1)} %copy-done.16, f32[256]{0:T(256)S(1)} %add_rsqrt_fusion, f32[256,1024]{1,0:T(8,128)S(1)} %convert_multiply_fusion, f32[128,1024]{1,0:T(8,128)S(1)} %copy.109, f32[128,1024]{1,0:T(8,128)S(1)} %copy.108), kind=kLoop, calls=%fused_computation.14 | loop fusion | flops 1310720 | bytes 2626560 | tf_op jit(solution)/shard_map/convert_element_type | solution.py:294
  (119 shorter events, 5.0 us)
Async XLA Ops:
  0.0 6.9 %copy-start = (bf16[256,1024]{1,0:T(8,128)(2,1)S(1)}, bf16[256,1024]{1,0:T(8,128)(2,1)}, u32[]{:S(2)}) copy-start(bf16[256,1024]{1,0:T(8,128)(2,1)} %param.9) | copy-start | bytes 1572868
  1.6 9.9 %collective-permute-start.1 = (bf16[3,1536]{1,0:T(4,128)(2,1)S(1)}, bf16[3,1536]{1,0:T(4,128)(2,1)S(1)}, u32[]{:S(2)}, u32[]{:S(2)}) collective-permute-start(bf16[3,1536]{1,0:T(4,128)(2,1)S(1)} %get-tuple-element.11), channel_id=1, source_target_pairs={{4,0},{8,4},{12,8},{16,12},{20,16},{24,20},{28,24},{5,1},{9,5},{13... | collective-permute-start | bytes 27656 | tf_op jit(solution)/shard_map/ppermute | solution.py:24
  2.9 9.2 %collective-permute-start = (bf16[3,1536]{1,0:T(4,128)(2,1)S(1)}, bf16[3,1536]{1,0:T(4,128)(2,1)S(1)}, u32[]{:S(2)}, u32[]{:S(2)}) collective-permute-start(bf16[3,1536]{1,0:T(4,128)(2,1)S(1)} %get-tuple-element.10), channel_id=1, source_target_pairs={{0,4},{4,8},{8,12},{12,16},{16,20},{20,24},{24,28},{1,5},{5,9},{9,... | collective-permute-start | bytes 27656 | tf_op jit(solution)/shard_map/ppermute | solution.py:23
  6.9 0.7 %copy-start.7 = (f32[256,16]{0,1:T(8,128)S(1)}, f32[256,16]{0,1:T(8,128)}, u32[]{:S(2)}) copy-start(f32[256,16]{0,1:T(8,128)} %param.12) | copy-start | bytes 49156
  7.6 0.7 %copy-start.23 = (f32[16]{0:T(128)S(1)}, f32[16]{0:T(128)}, u32[]{:S(2)}) copy-start(f32[16]{0:T(128)} %param.13) | copy-start | bytes 196
  9.0 0.7 %copy-start.13 = (f32[4,512]{1,0:T(4,128)S(1)}, f32[4,512]{1,0:T(4,128)}, u32[]{:S(2)}) copy-start(f32[4,512]{1,0:T(4,128)} %param.16) | copy-start | bytes 24580
  9.0 0.8 %copy-start.8 = (f32[4,1024]{1,0:T(4,128)S(1)}, f32[4,1024]{1,0:T(4,128)}, u32[]{:S(2)}) copy-start(f32[4,1024]{1,0:T(4,128)} %param.15) | copy-start | bytes 49156
  9.1 0.7 %copy-start.18 = (f32[16]{0:T(128)}, f32[16]{0:T(128)S(1)}, u32[]{:S(2)}) copy-start(f32[16]{0:T(128)S(1)} %fusion.98) | copy-start | bytes 196
  9.8 0.5 copy-start.20
  11.5 0.6 %copy-start.5 = (bf16[3,1536]{1,0:T(4,128)(2,1)}, bf16[3,1536]{1,0:T(4,128)(2,1)S(1)}, u32[]{:S(2)}) copy-start(bf16[3,1536]{1,0:T(4,128)(2,1)S(1)} %broadcast_select_fusion) | copy-start | bytes 27652
  13.0 0.7 %slice-start = ((bf16[3,1536]{1,0:T(4,128)(2,1)}), bf16[3,512]{1,0:T(4,128)(2,1)S(1)}, s32[]{:S(2)}) async-start(bf16[3,1536]{1,0:T(4,128)(2,1)} %copy-done.5), calls=%async_computation | async-start | bytes 8192 | tf_op jit(solution)/shard_map/slice | solution.py:243
  14.1 0.7 %copy-start.1 = (bf16[128,512]{1,0:T(8,128)(2,1)}, bf16[128,512]{1,0:T(8,128)(2,1)S(1)}, u32[]{:S(2)}) copy-start(bf16[128,512]{1,0:T(8,128)(2,1)S(1)} %get-tuple-element.74) | copy-start | bytes 393220
  14.1 0.7 %copy-start.3 = (bf16[128,512]{1,0:T(8,128)(2,1)}, bf16[128,512]{1,0:T(8,128)(2,1)S(1)}, u32[]{:S(2)}) copy-start(bf16[128,512]{1,0:T(8,128)(2,1)S(1)} %get-tuple-element.75) | copy-start | bytes 393220
  15.2 8.1 %collective-permute-start.2 = (f32[1032,128]{1,0:T(8,128)S(1)}, f32[1032,128]{1,0:T(8,128)S(1)}, u32[]{:S(2)}, u32[]{:S(2)}) collective-permute-start(f32[1032,128]{1,0:T(8,128)S(1)} %pad_maximum_fusion.1), channel_id=1, source_target_pairs={{0,4},{4,0},{8,12},{12,8},{16,20},{20,16},{24,28},{28,24},{1,5},{5... | collective-permute-start | bytes 1585160 | tf_op jit(solution)/shard_map/ppermute | solution.py:168
  17.8 0.5 %copy-start.9 = (pred[72]{0:T(512)(128)(4,1)}, pred[72]{0:T(512)(128)(4,1)S(1)}, u32[]{:S(2)}) copy-start(pred[72]{0:T(512)(128)(4,1)S(1)} %iota_compare_fusion.4) | copy-start | bytes 220
  21.7 1.4 %copy-start.2 = (bf16[128,512]{1,0:T(8,128)(2,1)S(1)}, bf16[128,512]{1,0:T(8,128)(2,1)}, u32[]{:S(2)}) copy-start(bf16[128,512]{1,0:T(8,128)(2,1)} %copy-done.1) | copy-start | bytes 393220
  23.2 0.7 %copy-start.19 = (f32[16]{0:T(128)S(1)}, f32[16]{0:T(128)}, u32[]{:S(2)}) copy-start(f32[16]{0:T(128)} %copy-done.18) | copy-start | bytes 196
  23.2 0.7 %copy-start.21 = (f32[16]{0:T(128)S(1)}, f32[16]{0:T(128)}, u32[]{:S(2)}) copy-start(f32[16]{0:T(128)} %copy-done.20) | copy-start | bytes 196
  24.7 0.6 %copy-start.17 = (pred[72]{0:T(512)(128)(4,1)S(1)}, pred[72]{0:T(512)(128)(4,1)}, u32[]{:S(2)}) copy-start(pred[72]{0:T(512)(128)(4,1)} %iota_compare_fusion.3) | copy-start | bytes 220
  25.3 2.6 %copy-start.12 = (f32[16,128]{1,0:T(8,128)S(1)}, f32[16,128]{1,0:T(8,128)}, u32[]{:S(2)}) copy-start(f32[16,128]{1,0:T(8,128)} %copy.86) | copy-start | bytes 24580
  25.3 2.6 %copy-start.15 = (f32[16,128]{1,0:T(8,128)S(1)}, f32[16,128]{1,0:T(8,128)}, u32[]{:S(2)}) copy-start(f32[16,128]{1,0:T(8,128)} %get-tuple-element.60) | copy-start | bytes 24580
  25.5 2.4 %copy-start.24 = (f32[16]{0:T(128)S(1)}, f32[16]{0:T(128)}, u32[]{:S(2)}) copy-start(f32[16]{0:T(128)} %param.14) | copy-start | bytes 196
  25.5 9.6 %collective-permute-start.3 = (bf16[2,8,72,128]{3,1,2,0:T(8,128)(2,1)S(1)}, bf16[2,8,72,128]{3,1,2,0:T(8,128)(2,1)S(1)}, u32[]{:S(2)}, u32[]{:S(2)}) collective-permute-start(bf16[2,8,72,128]{3,1,2,0:T(8,128)(2,1)S(1)} %fusion.38), channel_id=1, source_target_pairs={{0,8},{4,12},{8,0},{12,4},{16,24},{20,28},{24,16},{28,20},{1,9},{5... | collective-permute-start | bytes 884744 | tf_op jit(solution)/shard_map/ppermute | solution.py:109
  27.9 0.9 %copy-start.4 = (bf16[128,512]{1,0:T(8,128)(2,1)S(1)}, bf16[128,512]{1,0:T(8,128)(2,1)}, u32[]{:S(2)}) copy-start(bf16[128,512]{1,0:T(8,128)(2,1)} %copy-done.3) | copy-start | bytes 393220
  35.3 0.6 %copy-start.10 = (pred[72]{0:T(512)(128)(4,1)S(1)}, pred[72]{0:T(512)(128)(4,1)}, u32[]{:S(2)}) copy-start(pred[72]{0:T(512)(128)(4,1)} %copy-done.9) | copy-start | bytes 220
  35.3 0.7 %copy-start.22 = (f32[72]{0:T(128)S(1)}, f32[72]{0:T(128)}, u32[]{:S(2)}) copy-start(f32[72]{0:T(128)} %concatenate.84) | copy-start | bytes 868
  37.7 5.3 %collective-permute-start.4 = (bf16[1,8,72,128]{3,2,1,0:T(8,128)(2,1)S(1)}, bf16[1,8,72,128]{3,2,1,0:T(8,128)(2,1)S(1)}, u32[]{:S(2)}, u32[]{:S(2)}) collective-permute-start(bf16[1,8,72,128]{3,2,1,0:T(8,128)(2,1)S(1)} %fusion.65), channel_id=1, source_target_pairs={{0,16},{4,20},{8,24},{12,28},{16,0},{20,4},{24,8},{28,12},{1,17},{... | collective-permute-start | bytes 442376 | tf_op jit(solution)/shard_map/ppermute | solution.py:109
  43.2 1.0 %copy-start.11 = (f32[16,128]{1,0:T(8,128)S(1)}, f32[16,128]{1,0:T(8,128)}, u32[]{:S(2)}) copy-start(f32[16,128]{1,0:T(8,128)} %copy.82) | copy-start | bytes 24580
  43.2 1.0 %copy-start.14 = (f32[16,128]{1,0:T(8,128)S(1)}, f32[16,128]{1,0:T(8,128)}, u32[]{:S(2)}) copy-start(f32[16,128]{1,0:T(8,128)} %get-tuple-element.59) | copy-start | bytes 24580
  44.2 1.5 %collective-permute-start.5 = (f32[8,64,128]{2,1,0:T(8,128)S(1)}, f32[8,64,128]{2,1,0:T(8,128)S(1)}, u32[]{:S(2)}, u32[]{:S(2)}) collective-permute-start(f32[8,64,128]{2,1,0:T(8,128)S(1)} %get-tuple-element.23), channel_id=1, source_target_pairs={{0,4},{4,0},{8,12},{12,8},{16,20},{20,16},{24,28},{28,24},{1,5},{5... | collective-permute-start | bytes 786440 | tf_op jit(solution)/shard_map/ppermute | solution.py:186
  44.8 2.1 %collective-permute-start.6 = (f32[8,64,128]{2,1,0:T(8,128)}, f32[8,64,128]{2,1,0:T(8,128)}, u32[]{:S(2)}, u32[]{:S(2)}) collective-permute-start(f32[8,64,128]{2,1,0:T(8,128)} %get-tuple-element.44), channel_id=1, source_target_pairs={{0,4},{4,0},{8,12},{12,8},{16,20},{20,16},{24,28},{28,24},{1,5},{5... | collective-permute-start | bytes 786440 | tf_op jit(solution)/shard_map/ppermute | solution.py:186
  45.3 0.7 %copy-start.6 = (f32[128,16]{0,1:T(8,128)S(1)}, f32[128,16]{0,1:T(8,128)}, u32[]{:S(2)}) copy-start(f32[128,16]{0,1:T(8,128)} %copy.88) | copy-start | bytes 24580
  48.5 3.9 %copy-start.16 = (f32[1024]{0:T(1024)S(1)}, f32[1024]{0:T(1024)}, u32[]{:S(2)}) copy-start(f32[1024]{0:T(1024)} %param.17) | copy-start | bytes 12292
  48.7 3.6 %collective-permute-start.7 = (f32[256]{0:T(256)S(1)}, f32[256]{0:T(256)S(1)}, u32[]{:S(2)}, u32[]{:S(2)}) collective-permute-start(f32[256]{0:T(256)S(1)} %multiply_reduce_fusion), channel_id=1, source_target_pairs={{0,1},{1,0},{2,3},{3,2},{4,5},{5,4},{6,7},{7,6},{8,9},{9,8},{10,11... | collective-permute-start | bytes 3080 | tf_op jit(solution)/shard_map/ppermute | solution.py:30

commit v11 on v9

--- a/solution.py
+++ b/solution.py
@@ -182,7 +182,7 @@
     after_low = col(low_fe) * prefix + low_f
     before_high = col(high_ge) * wrapped + high_g
     own = (jnp.where(upper, after_low, prefix), jnp.where(upper, wrapped, before_high))
-    other = (jnp.where(upper, prefix, after_low), jnp.where(upper, before_high, wrapped))
+    other = jnp.stack([jnp.where(upper, prefix, after_low), jnp.where(upper, before_high, wrapped)])
     got_1, got_2 = lax.ppermute(other, "seq", pairs)
 
     def whole(own_half, got_half):

time: 46 us -> 46.1 us (level)
  waiting for transfers between devices: 13.1 us -> 14.4 us
  local copies, waits for them, and re-layouts: 10.2 us -> 9.7 us
  starting transfers between devices: 12.6 us -> 12.1 us
    ppermute x2 -> x1, waiting for transfers between devices: 0.29 us -> 1.06 us  [block_states(): got_1, got_2 = lax.ppermute(other, 'seq', pairs)]
    exp x4, local copies, waits for them, and re-layouts: 0.79 us -> 0.17 us  [finish_block(): total_out = partial_out + jnp.exp(log_cum)[:, :, None] * inter_out]
    ppermute x2 -> x1, starting transfers between devices: 0.63 us -> 0.07 us  [block_states(): got_1, got_2 = lax.ppermute(other, 'seq', pairs)]
    ppermute x1, waiting for transfers between devices: 0.01 us -> 0.56 us  [block_states(): got = lax.ppermute(sent, 'seq', pairs)]
    unnamed x20 -> x18, local copies, waits for them, and re-layouts: 3.67 us -> 4.03 us
  transfers between devices with their start and end apart: 8 -> 7, of which waited for: 4 -> 5; matrix products, arithmetic and copies ran while one was open for 13% -> 10% of each run, Pallas kernels for 0% -> 0%
where the time goes in v11:
time: 46.1 us; the launch traced here: 45.4 us
  waiting for transfers between devices  14.4 us (31%)
  starting transfers between devices  12.1 us (26%)
  local copies, waits for them, and re-layouts  9.7 us (21%)
  other arithmetic  6.01 us (13%)
  matrix products  2.63 us (6%)
  between operations  0.59 us (1%)
    ppermute x2, waiting for transfers between devices, butterfly_states(): got, got_e = from_link(lax.ppermute(msg, 'seq', pairs), rows)  10.8 us
    unnamed x18, local copies, waits for them, and re-layouts  4.03 us
    ppermute x2, starting transfers between devices, butterfly_states(): got, got_e = from_link(lax.ppermute(msg, 'seq', pairs), rows)  3.4 us
    ppermute x1, starting transfers between devices, extended_2(): low = lax.ppermute(tail, axis, forward)  3.03 us
    ppermute x1, starting transfers between devices, block_states(): got = lax.ppermute(sent, 'seq', pairs)  2.62 us
    ppermute x1, waiting for transfers between devices, partner(): lax.ppermute(array, axis, [(i, i ^ 1 << stride) for i in range(lax.axis_s...  1.99 us
    ppermute x1, starting transfers between devices, partner(): lax.ppermute(array, axis, [(i, i ^ 1 << stride) for i in range(lax.axis_s...  1.64 us
    slice x2, local copies, waits for them, and re-layouts, edges(): rows[tokens - rim_rows:]  1.53 us
  transfers between devices with their start and end apart: 7, of which 5 were waited for; matrix products, arithmetic and copies ran while one was open for 10% of the time, Pallas kernels for 0%

profile of v11, /device:TPU:0, one launch (start us, length us, event | category | flops | bytes accessed | tf_op | source)
XLA Modules:
  0.0 45.4 jit_solution(5958760745226543926)
XLA Ops:
  0.0 0.8 %fusion.97 = (bf16[3,1024]{1,0:T(4,128)(2,1)S(1)}, bf16[3,1024]{1,0:T(4,128)(2,1)S(1)}) fusion(bf16[256,1024]{1,0:T(8,128)(2,1)} %param.9), kind=kLoop, calls=%fused_computation.215 | loop fusion | bytes 24576 | tf_op jit(solution)/shard_map/slice | solution.py:222
  0.8 0.7 %fusion.99 = (bf16[3,512]{1,0:T(4,128)(2,1)S(1)}, bf16[3,512]{1,0:T(4,128)(2,1)S(1)}) fusion(bf16[256,512]{1,0:T(8,128)(2,1)} %param.11), kind=kLoop, calls=%fused_computation.217 | loop fusion | bytes 12288 | tf_op jit(solution)/shard_map/slice | solution.py:222
  1.6 1.3 %collective-permute-start.1 = (bf16[3,1536]{1,0:T(4,128)(2,1)S(1)}, bf16[3,1536]{1,0:T(4,128)(2,1)S(1)}, u32[]{:S(2)}, u32[]{:S(2)}) collective-permute-start(bf16[3,1536]{1,0:T(4,128)(2,1)S(1)} %get-tuple-element.8), channel_id=1, source_target_pairs={{4,0},{8,4},{12,8},{16,12},{20,16},{24,20},{28,24},{5,1},{9,5},{13... | collective-permute-start | bytes 27656 | tf_op jit(solution)/shard_map/ppermute | solution.py:24
  2.9 3.0 %collective-permute-start = (bf16[3,1536]{1,0:T(4,128)(2,1)S(1)}, bf16[3,1536]{1,0:T(4,128)(2,1)S(1)}, u32[]{:S(2)}, u32[]{:S(2)}) collective-permute-start(bf16[3,1536]{1,0:T(4,128)(2,1)S(1)} %get-tuple-element.7), channel_id=1, source_target_pairs={{0,4},{4,8},{8,12},{12,16},{16,20},{20,24},{24,28},{1,5},{5,9},{9,... | collective-permute-start | bytes 27656 | tf_op jit(solution)/shard_map/ppermute | solution.py:23
  5.9 1.0 %fusion.98 = (bf16[128,512]{1,0:T(8,128)(2,1)S(1)}, bf16[128,512]{1,0:T(8,128)(2,1)S(1)}) fusion(bf16[256,512]{1,0:T(8,128)(2,1)} %param.11), kind=kLoop, calls=%fused_computation.216 | loop fusion | bytes 524288 | tf_op jit(solution)/shard_map/slice | solution.py:271
  7.0 0.7 %copy-done.3 = f32[256,16]{0,1:T(8,128)S(1)} copy-done((f32[256,16]{0,1:T(8,128)S(1)}, f32[256,16]{0,1:T(8,128)}, u32[]{:S(2)}) %copy-start.3) | copy-done | bytes 16408
  7.7 0.6 %copy-done.7 = f32[16]{0:T(128)S(1)} copy-done((f32[16]{0:T(128)S(1)}, f32[16]{0:T(128)}, u32[]{:S(2)}) %copy-start.7) | copy-done | bytes 88
  8.5 0.2 reduce_window_sum.18
  8.8 0.2 reduce_window_sum.17
  9.1 0.7 %copy-done.5 = f32[4,512]{1,0:T(4,128)S(1)} copy-done((f32[4,512]{1,0:T(4,128)S(1)}, f32[4,512]{1,0:T(4,128)}, u32[]{:S(2)}) %copy-start.5) | copy-done | bytes 8216
  10.2 0.5 %copy-done.2 = bf16[3,1536]{1,0:T(4,128)(2,1)} copy-done((bf16[3,1536]{1,0:T(4,128)(2,1)}, bf16[3,1536]{1,0:T(4,128)(2,1)S(1)}, u32[]{:S(2)}) %copy-start.2) | copy-done | bytes 9240
  10.8 0.6 %multiply_convert_fusion.6 = (bf16[128,1024]{1,0:T(8,128)(2,1)S(1)}, bf16[128,1024]{1,0:T(8,128)(2,1)S(1)}) fusion(f32[131,1024]{1,0:T(8,128)S(1)} %maximum_convert_fusion, f32[1024]{0:T(1024)S(1)} %bitcast.153, f32[1024]{0:T(1024)S(1)} %bitcast.154, f32[1024]{0:T(1024)S(1)} %bitcast.152, f32[1024]{0:T(1024)S(1)} %bitcast.151, ...), kind=kLoop, calls=%fused_computation.65 | loop fusion | flops 3145728 | bytes 4734976 | tf_op jit(solution)/shard_map/convert_element_type | solution.py:239
  11.4 0.2 copy.92
  11.6 0.2 copy.86
  11.8 0.5 %slice-done = bf16[3,512]{1,0:T(4,128)(2,1)S(1)} async-done(((bf16[3,1536]{1,0:T(4,128)(2,1)}), bf16[3,512]{1,0:T(4,128)(2,1)S(1)}, s32[]{:S(2)}) %slice-start) | async-done | bytes 3096 | tf_op jit(solution)/shard_map/slice | solution.py:243
  12.4 0.3 multiply_convert_fusion.8
  12.7 0.2 fusion.45
  13.0 0.2 fusion.47
  13.3 2.6 %collective-permute-start.2 = (f32[1032,128]{1,0:T(8,128)S(1)}, f32[1032,128]{1,0:T(8,128)S(1)}, u32[]{:S(2)}, u32[]{:S(2)}) collective-permute-start(f32[1032,128]{1,0:T(8,128)S(1)} %pad_maximum_fusion.1), channel_id=1, source_target_pairs={{0,4},{4,0},{8,12},{12,8},{16,20},{20,16},{24,28},{28,24},{1,5},{5... | collective-permute-start | bytes 1585160 | tf_op jit(solution)/shard_map/ppermute | solution.py:168
  16.0 0.6 %slice.315 = pred[1]{0:T(512)(128)(4,1)} slice(pred[72]{0:T(512)(128)(4,1)S(1)} %iota_compare_fusion.4), slice={[64:65]} | slice | bytes 2 | tf_op jit(solution)/shard_map/slice | solution.py:87
  16.9 0.6 %collective-permute-done.2 = f32[1032,128]{1,0:T(8,128)S(1)} collective-permute-done((f32[1032,128]{1,0:T(8,128)S(1)}, f32[1032,128]{1,0:T(8,128)S(1)}, u32[]{:S(2)}, u32[]{:S(2)}) %collective-permute-start.2) | collective-permute-done | bytes 528416 | tf_op jit(solution)/shard_map/ppermute | solution.py:168
  17.6 0.3 fusion.55
  18.0 0.3 multiply_add_fusion
  18.4 0.1 fusion.39
  18.6 2.4 %collective-permute-start.3 = (bf16[2,8,72,128]{3,1,2,0:T(8,128)(2,1)S(1)}, bf16[2,8,72,128]{3,1,2,0:T(8,128)(2,1)S(1)}, u32[]{:S(2)}, u32[]{:S(2)}) collective-permute-start(bf16[2,8,72,128]{3,1,2,0:T(8,128)(2,1)S(1)} %fusion.39), channel_id=1, source_target_pairs={{0,8},{4,12},{8,0},{12,4},{16,24},{20,28},{24,16},{28,20},{1,9},{5... | collective-permute-start | bytes 884744 | tf_op jit(solution)/shard_map/ppermute | solution.py:109
  21.0 0.1 fusion.74
  21.1 0.7 %copy-done.8 = f32[16]{0:T(128)S(1)} copy-done((f32[16]{0:T(128)S(1)}, f32[16]{0:T(128)}, u32[]{:S(2)}) %copy-start.8) | copy-done | bytes 88
  21.8 0.6 %fusion.2 = f32[128,16,64]{0,2,1:T(8,128)S(1)} fusion(bf16[128,16,64]{0,2,1:T(8,128)(2,1)S(1)} %bitcast.143, f32[16,128]{1,0:T(8,128)S(1)} %get-tuple-element.55, f32[16,128]{1,0:T(8,128)S(1)} %copy.88, f32[128,128]{1,0:T(8,128)S(1)} %fusion.74, pred[128,128]{1,0:T(8,128)(4,1)S(1)} %iota_compare_fusion, f32[16]{0:T(128)S(1)} %copy-done.8), kind=kOutput, calls=%fused_computation.8 | convolution fusion | flops 35520512 | bytes 884800 | tf_op jit(solution)/shard_map/hts,shp->thp/dot_general | solution.py:252
  22.4 6.2 %collective-permute-done.3 = bf16[2,8,72,128]{3,1,2,0:T(8,128)(2,1)S(1)} collective-permute-done((bf16[2,8,72,128]{3,1,2,0:T(8,128)(2,1)S(1)}, bf16[2,8,72,128]{3,1,2,0:T(8,128)(2,1)S(1)}, u32[]{:S(2)}, u32[]{:S(2)}) %collective-permute-start.3) | collective-permute-done | bytes 294944 | tf_op jit(solution)/shard_map/ppermute | solution.py:109
  28.7 0.2 fusion.42
  28.9 0.2 copy_select_fusion
  29.1 0.7 %fusion.79 = (f32[8,128]{1,0:T(8,128)S(1)}, f32[8,1,128]{2,0,1:T(8,128)S(1)}) fusion(f32[8,1,128]{2,0,1:T(8,128)S(1)} %bitcast.147, pred[]{:T(512)S(6)} %eq.31, f32[8,128]{1,0:T(8,128)S(1)} %get-tuple-element.66, f32[8,128]{1,0:T(8,128)S(1)} %get-tuple-element.69, f32[8,72,128]{2,0,1:T(8,128)S(1)} %slice_bitcast_fusion, f32[8]{0:T(128)S(1)} %get-tuple-element.25, ...), kind=kLoop, calls=%fused_computation.161 | loop fusion | flops 9216 | bytes 319523 | tf_op jit(solution)/shard_map/jit(_where)/broadcast_in_dim | solution.py:98
  30.0 0.3 fusion.62
  30.3 1.0 %collective-permute-start.4 = (bf16[1,8,72,128]{3,1,2,0:T(8,128)(2,1)S(1)}, bf16[1,8,72,128]{3,1,2,0:T(8,128)(2,1)S(1)}, u32[]{:S(2)}, u32[]{:S(2)}) collective-permute-start(bf16[1,8,72,128]{3,1,2,0:T(8,128)(2,1)S(1)} %fusion.62), channel_id=1, source_target_pairs={{0,16},{4,20},{8,24},{12,28},{16,0},{20,4},{24,8},{28,12},{1,17},{... | collective-permute-start | bytes 442376 | tf_op jit(solution)/shard_map/ppermute | solution.py:109
  31.3 4.6 %collective-permute-done.4 = bf16[1,8,72,128]{3,1,2,0:T(8,128)(2,1)S(1)} collective-permute-done((bf16[1,8,72,128]{3,1,2,0:T(8,128)(2,1)S(1)}, bf16[1,8,72,128]{3,1,2,0:T(8,128)(2,1)S(1)}, u32[]{:S(2)}, u32[]{:S(2)}) %collective-permute-start.4) | collective-permute-done | bytes 147488 | tf_op jit(solution)/shard_map/ppermute | solution.py:109
  36.0 0.3 fusion.63
  36.4 0.1 fusion.69
  36.5 0.6 %fusion.3 = f32[128,16,64]{0,2,1:T(8,128)S(1)} fusion(bf16[128,16,64]{0,2,1:T(8,128)(2,1)S(1)} %bitcast.141, f32[16,128]{1,0:T(8,128)S(1)} %get-tuple-element.58, f32[16,128]{1,0:T(8,128)S(1)} %copy.114, f32[128,128]{1,0:T(8,128)S(1)} %fusion.69, pred[128,128]{1,0:T(8,128)(4,1)S(1)} %iota_compare_fusion, f32[16]{0:T(128)S(1)} %copy-done.8), kind=kOutput, calls=%fused_computation.9 | convolution fusion | flops 35520512 | bytes 884800 | tf_op jit(solution)/shard_map/hts,shp->thp/dot_general | solution.py:252
  37.2 1.1 %collective-permute-done.5 = f32[2,8,64,128]{3,2,1,0:T(8,128)S(1)} collective-permute-done((f32[2,8,64,128]{3,2,1,0:T(8,128)S(1)}, f32[2,8,64,128]{3,2,1,0:T(8,128)S(1)}, u32[]{:S(2)}, u32[]{:S(2)}) %collective-permute-start.5) | collective-permute-done | bytes 524320 | tf_op jit(solution)/shard_map/ppermute | solution.py:186
  38.3 0.4 fusion.1
  38.7 0.2 copy.118
  38.9 0.4 fusion
  39.3 0.2 copy.119
  39.5 0.8 %copy-done.1 = bf16[256,1024]{1,0:T(8,128)(2,1)S(1)} copy-done((bf16[256,1024]{1,0:T(8,128)(2,1)S(1)}, bf16[256,1024]{1,0:T(8,128)(2,1)}, u32[]{:S(2)}) %copy-start.1) | copy-done | bytes 524312
  40.4 0.4 multiply_reduce_fusion
  40.8 1.6 %collective-permute-start.6 = (f32[256]{0:T(256)S(1)}, f32[256]{0:T(256)S(1)}, u32[]{:S(2)}, u32[]{:S(2)}) collective-permute-start(f32[256]{0:T(256)S(1)} %get-tuple-element.9), channel_id=1, source_target_pairs={{0,1},{1,0},{2,3},{3,2},{4,5},{5,4},{6,7},{7,6},{8,9},{9,8},{10,11... | collective-permute-start | bytes 3080 | tf_op jit(solution)/shard_map/ppermute | solution.py:30
  42.4 2.0 %collective-permute-done.6 = f32[256]{0:T(256)S(1)} collective-permute-done((f32[256]{0:T(256)S(1)}, f32[256]{0:T(256)S(1)}, u32[]{:S(2)}, u32[]{:S(2)}) %collective-permute-start.6) | collective-permute-done | bytes 1056 | tf_op jit(solution)/shard_map/ppermute | solution.py:30
  44.4 1.0 %multiply_convert_fusion = bf16[256,1024]{1,0:T(8,128)(2,1)} fusion(f32[256,1024]{1,0:T(8,128)S(1)} %get-tuple-element.10, f32[1024]{0:T(1024)S(1)} %copy-done.6, f32[256]{0:T(256)S(1)} %add_rsqrt_fusion), kind=kLoop, calls=%fused_computation.14 | loop fusion | flops 786432 | bytes 1577984 | tf_op jit(solution)/shard_map/convert_element_type | solution.py:291
  (80 shorter events, 2.4 us)
Async XLA Ops:
  0.0 6.9 %copy-start = (bf16[256,1024]{1,0:T(8,128)(2,1)S(1)}, bf16[256,1024]{1,0:T(8,128)(2,1)}, u32[]{:S(2)}) copy-start(bf16[256,1024]{1,0:T(8,128)(2,1)} %param.9) | copy-start | bytes 1572868
  1.6 8.5 %collective-permute-start.1 = (bf16[3,1536]{1,0:T(4,128)(2,1)S(1)}, bf16[3,1536]{1,0:T(4,128)(2,1)S(1)}, u32[]{:S(2)}, u32[]{:S(2)}) collective-permute-start(bf16[3,1536]{1,0:T(4,128)(2,1)S(1)} %get-tuple-element.8), channel_id=1, source_target_pairs={{4,0},{8,4},{12,8},{16,12},{20,16},{24,20},{28,24},{5,1},{9,5},{13... | collective-permute-start | bytes 27656 | tf_op jit(solution)/shard_map/ppermute | solution.py:24
  2.9 7.8 %collective-permute-start = (bf16[3,1536]{1,0:T(4,128)(2,1)S(1)}, bf16[3,1536]{1,0:T(4,128)(2,1)S(1)}, u32[]{:S(2)}, u32[]{:S(2)}) collective-permute-start(bf16[3,1536]{1,0:T(4,128)(2,1)S(1)} %get-tuple-element.7), channel_id=1, source_target_pairs={{0,4},{4,8},{8,12},{12,16},{16,20},{20,24},{24,28},{1,5},{5,9},{9,... | collective-permute-start | bytes 27656 | tf_op jit(solution)/shard_map/ppermute | solution.py:23
  6.9 0.7 %copy-start.3 = (f32[256,16]{0,1:T(8,128)S(1)}, f32[256,16]{0,1:T(8,128)}, u32[]{:S(2)}) copy-start(f32[256,16]{0,1:T(8,128)} %param.12) | copy-start | bytes 49156
  7.6 0.7 %copy-start.7 = (f32[16]{0:T(128)S(1)}, f32[16]{0:T(128)}, u32[]{:S(2)}) copy-start(f32[16]{0:T(128)} %param.13) | copy-start | bytes 196
  9.0 0.7 %copy-start.5 = (f32[4,512]{1,0:T(4,128)S(1)}, f32[4,512]{1,0:T(4,128)}, u32[]{:S(2)}) copy-start(f32[4,512]{1,0:T(4,128)} %param.16) | copy-start | bytes 24580
  9.0 0.8 %copy-start.4 = (f32[4,1024]{1,0:T(4,128)S(1)}, f32[4,1024]{1,0:T(4,128)}, u32[]{:S(2)}) copy-start(f32[4,1024]{1,0:T(4,128)} %param.15) | copy-start | bytes 49156
  10.1 0.6 %copy-start.2 = (bf16[3,1536]{1,0:T(4,128)(2,1)}, bf16[3,1536]{1,0:T(4,128)(2,1)S(1)}, u32[]{:S(2)}) copy-start(bf16[3,1536]{1,0:T(4,128)(2,1)S(1)} %broadcast_select_fusion) | copy-start | bytes 27652
  11.6 0.7 %slice-start = ((bf16[3,1536]{1,0:T(4,128)(2,1)}), bf16[3,512]{1,0:T(4,128)(2,1)S(1)}, s32[]{:S(2)}) async-start(bf16[3,1536]{1,0:T(4,128)(2,1)} %copy-done.2), calls=%async_computation | async-start | bytes 8192 | tf_op jit(solution)/shard_map/slice | solution.py:243
  13.3 4.2 %collective-permute-start.2 = (f32[1032,128]{1,0:T(8,128)S(1)}, f32[1032,128]{1,0:T(8,128)S(1)}, u32[]{:S(2)}, u32[]{:S(2)}) collective-permute-start(f32[1032,128]{1,0:T(8,128)S(1)} %pad_maximum_fusion.1), channel_id=1, source_target_pairs={{0,4},{4,0},{8,12},{12,8},{16,20},{20,16},{24,28},{28,24},{1,5},{5... | collective-permute-start | bytes 1585160 | tf_op jit(solution)/shard_map/ppermute | solution.py:168
  18.6 10.0 %collective-permute-start.3 = (bf16[2,8,72,128]{3,1,2,0:T(8,128)(2,1)S(1)}, bf16[2,8,72,128]{3,1,2,0:T(8,128)(2,1)S(1)}, u32[]{:S(2)}, u32[]{:S(2)}) collective-permute-start(bf16[2,8,72,128]{3,1,2,0:T(8,128)(2,1)S(1)} %fusion.39), channel_id=1, source_target_pairs={{0,8},{4,12},{8,0},{12,4},{16,24},{20,28},{24,16},{28,20},{1,9},{5... | collective-permute-start | bytes 884744 | tf_op jit(solution)/shard_map/ppermute | solution.py:109
  21.1 0.7 %copy-start.8 = (f32[16]{0:T(128)S(1)}, f32[16]{0:T(128)}, u32[]{:S(2)}) copy-start(f32[16]{0:T(128)} %param.14) | copy-start | bytes 196
  30.3 5.6 %collective-permute-start.4 = (bf16[1,8,72,128]{3,1,2,0:T(8,128)(2,1)S(1)}, bf16[1,8,72,128]{3,1,2,0:T(8,128)(2,1)S(1)}, u32[]{:S(2)}, u32[]{:S(2)}) collective-permute-start(bf16[1,8,72,128]{3,1,2,0:T(8,128)(2,1)S(1)} %fusion.62), channel_id=1, source_target_pairs={{0,16},{4,20},{8,24},{12,28},{16,0},{20,4},{24,8},{28,12},{1,17},{... | collective-permute-start | bytes 442376 | tf_op jit(solution)/shard_map/ppermute | solution.py:109
  36.3 2.0 %collective-permute-start.5 = (f32[2,8,64,128]{3,2,1,0:T(8,128)S(1)}, f32[2,8,64,128]{3,2,1,0:T(8,128)S(1)}, u32[]{:S(2)}, u32[]{:S(2)}) collective-permute-start(f32[2,8,64,128]{3,2,1,0:T(8,128)S(1)} %pad_maximum_fusion.2), channel_id=1, source_target_pairs={{0,4},{4,0},{8,12},{12,8},{16,20},{20,16},{24,28},{28,24},{1,5},{5... | collective-permute-start | bytes 1572872 | tf_op jit(solution)/shard_map/ppermute | solution.py:186
  39.3 1.0 %copy-start.1 = (bf16[256,1024]{1,0:T(8,128)(2,1)S(1)}, bf16[256,1024]{1,0:T(8,128)(2,1)}, u32[]{:S(2)}) copy-start(bf16[256,1024]{1,0:T(8,128)(2,1)} %param.10) | copy-start | bytes 1572868
  40.8 3.7 %copy-start.6 = (f32[1024]{0:T(1024)S(1)}, f32[1024]{0:T(1024)}, u32[]{:S(2)}) copy-start(f32[1024]{0:T(1024)} %param.17) | copy-start | bytes 12292
  40.8 3.6 %collective-permute-start.6 = (f32[256]{0:T(256)S(1)}, f32[256]{0:T(256)S(1)}, u32[]{:S(2)}, u32[]{:S(2)}) collective-permute-start(f32[256]{0:T(256)S(1)} %get-tuple-element.9), channel_id=1, source_target_pairs={{0,1},{1,0},{2,3},{3,2},{4,5},{5,4},{6,7},{7,6},{8,9},{9,8},{10,11... | collective-permute-start | bytes 3080 | tf_op jit(solution)/shard_map/ppermute | solution.py:30

commit v12 on v11

--- a/solution.py
+++ b/solution.py
@@ -12,7 +12,7 @@
 def extended_2(block, sides, width):
     for axis, dim in sides:
         count = lax.axis_size(axis)
-        forward = [(i, i + 1) for i in range(count - 1)]
+        forward = [(i, (i + 1) % count) for i in range(count)]
         backward = [(target, source) for source, target in forward]
         tail, head = lax.optimization_barrier(
             (
@@ -22,6 +22,8 @@
         )
         low = lax.ppermute(tail, axis, forward)
         high = lax.ppermute(head, axis, backward)
+        low = jnp.where(lax.axis_index(axis) == 0, jnp.zeros_like(low), low)
+        high = jnp.where(lax.axis_index(axis) == count - 1, jnp.zeros_like(high), high)
         block = jnp.concatenate([low, block, high], axis=dim)
     return block
 

time: 46.1 us -> 44.2 us (0.959)
  starting transfers between devices: 12.1 us -> 8.55 us
  local copies, waits for them, and re-layouts: 9.7 us -> 11.7 us
  waiting for transfers between devices: 14.4 us -> 13.8 us
    ppermute x1, starting transfers between devices: 3.03 us -> 0.01 us  [extended_2(): low = lax.ppermute(tail, axis, forward)]
    ppermute x1, starting transfers between devices: 2.62 us -> 0.07 us  [block_states(): got = lax.ppermute(sent, 'seq', pairs)]
    ppermute x1, starting transfers between devices: 1.29 us -> 3.39 us  [extended_2(): high = lax.ppermute(head, axis, backward)]
    ppermute x2, waiting for transfers between devices: 10.8 us -> 9.93 us  [butterfly_states(): got, got_e = from_link(lax.ppermute(msg, 'seq', pairs), rows)]
    slice x2 -> x4, local copies, waits for them, and re-layouts: 0.01 us -> 0.73 us  [local_block(): inner_out = conv(lead_rows[:, :inner_width], inner_in, conv_inner)]
    unnamed x18 -> x20, local copies, waits for them, and re-layouts: 4.03 us -> 4.7 us
    slice x3 -> x4, local copies, waits for them, and re-layouts: 0.52 us -> 1.15 us  [local_block(): proj_out = conv(lead_rows[:, inner_width:], proj_in, conv_proj)]
where the time goes in v12:
time: 44.2 us; the launch traced here: 43.4 us
  waiting for transfers between devices  13.8 us (31%)
  local copies, waits for them, and re-layouts  11.7 us (26%)
  starting transfers between devices  8.55 us (19%)
  other arithmetic  6.01 us (14%)
  matrix products  2.62 us (6%)
  between operations  0.66 us (1%)
    ppermute x2, waiting for transfers between devices, butterfly_states(): got, got_e = from_link(lax.ppermute(msg, 'seq', pairs), rows)  9.93 us
    unnamed x20, local copies, waits for them, and re-layouts  4.7 us
    ppermute x1, starting transfers between devices, extended_2(): high = lax.ppermute(head, axis, backward)  3.39 us
    ppermute x2, starting transfers between devices, butterfly_states(): got, got_e = from_link(lax.ppermute(msg, 'seq', pairs), rows)  3.37 us
    ppermute x1, waiting for transfers between devices, partner(): lax.ppermute(array, axis, [(i, i ^ 1 << stride) for i in range(lax.axis_s...  1.99 us
    ppermute x1, starting transfers between devices, partner(): lax.ppermute(array, axis, [(i, i ^ 1 << stride) for i in range(lax.axis_s...  1.64 us
    slice x2, local copies, waits for them, and re-layouts, edges(): rows[tokens - rim_rows:]  1.53 us
    slice x4, local copies, waits for them, and re-layouts, local_block(): proj_out = conv(lead_rows[:, inner_width:], proj_in, conv_proj)  1.15 us
  transfers between devices with their start and end apart: 7, of which 5 were waited for; matrix products, arithmetic and copies ran while one was open for 10% of the time, Pallas kernels for 0%

profile of v12, /device:TPU:0, one launch (start us, length us, event | category | flops | bytes accessed | tf_op | source)
XLA Modules:
  0.0 43.4 jit_solution(5315352087537971534)
XLA Ops:
  0.0 0.8 %fusion.97 = (bf16[3,1024]{1,0:T(4,128)(2,1)S(1)}, bf16[3,1024]{1,0:T(4,128)(2,1)S(1)}) fusion(bf16[256,1024]{1,0:T(8,128)(2,1)} %param.9), kind=kLoop, calls=%fused_computation.216 | loop fusion | bytes 24576 | tf_op jit(solution)/shard_map/slice | solution.py:224
  0.8 0.7 %fusion.99 = (bf16[3,512]{1,0:T(4,128)(2,1)S(1)}, bf16[3,512]{1,0:T(4,128)(2,1)S(1)}) fusion(bf16[256,512]{1,0:T(8,128)(2,1)} %param.11), kind=kLoop, calls=%fused_computation.218 | loop fusion | bytes 12288 | tf_op jit(solution)/shard_map/slice | solution.py:224
  1.6 3.4 %collective-permute-start.1 = (bf16[3,1536]{1,0:T(4,128)(2,1)S(1)}, bf16[3,1536]{1,0:T(4,128)(2,1)S(1)}, u32[]{:S(2)}, u32[]{:S(2)}) collective-permute-start(bf16[3,1536]{1,0:T(4,128)(2,1)S(1)} %get-tuple-element.8), channel_id=1, source_target_pairs={{4,0},{8,4},{12,8},{16,12},{20,16},{24,20},{28,24},{0,28},{5,1},{9... | collective-permute-start | bytes 27656 | tf_op jit(solution)/shard_map/ppermute | solution.py:24
  5.0 1.0 %fusion.98 = (bf16[128,512]{1,0:T(8,128)(2,1)S(1)}, bf16[128,512]{1,0:T(8,128)(2,1)S(1)}) fusion(bf16[256,512]{1,0:T(8,128)(2,1)} %param.11), kind=kLoop, calls=%fused_computation.217 | loop fusion | bytes 524288 | tf_op jit(solution)/shard_map/slice | solution.py:273
  6.0 0.7 %copy-done.4 = f32[256,16]{0,1:T(8,128)S(1)} copy-done((f32[256,16]{0,1:T(8,128)S(1)}, f32[256,16]{0,1:T(8,128)}, u32[]{:S(2)}) %copy-start.4) | copy-done | bytes 16408
  6.7 0.6 %copy-done.8 = f32[16]{0:T(128)S(1)} copy-done((f32[16]{0:T(128)S(1)}, f32[16]{0:T(128)}, u32[]{:S(2)}) %copy-start.8) | copy-done | bytes 88
  7.5 0.2 reduce_window_sum.18
  7.9 0.2 reduce_window_sum.17
  8.2 0.7 %copy-done.6 = f32[4,512]{1,0:T(4,128)S(1)} copy-done((f32[4,512]{1,0:T(4,128)S(1)}, f32[4,512]{1,0:T(4,128)}, u32[]{:S(2)}) %copy-start.6) | copy-done | bytes 8216
  9.2 0.6 %copy-done.3 = bf16[3,1536]{1,0:T(4,128)(2,1)} copy-done((bf16[3,1536]{1,0:T(4,128)(2,1)}, bf16[3,1536]{1,0:T(4,128)(2,1)S(1)}, u32[]{:S(2)}) %copy-start.3) | copy-done | bytes 9240
  9.8 0.6 %copy-done.2 = bf16[3,1536]{1,0:T(4,128)(2,1)} copy-done((bf16[3,1536]{1,0:T(4,128)(2,1)}, bf16[3,1536]{1,0:T(4,128)(2,1)S(1)}, u32[]{:S(2)}) %copy-start.2) | copy-done | bytes 9240
  10.5 0.6 %slice-done.1 = bf16[3,1024]{1,0:T(4,128)(2,1)S(1)} async-done(((bf16[3,1536]{1,0:T(4,128)(2,1)}), bf16[3,1024]{1,0:T(4,128)(2,1)S(1)}, s32[]{:S(2)}) %slice-start.1) | async-done | bytes 6168 | tf_op jit(solution)/shard_map/slice | solution.py:244
  11.2 0.6 %multiply_convert_fusion.6 = (bf16[128,1024]{1,0:T(8,128)(2,1)S(1)}, bf16[128,1024]{1,0:T(8,128)(2,1)S(1)}) fusion(f32[131,1024]{1,0:T(8,128)S(1)} %maximum_convert_fusion, f32[1024]{0:T(1024)S(1)} %bitcast.153, f32[1024]{0:T(1024)S(1)} %bitcast.154, f32[1024]{0:T(1024)S(1)} %bitcast.152, f32[1024]{0:T(1024)S(1)} %bitcast.151, ...), kind=kLoop, calls=%fused_computation.65 | loop fusion | flops 3145728 | bytes 4734976 | tf_op jit(solution)/shard_map/convert_element_type | solution.py:241
  11.9 0.2 copy.92
  12.1 0.2 copy.86
  12.2 0.5 %slice-done.2 = bf16[3,512]{1,0:T(4,128)(2,1)S(1)} async-done(((bf16[3,1536]{1,0:T(4,128)(2,1)}), bf16[3,512]{1,0:T(4,128)(2,1)S(1)}, s32[]{:S(2)}) %slice-start.2) | async-done | bytes 3096 | tf_op jit(solution)/shard_map/slice | solution.py:245
  12.8 0.6 %slice-done = bf16[3,512]{1,0:T(4,128)(2,1)S(1)} async-done(((bf16[3,1536]{1,0:T(4,128)(2,1)}), bf16[3,512]{1,0:T(4,128)(2,1)S(1)}, s32[]{:S(2)}) %slice-start) | async-done | bytes 3096 | tf_op jit(solution)/shard_map/slice | solution.py:245
  13.5 0.3 multiply_convert_fusion.8
  13.8 0.2 fusion.45
  14.0 0.2 fusion.47
  14.6 0.6 %slice.315 = pred[1]{0:T(512)(128)(4,1)} slice(pred[72]{0:T(512)(128)(4,1)S(1)} %iota_compare_fusion.4), slice={[64:65]} | slice | bytes 2 | tf_op jit(solution)/shard_map/slice | solution.py:89
  15.5 0.8 %collective-permute-done.2 = f32[1032,128]{1,0:T(8,128)S(1)} collective-permute-done((f32[1032,128]{1,0:T(8,128)S(1)}, f32[1032,128]{1,0:T(8,128)S(1)}, u32[]{:S(2)}, u32[]{:S(2)}) %collective-permute-start.2) | collective-permute-done | bytes 528416 | tf_op jit(solution)/shard_map/ppermute | solution.py:170
  16.5 0.3 fusion.55
  16.9 0.3 multiply_add_fusion
  17.3 0.1 fusion.39
  17.5 1.8 %collective-permute-start.3 = (bf16[2,8,72,128]{3,1,2,0:T(8,128)(2,1)S(1)}, bf16[2,8,72,128]{3,1,2,0:T(8,128)(2,1)S(1)}, u32[]{:S(2)}, u32[]{:S(2)}) collective-permute-start(bf16[2,8,72,128]{3,1,2,0:T(8,128)(2,1)S(1)} %fusion.39), channel_id=1, source_target_pairs={{0,8},{4,12},{8,0},{12,4},{16,24},{20,28},{24,16},{28,20},{1,9},{5... | collective-permute-start | bytes 884744 | tf_op jit(solution)/shard_map/ppermute | solution.py:111
  19.4 0.7 %copy-done.9 = f32[16]{0:T(128)S(1)} copy-done((f32[16]{0:T(128)S(1)}, f32[16]{0:T(128)}, u32[]{:S(2)}) %copy-start.9) | copy-done | bytes 88
  20.1 0.6 %fusion.2 = f32[128,16,64]{0,2,1:T(8,128)S(1)} fusion(bf16[128,16,64]{0,2,1:T(8,128)(2,1)S(1)} %bitcast.143, f32[16,128]{1,0:T(8,128)S(1)} %get-tuple-element.55, f32[16,128]{1,0:T(8,128)S(1)} %copy.88, f32[128,128]{1,0:T(8,128)S(1)} %fusion.74, pred[128,128]{1,0:T(8,128)(4,1)S(1)} %iota_compare_fusion, f32[16]{0:T(128)S(1)} %copy-done.9), kind=kOutput, calls=%fused_computation.8 | convolution fusion | flops 35520512 | bytes 884800 | tf_op jit(solution)/shard_map/hts,shp->thp/dot_general | solution.py:254
  20.6 6.2 %collective-permute-done.3 = bf16[2,8,72,128]{3,1,2,0:T(8,128)(2,1)S(1)} collective-permute-done((bf16[2,8,72,128]{3,1,2,0:T(8,128)(2,1)S(1)}, bf16[2,8,72,128]{3,1,2,0:T(8,128)(2,1)S(1)}, u32[]{:S(2)}, u32[]{:S(2)}) %collective-permute-start.3) | collective-permute-done | bytes 294944 | tf_op jit(solution)/shard_map/ppermute | solution.py:111
  27.0 0.2 fusion.42
  27.2 0.2 copy_select_fusion
  27.4 0.7 %fusion.79 = (f32[8,128]{1,0:T(8,128)S(1)}, f32[8,1,128]{2,0,1:T(8,128)S(1)}) fusion(f32[8,1,128]{2,0,1:T(8,128)S(1)} %bitcast.147, pred[]{:T(512)S(6)} %eq.36, f32[8,128]{1,0:T(8,128)S(1)} %get-tuple-element.66, f32[8,128]{1,0:T(8,128)S(1)} %get-tuple-element.69, f32[8,72,128]{2,0,1:T(8,128)S(1)} %slice_bitcast_fusion, f32[8]{0:T(128)S(1)} %get-tuple-element.25, ...), kind=kLoop, calls=%fused_computation.162 | loop fusion | flops 9216 | bytes 319523 | tf_op jit(solution)/shard_map/jit(_where)/broadcast_in_dim | solution.py:100
  28.2 0.3 fusion.62
  28.5 1.6 %collective-permute-start.4 = (bf16[1,8,72,128]{3,1,2,0:T(8,128)(2,1)S(1)}, bf16[1,8,72,128]{3,1,2,0:T(8,128)(2,1)S(1)}, u32[]{:S(2)}, u32[]{:S(2)}) collective-permute-start(bf16[1,8,72,128]{3,1,2,0:T(8,128)(2,1)S(1)} %fusion.62), channel_id=1, source_target_pairs={{0,16},{4,20},{8,24},{12,28},{16,0},{20,4},{24,8},{28,12},{1,17},{... | collective-permute-start | bytes 442376 | tf_op jit(solution)/shard_map/ppermute | solution.py:111
  30.1 3.8 %collective-permute-done.4 = bf16[1,8,72,128]{3,1,2,0:T(8,128)(2,1)S(1)} collective-permute-done((bf16[1,8,72,128]{3,1,2,0:T(8,128)(2,1)S(1)}, bf16[1,8,72,128]{3,1,2,0:T(8,128)(2,1)S(1)}, u32[]{:S(2)}, u32[]{:S(2)}) %collective-permute-start.4) | collective-permute-done | bytes 147488 | tf_op jit(solution)/shard_map/ppermute | solution.py:111
  34.0 0.3 fusion.63
  34.4 0.1 fusion.69
  34.5 0.6 %fusion.3 = f32[128,16,64]{0,2,1:T(8,128)S(1)} fusion(bf16[128,16,64]{0,2,1:T(8,128)(2,1)S(1)} %bitcast.141, f32[16,128]{1,0:T(8,128)S(1)} %get-tuple-element.58, f32[16,128]{1,0:T(8,128)S(1)} %copy.114, f32[128,128]{1,0:T(8,128)S(1)} %fusion.69, pred[128,128]{1,0:T(8,128)(4,1)S(1)} %iota_compare_fusion, f32[16]{0:T(128)S(1)} %copy-done.9), kind=kOutput, calls=%fused_computation.9 | convolution fusion | flops 35520512 | bytes 884800 | tf_op jit(solution)/shard_map/hts,shp->thp/dot_general | solution.py:254
  35.2 1.1 %collective-permute-done.5 = f32[2,8,64,128]{3,2,1,0:T(8,128)S(1)} collective-permute-done((f32[2,8,64,128]{3,2,1,0:T(8,128)S(1)}, f32[2,8,64,128]{3,2,1,0:T(8,128)S(1)}, u32[]{:S(2)}, u32[]{:S(2)}) %collective-permute-start.5) | collective-permute-done | bytes 524320 | tf_op jit(solution)/shard_map/ppermute | solution.py:188
  36.3 0.4 fusion.1
  36.7 0.2 copy.118
  36.9 0.4 fusion
  37.4 0.2 copy.119
  37.6 0.8 %copy-done.1 = bf16[256,1024]{1,0:T(8,128)(2,1)S(1)} copy-done((bf16[256,1024]{1,0:T(8,128)(2,1)S(1)}, bf16[256,1024]{1,0:T(8,128)(2,1)}, u32[]{:S(2)}) %copy-start.1) | copy-done | bytes 524312
  38.4 0.4 multiply_reduce_fusion
  38.8 1.6 %collective-permute-start.6 = (f32[256]{0:T(256)S(1)}, f32[256]{0:T(256)S(1)}, u32[]{:S(2)}, u32[]{:S(2)}) collective-permute-start(f32[256]{0:T(256)S(1)} %get-tuple-element.9), channel_id=1, source_target_pairs={{0,1},{1,0},{2,3},{3,2},{4,5},{5,4},{6,7},{7,6},{8,9},{9,8},{10,11... | collective-permute-start | bytes 3080 | tf_op jit(solution)/shard_map/ppermute | solution.py:32
  40.4 2.0 %collective-permute-done.6 = f32[256]{0:T(256)S(1)} collective-permute-done((f32[256]{0:T(256)S(1)}, f32[256]{0:T(256)S(1)}, u32[]{:S(2)}, u32[]{:S(2)}) %collective-permute-start.6) | collective-permute-done | bytes 1056 | tf_op jit(solution)/shard_map/ppermute | solution.py:32
  42.4 1.0 %multiply_convert_fusion = bf16[256,1024]{1,0:T(8,128)(2,1)} fusion(f32[256,1024]{1,0:T(8,128)S(1)} %get-tuple-element.10, f32[1024]{0:T(1024)S(1)} %copy-done.7, f32[256]{0:T(256)S(1)} %add_rsqrt_fusion), kind=kLoop, calls=%fused_computation.14 | loop fusion | flops 786432 | bytes 1577984 | tf_op jit(solution)/shard_map/convert_element_type | solution.py:293
  (86 shorter events, 2.7 us)
Async XLA Ops:
  0.0 6.0 %copy-start = (bf16[256,1024]{1,0:T(8,128)(2,1)S(1)}, bf16[256,1024]{1,0:T(8,128)(2,1)}, u32[]{:S(2)}) copy-start(bf16[256,1024]{1,0:T(8,128)(2,1)} %param.9) | copy-start | bytes 1572868
  1.6 7.5 %collective-permute-start.1 = (bf16[3,1536]{1,0:T(4,128)(2,1)S(1)}, bf16[3,1536]{1,0:T(4,128)(2,1)S(1)}, u32[]{:S(2)}, u32[]{:S(2)}) collective-permute-start(bf16[3,1536]{1,0:T(4,128)(2,1)S(1)} %get-tuple-element.8), channel_id=1, source_target_pairs={{4,0},{8,4},{12,8},{16,12},{20,16},{24,20},{28,24},{0,28},{5,1},{9... | collective-permute-start | bytes 27656 | tf_op jit(solution)/shard_map/ppermute | solution.py:24
  5.0 4.8 %collective-permute-start = (bf16[3,1536]{1,0:T(4,128)(2,1)S(1)}, bf16[3,1536]{1,0:T(4,128)(2,1)S(1)}, u32[]{:S(2)}, u32[]{:S(2)}) collective-permute-start(bf16[3,1536]{1,0:T(4,128)(2,1)S(1)} %get-tuple-element.7), channel_id=1, source_target_pairs={{0,4},{4,8},{8,12},{12,16},{16,20},{20,24},{24,28},{28,0},{1,5},{5... | collective-permute-start | bytes 27656 | tf_op jit(solution)/shard_map/ppermute | solution.py:23
  6.0 0.7 %copy-start.4 = (f32[256,16]{0,1:T(8,128)S(1)}, f32[256,16]{0,1:T(8,128)}, u32[]{:S(2)}) copy-start(f32[256,16]{0,1:T(8,128)} %param.12) | copy-start | bytes 49156
  6.7 0.7 %copy-start.8 = (f32[16]{0:T(128)S(1)}, f32[16]{0:T(128)}, u32[]{:S(2)}) copy-start(f32[16]{0:T(128)} %param.13) | copy-start | bytes 196
  8.1 0.7 %copy-start.6 = (f32[4,512]{1,0:T(4,128)S(1)}, f32[4,512]{1,0:T(4,128)}, u32[]{:S(2)}) copy-start(f32[4,512]{1,0:T(4,128)} %param.16) | copy-start | bytes 24580
  8.1 0.8 %copy-start.5 = (f32[4,1024]{1,0:T(4,128)S(1)}, f32[4,1024]{1,0:T(4,128)}, u32[]{:S(2)}) copy-start(f32[4,1024]{1,0:T(4,128)} %param.15) | copy-start | bytes 49156
  9.1 0.6 %copy-start.3 = (bf16[3,1536]{1,0:T(4,128)(2,1)}, bf16[3,1536]{1,0:T(4,128)(2,1)S(1)}, u32[]{:S(2)}) copy-start(bf16[3,1536]{1,0:T(4,128)(2,1)S(1)} %select_select_fusion.1) | copy-start | bytes 27652
  9.8 0.6 %copy-start.2 = (bf16[3,1536]{1,0:T(4,128)(2,1)}, bf16[3,1536]{1,0:T(4,128)(2,1)S(1)}, u32[]{:S(2)}) copy-start(bf16[3,1536]{1,0:T(4,128)(2,1)S(1)} %broadcast_select_fusion) | copy-start | bytes 27652
  9.8 0.7 %slice-start.3 = ((bf16[3,1536]{1,0:T(4,128)(2,1)}), bf16[3,1024]{1,0:T(4,128)(2,1)S(1)}, s32[]{:S(2)}) async-start(bf16[3,1536]{1,0:T(4,128)(2,1)} %copy-done.3), calls=%async_computation.3 | async-start | bytes 16384 | tf_op jit(solution)/shard_map/slice | solution.py:244
  10.5 0.7 %slice-start.1 = ((bf16[3,1536]{1,0:T(4,128)(2,1)}), bf16[3,1024]{1,0:T(4,128)(2,1)S(1)}, s32[]{:S(2)}) async-start(bf16[3,1536]{1,0:T(4,128)(2,1)} %copy-done.2), calls=%async_computation.1 | async-start | bytes 16384 | tf_op jit(solution)/shard_map/slice | solution.py:244
  12.1 0.7 %slice-start.2 = ((bf16[3,1536]{1,0:T(4,128)(2,1)}), bf16[3,512]{1,0:T(4,128)(2,1)S(1)}, s32[]{:S(2)}) async-start(bf16[3,1536]{1,0:T(4,128)(2,1)} %copy-done.3), calls=%async_computation.2 | async-start | bytes 8192 | tf_op jit(solution)/shard_map/slice | solution.py:245
  12.8 0.7 %slice-start = ((bf16[3,1536]{1,0:T(4,128)(2,1)}), bf16[3,512]{1,0:T(4,128)(2,1)S(1)}, s32[]{:S(2)}) async-start(bf16[3,1536]{1,0:T(4,128)(2,1)} %copy-done.2), calls=%async_computation | async-start | bytes 8192 | tf_op jit(solution)/shard_map/slice | solution.py:245
  14.4 2.0 %collective-permute-start.2 = (f32[1032,128]{1,0:T(8,128)S(1)}, f32[1032,128]{1,0:T(8,128)S(1)}, u32[]{:S(2)}, u32[]{:S(2)}) collective-permute-start(f32[1032,128]{1,0:T(8,128)S(1)} %pad_maximum_fusion.1), channel_id=1, source_target_pairs={{0,4},{4,0},{8,12},{12,8},{16,20},{20,16},{24,28},{28,24},{1,5},{5... | collective-permute-start | bytes 1585160 | tf_op jit(solution)/shard_map/ppermute | solution.py:170
  17.5 9.3 %collective-permute-start.3 = (bf16[2,8,72,128]{3,1,2,0:T(8,128)(2,1)S(1)}, bf16[2,8,72,128]{3,1,2,0:T(8,128)(2,1)S(1)}, u32[]{:S(2)}, u32[]{:S(2)}) collective-permute-start(bf16[2,8,72,128]{3,1,2,0:T(8,128)(2,1)S(1)} %fusion.39), channel_id=1, source_target_pairs={{0,8},{4,12},{8,0},{12,4},{16,24},{20,28},{24,16},{28,20},{1,9},{5... | collective-permute-start | bytes 884744 | tf_op jit(solution)/shard_map/ppermute | solution.py:111
  19.4 0.7 %copy-start.9 = (f32[16]{0:T(128)S(1)}, f32[16]{0:T(128)}, u32[]{:S(2)}) copy-start(f32[16]{0:T(128)} %param.14) | copy-start | bytes 196
  28.5 5.4 %collective-permute-start.4 = (bf16[1,8,72,128]{3,1,2,0:T(8,128)(2,1)S(1)}, bf16[1,8,72,128]{3,1,2,0:T(8,128)(2,1)S(1)}, u32[]{:S(2)}, u32[]{:S(2)}) collective-permute-start(bf16[1,8,72,128]{3,1,2,0:T(8,128)(2,1)S(1)} %fusion.62), channel_id=1, source_target_pairs={{0,16},{4,20},{8,24},{12,28},{16,0},{20,4},{24,8},{28,12},{1,17},{... | collective-permute-start | bytes 442376 | tf_op jit(solution)/shard_map/ppermute | solution.py:111
  34.3 2.0 %collective-permute-start.5 = (f32[2,8,64,128]{3,2,1,0:T(8,128)S(1)}, f32[2,8,64,128]{3,2,1,0:T(8,128)S(1)}, u32[]{:S(2)}, u32[]{:S(2)}) collective-permute-start(f32[2,8,64,128]{3,2,1,0:T(8,128)S(1)} %pad_maximum_fusion.2), channel_id=1, source_target_pairs={{0,4},{4,0},{8,12},{12,8},{16,20},{20,16},{24,28},{28,24},{1,5},{5... | collective-permute-start | bytes 1572872 | tf_op jit(solution)/shard_map/ppermute | solution.py:188
  37.3 1.0 %copy-start.1 = (bf16[256,1024]{1,0:T(8,128)(2,1)S(1)}, bf16[256,1024]{1,0:T(8,128)(2,1)}, u32[]{:S(2)}) copy-start(bf16[256,1024]{1,0:T(8,128)(2,1)} %param.10) | copy-start | bytes 1572868
  38.8 3.7 %copy-start.7 = (f32[1024]{0:T(1024)S(1)}, f32[1024]{0:T(1024)}, u32[]{:S(2)}) copy-start(f32[1024]{0:T(1024)} %param.17) | copy-start | bytes 12292
  38.8 3.6 %collective-permute-start.6 = (f32[256]{0:T(256)S(1)}, f32[256]{0:T(256)S(1)}, u32[]{:S(2)}, u32[]{:S(2)}) collective-permute-start(f32[256]{0:T(256)S(1)} %get-tuple-element.9), channel_id=1, source_target_pairs={{0,1},{1,0},{2,3},{3,2},{4,5},{5,4},{6,7},{7,6},{8,9},{9,8},{10,11... | collective-permute-start | bytes 3080 | tf_op jit(solution)/shard_map/ppermute | solution.py:32

commit v13 on v11

--- a/solution.py
+++ b/solution.py
@@ -9,21 +9,16 @@
 KERNEL = 4
 
 
-def extended_2(block, sides, width):
-    for axis, dim in sides:
-        count = lax.axis_size(axis)
-        forward = [(i, i + 1) for i in range(count - 1)]
-        backward = [(target, source) for source, target in forward]
-        tail, head = lax.optimization_barrier(
-            (
-                lax.slice_in_dim(block, block.shape[dim] - width, None, axis=dim),
-                lax.slice_in_dim(block, 0, width, axis=dim),
-            )
-        )
-        low = lax.ppermute(tail, axis, forward)
-        high = lax.ppermute(head, axis, backward)
-        block = jnp.concatenate([low, block, high], axis=dim)
-    return block
+def exchange_rims(tails, heads, axis):
+    count = lax.axis_size(axis)
+    pos = lax.axis_index(axis)
+    forward = [(i, (i + 1) % count) for i in range(count)]
+    backward = [(target, source) for source, target in forward]
+    tails, heads = lax.optimization_barrier((tails, heads))
+    low = lax.ppermute(tails, axis, forward)
+    high = lax.ppermute(heads, axis, backward)
+    low = tuple(jnp.where(pos == 0, jnp.zeros_like(x), x) for x in low)
+    return low, high
 
 
 def partner(array, axis, stride):
@@ -217,17 +212,10 @@
     is_last = seq_pos == seq_count - 1
     my_group = lax.axis_index("head") * head_count // GROUP_HEADS
 
-    def edges(rows):
-        return jnp.concatenate(
-            [rows[tokens - rim_rows :], rows[half_rows - rim_rows : half_rows]], axis=0
-        )
-
-    edge_rows = jnp.concatenate([edges(inner_rows), edges(input_proj)], axis=1)
-    extended = extended_2(edge_rows, (("seq", 0),), rim_rows)
-    lead_first = extended[:rim_rows]
-    lead_second = jnp.where(
-        is_last, edge_rows[rim_rows:], extended[3 * rim_rows :]
-    )
+    tails = (inner_rows[half_rows - rim_rows : half_rows], input_proj[half_rows - rim_rows : half_rows])
+    heads = (inner_rows[tokens - rim_rows :], input_proj[tokens - rim_rows :])
+    lead_first, high = exchange_rims(tails, heads, "seq")
+    lead_second = tuple(jnp.where(is_last, t, h) for t, h in zip(tails, high))
     step_size = jax.nn.softplus(step_raw)
     causal = jnp.arange(half_rows)[:, None] >= jnp.arange(half_rows)[None, :]
 
@@ -239,8 +227,8 @@
         return jax.nn.silu(conv_sum).astype(jnp.bfloat16)
 
     def local_block(lead_rows, inner_in, proj_in, block_step):
-        inner_out = conv(lead_rows[:, :inner_width], inner_in, conv_inner)
-        proj_out = conv(lead_rows[:, inner_width:], proj_in, conv_proj)
+        inner_out = conv(lead_rows[0], inner_in, conv_inner)
+        proj_out = conv(lead_rows[1], proj_in, conv_proj)
         inner_conv = inner_out.reshape(half_rows, head_count, HEAD_SIZE)
         b_rows = lax.dynamic_slice_in_dim(proj_out, my_group * STATE, STATE, 1)
         c_rows = lax.dynamic_slice_in_dim(proj_out, (group_count + my_group) * STATE, STATE, 1)

time: 46.1 us -> 43.7 us (0.948)
  starting transfers between devices: 12.1 us -> 10.1 us
  local copies, waits for them, and re-layouts: 9.7 us -> 8.55 us
  other arithmetic: 6.01 us -> 6.72 us
    ppermute x1, starting transfers between devices: 2.62 us -> 0.82 us  [block_states(): got = lax.ppermute(sent, 'seq', pairs)]
    ppermute x2, waiting for transfers between devices: 10.8 us -> 11.9 us  [butterfly_states(): got, got_e = from_link(lax.ppermute(msg, 'seq', pairs), rows)]
    ppermute x1, waiting for transfers between devices: 1.06 us -> 0.08 us  [block_states(): got_1, got_2 = lax.ppermute(other, 'seq', pairs)]
    select_n x1 -> x4, other arithmetic: 0.02 us -> 0.74 us  [the longest x2 0.72 us: on_device(): lead_second = tuple((jnp.where(is_last, t, h) for t, h in zip(tails, high)))]
    unnamed x18 -> x16, local copies, waits for them, and re-layouts: 4.03 us -> 3.42 us
    slice x8 -> x2, local copies, waits for them, and re-layouts: 2.07 us -> 1.53 us  [on_device(): heads = (inner_rows[tokens - rim_rows:], input_proj[tokens - rim_rows:])]
    ppermute x2 -> x4, starting transfers between devices: 4.32 us -> 4.11 us  [the longest x2 3.62 us: exchange_rims(): high = lax.ppermute(heads, axis, backward)]
  transfers between devices with their start and end apart: 7 -> 9, of which waited for: 5 -> 5; matrix products, arithmetic and copies ran while one was open for 10% -> 13% of each run, Pallas kernels for 0% -> 0%
where the time goes in v13:
time: 43.7 us; the launch traced here: 43.1 us
  waiting for transfers between devices  14.5 us (33%)
  starting transfers between devices  10.1 us (23%)
  local copies, waits for them, and re-layouts  8.55 us (20%)
  other arithmetic  6.72 us (15%)
  matrix products  2.63 us (6%)
  between operations  0.58 us (1%)
    ppermute x2, waiting for transfers between devices, butterfly_states(): got, got_e = from_link(lax.ppermute(msg, 'seq', pairs), rows)  11.9 us
    ppermute x2, starting transfers between devices, exchange_rims(): high = lax.ppermute(heads, axis, backward)  3.62 us
    unnamed x16, local copies, waits for them, and re-layouts  3.42 us
    ppermute x2, starting transfers between devices, butterfly_states(): got, got_e = from_link(lax.ppermute(msg, 'seq', pairs), rows)  3.4 us
    ppermute x1, waiting for transfers between devices, partner(): lax.ppermute(array, axis, [(i, i ^ 1 << stride) for i in range(lax.axis_s...  1.99 us
    ppermute x1, starting transfers between devices, partner(): lax.ppermute(array, axis, [(i, i ^ 1 << stride) for i in range(lax.axis_s...  1.64 us
    slice x2, local copies, waits for them, and re-layouts, on_device(): heads = (inner_rows[tokens - rim_rows:], input_proj[tokens - rim_rows:])  1.53 us
    dot_general x2, matrix products, local_block(): jnp.einsum('hts,shp->thp', weights, inner_conv, preferred_element_type=jn...  1.12 us
  transfers between devices with their start and end apart: 9, of which 5 were waited for; matrix products, arithmetic and copies ran while one was open for 13% of the time, Pallas kernels for 0%

profile of v13, /device:TPU:0, one launch (start us, length us, event | category | flops | bytes accessed | tf_op | source)
XLA Modules:
  0.0 43.1 jit_solution(6668610845542001187)
XLA Ops:
  0.0 0.8 %fusion.97 = (bf16[3,1024]{1,0:T(4,128)(2,1)S(1)}, bf16[3,1024]{1,0:T(4,128)(2,1)S(1)}) fusion(bf16[256,1024]{1,0:T(8,128)(2,1)} %param.9), kind=kLoop, calls=%fused_computation.217 | loop fusion | bytes 24576 | tf_op jit(solution)/shard_map/slice | solution.py:216
  0.8 0.7 %fusion.99 = (bf16[3,512]{1,0:T(4,128)(2,1)S(1)}, bf16[3,512]{1,0:T(4,128)(2,1)S(1)}) fusion(bf16[256,512]{1,0:T(8,128)(2,1)} %param.11), kind=kLoop, calls=%fused_computation.219 | loop fusion | bytes 12288 | tf_op jit(solution)/shard_map/slice | solution.py:216
  1.5 0.5 %collective-permute-start.1 = (bf16[3,512]{1,0:T(4,128)(2,1)S(1)}, bf16[3,512]{1,0:T(4,128)(2,1)S(1)}, u32[]{:S(2)}, u32[]{:S(2)}) collective-permute-start(bf16[3,512]{1,0:T(4,128)(2,1)S(1)} %get-tuple-element.10), channel_id=1, source_target_pairs={{0,4},{4,8},{8,12},{12,16},{16,20},{20,24},{24,28},{28,0},{1,5},{5... | collective-permute-start | bytes 9224 | tf_op jit(solution)/shard_map/ppermute | solution.py:18
  2.0 2.9 %collective-permute-start.3 = (bf16[3,512]{1,0:T(4,128)(2,1)S(1)}, bf16[3,512]{1,0:T(4,128)(2,1)S(1)}, u32[]{:S(2)}, u32[]{:S(2)}) collective-permute-start(bf16[3,512]{1,0:T(4,128)(2,1)S(1)} %get-tuple-element.12), channel_id=1, source_target_pairs={{4,0},{8,4},{12,8},{16,12},{20,16},{24,20},{28,24},{0,28},{5,1},{9... | collective-permute-start | bytes 9224 | tf_op jit(solution)/shard_map/ppermute | solution.py:19
  5.0 0.7 %collective-permute-start.2 = (bf16[3,1024]{1,0:T(4,128)(2,1)S(1)}, bf16[3,1024]{1,0:T(4,128)(2,1)S(1)}, u32[]{:S(2)}, u32[]{:S(2)}) collective-permute-start(bf16[3,1024]{1,0:T(4,128)(2,1)S(1)} %get-tuple-element.11), channel_id=1, source_target_pairs={{4,0},{8,4},{12,8},{16,12},{20,16},{24,20},{28,24},{0,28},{5,1},{9... | collective-permute-start | bytes 18440 | tf_op jit(solution)/shard_map/ppermute | solution.py:19
  5.7 1.0 %fusion.98 = (bf16[128,512]{1,0:T(8,128)(2,1)S(1)}, bf16[128,512]{1,0:T(8,128)(2,1)S(1)}) fusion(bf16[256,512]{1,0:T(8,128)(2,1)} %param.11), kind=kLoop, calls=%fused_computation.218 | loop fusion | bytes 524288 | tf_op jit(solution)/shard_map/slice | solution.py:259
  6.7 0.7 %copy-done.2 = f32[256,16]{0,1:T(8,128)S(1)} copy-done((f32[256,16]{0,1:T(8,128)S(1)}, f32[256,16]{0,1:T(8,128)}, u32[]{:S(2)}) %copy-start.2) | copy-done | bytes 16408
  7.4 0.6 %copy-done.6 = f32[16]{0:T(128)S(1)} copy-done((f32[16]{0:T(128)S(1)}, f32[16]{0:T(128)}, u32[]{:S(2)}) %copy-start.6) | copy-done | bytes 88
  8.2 0.2 reduce_window_sum.18
  8.4 0.1 copy.87
  8.5 0.2 reduce_window_sum.17
  8.8 0.7 %copy-done.4 = f32[4,512]{1,0:T(4,128)S(1)} copy-done((f32[4,512]{1,0:T(4,128)S(1)}, f32[4,512]{1,0:T(4,128)}, u32[]{:S(2)}) %copy-start.4) | copy-done | bytes 8216
  9.9 0.7 %broadcast_select_fusion.2 = bf16[3,512]{1,0:T(4,128)(2,1)S(1)} fusion(bf16[3,512]{1,0:T(4,128)(2,1)S(1)} %collective-permute-done.3, pred[]{:T(512)S(6)} %eq.40, bf16[256,512]{1,0:T(8,128)(2,1)} %param.11), kind=kLoop, calls=%fused_computation.171 | loop fusion | flops 1536 | bytes 9217 | tf_op jit(solution)/shard_map/jit(_where)/select_n | solution.py:218
  10.6 0.3 multiply_convert_fusion.8
  11.2 0.6 %multiply_convert_fusion.6 = (bf16[128,1024]{1,0:T(8,128)(2,1)S(1)}, bf16[128,1024]{1,0:T(8,128)(2,1)S(1)}) fusion(f32[131,1024]{1,0:T(8,128)S(1)} %maximum_convert_fusion, f32[1024]{0:T(1024)S(1)} %bitcast.153, f32[1024]{0:T(1024)S(1)} %bitcast.154, f32[1024]{0:T(1024)S(1)} %bitcast.152, f32[1024]{0:T(1024)S(1)} %bitcast.151, ...), kind=kLoop, calls=%fused_computation.65 | loop fusion | flops 3145728 | bytes 4734976 | tf_op jit(solution)/shard_map/convert_element_type | solution.py:227
  11.8 0.2 copy.92
  12.0 0.2 copy.86
  12.2 0.2 fusion.45
  12.4 0.2 fusion.47
  12.8 0.8 %collective-permute-start.4 = (f32[1032,128]{1,0:T(8,128)S(1)}, f32[1032,128]{1,0:T(8,128)S(1)}, u32[]{:S(2)}, u32[]{:S(2)}) collective-permute-start(f32[1032,128]{1,0:T(8,128)S(1)} %pad_maximum_fusion.1), channel_id=1, source_target_pairs={{0,4},{4,0},{8,12},{12,8},{16,20},{20,16},{24,28},{28,24},{1,5},{5... | collective-permute-start | bytes 1585160 | tf_op jit(solution)/shard_map/ppermute | solution.py:163
  13.7 0.6 %slice.284 = pred[1]{0:T(512)(128)(4,1)} slice(pred[72]{0:T(512)(128)(4,1)S(1)} %iota_compare_fusion.4), slice={[64:65]} | slice | bytes 2 | tf_op jit(solution)/shard_map/slice | solution.py:82
  14.5 0.6 %collective-permute-done.4 = f32[1032,128]{1,0:T(8,128)S(1)} collective-permute-done((f32[1032,128]{1,0:T(8,128)S(1)}, f32[1032,128]{1,0:T(8,128)S(1)}, u32[]{:S(2)}, u32[]{:S(2)}) %collective-permute-start.4) | collective-permute-done | bytes 528416 | tf_op jit(solution)/shard_map/ppermute | solution.py:163
  15.2 0.3 fusion.55
  15.6 0.3 multiply_add_fusion
  16.1 0.1 fusion.39
  16.2 2.5 %collective-permute-start.5 = (bf16[2,8,72,128]{3,1,2,0:T(8,128)(2,1)S(1)}, bf16[2,8,72,128]{3,1,2,0:T(8,128)(2,1)S(1)}, u32[]{:S(2)}, u32[]{:S(2)}) collective-permute-start(bf16[2,8,72,128]{3,1,2,0:T(8,128)(2,1)S(1)} %fusion.39), channel_id=1, source_target_pairs={{0,8},{4,12},{8,0},{12,4},{16,24},{20,28},{24,16},{28,20},{1,9},{5... | collective-permute-start | bytes 884744 | tf_op jit(solution)/shard_map/ppermute | solution.py:104
  18.7 0.1 fusion.74
  18.8 0.1 fusion.69
  19.0 7.2 %collective-permute-done.5 = bf16[2,8,72,128]{3,1,2,0:T(8,128)(2,1)S(1)} collective-permute-done((bf16[2,8,72,128]{3,1,2,0:T(8,128)(2,1)S(1)}, bf16[2,8,72,128]{3,1,2,0:T(8,128)(2,1)S(1)}, u32[]{:S(2)}, u32[]{:S(2)}) %collective-permute-start.5) | collective-permute-done | bytes 294944 | tf_op jit(solution)/shard_map/ppermute | solution.py:104
  26.4 0.2 fusion.42
  26.6 0.2 copy_select_fusion
  26.8 0.7 %fusion.79 = (f32[8,128]{1,0:T(8,128)S(1)}, f32[8,1,128]{2,0,1:T(8,128)S(1)}) fusion(f32[8,1,128]{2,0,1:T(8,128)S(1)} %bitcast.147, pred[]{:T(512)S(6)} %eq.36, f32[8,128]{1,0:T(8,128)S(1)} %get-tuple-element.68, f32[8,128]{1,0:T(8,128)S(1)} %get-tuple-element.71, f32[8,72,128]{2,0,1:T(8,128)S(1)} %slice_bitcast_fusion, f32[8]{0:T(128)S(1)} %get-tuple-element.29, ...), kind=kLoop, calls=%fused_computation.161 | loop fusion | flops 9216 | bytes 319523 | tf_op jit(solution)/shard_map/jit(_where)/broadcast_in_dim | solution.py:93
  27.7 0.3 fusion.62
  27.9 0.9 %collective-permute-start.6 = (bf16[1,8,72,128]{3,1,2,0:T(8,128)(2,1)S(1)}, bf16[1,8,72,128]{3,1,2,0:T(8,128)(2,1)S(1)}, u32[]{:S(2)}, u32[]{:S(2)}) collective-permute-start(bf16[1,8,72,128]{3,1,2,0:T(8,128)(2,1)S(1)} %fusion.62), channel_id=1, source_target_pairs={{0,16},{4,20},{8,24},{12,28},{16,0},{20,4},{24,8},{28,12},{1,17},{... | collective-permute-start | bytes 442376 | tf_op jit(solution)/shard_map/ppermute | solution.py:104
  28.9 4.6 %collective-permute-done.6 = bf16[1,8,72,128]{3,1,2,0:T(8,128)(2,1)S(1)} collective-permute-done((bf16[1,8,72,128]{3,1,2,0:T(8,128)(2,1)S(1)}, bf16[1,8,72,128]{3,1,2,0:T(8,128)(2,1)S(1)}, u32[]{:S(2)}, u32[]{:S(2)}) %collective-permute-start.6) | collective-permute-done | bytes 147488 | tf_op jit(solution)/shard_map/ppermute | solution.py:104
  33.6 0.3 fusion.63
  34.1 0.6 %copy-done.7 = f32[16]{0:T(128)S(1)} copy-done((f32[16]{0:T(128)S(1)}, f32[16]{0:T(128)}, u32[]{:S(2)}) %copy-start.7) | copy-done | bytes 88
  34.6 0.6 %fusion.2 = f32[128,16,64]{0,2,1:T(8,128)S(1)} fusion(bf16[128,16,64]{0,2,1:T(8,128)(2,1)S(1)} %bitcast.143, f32[16,128]{1,0:T(8,128)S(1)} %get-tuple-element.57, f32[16,128]{1,0:T(8,128)S(1)} %copy.88, f32[128,128]{1,0:T(8,128)S(1)} %fusion.74, pred[128,128]{1,0:T(8,128)(4,1)S(1)} %iota_compare_fusion, f32[16]{0:T(128)S(1)} %copy-done.7), kind=kOutput, calls=%fused_computation.8 | convolution fusion | flops 35520512 | bytes 884800 | tf_op jit(solution)/shard_map/hts,shp->thp/dot_general | solution.py:240
  35.2 0.6 %fusion.3 = f32[128,16,64]{0,2,1:T(8,128)S(1)} fusion(bf16[128,16,64]{0,2,1:T(8,128)(2,1)S(1)} %bitcast.141, f32[16,128]{1,0:T(8,128)S(1)} %get-tuple-element.60, f32[16,128]{1,0:T(8,128)S(1)} %copy.114, f32[128,128]{1,0:T(8,128)S(1)} %fusion.69, pred[128,128]{1,0:T(8,128)(4,1)S(1)} %iota_compare_fusion, f32[16]{0:T(128)S(1)} %copy-done.7), kind=kOutput, calls=%fused_computation.9 | convolution fusion | flops 35520512 | bytes 884800 | tf_op jit(solution)/shard_map/hts,shp->thp/dot_general | solution.py:240
  36.0 0.4 fusion.1
  36.4 0.2 copy.118
  36.6 0.4 fusion
  37.0 0.2 copy.119
  37.2 0.8 %copy-done.1 = bf16[256,1024]{1,0:T(8,128)(2,1)S(1)} copy-done((bf16[256,1024]{1,0:T(8,128)(2,1)S(1)}, bf16[256,1024]{1,0:T(8,128)(2,1)}, u32[]{:S(2)}) %copy-start.1) | copy-done | bytes 524312
  38.0 0.4 multiply_reduce_fusion
  38.5 1.6 %collective-permute-start.8 = (f32[256]{0:T(256)S(1)}, f32[256]{0:T(256)S(1)}, u32[]{:S(2)}, u32[]{:S(2)}) collective-permute-start(f32[256]{0:T(256)S(1)} %get-tuple-element.13), channel_id=1, source_target_pairs={{0,1},{1,0},{2,3},{3,2},{4,5},{5,4},{6,7},{7,6},{8,9},{9,8},{10,11... | collective-permute-start | bytes 3080 | tf_op jit(solution)/shard_map/ppermute | solution.py:25
  40.1 2.0 %collective-permute-done.8 = f32[256]{0:T(256)S(1)} collective-permute-done((f32[256]{0:T(256)S(1)}, f32[256]{0:T(256)S(1)}, u32[]{:S(2)}, u32[]{:S(2)}) %collective-permute-start.8) | collective-permute-done | bytes 1056 | tf_op jit(solution)/shard_map/ppermute | solution.py:25
  42.1 1.0 %multiply_convert_fusion = bf16[256,1024]{1,0:T(8,128)(2,1)} fusion(f32[256,1024]{1,0:T(8,128)S(1)} %get-tuple-element.14, f32[1024]{0:T(1024)S(1)} %copy-done.5, f32[256]{0:T(256)S(1)} %add_rsqrt_fusion), kind=kLoop, calls=%fused_computation.14 | loop fusion | flops 786432 | bytes 1577984 | tf_op jit(solution)/shard_map/convert_element_type | solution.py:279
  (78 shorter events, 2.4 us)
Async XLA Ops:
  0.0 6.6 %copy-start = (bf16[256,1024]{1,0:T(8,128)(2,1)S(1)}, bf16[256,1024]{1,0:T(8,128)(2,1)}, u32[]{:S(2)}) copy-start(bf16[256,1024]{1,0:T(8,128)(2,1)} %param.9) | copy-start | bytes 1572868
  1.5 8.3 %collective-permute-start.1 = (bf16[3,512]{1,0:T(4,128)(2,1)S(1)}, bf16[3,512]{1,0:T(4,128)(2,1)S(1)}, u32[]{:S(2)}, u32[]{:S(2)}) collective-permute-start(bf16[3,512]{1,0:T(4,128)(2,1)S(1)} %get-tuple-element.10), channel_id=1, source_target_pairs={{0,4},{4,8},{8,12},{12,16},{16,20},{20,24},{24,28},{28,0},{1,5},{5... | collective-permute-start | bytes 9224 | tf_op jit(solution)/shard_map/ppermute | solution.py:18
  2.0 7.8 %collective-permute-start.3 = (bf16[3,512]{1,0:T(4,128)(2,1)S(1)}, bf16[3,512]{1,0:T(4,128)(2,1)S(1)}, u32[]{:S(2)}, u32[]{:S(2)}) collective-permute-start(bf16[3,512]{1,0:T(4,128)(2,1)S(1)} %get-tuple-element.12), channel_id=1, source_target_pairs={{4,0},{8,4},{12,8},{16,12},{20,16},{24,20},{28,24},{0,28},{5,1},{9... | collective-permute-start | bytes 9224 | tf_op jit(solution)/shard_map/ppermute | solution.py:19
  5.0 6.0 %collective-permute-start.2 = (bf16[3,1024]{1,0:T(4,128)(2,1)S(1)}, bf16[3,1024]{1,0:T(4,128)(2,1)S(1)}, u32[]{:S(2)}, u32[]{:S(2)}) collective-permute-start(bf16[3,1024]{1,0:T(4,128)(2,1)S(1)} %get-tuple-element.11), channel_id=1, source_target_pairs={{4,0},{8,4},{12,8},{16,12},{20,16},{24,20},{28,24},{0,28},{5,1},{9... | collective-permute-start | bytes 18440 | tf_op jit(solution)/shard_map/ppermute | solution.py:19
  5.6 5.4 %collective-permute-start = (bf16[3,1024]{1,0:T(4,128)(2,1)S(1)}, bf16[3,1024]{1,0:T(4,128)(2,1)S(1)}, u32[]{:S(2)}, u32[]{:S(2)}) collective-permute-start(bf16[3,1024]{1,0:T(4,128)(2,1)S(1)} %get-tuple-element.9), channel_id=1, source_target_pairs={{0,4},{4,8},{8,12},{12,16},{16,20},{20,24},{24,28},{28,0},{1,5},{5... | collective-permute-start | bytes 18440 | tf_op jit(solution)/shard_map/ppermute | solution.py:18
  6.7 0.7 %copy-start.2 = (f32[256,16]{0,1:T(8,128)S(1)}, f32[256,16]{0,1:T(8,128)}, u32[]{:S(2)}) copy-start(f32[256,16]{0,1:T(8,128)} %param.12) | copy-start | bytes 49156
  7.4 0.7 %copy-start.6 = (f32[16]{0:T(128)S(1)}, f32[16]{0:T(128)}, u32[]{:S(2)}) copy-start(f32[16]{0:T(128)} %param.13) | copy-start | bytes 196
  8.8 0.7 %copy-start.4 = (f32[4,512]{1,0:T(4,128)S(1)}, f32[4,512]{1,0:T(4,128)}, u32[]{:S(2)}) copy-start(f32[4,512]{1,0:T(4,128)} %param.16) | copy-start | bytes 24580
  8.8 0.8 %copy-start.3 = (f32[4,1024]{1,0:T(4,128)S(1)}, f32[4,1024]{1,0:T(4,128)}, u32[]{:S(2)}) copy-start(f32[4,1024]{1,0:T(4,128)} %param.15) | copy-start | bytes 49156
  12.8 2.4 %collective-permute-start.4 = (f32[1032,128]{1,0:T(8,128)S(1)}, f32[1032,128]{1,0:T(8,128)S(1)}, u32[]{:S(2)}, u32[]{:S(2)}) collective-permute-start(f32[1032,128]{1,0:T(8,128)S(1)} %pad_maximum_fusion.1), channel_id=1, source_target_pairs={{0,4},{4,0},{8,12},{12,8},{16,20},{20,16},{24,28},{28,24},{1,5},{5... | collective-permute-start | bytes 1585160 | tf_op jit(solution)/shard_map/ppermute | solution.py:163
  16.2 10.0 %collective-permute-start.5 = (bf16[2,8,72,128]{3,1,2,0:T(8,128)(2,1)S(1)}, bf16[2,8,72,128]{3,1,2,0:T(8,128)(2,1)S(1)}, u32[]{:S(2)}, u32[]{:S(2)}) collective-permute-start(bf16[2,8,72,128]{3,1,2,0:T(8,128)(2,1)S(1)} %fusion.39), channel_id=1, source_target_pairs={{0,8},{4,12},{8,0},{12,4},{16,24},{20,28},{24,16},{28,20},{1,9},{5... | collective-permute-start | bytes 884744 | tf_op jit(solution)/shard_map/ppermute | solution.py:104
  27.9 5.6 %collective-permute-start.6 = (bf16[1,8,72,128]{3,1,2,0:T(8,128)(2,1)S(1)}, bf16[1,8,72,128]{3,1,2,0:T(8,128)(2,1)S(1)}, u32[]{:S(2)}, u32[]{:S(2)}) collective-permute-start(bf16[1,8,72,128]{3,1,2,0:T(8,128)(2,1)S(1)} %fusion.62), channel_id=1, source_target_pairs={{0,16},{4,20},{8,24},{12,28},{16,0},{20,4},{24,8},{28,12},{1,17},{... | collective-permute-start | bytes 442376 | tf_op jit(solution)/shard_map/ppermute | solution.py:104
  34.0 0.7 %copy-start.7 = (f32[16]{0:T(128)S(1)}, f32[16]{0:T(128)}, u32[]{:S(2)}) copy-start(f32[16]{0:T(128)} %param.14) | copy-start | bytes 196
  34.0 2.0 %collective-permute-start.7 = (f32[2,8,64,128]{3,2,1,0:T(8,128)S(1)}, f32[2,8,64,128]{3,2,1,0:T(8,128)S(1)}, u32[]{:S(2)}, u32[]{:S(2)}) collective-permute-start(f32[2,8,64,128]{3,2,1,0:T(8,128)S(1)} %pad_maximum_fusion.2), channel_id=1, source_target_pairs={{0,4},{4,0},{8,12},{12,8},{16,20},{20,16},{24,28},{28,24},{1,5},{5... | collective-permute-start | bytes 1572872 | tf_op jit(solution)/shard_map/ppermute | solution.py:181
  37.0 1.0 %copy-start.1 = (bf16[256,1024]{1,0:T(8,128)(2,1)S(1)}, bf16[256,1024]{1,0:T(8,128)(2,1)}, u32[]{:S(2)}) copy-start(bf16[256,1024]{1,0:T(8,128)(2,1)} %param.10) | copy-start | bytes 1572868
  38.4 3.7 %copy-start.5 = (f32[1024]{0:T(1024)S(1)}, f32[1024]{0:T(1024)}, u32[]{:S(2)}) copy-start(f32[1024]{0:T(1024)} %param.17) | copy-start | bytes 12292
  38.5 3.6 %collective-permute-start.8 = (f32[256]{0:T(256)S(1)}, f32[256]{0:T(256)S(1)}, u32[]{:S(2)}, u32[]{:S(2)}) collective-permute-start(f32[256]{0:T(256)S(1)} %get-tuple-element.13), channel_id=1, source_target_pairs={{0,1},{1,0},{2,3},{3,2},{4,5},{5,4},{6,7},{7,6},{8,9},{9,8},{10,11... | collective-permute-start | bytes 3080 | tf_op jit(solution)/shard_map/ppermute | solution.py:25

commit v14 on v13

--- a/solution.py
+++ b/solution.py
@@ -219,16 +219,19 @@
     step_size = jax.nn.softplus(step_raw)
     causal = jnp.arange(half_rows)[:, None] >= jnp.arange(half_rows)[None, :]
 
-    def conv(lead_rows, rows_in, taps):
-        padded = jnp.concatenate([lead_rows, rows_in], axis=0).astype(jnp.float32)
-        conv_sum = jnp.zeros((half_rows, rows_in.shape[1]), jnp.float32)
+    def conv(leads, rows_in, taps):
+        width = rows_in.shape[1]
+        blocks = rows_in.reshape(2, half_rows, width)
+        padded = jnp.concatenate([jnp.stack(leads), blocks], axis=1).astype(jnp.float32)
+        conv_sum = jnp.zeros((2, half_rows, width), jnp.float32)
         for offset in range(KERNEL):
-            conv_sum = conv_sum + taps[offset][None, :] * padded[offset : offset + half_rows]
+            conv_sum = conv_sum + taps[offset][None, None, :] * padded[:, offset : offset + half_rows]
         return jax.nn.silu(conv_sum).astype(jnp.bfloat16)
 
-    def local_block(lead_rows, inner_in, proj_in, block_step):
-        inner_out = conv(lead_rows[0], inner_in, conv_inner)
-        proj_out = conv(lead_rows[1], proj_in, conv_proj)
+    inner_all = conv((lead_first[0], lead_second[0]), inner_rows, conv_inner)
+    proj_all = conv((lead_first[1], lead_second[1]), input_proj, conv_proj)
+
+    def local_block(inner_out, proj_out, block_step):
         inner_conv = inner_out.reshape(half_rows, head_count, HEAD_SIZE)
         b_rows = lax.dynamic_slice_in_dim(proj_out, my_group * STATE, STATE, 1)
         c_rows = lax.dynamic_slice_in_dim(proj_out, (group_count + my_group) * STATE, STATE, 1)
@@ -256,10 +259,10 @@
         return total_out.reshape(half_rows, inner_width)
 
     first_out, first_cum, first_c, first_elem = local_block(
-        lead_first, inner_rows[:half_rows], input_proj[:half_rows], step_size[:half_rows]
+        inner_all[0], proj_all[0], step_size[:half_rows]
     )
     second_out, second_cum, second_c, second_elem = local_block(
-        lead_second, inner_rows[half_rows:], input_proj[half_rows:], step_size[half_rows:]
+        inner_all[1], proj_all[1], step_size[half_rows:]
     )
     first_in, second_in = block_states(
         first_elem[1], second_elem[1], first_cum[-1], second_cum[-1], seq_pos, seq_count

time: 43.7 us -> 47.3 us (1.082)
  other arithmetic: 6.72 us -> 10.2 us
  starting transfers between devices: 10.1 us -> 11.2 us
  local copies, waits for them, and re-layouts: 8.55 us -> 7.66 us
    unnamed x16 -> x8, local copies, waits for them, and re-layouts: 3.42 us -> 0.47 us
    ppermute x2, starting transfers between devices: 3.62 us -> 6.01 us  [exchange_rims(): high = lax.ppermute(heads, axis, backward)]
    another operation x0 -> x5, other arithmetic: none -> 1.48 us  [conv(): jnp.stack(leads)]
    reshape x0 -> x1, local copies, waits for them, and re-layouts: none -> 1.31 us  [conv(): blocks = rows_in.reshape(2, half_rows, width)]
    convert_element_type x2, other arithmetic: 0.97 us -> 1.9 us  [conv(): return jax.nn.silu(conv_sum).astype(jnp.bfloat16)]
    slice x4, local copies, waits for them, and re-layouts: 1.04 us -> 1.81 us  [the longest x2 1.74 us: conv(): taps[offset][None, None, :] * padded[:, offset:offset + half_rows]]
    ppermute x2, waiting for transfers between devices: 11.9 us -> 11.1 us  [butterfly_states(): got, got_e = from_link(lax.ppermute(msg, 'seq', pairs), rows)]
    ppermute x1, starting transfers between devices: 0.82 us -> 0.07 us  [block_states(): got = lax.ppermute(sent, 'seq', pairs)]
  transfers between devices with their start and end apart: 9 -> 9, of which waited for: 5 -> 5; matrix products, arithmetic and copies ran while one was open for 13% -> 21% of each run, Pallas kernels for 0% -> 0%
where the time goes in v14:
time: 47.3 us; the launch traced here: 46.5 us
  waiting for transfers between devices  14.2 us (30%)
  starting transfers between devices  11.2 us (24%)
  other arithmetic  10.2 us (22%)
  local copies, waits for them, and re-layouts  7.66 us (16%)
  matrix products  2.6 us (5%)
  between operations  0.64 us (1%)
    ppermute x2, waiting for transfers between devices, butterfly_states(): got, got_e = from_link(lax.ppermute(msg, 'seq', pairs), rows)  11.1 us
    ppermute x2, starting transfers between devices, exchange_rims(): high = lax.ppermute(heads, axis, backward)  6.01 us
    ppermute x2, starting transfers between devices, butterfly_states(): got, got_e = from_link(lax.ppermute(msg, 'seq', pairs), rows)  3.37 us
    ppermute x1, waiting for transfers between devices, partner(): lax.ppermute(array, axis, [(i, i ^ 1 << stride) for i in range(lax.axis_s...  1.99 us
    convert_element_type x2, other arithmetic, conv(): return jax.nn.silu(conv_sum).astype(jnp.bfloat16)  1.9 us
    slice x2, local copies, waits for them, and re-layouts, conv(): taps[offset][None, None, :] * padded[:, offset:offset + half_rows]  1.74 us
    ppermute x1, starting transfers between devices, partner(): lax.ppermute(array, axis, [(i, i ^ 1 << stride) for i in range(lax.axis_s...  1.64 us
    slice x2, local copies, waits for them, and re-layouts, on_device(): heads = (inner_rows[tokens - rim_rows:], input_proj[tokens - rim_rows:])  1.51 us
  transfers between devices with their start and end apart: 9, of which 5 were waited for; matrix products, arithmetic and copies ran while one was open for 21% of the time, Pallas kernels for 0%

profile of v14, /device:TPU:0, one launch (start us, length us, event | category | flops | bytes accessed | tf_op | source)
XLA Modules:
  0.0 46.5 jit_solution(11628906522562332147)
XLA Ops:
  0.0 0.8 %fusion.91 = (bf16[3,1024]{1,0:T(4,128)(2,1)S(1)}, bf16[3,1024]{1,0:T(4,128)(2,1)S(1)}) fusion(bf16[256,1024]{1,0:T(8,128)(2,1)} %param.9), kind=kLoop, calls=%fused_computation.200 | loop fusion | bytes 24576 | tf_op jit(solution)/shard_map/slice | solution.py:216
  0.8 0.7 %fusion.93 = (bf16[3,512]{1,0:T(4,128)(2,1)S(1)}, bf16[3,512]{1,0:T(4,128)(2,1)S(1)}) fusion(bf16[256,512]{1,0:T(8,128)(2,1)} %param.11), kind=kLoop, calls=%fused_computation.202 | loop fusion | bytes 12288 | tf_op jit(solution)/shard_map/slice | solution.py:216
  1.5 3.4 %collective-permute-start.1 = (bf16[3,1024]{1,0:T(4,128)(2,1)S(1)}, bf16[3,1024]{1,0:T(4,128)(2,1)S(1)}, u32[]{:S(2)}, u32[]{:S(2)}) collective-permute-start(bf16[3,1024]{1,0:T(4,128)(2,1)S(1)} %get-tuple-element.10), channel_id=1, source_target_pairs={{4,0},{8,4},{12,8},{16,12},{20,16},{24,20},{28,24},{0,28},{5,1},{9... | collective-permute-start | bytes 18440 | tf_op jit(solution)/shard_map/ppermute | solution.py:19
  4.9 2.6 %collective-permute-start.3 = (bf16[3,512]{1,0:T(4,128)(2,1)S(1)}, bf16[3,512]{1,0:T(4,128)(2,1)S(1)}, u32[]{:S(2)}, u32[]{:S(2)}) collective-permute-start(bf16[3,512]{1,0:T(4,128)(2,1)S(1)} %get-tuple-element.12), channel_id=1, source_target_pairs={{4,0},{8,4},{12,8},{16,12},{20,16},{24,20},{28,24},{0,28},{5,1},{9... | collective-permute-start | bytes 9224 | tf_op jit(solution)/shard_map/ppermute | solution.py:19
  7.5 0.7 %compare_select_fusion = f32[256,16]{0,1:T(8,128)S(1)} fusion(f32[256,16]{0,1:T(8,128)} %param.12), kind=kLoop, calls=%fused_computation.111 | loop fusion | flops 24576 | bytes 32768 | tf_op jit(solution)/shard_map/jit(softplus)/select_n | solution.py:219
  8.3 0.7 %negate_multiply_fusion.1 = (f32[128,16]{0,1:T(8,128)S(1)}, f32[128,16]{0,1:T(8,128)S(1)}) fusion(f32[256,16]{0,1:T(8,128)S(1)} %compare_select_fusion, f32[16]{0:T(128)} %param.13), kind=kLoop, calls=%fused_computation.137 | loop fusion | flops 8192 | bytes 32832 | tf_op jit(solution)/shard_map/mul | solution.py:238
  9.1 0.2 reduce_window_sum.18
  9.5 0.2 reduce_window_sum.17
  9.7 0.9 %fusion.94 = (f32[1,1024]{1,0:T(1,128)S(1)}, f32[1,1024]{1,0:T(1,128)S(1)}, f32[1,1024]{1,0:T(1,128)S(1)}, f32[1,1024]{1,0:T(1,128)S(1)}) fusion(f32[4,1024]{1,0:T(4,128)} %param.15), kind=kLoop, calls=%fused_computation.203 | loop fusion | bytes 32768 | tf_op jit(solution)/shard_map/slice | solution.py:228
  10.6 0.9 %fusion.95 = (f32[1,512]{1,0:T(1,128)S(1)}, f32[1,512]{1,0:T(1,128)S(1)}, f32[1,512]{1,0:T(1,128)S(1)}, f32[1,512]{1,0:T(1,128)S(1)}) fusion(f32[4,512]{1,0:T(4,128)} %param.16), kind=kLoop, calls=%fused_computation.204 | loop fusion | bytes 16384 | tf_op jit(solution)/shard_map/slice | solution.py:228
  11.7 1.3 %copy.87 = bf16[2,128,1024]{1,2,0:T(8,128)(2,1)S(1)} copy(bf16[2,128,1024]{2,1,0:T(8,128)(2,1)} %bitcast.178) | data formatting | bytes 1048576 | tf_op jit(solution)/shard_map/reshape | solution.py:224
  13.1 0.7 %select_bitcast_fusion.4 = bf16[1,3,512]{2,1,0:T(4,128)(2,1)S(1)} fusion(bf16[3,512]{1,0:T(4,128)(2,1)S(1)} %collective-permute-done.3, pred[]{:T(512)S(6)} %eq.35, bf16[256,512]{1,0:T(8,128)(2,1)} %param.11), kind=kLoop, calls=%fused_computation.154 | loop fusion | flops 1536 | bytes 9217 | tf_op jit(solution)/shard_map/stack | solution.py:225
  13.9 0.3 multiply_convert_fusion.6
  14.3 0.7 %select_bitcast_fusion.2 = bf16[1,3,1024]{2,1,0:T(4,128)(2,1)S(1)} fusion(bf16[3,1024]{1,0:T(4,128)(2,1)S(1)} %collective-permute-done.1, pred[]{:T(512)S(6)} %eq.35, bf16[256,1024]{1,0:T(8,128)(2,1)} %param.9), kind=kLoop, calls=%fused_computation.138 | loop fusion | flops 3072 | bytes 18433 | tf_op jit(solution)/shard_map/stack | solution.py:225
  15.0 0.3 copy.86
  15.4 0.4 maximum_convert_fusion
  15.8 1.6 %multiply_convert_fusion.3 = bf16[2,128,1024]{1,2,0:T(8,128)(2,1)S(1)} fusion(f32[2,131,1024]{1,2,0:T(8,128)S(1)} %maximum_convert_fusion, f32[1024]{0:T(1024)S(1)} %bitcast.189, f32[1024]{0:T(1024)S(1)} %bitcast.190, f32[1024]{0:T(1024)S(1)} %bitcast.188, f32[1024]{0:T(1024)S(1)} %bitcast.187), kind=kLoop, calls=%fused_computation.26 | loop fusion | flops 3145728 | bytes 4734976 | tf_op jit(solution)/shard_map/convert_element_type | solution.py:229
  17.5 0.2 fusion.55
  17.7 0.2 fusion.58
  18.3 0.6 %slice.240 = pred[1]{0:T(512)(128)(4,1)} slice(pred[72]{0:T(512)(128)(4,1)S(1)} %iota_compare_fusion.4), slice={[64:65]} | slice | bytes 2 | tf_op jit(solution)/shard_map/slice | solution.py:82
  19.2 0.1 fusion.61
  19.3 0.7 %collective-permute-done.4 = f32[1032,128]{1,0:T(8,128)S(1)} collective-permute-done((f32[1032,128]{1,0:T(8,128)S(1)}, f32[1032,128]{1,0:T(8,128)S(1)}, u32[]{:S(2)}, u32[]{:S(2)}) %collective-permute-start.4) | collective-permute-done | bytes 528416 | tf_op jit(solution)/shard_map/ppermute | solution.py:163
  20.2 0.3 fusion.45
  20.6 0.3 multiply_add_fusion
  21.0 0.1 fusion.39
  21.1 1.8 %collective-permute-start.5 = (bf16[2,8,72,128]{3,1,2,0:T(8,128)(2,1)S(1)}, bf16[2,8,72,128]{3,1,2,0:T(8,128)(2,1)S(1)}, u32[]{:S(2)}, u32[]{:S(2)}) collective-permute-start(bf16[2,8,72,128]{3,1,2,0:T(8,128)(2,1)S(1)} %fusion.39), channel_id=1, source_target_pairs={{0,8},{4,12},{8,0},{12,4},{16,24},{20,28},{24,16},{28,20},{1,9},{5... | collective-permute-start | bytes 884744 | tf_op jit(solution)/shard_map/ppermute | solution.py:104
  22.9 0.1 fusion.53
  23.1 7.3 %collective-permute-done.5 = bf16[2,8,72,128]{3,1,2,0:T(8,128)(2,1)S(1)} collective-permute-done((bf16[2,8,72,128]{3,1,2,0:T(8,128)(2,1)S(1)}, bf16[2,8,72,128]{3,1,2,0:T(8,128)(2,1)S(1)}, u32[]{:S(2)}, u32[]{:S(2)}) %collective-permute-start.5) | collective-permute-done | bytes 294944 | tf_op jit(solution)/shard_map/ppermute | solution.py:104
  30.6 0.2 fusion.42
  30.8 0.2 copy_select_fusion
  31.0 0.7 %fusion.73 = (f32[8,128]{1,0:T(8,128)S(1)}, f32[8,1,128]{2,0,1:T(8,128)S(1)}) fusion(f32[8,1,128]{2,0,1:T(8,128)S(1)} %bitcast.183, pred[]{:T(512)S(6)} %eq.37, f32[8,128]{1,0:T(8,128)S(1)} %get-tuple-element.68, f32[8,128]{1,0:T(8,128)S(1)} %get-tuple-element.71, f32[8,72,128]{2,0,1:T(8,128)S(1)} %slice_bitcast_fusion, f32[8]{0:T(128)S(1)} %get-tuple-element.29, ...), kind=kLoop, calls=%fused_computation.144 | loop fusion | flops 9216 | bytes 319523 | tf_op jit(solution)/shard_map/jit(_where)/broadcast_in_dim | solution.py:93
  31.9 0.3 fusion.50
  32.2 1.6 %collective-permute-start.6 = (bf16[1,8,72,128]{3,1,2,0:T(8,128)(2,1)S(1)}, bf16[1,8,72,128]{3,1,2,0:T(8,128)(2,1)S(1)}, u32[]{:S(2)}, u32[]{:S(2)}) collective-permute-start(bf16[1,8,72,128]{3,1,2,0:T(8,128)(2,1)S(1)} %fusion.50), channel_id=1, source_target_pairs={{0,16},{4,20},{8,24},{12,28},{16,0},{20,4},{24,8},{28,12},{1,17},{... | collective-permute-start | bytes 442376 | tf_op jit(solution)/shard_map/ppermute | solution.py:104
  33.8 3.8 %collective-permute-done.6 = bf16[1,8,72,128]{3,1,2,0:T(8,128)(2,1)S(1)} collective-permute-done((bf16[1,8,72,128]{3,1,2,0:T(8,128)(2,1)S(1)}, bf16[1,8,72,128]{3,1,2,0:T(8,128)(2,1)S(1)}, u32[]{:S(2)}, u32[]{:S(2)}) %collective-permute-start.6) | collective-permute-done | bytes 147488 | tf_op jit(solution)/shard_map/ppermute | solution.py:104
  37.7 0.3 fusion.51
  38.1 0.2 copy-done.3
  38.3 0.6 %fusion.2 = f32[128,16,64]{0,2,1:T(8,128)S(1)} fusion(bf16[128,16,64]{0,2,1:T(8,128)(2,1)S(1)} %bitcast.181, f32[16,128]{1,0:T(8,128)S(1)} %get-tuple-element.59, f32[16,128]{1,0:T(8,128)S(1)} %copy.89, f32[128,128]{1,0:T(8,128)S(1)} %fusion.61, pred[128,128]{1,0:T(8,128)(4,1)S(1)} %iota_compare_fusion, f32[16]{0:T(128)S(1)} %copy-done.3), kind=kOutput, calls=%fused_computation.8 | convolution fusion | flops 35520512 | bytes 884800 | tf_op jit(solution)/shard_map/hts,shp->thp/dot_general | solution.py:243
  38.9 0.6 %fusion.3 = f32[128,16,64]{0,2,1:T(8,128)S(1)} fusion(bf16[128,16,64]{0,2,1:T(8,128)(2,1)S(1)} %bitcast.180, f32[16,128]{1,0:T(8,128)S(1)} %get-tuple-element.62, f32[16,128]{1,0:T(8,128)S(1)} %copy.114, f32[128,128]{1,0:T(8,128)S(1)} %fusion.53, pred[128,128]{1,0:T(8,128)(4,1)S(1)} %iota_compare_fusion, f32[16]{0:T(128)S(1)} %copy-done.3), kind=kOutput, calls=%fused_computation.9 | convolution fusion | flops 35520512 | bytes 884800 | tf_op jit(solution)/shard_map/hts,shp->thp/dot_general | solution.py:243
  39.6 0.4 collective-permute-done.7
  40.0 0.4 fusion.1
  40.4 0.2 copy.118
  40.6 0.4 fusion
  41.0 0.2 copy.119
  41.2 0.2 copy-done
  41.5 0.4 multiply_reduce_fusion
  41.9 1.6 %collective-permute-start.8 = (f32[256]{0:T(256)S(1)}, f32[256]{0:T(256)S(1)}, u32[]{:S(2)}, u32[]{:S(2)}) collective-permute-start(f32[256]{0:T(256)S(1)} %get-tuple-element.13), channel_id=1, source_target_pairs={{0,1},{1,0},{2,3},{3,2},{4,5},{5,4},{6,7},{7,6},{8,9},{9,8},{10,11... | collective-permute-start | bytes 3080 | tf_op jit(solution)/shard_map/ppermute | solution.py:25
  43.5 2.0 %collective-permute-done.8 = f32[256]{0:T(256)S(1)} collective-permute-done((f32[256]{0:T(256)S(1)}, f32[256]{0:T(256)S(1)}, u32[]{:S(2)}, u32[]{:S(2)}) %collective-permute-start.8) | collective-permute-done | bytes 1056 | tf_op jit(solution)/shard_map/ppermute | solution.py:25
  45.5 1.0 %multiply_convert_fusion = bf16[256,1024]{1,0:T(8,128)(2,1)} fusion(f32[256,1024]{1,0:T(8,128)S(1)} %get-tuple-element.14, f32[1024]{0:T(1024)S(1)} %copy-done.2, f32[256]{0:T(256)S(1)} %add_rsqrt_fusion), kind=kLoop, calls=%fused_computation.22 | loop fusion | flops 786432 | bytes 1577984 | tf_op jit(solution)/shard_map/convert_element_type | solution.py:282
  (70 shorter events, 2.3 us)
Async XLA Ops:
  0.0 13.8 %copy-start.1 = (bf16[256,512]{1,0:T(8,128)(2,1)S(1)}, bf16[256,512]{1,0:T(8,128)(2,1)}, u32[]{:S(2)}) copy-start(bf16[256,512]{1,0:T(8,128)(2,1)} %param.11) | copy-start | bytes 786436
  1.5 12.7 %collective-permute-start.1 = (bf16[3,1024]{1,0:T(4,128)(2,1)S(1)}, bf16[3,1024]{1,0:T(4,128)(2,1)S(1)}, u32[]{:S(2)}, u32[]{:S(2)}) collective-permute-start(bf16[3,1024]{1,0:T(4,128)(2,1)S(1)} %get-tuple-element.10), channel_id=1, source_target_pairs={{4,0},{8,4},{12,8},{16,12},{20,16},{24,20},{28,24},{0,28},{5,1},{9... | collective-permute-start | bytes 18440 | tf_op jit(solution)/shard_map/ppermute | solution.py:19
  4.9 10.1 %collective-permute-start = (bf16[3,1024]{1,0:T(4,128)(2,1)S(1)}, bf16[3,1024]{1,0:T(4,128)(2,1)S(1)}, u32[]{:S(2)}, u32[]{:S(2)}) collective-permute-start(bf16[3,1024]{1,0:T(4,128)(2,1)S(1)} %get-tuple-element.9), channel_id=1, source_target_pairs={{0,4},{4,8},{8,12},{12,16},{16,20},{20,24},{24,28},{28,0},{1,5},{5... | collective-permute-start | bytes 18440 | tf_op jit(solution)/shard_map/ppermute | solution.py:18
  4.9 8.2 %collective-permute-start.3 = (bf16[3,512]{1,0:T(4,128)(2,1)S(1)}, bf16[3,512]{1,0:T(4,128)(2,1)S(1)}, u32[]{:S(2)}, u32[]{:S(2)}) collective-permute-start(bf16[3,512]{1,0:T(4,128)(2,1)S(1)} %get-tuple-element.12), channel_id=1, source_target_pairs={{4,0},{8,4},{12,8},{16,12},{20,16},{24,20},{28,24},{0,28},{5,1},{9... | collective-permute-start | bytes 9224 | tf_op jit(solution)/shard_map/ppermute | solution.py:19
  7.5 6.2 %collective-permute-start.2 = (bf16[3,512]{1,0:T(4,128)(2,1)S(1)}, bf16[3,512]{1,0:T(4,128)(2,1)S(1)}, u32[]{:S(2)}, u32[]{:S(2)}) collective-permute-start(bf16[3,512]{1,0:T(4,128)(2,1)S(1)} %get-tuple-element.11), channel_id=1, source_target_pairs={{0,4},{4,8},{8,12},{12,16},{16,20},{20,24},{24,28},{28,0},{1,5},{5... | collective-permute-start | bytes 9224 | tf_op jit(solution)/shard_map/ppermute | solution.py:18
  18.1 2.0 %collective-permute-start.4 = (f32[1032,128]{1,0:T(8,128)S(1)}, f32[1032,128]{1,0:T(8,128)S(1)}, u32[]{:S(2)}, u32[]{:S(2)}) collective-permute-start(f32[1032,128]{1,0:T(8,128)S(1)} %pad_maximum_fusion.1), channel_id=1, source_target_pairs={{0,4},{4,0},{8,12},{12,8},{16,20},{20,16},{24,28},{28,24},{1,5},{5... | collective-permute-start | bytes 1585160 | tf_op jit(solution)/shard_map/ppermute | solution.py:163
  21.1 9.3 %collective-permute-start.5 = (bf16[2,8,72,128]{3,1,2,0:T(8,128)(2,1)S(1)}, bf16[2,8,72,128]{3,1,2,0:T(8,128)(2,1)S(1)}, u32[]{:S(2)}, u32[]{:S(2)}) collective-permute-start(bf16[2,8,72,128]{3,1,2,0:T(8,128)(2,1)S(1)} %fusion.39), channel_id=1, source_target_pairs={{0,8},{4,12},{8,0},{12,4},{16,24},{20,28},{24,16},{28,20},{1,9},{5... | collective-permute-start | bytes 884744 | tf_op jit(solution)/shard_map/ppermute | solution.py:104
  32.2 5.4 %collective-permute-start.6 = (bf16[1,8,72,128]{3,1,2,0:T(8,128)(2,1)S(1)}, bf16[1,8,72,128]{3,1,2,0:T(8,128)(2,1)S(1)}, u32[]{:S(2)}, u32[]{:S(2)}) collective-permute-start(bf16[1,8,72,128]{3,1,2,0:T(8,128)(2,1)S(1)} %fusion.50), channel_id=1, source_target_pairs={{0,16},{4,20},{8,24},{12,28},{16,0},{20,4},{24,8},{28,12},{1,17},{... | collective-permute-start | bytes 442376 | tf_op jit(solution)/shard_map/ppermute | solution.py:104
  37.6 0.7 %copy-start.3 = (f32[16]{0:T(128)S(1)}, f32[16]{0:T(128)}, u32[]{:S(2)}) copy-start(f32[16]{0:T(128)} %param.14) | copy-start | bytes 196
  38.0 2.0 %collective-permute-start.7 = (f32[2,8,64,128]{3,2,1,0:T(8,128)S(1)}, f32[2,8,64,128]{3,2,1,0:T(8,128)S(1)}, u32[]{:S(2)}, u32[]{:S(2)}) collective-permute-start(f32[2,8,64,128]{3,2,1,0:T(8,128)S(1)} %pad_maximum_fusion.2), channel_id=1, source_target_pairs={{0,4},{4,0},{8,12},{12,8},{16,20},{20,16},{24,28},{28,24},{1,5},{5... | collective-permute-start | bytes 1572872 | tf_op jit(solution)/shard_map/ppermute | solution.py:181
  40.4 1.0 %copy-start = (bf16[256,1024]{1,0:T(8,128)(2,1)S(1)}, bf16[256,1024]{1,0:T(8,128)(2,1)}, u32[]{:S(2)}) copy-start(bf16[256,1024]{1,0:T(8,128)(2,1)} %param.10) | copy-start | bytes 1572868
  41.0 4.5 %copy-start.2 = (f32[1024]{0:T(1024)S(1)}, f32[1024]{0:T(1024)}, u32[]{:S(2)}) copy-start(f32[1024]{0:T(1024)} %param.17) | copy-start | bytes 12292
  41.9 3.6 %collective-permute-start.8 = (f32[256]{0:T(256)S(1)}, f32[256]{0:T(256)S(1)}, u32[]{:S(2)}, u32[]{:S(2)}) collective-permute-start(f32[256]{0:T(256)S(1)} %get-tuple-element.13), channel_id=1, source_target_pairs={{0,1},{1,0},{2,3},{3,2},{4,5},{5,4},{6,7},{7,6},{8,9},{9,8},{10,11... | collective-permute-start | bytes 3080 | tf_op jit(solution)/shard_map/ppermute | solution.py:25

commit v15 on v13

--- a/solution.py
+++ b/solution.py
@@ -158,7 +158,7 @@
 
     theirs = 1 - core
     sent = pack(
-        (part(first_loc, theirs), part(second_loc, theirs)), (part(e1, theirs), part(e2, theirs)), jnp.float32
+        (part(first_loc, theirs), part(second_loc, theirs)), (part(e1, theirs), part(e2, theirs)), LINK
     )
     got = lax.ppermute(sent, "seq", pairs)
     (p1, p2), (q1, q2) = unpack(got, 2, (half, *first_loc.shape[1:]))

time: 43.7 us -> 43.2 us (0.989)
  no operation moved by 1% of the time
where the time goes in v15:
time: 43.2 us; the launch traced here: 42.6 us
  waiting for transfers between devices  14.1 us (33%)
  starting transfers between devices  10.1 us (23%)
  local copies, waits for them, and re-layouts  8.44 us (20%)
  other arithmetic  6.75 us (16%)
  matrix products  2.63 us (6%)
  between operations  0.6 us (1%)
    ppermute x2, waiting for transfers between devices, butterfly_states(): got, got_e = from_link(lax.ppermute(msg, 'seq', pairs), rows)  11.9 us
    ppermute x2, starting transfers between devices, exchange_rims(): high = lax.ppermute(heads, axis, backward)  3.62 us
    ppermute x2, starting transfers between devices, butterfly_states(): got, got_e = from_link(lax.ppermute(msg, 'seq', pairs), rows)  3.4 us
    unnamed x16, local copies, waits for them, and re-layouts  3.31 us
    ppermute x1, waiting for transfers between devices, partner(): lax.ppermute(array, axis, [(i, i ^ 1 << stride) for i in range(lax.axis_s...  1.99 us
    ppermute x1, starting transfers between devices, partner(): lax.ppermute(array, axis, [(i, i ^ 1 << stride) for i in range(lax.axis_s...  1.64 us
    slice x2, local copies, waits for them, and re-layouts, on_device(): heads = (inner_rows[tokens - rim_rows:], input_proj[tokens - rim_rows:])  1.53 us
    dot_general x2, matrix products, local_block(): jnp.einsum('hts,shp->thp', weights, inner_conv, preferred_element_type=jn...  1.12 us
  transfers between devices with their start and end apart: 9, of which 5 were waited for; matrix products, arithmetic and copies ran while one was open for 13% of the time, Pallas kernels for 0%

profile of v15, /device:TPU:0, one launch (start us, length us, event | category | flops | bytes accessed | tf_op | source)
XLA Modules:
  0.0 42.6 jit_solution(9556923187732361033)
XLA Ops:
  0.0 0.8 %fusion.101 = (bf16[3,1024]{1,0:T(4,128)(2,1)S(1)}, bf16[3,1024]{1,0:T(4,128)(2,1)S(1)}) fusion(bf16[256,1024]{1,0:T(8,128)(2,1)} %param.9), kind=kLoop, calls=%fused_computation.221 | loop fusion | bytes 24576 | tf_op jit(solution)/shard_map/slice | solution.py:216
  0.8 0.7 %fusion.104 = (bf16[3,512]{1,0:T(4,128)(2,1)S(1)}, bf16[3,512]{1,0:T(4,128)(2,1)S(1)}) fusion(bf16[256,512]{1,0:T(8,128)(2,1)} %param.11), kind=kLoop, calls=%fused_computation.224 | loop fusion | bytes 12288 | tf_op jit(solution)/shard_map/slice | solution.py:216
  1.5 0.5 %collective-permute-start.1 = (bf16[3,512]{1,0:T(4,128)(2,1)S(1)}, bf16[3,512]{1,0:T(4,128)(2,1)S(1)}, u32[]{:S(2)}, u32[]{:S(2)}) collective-permute-start(bf16[3,512]{1,0:T(4,128)(2,1)S(1)} %get-tuple-element.10), channel_id=1, source_target_pairs={{0,4},{4,8},{8,12},{12,16},{16,20},{20,24},{24,28},{28,0},{1,5},{5... | collective-permute-start | bytes 9224 | tf_op jit(solution)/shard_map/ppermute | solution.py:18
  2.0 2.9 %collective-permute-start.3 = (bf16[3,512]{1,0:T(4,128)(2,1)S(1)}, bf16[3,512]{1,0:T(4,128)(2,1)S(1)}, u32[]{:S(2)}, u32[]{:S(2)}) collective-permute-start(bf16[3,512]{1,0:T(4,128)(2,1)S(1)} %get-tuple-element.12), channel_id=1, source_target_pairs={{4,0},{8,4},{12,8},{16,12},{20,16},{24,20},{28,24},{0,28},{5,1},{9... | collective-permute-start | bytes 9224 | tf_op jit(solution)/shard_map/ppermute | solution.py:19
  5.0 0.7 %collective-permute-start.2 = (bf16[3,1024]{1,0:T(4,128)(2,1)S(1)}, bf16[3,1024]{1,0:T(4,128)(2,1)S(1)}, u32[]{:S(2)}, u32[]{:S(2)}) collective-permute-start(bf16[3,1024]{1,0:T(4,128)(2,1)S(1)} %get-tuple-element.11), channel_id=1, source_target_pairs={{4,0},{8,4},{12,8},{16,12},{20,16},{24,20},{28,24},{0,28},{5,1},{9... | collective-permute-start | bytes 18440 | tf_op jit(solution)/shard_map/ppermute | solution.py:19
  5.7 1.0 %fusion.103 = (bf16[128,512]{1,0:T(8,128)(2,1)S(1)}, bf16[128,512]{1,0:T(8,128)(2,1)S(1)}) fusion(bf16[256,512]{1,0:T(8,128)(2,1)} %param.11), kind=kLoop, calls=%fused_computation.223 | loop fusion | bytes 524288 | tf_op jit(solution)/shard_map/slice | solution.py:259
  6.7 0.7 %copy-done.2 = f32[256,16]{0,1:T(8,128)S(1)} copy-done((f32[256,16]{0,1:T(8,128)S(1)}, f32[256,16]{0,1:T(8,128)}, u32[]{:S(2)}) %copy-start.2) | copy-done | bytes 16408
  7.4 0.6 %copy-done.6 = f32[16]{0:T(128)S(1)} copy-done((f32[16]{0:T(128)S(1)}, f32[16]{0:T(128)}, u32[]{:S(2)}) %copy-start.6) | copy-done | bytes 88
  8.2 0.2 reduce_window_sum.18
  8.4 0.1 copy.87
  8.5 0.2 reduce_window_sum.17
  9.0 0.6 %copy-done.4 = f32[4,512]{1,0:T(4,128)S(1)} copy-done((f32[4,512]{1,0:T(4,128)S(1)}, f32[4,512]{1,0:T(4,128)}, u32[]{:S(2)}) %copy-start.4) | copy-done | bytes 8216
  9.8 0.7 %broadcast_select_fusion.2 = bf16[3,512]{1,0:T(4,128)(2,1)S(1)} fusion(bf16[3,512]{1,0:T(4,128)(2,1)S(1)} %collective-permute-done.3, pred[]{:T(512)S(6)} %eq.40, bf16[256,512]{1,0:T(8,128)(2,1)} %param.11), kind=kLoop, calls=%fused_computation.174 | loop fusion | flops 1536 | bytes 9217 | tf_op jit(solution)/shard_map/jit(_where)/select_n | solution.py:218
  10.5 0.3 multiply_convert_fusion.8
  11.1 0.6 %multiply_convert_fusion.6 = (bf16[128,1024]{1,0:T(8,128)(2,1)S(1)}, bf16[128,1024]{1,0:T(8,128)(2,1)S(1)}) fusion(f32[131,1024]{1,0:T(8,128)S(1)} %maximum_convert_fusion, f32[1024]{0:T(1024)S(1)} %bitcast.147, f32[1024]{0:T(1024)S(1)} %bitcast.148, f32[1024]{0:T(1024)S(1)} %bitcast.146, f32[1024]{0:T(1024)S(1)} %bitcast.145, ...), kind=kLoop, calls=%fused_computation.64 | loop fusion | flops 3145728 | bytes 4734976 | tf_op jit(solution)/shard_map/convert_element_type | solution.py:227
  11.7 0.2 copy.86
  11.9 0.2 copy.92
  12.1 0.2 fusion.47
  12.3 0.2 fusion.45
  12.6 0.8 %collective-permute-start.4 = (bf16[1032,128]{1,0:T(8,128)(2,1)S(1)}, bf16[1032,128]{1,0:T(8,128)(2,1)S(1)}, u32[]{:S(2)}, u32[]{:S(2)}) collective-permute-start(bf16[1032,128]{1,0:T(8,128)(2,1)S(1)} %pad_maximum_fusion.6), channel_id=1, source_target_pairs={{0,4},{4,0},{8,12},{12,8},{16,20},{20,16},{24,28},{28,24},{1,5},{5... | collective-permute-start | bytes 792584 | tf_op jit(solution)/shard_map/ppermute | solution.py:163
  13.5 0.6 %slice.280 = pred[1]{0:T(512)(128)(4,1)} slice(pred[72]{0:T(512)(128)(4,1)S(1)} %iota_compare_fusion.4), slice={[64:65]} | slice | bytes 2 | tf_op jit(solution)/shard_map/slice | solution.py:82
  14.5 0.2 collective-permute-done.4
  14.8 0.3 fusion.55
  15.2 0.3 multiply_add_fusion
  15.6 0.1 fusion.39
  15.7 2.5 %collective-permute-start.5 = (bf16[2,8,72,128]{3,1,2,0:T(8,128)(2,1)S(1)}, bf16[2,8,72,128]{3,1,2,0:T(8,128)(2,1)S(1)}, u32[]{:S(2)}, u32[]{:S(2)}) collective-permute-start(bf16[2,8,72,128]{3,1,2,0:T(8,128)(2,1)S(1)} %fusion.39), channel_id=1, source_target_pairs={{0,8},{4,12},{8,0},{12,4},{16,24},{20,28},{24,16},{28,20},{1,9},{5... | collective-permute-start | bytes 884744 | tf_op jit(solution)/shard_map/ppermute | solution.py:104
  18.2 0.1 fusion.74
  18.4 0.1 fusion.69
  18.5 7.2 %collective-permute-done.5 = bf16[2,8,72,128]{3,1,2,0:T(8,128)(2,1)S(1)} collective-permute-done((bf16[2,8,72,128]{3,1,2,0:T(8,128)(2,1)S(1)}, bf16[2,8,72,128]{3,1,2,0:T(8,128)(2,1)S(1)}, u32[]{:S(2)}, u32[]{:S(2)}) %collective-permute-start.5) | collective-permute-done | bytes 294944 | tf_op jit(solution)/shard_map/ppermute | solution.py:104
  25.9 0.2 fusion.42
  26.1 0.2 copy_select_fusion
  26.3 0.7 %fusion.79 = (f32[8,128]{1,0:T(8,128)S(1)}, f32[8,1,128]{2,0,1:T(8,128)S(1)}) fusion(f32[8,1,128]{2,0,1:T(8,128)S(1)} %bitcast.141, pred[]{:T(512)S(6)} %eq.36, f32[8,128]{1,0:T(8,128)S(1)} %get-tuple-element.56, f32[8,128]{1,0:T(8,128)S(1)} %get-tuple-element.59, f32[8,72,128]{2,0,1:T(8,128)S(1)} %slice_bitcast_fusion, f32[8]{0:T(128)S(1)} %get-tuple-element.72, ...), kind=kLoop, calls=%fused_computation.163 | loop fusion | flops 9216 | bytes 319523 | tf_op jit(solution)/shard_map/jit(_where)/broadcast_in_dim | solution.py:93
  27.2 0.3 fusion.62
  27.5 0.9 %collective-permute-start.6 = (bf16[1,8,72,128]{3,1,2,0:T(8,128)(2,1)S(1)}, bf16[1,8,72,128]{3,1,2,0:T(8,128)(2,1)S(1)}, u32[]{:S(2)}, u32[]{:S(2)}) collective-permute-start(bf16[1,8,72,128]{3,1,2,0:T(8,128)(2,1)S(1)} %fusion.62), channel_id=1, source_target_pairs={{0,16},{4,20},{8,24},{12,28},{16,0},{20,4},{24,8},{28,12},{1,17},{... | collective-permute-start | bytes 442376 | tf_op jit(solution)/shard_map/ppermute | solution.py:104
  28.4 4.6 %collective-permute-done.6 = bf16[1,8,72,128]{3,1,2,0:T(8,128)(2,1)S(1)} collective-permute-done((bf16[1,8,72,128]{3,1,2,0:T(8,128)(2,1)S(1)}, bf16[1,8,72,128]{3,1,2,0:T(8,128)(2,1)S(1)}, u32[]{:S(2)}, u32[]{:S(2)}) %collective-permute-start.6) | collective-permute-done | bytes 147488 | tf_op jit(solution)/shard_map/ppermute | solution.py:104
  33.2 0.3 fusion.63
  33.6 0.6 %copy-done.7 = f32[16]{0:T(128)S(1)} copy-done((f32[16]{0:T(128)S(1)}, f32[16]{0:T(128)}, u32[]{:S(2)}) %copy-start.7) | copy-done | bytes 88
  34.1 0.6 %fusion.2 = f32[128,16,64]{0,2,1:T(8,128)S(1)} fusion(bf16[128,16,64]{0,2,1:T(8,128)(2,1)S(1)} %bitcast.136, f32[16,128]{1,0:T(8,128)S(1)} %get-tuple-element.45, f32[16,128]{1,0:T(8,128)S(1)} %copy.88, f32[128,128]{1,0:T(8,128)S(1)} %fusion.74, pred[128,128]{1,0:T(8,128)(4,1)S(1)} %iota_compare_fusion, f32[16]{0:T(128)S(1)} %copy-done.7), kind=kOutput, calls=%fused_computation.8 | convolution fusion | flops 35520512 | bytes 884800 | tf_op jit(solution)/shard_map/hts,shp->thp/dot_general | solution.py:240
  34.7 0.6 %fusion.3 = f32[128,16,64]{0,2,1:T(8,128)S(1)} fusion(bf16[128,16,64]{0,2,1:T(8,128)(2,1)S(1)} %bitcast.134, f32[16,128]{1,0:T(8,128)S(1)} %get-tuple-element.48, f32[16,128]{1,0:T(8,128)S(1)} %copy.114, f32[128,128]{1,0:T(8,128)S(1)} %fusion.69, pred[128,128]{1,0:T(8,128)(4,1)S(1)} %iota_compare_fusion, f32[16]{0:T(128)S(1)} %copy-done.7), kind=kOutput, calls=%fused_computation.9 | convolution fusion | flops 35520512 | bytes 884800 | tf_op jit(solution)/shard_map/hts,shp->thp/dot_general | solution.py:240
  35.5 0.4 fusion.1
  35.9 0.2 copy.118
  36.1 0.4 fusion
  36.5 0.2 copy.119
  36.7 0.8 %copy-done.1 = bf16[256,1024]{1,0:T(8,128)(2,1)S(1)} copy-done((bf16[256,1024]{1,0:T(8,128)(2,1)S(1)}, bf16[256,1024]{1,0:T(8,128)(2,1)}, u32[]{:S(2)}) %copy-start.1) | copy-done | bytes 524312
  37.6 0.4 multiply_reduce_fusion
  38.0 1.6 %collective-permute-start.8 = (f32[256]{0:T(256)S(1)}, f32[256]{0:T(256)S(1)}, u32[]{:S(2)}, u32[]{:S(2)}) collective-permute-start(f32[256]{0:T(256)S(1)} %get-tuple-element.13), channel_id=1, source_target_pairs={{0,1},{1,0},{2,3},{3,2},{4,5},{5,4},{6,7},{7,6},{8,9},{9,8},{10,11... | collective-permute-start | bytes 3080 | tf_op jit(solution)/shard_map/ppermute | solution.py:25
  39.6 2.0 %collective-permute-done.8 = f32[256]{0:T(256)S(1)} collective-permute-done((f32[256]{0:T(256)S(1)}, f32[256]{0:T(256)S(1)}, u32[]{:S(2)}, u32[]{:S(2)}) %collective-permute-start.8) | collective-permute-done | bytes 1056 | tf_op jit(solution)/shard_map/ppermute | solution.py:25
  41.6 1.0 %multiply_convert_fusion = bf16[256,1024]{1,0:T(8,128)(2,1)} fusion(f32[256,1024]{1,0:T(8,128)S(1)} %get-tuple-element.14, f32[1024]{0:T(1024)S(1)} %copy-done.5, f32[256]{0:T(256)S(1)} %add_rsqrt_fusion), kind=kLoop, calls=%fused_computation.14 | loop fusion | flops 786432 | bytes 1577984 | tf_op jit(solution)/shard_map/convert_element_type | solution.py:279
  (83 shorter events, 2.4 us)
Async XLA Ops:
  0.0 6.6 %copy-start = (bf16[256,1024]{1,0:T(8,128)(2,1)S(1)}, bf16[256,1024]{1,0:T(8,128)(2,1)}, u32[]{:S(2)}) copy-start(bf16[256,1024]{1,0:T(8,128)(2,1)} %param.9) | copy-start | bytes 1572868
  1.5 8.2 %collective-permute-start.1 = (bf16[3,512]{1,0:T(4,128)(2,1)S(1)}, bf16[3,512]{1,0:T(4,128)(2,1)S(1)}, u32[]{:S(2)}, u32[]{:S(2)}) collective-permute-start(bf16[3,512]{1,0:T(4,128)(2,1)S(1)} %get-tuple-element.10), channel_id=1, source_target_pairs={{0,4},{4,8},{8,12},{12,16},{16,20},{20,24},{24,28},{28,0},{1,5},{5... | collective-permute-start | bytes 9224 | tf_op jit(solution)/shard_map/ppermute | solution.py:18
  2.0 7.8 %collective-permute-start.3 = (bf16[3,512]{1,0:T(4,128)(2,1)S(1)}, bf16[3,512]{1,0:T(4,128)(2,1)S(1)}, u32[]{:S(2)}, u32[]{:S(2)}) collective-permute-start(bf16[3,512]{1,0:T(4,128)(2,1)S(1)} %get-tuple-element.12), channel_id=1, source_target_pairs={{4,0},{8,4},{12,8},{16,12},{20,16},{24,20},{28,24},{0,28},{5,1},{9... | collective-permute-start | bytes 9224 | tf_op jit(solution)/shard_map/ppermute | solution.py:19
  5.0 5.9 %collective-permute-start.2 = (bf16[3,1024]{1,0:T(4,128)(2,1)S(1)}, bf16[3,1024]{1,0:T(4,128)(2,1)S(1)}, u32[]{:S(2)}, u32[]{:S(2)}) collective-permute-start(bf16[3,1024]{1,0:T(4,128)(2,1)S(1)} %get-tuple-element.11), channel_id=1, source_target_pairs={{4,0},{8,4},{12,8},{16,12},{20,16},{24,20},{28,24},{0,28},{5,1},{9... | collective-permute-start | bytes 18440 | tf_op jit(solution)/shard_map/ppermute | solution.py:19
  5.6 5.3 %collective-permute-start = (bf16[3,1024]{1,0:T(4,128)(2,1)S(1)}, bf16[3,1024]{1,0:T(4,128)(2,1)S(1)}, u32[]{:S(2)}, u32[]{:S(2)}) collective-permute-start(bf16[3,1024]{1,0:T(4,128)(2,1)S(1)} %get-tuple-element.9), channel_id=1, source_target_pairs={{0,4},{4,8},{8,12},{12,16},{16,20},{20,24},{24,28},{28,0},{1,5},{5... | collective-permute-start | bytes 18440 | tf_op jit(solution)/shard_map/ppermute | solution.py:18
  6.7 0.7 %copy-start.2 = (f32[256,16]{0,1:T(8,128)S(1)}, f32[256,16]{0,1:T(8,128)}, u32[]{:S(2)}) copy-start(f32[256,16]{0,1:T(8,128)} %param.12) | copy-start | bytes 49156
  7.4 0.7 %copy-start.6 = (f32[16]{0:T(128)S(1)}, f32[16]{0:T(128)}, u32[]{:S(2)}) copy-start(f32[16]{0:T(128)} %param.13) | copy-start | bytes 196
  8.8 0.7 %copy-start.4 = (f32[4,512]{1,0:T(4,128)S(1)}, f32[4,512]{1,0:T(4,128)}, u32[]{:S(2)}) copy-start(f32[4,512]{1,0:T(4,128)} %param.16) | copy-start | bytes 24580
  8.8 0.7 %copy-start.3 = (f32[4,1024]{1,0:T(4,128)S(1)}, f32[4,1024]{1,0:T(4,128)}, u32[]{:S(2)}) copy-start(f32[4,1024]{1,0:T(4,128)} %param.15) | copy-start | bytes 49156
  12.6 2.0 %collective-permute-start.4 = (bf16[1032,128]{1,0:T(8,128)(2,1)S(1)}, bf16[1032,128]{1,0:T(8,128)(2,1)S(1)}, u32[]{:S(2)}, u32[]{:S(2)}) collective-permute-start(bf16[1032,128]{1,0:T(8,128)(2,1)S(1)} %pad_maximum_fusion.6), channel_id=1, source_target_pairs={{0,4},{4,0},{8,12},{12,8},{16,20},{20,16},{24,28},{28,24},{1,5},{5... | collective-permute-start | bytes 792584 | tf_op jit(solution)/shard_map/ppermute | solution.py:163
  15.7 10.0 %collective-permute-start.5 = (bf16[2,8,72,128]{3,1,2,0:T(8,128)(2,1)S(1)}, bf16[2,8,72,128]{3,1,2,0:T(8,128)(2,1)S(1)}, u32[]{:S(2)}, u32[]{:S(2)}) collective-permute-start(bf16[2,8,72,128]{3,1,2,0:T(8,128)(2,1)S(1)} %fusion.39), channel_id=1, source_target_pairs={{0,8},{4,12},{8,0},{12,4},{16,24},{20,28},{24,16},{28,20},{1,9},{5... | collective-permute-start | bytes 884744 | tf_op jit(solution)/shard_map/ppermute | solution.py:104
  27.5 5.6 %collective-permute-start.6 = (bf16[1,8,72,128]{3,1,2,0:T(8,128)(2,1)S(1)}, bf16[1,8,72,128]{3,1,2,0:T(8,128)(2,1)S(1)}, u32[]{:S(2)}, u32[]{:S(2)}) collective-permute-start(bf16[1,8,72,128]{3,1,2,0:T(8,128)(2,1)S(1)} %fusion.62), channel_id=1, source_target_pairs={{0,16},{4,20},{8,24},{12,28},{16,0},{20,4},{24,8},{28,12},{1,17},{... | collective-permute-start | bytes 442376 | tf_op jit(solution)/shard_map/ppermute | solution.py:104
  33.5 0.7 %copy-start.7 = (f32[16]{0:T(128)S(1)}, f32[16]{0:T(128)}, u32[]{:S(2)}) copy-start(f32[16]{0:T(128)} %param.14) | copy-start | bytes 196
  33.5 2.0 %collective-permute-start.7 = (f32[2,8,64,128]{3,2,1,0:T(8,128)S(1)}, f32[2,8,64,128]{3,2,1,0:T(8,128)S(1)}, u32[]{:S(2)}, u32[]{:S(2)}) collective-permute-start(f32[2,8,64,128]{3,2,1,0:T(8,128)S(1)} %pad_maximum_fusion.1), channel_id=1, source_target_pairs={{0,4},{4,0},{8,12},{12,8},{16,20},{20,16},{24,28},{28,24},{1,5},{5... | collective-permute-start | bytes 1572872 | tf_op jit(solution)/shard_map/ppermute | solution.py:181
  36.5 1.0 %copy-start.1 = (bf16[256,1024]{1,0:T(8,128)(2,1)S(1)}, bf16[256,1024]{1,0:T(8,128)(2,1)}, u32[]{:S(2)}) copy-start(bf16[256,1024]{1,0:T(8,128)(2,1)} %param.10) | copy-start | bytes 1572868
  38.0 3.7 %copy-start.5 = (f32[1024]{0:T(1024)S(1)}, f32[1024]{0:T(1024)}, u32[]{:S(2)}) copy-start(f32[1024]{0:T(1024)} %param.17) | copy-start | bytes 12292
  38.0 3.6 %collective-permute-start.8 = (f32[256]{0:T(256)S(1)}, f32[256]{0:T(256)S(1)}, u32[]{:S(2)}, u32[]{:S(2)}) collective-permute-start(f32[256]{0:T(256)S(1)} %get-tuple-element.13), channel_id=1, source_target_pairs={{0,1},{1,0},{2,3},{3,2},{4,5},{5,4},{6,7},{7,6},{8,9},{9,8},{10,11... | collective-permute-start | bytes 3080 | tf_op jit(solution)/shard_map/ppermute | solution.py:25
